TPU v7x, 32 devices: a whole 2x2x4 slice. The times are simulated.
32 devices in a mesh: sec: 4 (over z), blk: 8 (over y, x, core).
Axes of the slice: x: 2, y: 2, z: 4, core: 2. Of those that a mesh axis runs over, the one named last changes fastest.
Arguments:
- receptor: bfloat16 [16384, 1024], P(('sec', 'blk')), may hold values from -6 to 6
- poses: bfloat16 [4096, 1024], P(('sec', 'blk')), may hold values from -6 to 6
- pairs: int32 [8192, 2], P(('sec', 'blk')), may hold values from 0 to 127
- block_complex: int32 [32], replicated, may hold values from 0 to 15, never falling along the last dimension, each value on 1 to 4 neighbouring positions
- w_key: bfloat16 [1024, 1024], P('blk'), may hold values from -0.1875 to 0.1875
- w_value: bfloat16 [1024, 1024], P('blk'), may hold values from -0.1875 to 0.1875
- w_query: bfloat16 [1024, 1024], replicated, may hold values from -0.1875 to 0.1875
- score_weight: float32 [1024], replicated, may hold values from -24 to 24
Outputs:
- pair_loss: float32 [8192], P(('sec', 'blk'))
- pose_grad: bfloat16 [4096, 1024], P(('sec', 'blk'))
- receptor_grad: bfloat16 [16384, 1024], P(('sec', 'blk'))
Inputs may be any that keep to these rules, and one draw needn't show every extreme that they name: `block_complex`: never falls from one block to the next; each complex holds 1 to 4 consecutive blocks, and some complex holds exactly 4. `pairs`: indices among the 128 poses beside the pair's block.
All inputs are finite; a program needn't handle non-finite values.
Results may differ from a plain program's by a relative error of at most 0.014.
Values may be sent and summed in bfloat16 or wider, within the bound.
No kernel may reach another device: no remote copies, remote signals or barrier semaphores. Data moves between devices by JAX's collectives and lax.ppermute only.
A program may use at most 64 MiB of HBM per device.

v0:
```python
import jax
import jax.numpy as jnp
from jax import lax
from jax.sharding import PartitionSpec as P

H = 16
DH = 64
MOSTB = 4


highest = lax.Precision.HIGHEST


def from_behind(value, axis, steps):
    count = lax.axis_size(axis)
    initial, last = (max(0, -steps), min(count, count - steps))
    return lax.ppermute(value, axis, [(source, source + steps) for source in range(initial, last)])


def features(values):
    return jnp.where(values > 0, values + 1.0, jnp.exp(jnp.minimum(values, 0.0)))


def slope(values):
    return jnp.where(values > 0, jnp.ones_like(values), jnp.exp(jnp.minimum(values, 0.0)))


def local_state(key_feat, val_round):
    rows = key_feat.shape[0]
    key_heads = key_feat.reshape(rows, H, DH)
    val_heads = val_round.reshape(rows, H, DH)
    outer = jnp.einsum(
        "thd,the->dhe", key_heads, val_heads, preferred_element_type=jnp.float32
    ).reshape(DH, H * DH)
    norm_row = jnp.sum(key_feat, axis=0, dtype=jnp.float32)
    return jnp.concatenate([outer, norm_row[None, :]], axis=0)


def complex_total(own, block_complex):
    position = lax.axis_index(("sec", "blk"))
    blocks = block_complex.shape[0]
    mine = jnp.take(block_complex, position)
    total = own
    for reach in range(1, MOSTB):
        lower = from_behind(own.astype(jnp.bfloat16), ("sec", "blk"), reach).astype(own.dtype)
        upper = from_behind(own.astype(jnp.bfloat16), ("sec", "blk"), -reach).astype(own.dtype)
        below = jnp.take(block_complex, jnp.maximum(position - reach, 0))
        above = jnp.take(block_complex, jnp.minimum(position + reach, blocks - 1))
        take_lower = jnp.logical_and(position - reach >= 0, below == mine)
        take_upper = jnp.logical_and(position + reach < blocks, above == mine)
        total = total + jnp.where(take_lower, lower, 0.0) + jnp.where(take_upper, upper, 0.0)
    return total


def pose_side(pose_rows, pair_rows, state, w_query, score_weight):
    count = pose_rows.shape[0]
    queries = jnp.dot(pose_rows, w_query, preferred_element_type=jnp.float32)
    query_heads = features(queries).reshape(count, H, DH)
    state_heads = state[:DH].reshape(DH, H, DH)
    norm_heads = state[DH].reshape(H, DH)
    numer = jnp.einsum("phd,dhe->phe", query_heads, state_heads, precision=highest)
    denom = jnp.sum(query_heads * norm_heads[None], axis=2)
    attended = numer / denom[:, :, None]
    weight_heads = score_weight.reshape(H, DH)
    scores = jnp.sum(attended * weight_heads[None], axis=(1, 2))
    better = jnp.take(scores, pair_rows[:, 0])
    worse = jnp.take(scores, pair_rows[:, 1])
    delta = worse - better
    pair_loss = jax.nn.softplus(delta)
    push = jax.nn.sigmoid(delta)
    slots = lax.broadcasted_iota(jnp.int32, (pair_rows.shape[0], count), 1)
    score_grad = jnp.sum(
        jnp.where(slots == pair_rows[:, 1:2], push[:, None], 0.0)
        - jnp.where(slots == pair_rows[:, 0:1], push[:, None], 0.0),
        axis=0,
    )
    attended_grad = score_grad[:, None, None] * weight_heads[None]
    numer_grad = attended_grad / denom[:, :, None]
    denom_grad = -jnp.sum(attended_grad * attended, axis=2) / denom
    outer_grad = jnp.einsum("phd,phe->dhe", query_heads, numer_grad, precision=highest).reshape(
        DH, H * DH
    )
    norm_grad = jnp.sum(query_heads * denom_grad[:, :, None], axis=0).reshape(H * DH)
    pose_state = jnp.concatenate([outer_grad, norm_grad[None, :]], axis=0)
    feat_grad = (
        jnp.einsum("phe,dhe->phd", numer_grad, state_heads, precision=highest)
        + denom_grad[:, :, None] * norm_heads[None]
    )
    query_grad = (feat_grad.reshape(count, H * DH) * slope(queries)).astype(jnp.bfloat16)
    pose_grad = lax.dot_general(
        query_grad, w_query, (((1,), (1,)), ((), ())), preferred_element_type=jnp.float32
    )
    return (pair_loss, pose_grad.astype(jnp.bfloat16), pose_state)


def shards(receptor, poses, pairs, block_complex, w_key, w_value, w_query, score_weight):
    rows = receptor.shape[0]
    width = receptor.shape[1]
    contract = (((1,), (1,)), ((), ()))
    full_key, full_value = (
        lax.all_gather(w_key, "blk", axis=0, tiled=True),
        lax.all_gather(w_value, "blk", axis=0, tiled=True),
    )
    keys = jnp.dot(receptor, full_key, preferred_element_type=jnp.float32)
    values = jnp.dot(receptor, full_value, preferred_element_type=jnp.float32)
    key_feat = features(keys).astype(jnp.bfloat16)
    val_round = values.astype(jnp.bfloat16)
    state = complex_total(local_state(key_feat, val_round), block_complex)
    pair_loss, pose_grad, pose_state = pose_side(poses, pairs, state, w_query, score_weight)
    state_grad = complex_total(pose_state, block_complex).astype(jnp.bfloat16)
    key_heads = key_feat.reshape(rows, H, DH)
    val_heads = val_round.reshape(rows, H, DH)
    grad_heads = state_grad[:DH].reshape(DH, H, DH)
    norm_back = state_grad[DH].astype(jnp.float32).reshape(H, DH)
    feat_grad = (
        jnp.einsum("the,dhe->thd", val_heads, grad_heads, preferred_element_type=jnp.float32)
        + norm_back[None]
    )
    key_grad = (feat_grad.reshape(rows, width) * slope(keys)).astype(jnp.bfloat16)
    value_grad = (
        jnp.einsum("thd,dhe->the", key_heads, grad_heads, preferred_element_type=jnp.float32)
        .reshape(rows, width)
        .astype(jnp.bfloat16)
    )
    total = lax.dot_general(key_grad, full_key, contract, preferred_element_type=jnp.float32)
    total = total + lax.dot_general(
        value_grad, full_value, contract, preferred_element_type=jnp.float32
    )
    return (pair_loss, pose_grad, total.astype(jnp.bfloat16))


def solution(mesh):
    placed = (
        P(("sec", "blk"), None),
        P(("sec", "blk"), None),
        P(("sec", "blk"), None),
        P(),
        P("blk", None),
        P("blk", None),
        P(),
        P(),
    )
    return jax.shard_map(
        shards,
        mesh=mesh,
        in_specs=placed,
        out_specs=(P(("sec", "blk")), P(("sec", "blk"), None), P(("sec", "blk"), None)),
        check_vma=False,
    )
```

profile of v0, /device:TPU:16, one launch (start us, length us, event | category | flops | bytes accessed | tf_op | source)
XLA Modules:
  0.0 189.2 jit_solution(2240963160841617710)
XLA Ops:
  8.0 0.7 all-gather.5.cloned.1.call-update
  8.7 1.3 fusion.24
  10.6 2.4 %add_select_fusion = (f32[128,1024]{1,0:T(8,128)}, f32[128,1024]{1,0:T(8,128)}) fusion(bf16[128,1024]{1,0:T(8,128)(2,1)} %param.11, bf16[1024,1024]{1,0:T(8,128)(2,1)S(1)} %copy-done), kind=kOutput, calls=%fused_computation.27 | convolution fusion | flops 268959744 | bytes 3407872 | tf_op jit(solution)/shard_map/dot_general | solution.py:57
  13.0 25.9 %all-gather.3.cloned.1.call-done = bf16[1024,1024]{1,0:T(8,128)(2,1)} async-done(((bf16[128,1024]{1,0:T(8,128)(2,1)}), bf16[1024,1024]{1,0:T(8,128)(2,1)}) %all-gather.3.cloned.1.call-update) | async-done | bytes 2097168 | tf_op jit(solution)/shard_map/all_gather | solution.py:102
  38.9 4.1 %convolution_convert_fusion.1 = bf16[512,1024]{1,0:T(8,128)(2,1)} fusion(bf16[512,1024]{1,0:T(8,128)(2,1)} %param.10, bf16[1024,1024]{1,0:T(8,128)(2,1)} %all-gather.3.cloned.1.call-done), kind=kOutput, calls=%fused_computation.9 | convolution fusion | flops 1074266112 | bytes 4194304 | tf_op jit(solution)/shard_map/dot_general | solution.py:105
  43.0 1.5 copy.35
  44.5 24.2 %all-gather.5.cloned.1.call-done = bf16[1024,1024]{1,0:T(8,128)(2,1)} async-done(((bf16[128,1024]{1,0:T(8,128)(2,1)}), bf16[1024,1024]{1,0:T(8,128)(2,1)}) %all-gather.5.cloned.1.call-update) | async-done | bytes 2097168 | tf_op jit(solution)/shard_map/all_gather | solution.py:101
  68.7 5.0 %convert_reduce_fusion = (f32[1024]{0:T(1024)S(1)}, bf16[512,1024]{1,0:T(8,128)(2,1)}, f32[512,1024]{1,0:T(8,128)}) fusion(bf16[512,1024]{1,0:T(8,128)(2,1)} %param.10, bf16[1024,1024]{1,0:T(8,128)(2,1)} %all-gather.5.cloned.1.call-done), kind=kOutput, calls=%fused_computation.4 | convolution fusion | flops 1077410816 | bytes 6295552 | tf_op jit(solution)/shard_map/dot_general | solution.py:104
  73.7 2.3 %copy.36 = bf16[512,1024]{0,1:T(8,128)(2,1)} copy(bf16[512,1024]{1,0:T(8,128)(2,1)} %get-tuple-element.84) | data formatting | bytes 2097152 | tf_op jit(solution)/shard_map/convert_element_type | solution.py:106
  76.0 2.4 %fusion.26 = f32[16,64,64]{2,1,0:T(8,128)} fusion(bf16[512,16,64]{0,2,1:T(8,128)(2,1)S(1)} %bitcast.65, bf16[512,16,64]{0,2,1:T(8,128)(2,1)} %bitcast.67), kind=kOutput, calls=%fused_computation.66 | convolution fusion | flops 67108864 | bytes 2359296 | tf_op jit(solution)/shard_map/thd,the->dhe/dot_general | solution.py:32
  78.4 1.2 copy.37
  80.3 3.1 %collective-permute-start.5 = (bf16[65,1024]{1,0:T(8,128)(2,1)}, bf16[65,1024]{1,0:T(8,128)(2,1)S(1)}, u32[]{:S(2)}, u32[]{:S(2)}) collective-permute-start(bf16[65,1024]{1,0:T(8,128)(2,1)} %fusion.16), channel_id=1, source_target_pairs={{3,0},{4,1},{5,2},{6,3},{7,4},{8,5},{9,6},{10,7},{11,8},{12,9},{13... | collective-permute-start | bytes 399368 | tf_op jit(solution)/shard_map/ppermute | solution.py:17
  84.2 2.4 %collective-permute-start.4 = (bf16[65,1024]{1,0:T(8,128)(2,1)}, bf16[65,1024]{1,0:T(8,128)(2,1)}, u32[]{:S(2)}, u32[]{:S(2)}) collective-permute-start(bf16[65,1024]{1,0:T(8,128)(2,1)} %fusion.16), channel_id=1, source_target_pairs={{0,3},{1,4},{2,5},{3,6},{4,7},{5,8},{6,9},{7,10},{8,11},{9,12},{10... | collective-permute-start | bytes 399368 | tf_op jit(solution)/shard_map/ppermute | solution.py:17
  86.6 5.1 %collective-permute-start.3 = (bf16[65,1024]{1,0:T(8,128)(2,1)}, bf16[65,1024]{1,0:T(8,128)(2,1)}, u32[]{:S(2)}, u32[]{:S(2)}) collective-permute-start(bf16[65,1024]{1,0:T(8,128)(2,1)} %fusion.16), channel_id=1, source_target_pairs={{2,0},{3,1},{4,2},{5,3},{6,4},{7,5},{8,6},{9,7},{10,8},{11,9},{12,... | collective-permute-start | bytes 399368 | tf_op jit(solution)/shard_map/ppermute | solution.py:17
  91.7 1.9 %collective-permute-start.2 = (bf16[65,1024]{1,0:T(8,128)(2,1)}, bf16[65,1024]{1,0:T(8,128)(2,1)}, u32[]{:S(2)}, u32[]{:S(2)}) collective-permute-start(bf16[65,1024]{1,0:T(8,128)(2,1)} %fusion.16), channel_id=1, source_target_pairs={{0,2},{1,3},{2,4},{3,5},{4,6},{5,7},{6,8},{7,9},{8,10},{9,11},{10,... | collective-permute-start | bytes 399368 | tf_op jit(solution)/shard_map/ppermute | solution.py:17
  93.7 4.1 %collective-permute-start.1 = (bf16[65,1024]{1,0:T(8,128)(2,1)}, bf16[65,1024]{1,0:T(8,128)(2,1)}, u32[]{:S(2)}, u32[]{:S(2)}) collective-permute-start(bf16[65,1024]{1,0:T(8,128)(2,1)} %fusion.16), channel_id=1, source_target_pairs={{1,0},{2,1},{3,2},{4,3},{5,4},{6,5},{7,6},{8,7},{9,8},{10,9},{11,1... | collective-permute-start | bytes 399368 | tf_op jit(solution)/shard_map/ppermute | solution.py:17
  97.8 1.9 %collective-permute-start = (bf16[65,1024]{1,0:T(8,128)(2,1)}, bf16[65,1024]{1,0:T(8,128)(2,1)}, u32[]{:S(2)}, u32[]{:S(2)}) collective-permute-start(bf16[65,1024]{1,0:T(8,128)(2,1)} %fusion.16), channel_id=1, source_target_pairs={{0,1},{1,2},{2,3},{3,4},{4,5},{5,6},{6,7},{7,8},{8,9},{9,10},{10,1... | collective-permute-start | bytes 399368 | tf_op jit(solution)/shard_map/ppermute | solution.py:17
  100.3 1.6 fusion.25
  106.4 1.4 mul.68
  107.8 2.0 %copy.39 = f32[128,1024]{0,1:T(8,128)} copy(f32[128,1024]{1,0:T(8,128)} %get-tuple-element.95) | data formatting | bytes 1048576 | tf_op jit(solution)/shard_map/jit(_where)/select_n | solution.py:21
  109.8 1.3 pad_clamp_fusion
  111.1 1.4 select_add_fusion
  112.7 1.0 copy.38
  113.7 1.2 multiply_reduce_fusion.2
  115.0 2.7 %multiply_reduce_fusion.1 = (f32[128]{0:T(128)S(1)}, f32[128,16,64]{0,2,1:T(8,128)}) fusion(f32[16,64]{1,0:T(8,128)} %mul.68, f32[128,16]{0,1:T(8,128)S(1)} %multiply_reduce_fusion.2, f32[64,16,64]{0,2,1:T(8,128)} %bitcast.77, f32[128,16,64]{0,2,1:T(8,128)} %bitcast.73), kind=kOutput, calls=%fused_computation.24 | convolution fusion | flops 101056384 | bytes 1323520 | tf_op jit(solution)/shard_map/phd,dhe->phe/dot_general | solution.py:61
  117.7 2.0 %gather_fusion.1 = f32[256]{0:T(256)S(1)} fusion(f32[128]{0:T(128)S(1)} %get-tuple-element.97, s32[1024]{0:T(1024)} %pad_clamp_fusion), kind=kCustom, calls=%fused_computation.1.clone | custom fusion | bytes 3072 | tf_op jit(solution)/shard_map/jit(_take)/gather | solution.py:66
  119.7 2.0 %gather_fusion = f32[256]{0:T(256)S(1)} fusion(f32[128]{0:T(128)S(1)} %get-tuple-element.97, s32[1024]{0:T(1024)} %pad_clamp_fusion.1), kind=kCustom, calls=%fused_computation.clone | custom fusion | bytes 3072 | tf_op jit(solution)/shard_map/jit(_take)/gather | solution.py:67
  122.5 2.9 %fusion.6 = f32[16,64,64]{2,1,0:T(8,128)} fusion(f32[128,16,64]{0,2,1:T(8,128)} %bitcast.74, f32[128]{0:T(128)S(1)} %subtract_reduce_fusion, f32[16,64]{1,0:T(8,128)S(1)} %copy-done.6, f32[128,16]{0,1:T(8,128)S(1)} %multiply_reduce_fusion.2), kind=kOutput, calls=%fused_computation.28 | convolution fusion | flops 100925440 | bytes 799232 | tf_op jit(solution)/shard_map/phd,phe->dhe/dot_general | solution.py:80
  125.6 2.0 %fusion = f32[128,16,64]{0,2,1:T(8,128)} fusion(f32[64,16,64]{0,2,1:T(8,128)S(1)} %bitcast.78, f32[128,16]{0,1:T(8,128)S(1)} %negate_divide_fusion, f32[128]{0:T(128)S(1)} %subtract_reduce_fusion, f32[16,64]{1,0:T(8,128)S(1)} %copy-done.6, f32[128,16]{0,1:T(8,128)S(1)} %multiply_reduce_fusion.2, f32[16,64]{1,0:T(8,128)S(1)} %mul.65), kind=kOutput, calls=%fused_computation.11 | convolution fusion | flops 101187584 | bytes 811520 | tf_op jit(solution)/shard_map/phe,dhe->phd/dot_general | solution.py:86
  127.6 1.2 copy.43
  128.8 0.9 mul.74
  129.7 2.1 %copy.42 = f32[128,1024]{1,0:T(8,128)} copy(f32[128,1024]{0,1:T(8,128)} %bitcast.75) | data formatting | bytes 1048576 | tf_op jit(solution)/shard_map/mul | solution.py:87
  131.8 1.4 multiply_reduce_fusion
  134.4 3.8 %collective-permute-start.11 = (bf16[65,1024]{1,0:T(8,128)(2,1)}, bf16[65,1024]{1,0:T(8,128)(2,1)S(1)}, u32[]{:S(2)}, u32[]{:S(2)}) collective-permute-start(bf16[65,1024]{1,0:T(8,128)(2,1)} %fusion.15), channel_id=1, source_target_pairs={{3,0},{4,1},{5,2},{6,3},{7,4},{8,5},{9,6},{10,7},{11,8},{12,9},{13... | collective-permute-start | bytes 399368 | tf_op jit(solution)/shard_map/ppermute | solution.py:17
  138.2 1.9 %collective-permute-start.10 = (bf16[65,1024]{1,0:T(8,128)(2,1)}, bf16[65,1024]{1,0:T(8,128)(2,1)}, u32[]{:S(2)}, u32[]{:S(2)}) collective-permute-start(bf16[65,1024]{1,0:T(8,128)(2,1)} %fusion.15), channel_id=1, source_target_pairs={{0,3},{1,4},{2,5},{3,6},{4,7},{5,8},{6,9},{7,10},{8,11},{9,12},{10... | collective-permute-start | bytes 399368 | tf_op jit(solution)/shard_map/ppermute | solution.py:17
  140.1 5.7 %collective-permute-start.9 = (bf16[65,1024]{1,0:T(8,128)(2,1)}, bf16[65,1024]{1,0:T(8,128)(2,1)}, u32[]{:S(2)}, u32[]{:S(2)}) collective-permute-start(bf16[65,1024]{1,0:T(8,128)(2,1)} %fusion.15), channel_id=1, source_target_pairs={{2,0},{3,1},{4,2},{5,3},{6,4},{7,5},{8,6},{9,7},{10,8},{11,9},{12,... | collective-permute-start | bytes 399368 | tf_op jit(solution)/shard_map/ppermute | solution.py:17
  145.8 1.9 %collective-permute-start.8 = (bf16[65,1024]{1,0:T(8,128)(2,1)}, bf16[65,1024]{1,0:T(8,128)(2,1)}, u32[]{:S(2)}, u32[]{:S(2)}) collective-permute-start(bf16[65,1024]{1,0:T(8,128)(2,1)} %fusion.15), channel_id=1, source_target_pairs={{0,2},{1,3},{2,4},{3,5},{4,6},{5,7},{6,8},{7,9},{8,10},{9,11},{10,... | collective-permute-start | bytes 399368 | tf_op jit(solution)/shard_map/ppermute | solution.py:17
  147.7 5.7 %collective-permute-start.7 = (bf16[65,1024]{1,0:T(8,128)(2,1)}, bf16[65,1024]{1,0:T(8,128)(2,1)}, u32[]{:S(2)}, u32[]{:S(2)}) collective-permute-start(bf16[65,1024]{1,0:T(8,128)(2,1)} %fusion.15), channel_id=1, source_target_pairs={{1,0},{2,1},{3,2},{4,3},{5,4},{6,5},{7,6},{8,7},{9,8},{10,9},{11,1... | collective-permute-start | bytes 399368 | tf_op jit(solution)/shard_map/ppermute | solution.py:17
  153.4 2.1 %copy.41 = f32[128,1024]{1,0:T(8,128)} copy(f32[128,1024]{0,1:T(8,128)} %bitcast.80) | data formatting | bytes 1048576 | tf_op jit(solution)/shard_map/reshape | solution.py:89
  155.5 2.7 %convolution_convert_fusion.2 = bf16[128,1024]{1,0:T(8,128)(2,1)} fusion(bf16[1024,1024]{1,0:T(8,128)(2,1)S(1)} %copy-done, f32[128,1024]{1,0:T(8,128)} %copy.41, f32[128,1024]{1,0:T(8,128)} %get-tuple-element.96), kind=kOutput, calls=%fused_computation.14 | convolution fusion | flops 269221888 | bytes 3407872 | tf_op jit(solution)/shard_map/dot_general | solution.py:90
  158.2 2.1 %collective-permute-start.6 = (bf16[65,1024]{1,0:T(8,128)(2,1)}, bf16[65,1024]{1,0:T(8,128)(2,1)S(1)}, u32[]{:S(2)}, u32[]{:S(2)}) collective-permute-start(bf16[65,1024]{1,0:T(8,128)(2,1)} %fusion.15), channel_id=1, source_target_pairs={{0,1},{1,2},{2,3},{3,4},{4,5},{5,6},{6,7},{7,8},{8,9},{9,10},{10,1... | collective-permute-start | bytes 399368 | tf_op jit(solution)/shard_map/ppermute | solution.py:17
  161.0 5.7 %collective-permute-done.6 = bf16[65,1024]{1,0:T(8,128)(2,1)S(1)} collective-permute-done((bf16[65,1024]{1,0:T(8,128)(2,1)}, bf16[65,1024]{1,0:T(8,128)(2,1)S(1)}, u32[]{:S(2)}, u32[]{:S(2)}) %collective-permute-start.6) | collective-permute-done | bytes 133152 | tf_op jit(solution)/shard_map/ppermute | solution.py:17
  166.7 1.3 add_convert_fusion.1
  168.3 2.6 %convolution_convert_fusion = bf16[16,64,512]{2,1,0:T(8,128)(2,1)} fusion(bf16[64,16,64]{0,2,1:T(8,128)(2,1)S(1)} %bitcast.70, bf16[512,16,64]{0,2,1:T(8,128)(2,1)} %bitcast.68), kind=kOutput, calls=%fused_computation.8 | convolution fusion | flops 67633152 | bytes 2228224 | tf_op jit(solution)/shard_map/thd,dhe->the/dot_general | solution.py:121
  170.9 1.9 convolution_add_fusion
  172.8 2.9 %copy.45 = f32[512,1024]{1,0:T(8,128)} copy(f32[512,1024]{0,1:T(8,128)} %bitcast.69) | data formatting | bytes 4194304 | tf_op jit(solution)/shard_map/reshape | solution.py:119
  175.7 4.3 %fusion.2 = f32[512,1024]{1,0:T(8,128)S(1)} fusion(bf16[1024,1024]{1,0:T(8,128)(2,1)} %all-gather.5.cloned.1.call-done, f32[512,1024]{1,0:T(8,128)} %copy.45, f32[512,1024]{1,0:T(8,128)} %get-tuple-element.94), kind=kOutput, calls=%fused_computation.15 | convolution fusion | flops 1076363264 | bytes 8388608 | tf_op jit(solution)/shard_map/dot_general | solution.py:125
  180.0 2.3 %add_convert_fusion = bf16[512,1024]{1,0:T(8,128)(2,1)} fusion(f32[512,1024]{1,0:T(8,128)S(1)} %fusion.2, bf16[512,1024]{0,1:T(8,128)(2,1)S(1)} %bitcast.76, bf16[1024,1024]{1,0:T(8,128)(2,1)S(1)} %copy-done.12), kind=kOutput, calls=%fused_computation.2 | convolution fusion | flops 1074790400 | bytes 6291456 | tf_op jit(solution)/shard_map/dot_general | solution.py:126
  (57 shorter events, 6.6 us)
Async XLA Ops:
  7.2 3.4 %copy-start = (bf16[1024,1024]{1,0:T(8,128)(2,1)S(1)}, bf16[1024,1024]{1,0:T(8,128)(2,1)}, u32[]{:S(2)}) copy-start(bf16[1024,1024]{1,0:T(8,128)(2,1)} %param.16) | copy-start | bytes 6291460
  7.2 31.7 %all-gather.3.cloned.1.call-start = ((), (), s32[]{:S(2)}) async-start(), calls=%async_computation | async-start | bytes 2359296 | tf_op jit(solution)/shard_map/all_gather | solution.py:102
  7.9 60.8 %all-gather.5.cloned.1.call-start = ((), (), s32[]{:S(2)}) async-start(), calls=%async_computation.1 | async-start | bytes 2359296 | tf_op jit(solution)/shard_map/all_gather | solution.py:101
  10.0 28.9 %copy-start.9 = (s32[256,1]{0,1:T(1,128)}, s32[256,1]{0,1:T(1,128)S(1)}, u32[]{:S(2)}) copy-start(s32[256,1]{0,1:T(1,128)S(1)} %get-tuple-element.86) | copy-start | bytes 3076
  73.7 5.9 %copy-start.7 = (f32[1024]{0:T(1024)}, f32[1024]{0:T(1024)S(1)}, u32[]{:S(2)}) copy-start(f32[1024]{0:T(1024)S(1)} %get-tuple-element.83) | copy-start | bytes 12292
  80.3 17.5 %collective-permute-start.5 = (bf16[65,1024]{1,0:T(8,128)(2,1)}, bf16[65,1024]{1,0:T(8,128)(2,1)S(1)}, u32[]{:S(2)}, u32[]{:S(2)}) collective-permute-start(bf16[65,1024]{1,0:T(8,128)(2,1)} %fusion.16), channel_id=1, source_target_pairs={{3,0},{4,1},{5,2},{6,3},{7,4},{8,5},{9,6},{10,7},{11,8},{12,9},{13... | collective-permute-start | bytes 399368 | tf_op jit(solution)/shard_map/ppermute | solution.py:17
  84.2 27.0 %collective-permute-start.4 = (bf16[65,1024]{1,0:T(8,128)(2,1)}, bf16[65,1024]{1,0:T(8,128)(2,1)}, u32[]{:S(2)}, u32[]{:S(2)}) collective-permute-start(bf16[65,1024]{1,0:T(8,128)(2,1)} %fusion.16), channel_id=1, source_target_pairs={{0,3},{1,4},{2,5},{3,6},{4,7},{5,8},{6,9},{7,10},{8,11},{9,12},{10... | collective-permute-start | bytes 399368 | tf_op jit(solution)/shard_map/ppermute | solution.py:17
  86.6 24.5 %collective-permute-start.3 = (bf16[65,1024]{1,0:T(8,128)(2,1)}, bf16[65,1024]{1,0:T(8,128)(2,1)}, u32[]{:S(2)}, u32[]{:S(2)}) collective-permute-start(bf16[65,1024]{1,0:T(8,128)(2,1)} %fusion.16), channel_id=1, source_target_pairs={{2,0},{3,1},{4,2},{5,3},{6,4},{7,5},{8,6},{9,7},{10,8},{11,9},{12,... | collective-permute-start | bytes 399368 | tf_op jit(solution)/shard_map/ppermute | solution.py:17
  91.7 19.4 %collective-permute-start.2 = (bf16[65,1024]{1,0:T(8,128)(2,1)}, bf16[65,1024]{1,0:T(8,128)(2,1)}, u32[]{:S(2)}, u32[]{:S(2)}) collective-permute-start(bf16[65,1024]{1,0:T(8,128)(2,1)} %fusion.16), channel_id=1, source_target_pairs={{0,2},{1,3},{2,4},{3,5},{4,6},{5,7},{6,8},{7,9},{8,10},{9,11},{10,... | collective-permute-start | bytes 399368 | tf_op jit(solution)/shard_map/ppermute | solution.py:17
  93.7 17.5 %collective-permute-start.1 = (bf16[65,1024]{1,0:T(8,128)(2,1)}, bf16[65,1024]{1,0:T(8,128)(2,1)}, u32[]{:S(2)}, u32[]{:S(2)}) collective-permute-start(bf16[65,1024]{1,0:T(8,128)(2,1)} %fusion.16), channel_id=1, source_target_pairs={{1,0},{2,1},{3,2},{4,3},{5,4},{6,5},{7,6},{8,7},{9,8},{10,9},{11,1... | collective-permute-start | bytes 399368 | tf_op jit(solution)/shard_map/ppermute | solution.py:17
  97.8 13.3 %collective-permute-start = (bf16[65,1024]{1,0:T(8,128)(2,1)}, bf16[65,1024]{1,0:T(8,128)(2,1)}, u32[]{:S(2)}, u32[]{:S(2)}) collective-permute-start(bf16[65,1024]{1,0:T(8,128)(2,1)} %fusion.16), channel_id=1, source_target_pairs={{0,1},{1,2},{2,3},{3,4},{4,5},{5,6},{6,7},{7,8},{8,9},{9,10},{10,1... | collective-permute-start | bytes 399368 | tf_op jit(solution)/shard_map/ppermute | solution.py:17
  115.0 6.8 %copy-start.8 = (s32[256,1]{0,1:T(1,128)S(1)}, s32[256,1]{0,1:T(1,128)}, u32[]{:S(2)}) copy-start(s32[256,1]{0,1:T(1,128)} %get-tuple-element.85) | copy-start | bytes 3076
  115.0 6.8 %copy-start.10 = (s32[256,1]{0,1:T(1,128)S(1)}, s32[256,1]{0,1:T(1,128)}, u32[]{:S(2)}) copy-start(s32[256,1]{0,1:T(1,128)} %copy-done.9) | copy-start | bytes 3076
  115.0 7.5 %copy-start.6 = (f32[16,64]{1,0:T(8,128)S(1)}, f32[16,64]{1,0:T(8,128)}, u32[]{:S(2)}) copy-start(f32[16,64]{1,0:T(8,128)} %mul.68) | copy-start | bytes 12292
  121.7 3.7 %copy-start.3 = (f32[128,16,64]{0,2,1:T(8,128)S(1)}, f32[128,16,64]{0,2,1:T(8,128)}, u32[]{:S(2)}) copy-start(f32[128,16,64]{0,2,1:T(8,128)} %get-tuple-element.98) | copy-start | bytes 1572868
  121.7 3.9 %copy-start.2 = (f32[64,1024]{0,1:T(8,128)S(1)}, f32[64,1024]{0,1:T(8,128)}, u32[]{:S(2)}) copy-start(f32[64,1024]{0,1:T(8,128)} %copy.38) | copy-start | bytes 786436
  133.1 0.6 copy-start.4
  134.4 23.8 %collective-permute-start.11 = (bf16[65,1024]{1,0:T(8,128)(2,1)}, bf16[65,1024]{1,0:T(8,128)(2,1)S(1)}, u32[]{:S(2)}, u32[]{:S(2)}) collective-permute-start(bf16[65,1024]{1,0:T(8,128)(2,1)} %fusion.15), channel_id=1, source_target_pairs={{3,0},{4,1},{5,2},{6,3},{7,4},{8,5},{9,6},{10,7},{11,8},{12,9},{13... | collective-permute-start | bytes 399368 | tf_op jit(solution)/shard_map/ppermute | solution.py:17
  138.2 22.8 %collective-permute-start.10 = (bf16[65,1024]{1,0:T(8,128)(2,1)}, bf16[65,1024]{1,0:T(8,128)(2,1)}, u32[]{:S(2)}, u32[]{:S(2)}) collective-permute-start(bf16[65,1024]{1,0:T(8,128)(2,1)} %fusion.15), channel_id=1, source_target_pairs={{0,3},{1,4},{2,5},{3,6},{4,7},{5,8},{6,9},{7,10},{8,11},{9,12},{10... | collective-permute-start | bytes 399368 | tf_op jit(solution)/shard_map/ppermute | solution.py:17
  140.1 20.8 %collective-permute-start.9 = (bf16[65,1024]{1,0:T(8,128)(2,1)}, bf16[65,1024]{1,0:T(8,128)(2,1)}, u32[]{:S(2)}, u32[]{:S(2)}) collective-permute-start(bf16[65,1024]{1,0:T(8,128)(2,1)} %fusion.15), channel_id=1, source_target_pairs={{2,0},{3,1},{4,2},{5,3},{6,4},{7,5},{8,6},{9,7},{10,8},{11,9},{12,... | collective-permute-start | bytes 399368 | tf_op jit(solution)/shard_map/ppermute | solution.py:17
  145.8 15.2 %collective-permute-start.8 = (bf16[65,1024]{1,0:T(8,128)(2,1)}, bf16[65,1024]{1,0:T(8,128)(2,1)}, u32[]{:S(2)}, u32[]{:S(2)}) collective-permute-start(bf16[65,1024]{1,0:T(8,128)(2,1)} %fusion.15), channel_id=1, source_target_pairs={{0,2},{1,3},{2,4},{3,5},{4,6},{5,7},{6,8},{7,9},{8,10},{9,11},{10,... | collective-permute-start | bytes 399368 | tf_op jit(solution)/shard_map/ppermute | solution.py:17
  147.7 13.2 %collective-permute-start.7 = (bf16[65,1024]{1,0:T(8,128)(2,1)}, bf16[65,1024]{1,0:T(8,128)(2,1)}, u32[]{:S(2)}, u32[]{:S(2)}) collective-permute-start(bf16[65,1024]{1,0:T(8,128)(2,1)} %fusion.15), channel_id=1, source_target_pairs={{1,0},{2,1},{3,2},{4,3},{5,4},{6,5},{7,6},{8,7},{9,8},{10,9},{11,1... | collective-permute-start | bytes 399368 | tf_op jit(solution)/shard_map/ppermute | solution.py:17
  155.5 4.9 %copy-start.11 = (f32[256]{0:T(256)S(1)}, f32[256]{0:T(256)}, u32[]{:S(2)}) copy-start(f32[256]{0:T(256)} %get-tuple-element.82) | copy-start | bytes 3076
  155.5 11.2 %copy-start.5 = (f32[1024]{0:T(1024)S(1)}, f32[1024]{0:T(1024)}, u32[]{:S(2)}) copy-start(f32[1024]{0:T(1024)} %copy-done.4) | copy-start | bytes 12292
  158.2 8.5 %collective-permute-start.6 = (bf16[65,1024]{1,0:T(8,128)(2,1)}, bf16[65,1024]{1,0:T(8,128)(2,1)S(1)}, u32[]{:S(2)}, u32[]{:S(2)}) collective-permute-start(bf16[65,1024]{1,0:T(8,128)(2,1)} %fusion.15), channel_id=1, source_target_pairs={{0,1},{1,2},{2,3},{3,4},{4,5},{5,6},{6,7},{7,8},{8,9},{9,10},{10,1... | collective-permute-start | bytes 399368 | tf_op jit(solution)/shard_map/ppermute | solution.py:17
  175.7 4.3 %copy-start.1 = (bf16[16,64,512]{2,1,0:T(8,128)(2,1)S(1)}, bf16[16,64,512]{2,1,0:T(8,128)(2,1)}, u32[]{:S(2)}) copy-start(bf16[16,64,512]{2,1,0:T(8,128)(2,1)} %convolution_convert_fusion) | copy-start | bytes 3145732
  175.7 4.3 %copy-start.12 = (bf16[1024,1024]{1,0:T(8,128)(2,1)S(1)}, bf16[1024,1024]{1,0:T(8,128)(2,1)}, u32[]{:S(2)}) copy-start(bf16[1024,1024]{1,0:T(8,128)(2,1)} %all-gather.3.cloned.1.call-done) | copy-start | bytes 6291460
Sparse Core Ops, SparseCore 0:
  9.9 28.9 all-gather.2
  40.8 27.8 all-gather.4
where the time goes:
time: 190 us; the launch traced here: 189 us
  waiting for transfers between devices  57.2 us (30%)
  starting transfers between devices  39.8 us (21%)
  matrix products  35.4 us (19%)
  local copies, waits for them, and re-layouts  26.5 us (14%)
  between operations  18.9 us (10%)
  other arithmetic  11.4 us (6%)
    ppermute x12, starting transfers between devices, from_behind(): lax.ppermute(value, axis, [(source, source + steps) for source in range(i...  39.7 us
    all_gather x1, waiting for transfers between devices, shards(): lax.all_gather(w_value, 'blk', axis=0, tiled=True)  25.9 us
    all_gather x1, waiting for transfers between devices, shards(): lax.all_gather(w_key, 'blk', axis=0, tiled=True)  24.2 us
    ppermute x12, waiting for transfers between devices, from_behind(): lax.ppermute(value, axis, [(source, source + steps) for source in range(i...  5.78 us
    dot_general x1, matrix products, shards(): keys = jnp.dot(receptor, full_key, preferred_element_type=jnp.float32)  5.01 us
    dot_general x1, matrix products, shards(): lax.dot_general(key_grad, full_key, contract, preferred_element_type=jnp....  4.29 us
    dot_general x1, matrix products, shards(): values = jnp.dot(receptor, full_value, preferred_element_type=jnp.float32)  4.14 us
  transfers between devices with their start and end apart: 14, of which 3 were waited for; matrix products, arithmetic and copies ran while one was open for 12% of the time, Pallas kernels for 0%

commit v1 on v0

--- a/solution.py
+++ b/solution.py
@@ -93,16 +93,35 @@
     return (pair_loss, pose_grad.astype(jnp.bfloat16), pose_state)
 
 
+def gather_rows(shard):
+    count = lax.axis_size("blk")
+    if count > 16 or count % 2:
+        return lax.all_gather(shard, "blk", axis=0, tiled=True)
+    position = lax.axis_index("blk")
+    rows = shard.shape[0]
+    got = [shard] + [
+        lax.ppermute(shard, "blk", [(s, (s + 2 * k) % count) for s in range(count)])
+        for k in range(1, count // 2)
+    ]
+    mine = jnp.stack(got)
+    sibling = lax.ppermute(mine, "blk", [(s, s ^ 1) for s in range(count)])
+    full = jnp.zeros((count,) + shard.shape, shard.dtype)
+    for k in range(count // 2):
+        full = lax.dynamic_update_slice(full, mine[k][None], ((position - 2 * k) % count, 0, 0))
+        full = lax.dynamic_update_slice(
+            full, sibling[k][None], (((position ^ 1) - 2 * k) % count, 0, 0)
+        )
+    return full.reshape(count * rows, shard.shape[1])
+
+
 def shards(receptor, poses, pairs, block_complex, w_key, w_value, w_query, score_weight):
     rows = receptor.shape[0]
     width = receptor.shape[1]
     contract = (((1,), (1,)), ((), ()))
-    full_key, full_value = (
-        lax.all_gather(w_key, "blk", axis=0, tiled=True),
-        lax.all_gather(w_value, "blk", axis=0, tiled=True),
-    )
-    keys = jnp.dot(receptor, full_key, preferred_element_type=jnp.float32)
-    values = jnp.dot(receptor, full_value, preferred_element_type=jnp.float32)
+    full_both = gather_rows(jnp.concatenate([w_key, w_value], axis=1))
+    both = jnp.dot(receptor, full_both, preferred_element_type=jnp.float32)
+    keys = both[:, :width]
+    values = both[:, width:]
     key_feat = features(keys).astype(jnp.bfloat16)
     val_round = values.astype(jnp.bfloat16)
     state = complex_total(local_state(key_feat, val_round), block_complex)
@@ -122,10 +141,8 @@
         .reshape(rows, width)
         .astype(jnp.bfloat16)
     )
-    total = lax.dot_general(key_grad, full_key, contract, preferred_element_type=jnp.float32)
-    total = total + lax.dot_general(
-        value_grad, full_value, contract, preferred_element_type=jnp.float32
-    )
+    both_grad = jnp.concatenate([key_grad, value_grad], axis=1)
+    total = lax.dot_general(both_grad, full_both, contract, preferred_element_type=jnp.float32)
     return (pair_loss, pose_grad, total.astype(jnp.bfloat16))
 
 

time: 190 us -> 147 us (0.77)
  waiting for transfers between devices: 57.2 us -> 31.2 us
  matrix products: 35.4 us -> 22 us
  between operations: 18.9 us -> 5.85 us
  other arithmetic: 11.4 us -> 17.3 us
  starting transfers between devices: 39.8 us -> 42.2 us
    all_gather x2 -> x0, waiting for transfers between devices: 50.1 us -> none  [the longest x1 25.9 us: shards(): lax.all_gather(w_value, 'blk', axis=0, tiled=True)]
    ppermute x0 -> x4, waiting for transfers between devices: none -> 25.2 us  [the longest x3 23.5 us: gather_rows(): lax.ppermute(shard, 'blk', [(s, (s + 2 * k) % count) for s in range(count)])]
    dot_general x4 -> x2, matrix products: 15.7 us -> 5.83 us  [the longest x1 3.35 us: shards(): lax.dot_general(both_grad, full_both, contract, preferred_element_type=jn...]
    dynamic_update_slice x0 -> x8, local copies, waits for them, and re-layouts: none -> 4.6 us  [the longest x4 4.4 us: gather_rows(): lax.dynamic_update_slice(full, sibling[k][None], (((position ^ 1) - 2 * k...]
    convert_element_type x2 -> x0, local copies, waits for them, and re-layouts: 3.76 us -> none  [the longest x1 2.27 us: shards(): key_feat = features(keys).astype(jnp.bfloat16)]
    ppermute x0 -> x4, starting transfers between devices: none -> 3.6 us  [the longest x3 3.6 us: gather_rows(): lax.ppermute(shard, 'blk', [(s, (s + 2 * k) % count) for s in range(count)])]
    reshape x1 -> x0, local copies, waits for them, and re-layouts: 2.92 us -> none  [shards(): feat_grad.reshape(rows, width) * slope(keys)]
    convert_element_type x0 -> x1, other arithmetic: none -> 2.5 us  [shards(): (feat_grad.reshape(rows, width) * slope(keys)).astype(jnp.bfloat16)]
  transfers between devices with their start and end apart: 14 -> 16, of which waited for: 3 -> 4; matrix products, arithmetic and copies ran while one was open for 12% -> 11% of each run, Pallas kernels for 0% -> 0%
where the time goes in v1:
time: 147 us; the launch traced here: 146 us
  starting transfers between devices  42.2 us (29%)
  waiting for transfers between devices  31.2 us (21%)
  local copies, waits for them, and re-layouts  27.6 us (19%)
  matrix products  22 us (15%)
  other arithmetic  17.3 us (12%)
  between operations  5.85 us (4%)
    ppermute x12, starting transfers between devices, from_behind(): lax.ppermute(value, axis, [(source, source + steps) for source in range(i...  38.6 us
    ppermute x3, waiting for transfers between devices, gather_rows(): lax.ppermute(shard, 'blk', [(s, (s + 2 * k) % count) for s in range(count)])  23.5 us
    ppermute x12, waiting for transfers between devices, from_behind(): lax.ppermute(value, axis, [(source, source + steps) for source in range(i...  5.96 us
    dynamic_update_slice x4, local copies, waits for them, and re-layouts, gather_rows(): lax.dynamic_update_slice(full, sibling[k][None], (((position ^ 1) - 2 * k...  4.4 us
    ppermute x3, starting transfers between devices, gather_rows(): lax.ppermute(shard, 'blk', [(s, (s + 2 * k) % count) for s in range(count)])  3.6 us
    dot_general x1, matrix products, shards(): lax.dot_general(both_grad, full_both, contract, preferred_element_type=jn...  3.35 us
    unnamed x47, local copies, waits for them, and re-layouts  3.04 us
  transfers between devices with their start and end apart: 16, of which 4 were waited for; matrix products, arithmetic and copies ran while one was open for 11% of the time, Pallas kernels for 0%

profile of v1, /device:TPU:16, one launch (start us, length us, event | category | flops | bytes accessed | tf_op | source)
XLA Modules:
  0.0 146.2 jit_solution(18060744458048302182)
XLA Ops:
  0.6 1.1 constant_dynamic-update-slice_fusion.1
  2.7 2.5 %collective-permute-start.2 = (bf16[128,2048]{1,0:T(8,128)(2,1)S(1)}, bf16[128,2048]{1,0:T(8,128)(2,1)S(1)}, u32[]{:S(2)}, u32[]{:S(2)}) collective-permute-start(bf16[128,2048]{1,0:T(8,128)(2,1)S(1)} %constant_dynamic-update-slice_fusion), channel_id=1, source_target_pairs={{0,6},{1,7},{2,0},{3,1},{4,2},{5,3},{6,4},{7,5},{8,14},{9,15},{10,... | collective-permute-start | bytes 1572872 | tf_op jit(solution)/shard_map/ppermute | solution.py:103
  6.3 11.3 %collective-permute-done.2 = bf16[128,2048]{1,0:T(8,128)(2,1)S(1)} collective-permute-done((bf16[128,2048]{1,0:T(8,128)(2,1)S(1)}, bf16[128,2048]{1,0:T(8,128)(2,1)S(1)}, u32[]{:S(2)}, u32[]{:S(2)}) %collective-permute-start.2) | collective-permute-done | bytes 524320 | tf_op jit(solution)/shard_map/ppermute | solution.py:103
  17.6 12.3 %collective-permute-done.1 = bf16[128,2048]{1,0:T(8,128)(2,1)S(1)} collective-permute-done((bf16[128,2048]{1,0:T(8,128)(2,1)S(1)}, bf16[128,2048]{1,0:T(8,128)(2,1)S(1)}, u32[]{:S(2)}, u32[]{:S(2)}) %collective-permute-start.1) | collective-permute-done | bytes 524320 | tf_op jit(solution)/shard_map/ppermute | solution.py:103
  29.9 1.6 %pad_maximum_fusion = bf16[4,128,2048]{2,1,0:T(8,128)(2,1)} fusion(bf16[1,128,2048]{2,1,0:T(8,128)(2,1)S(1)} %bitcast.88, bf16[1,128,2048]{2,1,0:T(8,128)(2,1)S(1)} %bitcast.89, bf16[1,128,2048]{2,1,0:T(8,128)(2,1)S(1)} %bitcast.90, bf16[1,128,2048]{2,1,0:T(8,128)(2,1)S(1)} %bitcast.81), kind=kLoop, calls=%fused_computation.4 | loop fusion | flops 3145728 | bytes 4194304 | tf_op jit(solution)/shard_map/stack | solution.py:106
  32.2 1.5 %add_select_fusion = (f32[128,1024]{1,0:T(8,128)}, f32[128,1024]{1,0:T(8,128)}) fusion(bf16[128,1024]{1,0:T(8,128)(2,1)S(1)} %copy-done.13, bf16[1024,1024]{1,0:T(8,128)(2,1)S(1)} %copy-done), kind=kOutput, calls=%fused_computation.35 | convolution fusion | flops 268959744 | bytes 3407872 | tf_op jit(solution)/shard_map/dot_general | solution.py:57
  34.3 1.7 %collective-permute-done.3 = bf16[4,128,2048]{2,1,0:T(8,128)(2,1)} collective-permute-done((bf16[4,128,2048]{2,1,0:T(8,128)(2,1)}, bf16[4,128,2048]{2,1,0:T(8,128)(2,1)}, u32[]{:S(2)}, u32[]{:S(2)}) %collective-permute-start.3) | collective-permute-done | bytes 2097184 | tf_op jit(solution)/shard_map/ppermute | solution.py:107
  37.2 1.1 slice_dynamic-update-slice_fusion.2
  38.3 1.2 slice_dynamic-update-slice_fusion.1
  39.6 1.1 slice_dynamic-update-slice_fusion
  40.7 2.5 %convolution_bitcast_fusion = f32[512,2048]{0,1:T(8,128)S(1)} fusion(bf16[1024,2048]{1,0:T(8,128)(2,1)S(1)} %bitcast.79, bf16[512,1024]{1,0:T(8,128)(2,1)S(1)} %copy-done.22), kind=kOutput, calls=%fused_computation.2 | convolution fusion | flops 2147483648 | bytes 9437184 | tf_op jit(solution)/shard_map/dot_general | solution.py:122
  43.2 2.0 %convert_reduce_fusion = (f32[1024]{0:T(1024)S(1)}, bf16[512,1024]{0,1:T(8,128)(2,1)S(1)}, pred[512,1024]{0,1:T(8,128)(4,1)}) fusion(f32[512,2048]{0,1:T(8,128)S(1)} %convolution_bitcast_fusion), kind=kLoop, calls=%fused_computation.11 | loop fusion | flops 3668992 | bytes 3674112 | tf_op jit(solution)/shard_map/reduce_sum | solution.py:35
  45.3 1.3 fusion.30
  46.6 1.2 copy.27
  48.5 2.0 %collective-permute-start.9 = (bf16[65,1024]{1,0:T(8,128)(2,1)}, bf16[65,1024]{1,0:T(8,128)(2,1)S(1)}, u32[]{:S(2)}, u32[]{:S(2)}) collective-permute-start(bf16[65,1024]{1,0:T(8,128)(2,1)} %fusion.21), channel_id=1, source_target_pairs={{3,0},{4,1},{5,2},{6,3},{7,4},{8,5},{9,6},{10,7},{11,8},{12,9},{13... | collective-permute-start | bytes 399368 | tf_op jit(solution)/shard_map/ppermute | solution.py:17
  50.5 1.2 compare_select_fusion
  51.8 3.5 %collective-permute-start.8 = (bf16[65,1024]{1,0:T(8,128)(2,1)}, bf16[65,1024]{1,0:T(8,128)(2,1)}, u32[]{:S(2)}, u32[]{:S(2)}) collective-permute-start(bf16[65,1024]{1,0:T(8,128)(2,1)} %fusion.21), channel_id=1, source_target_pairs={{0,3},{1,4},{2,5},{3,6},{4,7},{5,8},{6,9},{7,10},{8,11},{9,12},{10... | collective-permute-start | bytes 399368 | tf_op jit(solution)/shard_map/ppermute | solution.py:17
  55.3 4.1 %collective-permute-start.7 = (bf16[65,1024]{1,0:T(8,128)(2,1)}, bf16[65,1024]{1,0:T(8,128)(2,1)}, u32[]{:S(2)}, u32[]{:S(2)}) collective-permute-start(bf16[65,1024]{1,0:T(8,128)(2,1)} %fusion.21), channel_id=1, source_target_pairs={{2,0},{3,1},{4,2},{5,3},{6,4},{7,5},{8,6},{9,7},{10,8},{11,9},{12,... | collective-permute-start | bytes 399368 | tf_op jit(solution)/shard_map/ppermute | solution.py:17
  59.4 1.9 %collective-permute-start.6 = (bf16[65,1024]{1,0:T(8,128)(2,1)}, bf16[65,1024]{1,0:T(8,128)(2,1)}, u32[]{:S(2)}, u32[]{:S(2)}) collective-permute-start(bf16[65,1024]{1,0:T(8,128)(2,1)} %fusion.21), channel_id=1, source_target_pairs={{0,2},{1,3},{2,4},{3,5},{4,6},{5,7},{6,8},{7,9},{8,10},{9,11},{10,... | collective-permute-start | bytes 399368 | tf_op jit(solution)/shard_map/ppermute | solution.py:17
  61.3 4.0 %collective-permute-start.5 = (bf16[65,1024]{1,0:T(8,128)(2,1)}, bf16[65,1024]{1,0:T(8,128)(2,1)}, u32[]{:S(2)}, u32[]{:S(2)}) collective-permute-start(bf16[65,1024]{1,0:T(8,128)(2,1)} %fusion.21), channel_id=1, source_target_pairs={{1,0},{2,1},{3,2},{4,3},{5,4},{6,5},{7,6},{8,7},{9,8},{10,9},{11,1... | collective-permute-start | bytes 399368 | tf_op jit(solution)/shard_map/ppermute | solution.py:17
  65.4 1.9 %collective-permute-start.4 = (bf16[65,1024]{1,0:T(8,128)(2,1)}, bf16[65,1024]{1,0:T(8,128)(2,1)}, u32[]{:S(2)}, u32[]{:S(2)}) collective-permute-start(bf16[65,1024]{1,0:T(8,128)(2,1)} %fusion.21), channel_id=1, source_target_pairs={{0,1},{1,2},{2,3},{3,4},{4,5},{5,6},{6,7},{7,8},{8,9},{9,10},{10,1... | collective-permute-start | bytes 399368 | tf_op jit(solution)/shard_map/ppermute | solution.py:17
  67.9 1.4 mul.68
  69.2 1.6 %fusion.29 = (s32[1]{0:T(128)}, s32[1]{0:T(128)}, s32[1]{0:T(128)}, s32[1]{0:T(128)}, s32[1]{0:T(128)}, /*index=5*/s32[1]{0:T(128)}, s32[1]{0:T(128)}) fusion(s32[32]{0:T(128)} %param.13, s32[]{:T(128)S(6)} %max.20, s32[]{:T(128)S(6)} %select_n.234, s32[]{:T(128)S(6)} %max.21, s32[]{:T(128)S(6)} %select_n.227, s32[]{:T(128)S(6)} %select_n.223, ...), kind=kLoop, calls=%fused_computation.78 | loop fusion | bytes 84 | solution.py:47
  75.4 2.1 %copy.29 = f32[128,1024]{0,1:T(8,128)} copy(f32[128,1024]{1,0:T(8,128)} %get-tuple-element.95) | data formatting | bytes 1048576 | tf_op jit(solution)/shard_map/jit(_where)/select_n | solution.py:21
  77.5 1.2 pad_clamp_fusion.1
  78.8 1.4 select_add_fusion
  81.3 1.2 multiply_reduce_fusion.2
  82.6 2.7 %multiply_reduce_fusion.1 = (f32[128]{0:T(128)S(1)}, f32[128,16,64]{0,2,1:T(8,128)}) fusion(f32[16,64]{1,0:T(8,128)} %mul.68, f32[128,16]{0,1:T(8,128)S(1)} %multiply_reduce_fusion.2, f32[64,16,64]{0,2,1:T(8,128)} %bitcast.92, f32[128,16,64]{0,2,1:T(8,128)} %bitcast.85), kind=kOutput, calls=%fused_computation.32 | convolution fusion | flops 101056384 | bytes 1323520 | tf_op jit(solution)/shard_map/phd,dhe->phe/dot_general | solution.py:61
  85.2 2.0 %gather_fusion.1 = f32[256]{0:T(256)S(1)} fusion(f32[128]{0:T(128)S(1)} %get-tuple-element.97, s32[1024]{0:T(1024)} %pad_clamp_fusion), kind=kCustom, calls=%fused_computation.1.clone | custom fusion | bytes 3072 | tf_op jit(solution)/shard_map/jit(_take)/gather | solution.py:66
  87.3 2.0 %gather_fusion = f32[256]{0:T(256)S(1)} fusion(f32[128]{0:T(128)S(1)} %get-tuple-element.97, s32[1024]{0:T(1024)} %pad_clamp_fusion.1), kind=kCustom, calls=%fused_computation.clone | custom fusion | bytes 3072 | tf_op jit(solution)/shard_map/jit(_take)/gather | solution.py:67
  90.1 2.9 %fusion.11 = f32[16,64,64]{2,1,0:T(8,128)} fusion(f32[128,16,64]{0,2,1:T(8,128)} %bitcast.86, f32[128]{0:T(128)S(1)} %subtract_reduce_fusion, f32[16,64]{1,0:T(8,128)S(1)} %copy-done.17, f32[128,16]{0,1:T(8,128)S(1)} %multiply_reduce_fusion.2), kind=kOutput, calls=%fused_computation.36 | convolution fusion | flops 100925440 | bytes 799232 | tf_op jit(solution)/shard_map/phd,phe->dhe/dot_general | solution.py:80
  93.2 2.0 %fusion.8 = f32[128,16,64]{0,2,1:T(8,128)} fusion(f32[64,16,64]{0,2,1:T(8,128)S(1)} %bitcast.93, f32[128,16]{0,1:T(8,128)S(1)} %negate_divide_fusion, f32[128]{0:T(128)S(1)} %subtract_reduce_fusion, f32[16,64]{1,0:T(8,128)S(1)} %copy-done.17, f32[128,16]{0,1:T(8,128)S(1)} %multiply_reduce_fusion.2, f32[16,64]{1,0:T(8,128)S(1)} %mul.65), kind=kOutput, calls=%fused_computation.19 | convolution fusion | flops 101187584 | bytes 811520 | tf_op jit(solution)/shard_map/phe,dhe->phd/dot_general | solution.py:86
  96.0 2.1 %copy.32 = f32[128,1024]{1,0:T(8,128)} copy(f32[128,1024]{0,1:T(8,128)} %bitcast.87) | data formatting | bytes 1048576 | tf_op jit(solution)/shard_map/mul | solution.py:87
  98.1 1.2 copy.33
  99.3 1.4 multiply_reduce_fusion
  101.9 3.9 %collective-permute-start.15 = (bf16[65,1024]{1,0:T(8,128)(2,1)}, bf16[65,1024]{1,0:T(8,128)(2,1)S(1)}, u32[]{:S(2)}, u32[]{:S(2)}) collective-permute-start(bf16[65,1024]{1,0:T(8,128)(2,1)} %fusion.20), channel_id=1, source_target_pairs={{3,0},{4,1},{5,2},{6,3},{7,4},{8,5},{9,6},{10,7},{11,8},{12,9},{13... | collective-permute-start | bytes 399368 | tf_op jit(solution)/shard_map/ppermute | solution.py:17
  105.8 1.9 %collective-permute-start.14 = (bf16[65,1024]{1,0:T(8,128)(2,1)}, bf16[65,1024]{1,0:T(8,128)(2,1)}, u32[]{:S(2)}, u32[]{:S(2)}) collective-permute-start(bf16[65,1024]{1,0:T(8,128)(2,1)} %fusion.20), channel_id=1, source_target_pairs={{0,3},{1,4},{2,5},{3,6},{4,7},{5,8},{6,9},{7,10},{8,11},{9,12},{10... | collective-permute-start | bytes 399368 | tf_op jit(solution)/shard_map/ppermute | solution.py:17
  107.7 5.8 %collective-permute-start.13 = (bf16[65,1024]{1,0:T(8,128)(2,1)}, bf16[65,1024]{1,0:T(8,128)(2,1)}, u32[]{:S(2)}, u32[]{:S(2)}) collective-permute-start(bf16[65,1024]{1,0:T(8,128)(2,1)} %fusion.20), channel_id=1, source_target_pairs={{2,0},{3,1},{4,2},{5,3},{6,4},{7,5},{8,6},{9,7},{10,8},{11,9},{12,... | collective-permute-start | bytes 399368 | tf_op jit(solution)/shard_map/ppermute | solution.py:17
  113.6 1.9 %collective-permute-start.12 = (bf16[65,1024]{1,0:T(8,128)(2,1)}, bf16[65,1024]{1,0:T(8,128)(2,1)}, u32[]{:S(2)}, u32[]{:S(2)}) collective-permute-start(bf16[65,1024]{1,0:T(8,128)(2,1)} %fusion.20), channel_id=1, source_target_pairs={{0,2},{1,3},{2,4},{3,5},{4,6},{5,7},{6,8},{7,9},{8,10},{9,11},{10,... | collective-permute-start | bytes 399368 | tf_op jit(solution)/shard_map/ppermute | solution.py:17
  115.5 5.6 %collective-permute-start.11 = (bf16[65,1024]{1,0:T(8,128)(2,1)}, bf16[65,1024]{1,0:T(8,128)(2,1)}, u32[]{:S(2)}, u32[]{:S(2)}) collective-permute-start(bf16[65,1024]{1,0:T(8,128)(2,1)} %fusion.20), channel_id=1, source_target_pairs={{1,0},{2,1},{3,2},{4,3},{5,4},{6,5},{7,6},{8,7},{9,8},{10,9},{11,1... | collective-permute-start | bytes 399368 | tf_op jit(solution)/shard_map/ppermute | solution.py:17
  121.1 2.1 %copy.31 = f32[128,1024]{1,0:T(8,128)} copy(f32[128,1024]{0,1:T(8,128)} %bitcast.95) | data formatting | bytes 1048576 | tf_op jit(solution)/shard_map/reshape | solution.py:89
  123.2 2.7 %convolution_convert_fusion.1 = bf16[128,1024]{1,0:T(8,128)(2,1)} fusion(bf16[1024,1024]{1,0:T(8,128)(2,1)S(1)} %copy-done, f32[128,1024]{1,0:T(8,128)} %copy.31, f32[128,1024]{1,0:T(8,128)} %get-tuple-element.96), kind=kOutput, calls=%fused_computation.22 | convolution fusion | flops 269221888 | bytes 3407872 | tf_op jit(solution)/shard_map/dot_general | solution.py:90
  125.9 1.9 %collective-permute-start.10 = (bf16[65,1024]{1,0:T(8,128)(2,1)}, bf16[65,1024]{1,0:T(8,128)(2,1)S(1)}, u32[]{:S(2)}, u32[]{:S(2)}) collective-permute-start(bf16[65,1024]{1,0:T(8,128)(2,1)} %fusion.20), channel_id=1, source_target_pairs={{0,1},{1,2},{2,3},{3,4},{4,5},{5,6},{6,7},{7,8},{8,9},{9,10},{10,1... | collective-permute-start | bytes 399368 | tf_op jit(solution)/shard_map/ppermute | solution.py:17
  128.5 5.9 %collective-permute-done.10 = bf16[65,1024]{1,0:T(8,128)(2,1)S(1)} collective-permute-done((bf16[65,1024]{1,0:T(8,128)(2,1)}, bf16[65,1024]{1,0:T(8,128)(2,1)S(1)}, u32[]{:S(2)}, u32[]{:S(2)}) %collective-permute-start.10) | collective-permute-done | bytes 133152 | tf_op jit(solution)/shard_map/ppermute | solution.py:17
  134.4 1.3 add_convert_fusion
  135.9 2.7 %convolution_convert_fusion = bf16[16,64,512]{2,1,0:T(8,128)(2,1)} fusion(bf16[64,16,64]{0,2,1:T(8,128)(2,1)S(1)} %bitcast.82, bf16[512,16,64]{0,2,1:T(8,128)(2,1)} %bitcast.78), kind=kOutput, calls=%fused_computation.17 | convolution fusion | flops 67633152 | bytes 2228224 | tf_op jit(solution)/shard_map/thd,dhe->the/dot_general | solution.py:140
  139.7 2.5 %fusion.4 = bf16[512,1024]{0,1:T(8,128)(2,1)S(1)} fusion(f32[16,64,512]{2,1,0:T(8,128)S(1)} %convolution_add_fusion, pred[512,1024]{0,1:T(8,128)(4,1)S(1)} %copy-done.5, f32[512,2048]{0,1:T(8,128)} %copy-done.2), kind=kLoop, calls=%fused_computation.10 | loop fusion | flops 2097152 | bytes 5767168 | tf_op jit(solution)/shard_map/convert_element_type | solution.py:138
  142.8 3.4 %fusion.5 = bf16[512,1024]{1,0:T(8,128)(2,1)} fusion(bf16[1024,2048]{1,0:T(8,128)(2,1)S(1)} %bitcast.80, bf16[512,1024]{0,1:T(8,128)(2,1)S(1)} %bitcast.91, bf16[512,1024]{0,1:T(8,128)(2,1)S(1)} %fusion.4), kind=kOutput, calls=%fused_computation.16 | convolution fusion | flops 2152202240 | bytes 7340032 | tf_op jit(solution)/shard_map/dot_general | solution.py:145
  (88 shorter events, 12.7 us)
Async XLA Ops:
  0.6 31.6 %copy-start = (bf16[1024,1024]{1,0:T(8,128)(2,1)S(1)}, bf16[1024,1024]{1,0:T(8,128)(2,1)}, u32[]{:S(2)}) copy-start(bf16[1024,1024]{1,0:T(8,128)(2,1)} %param.16) | copy-start | bytes 6291460
  2.7 14.9 %collective-permute-start.2 = (bf16[128,2048]{1,0:T(8,128)(2,1)S(1)}, bf16[128,2048]{1,0:T(8,128)(2,1)S(1)}, u32[]{:S(2)}, u32[]{:S(2)}) collective-permute-start(bf16[128,2048]{1,0:T(8,128)(2,1)S(1)} %constant_dynamic-update-slice_fusion), channel_id=1, source_target_pairs={{0,6},{1,7},{2,0},{3,1},{4,2},{5,3},{6,4},{7,5},{8,14},{9,15},{10,... | collective-permute-start | bytes 1572872 | tf_op jit(solution)/shard_map/ppermute | solution.py:103
  5.2 24.6 %collective-permute-start.1 = (bf16[128,2048]{1,0:T(8,128)(2,1)S(1)}, bf16[128,2048]{1,0:T(8,128)(2,1)S(1)}, u32[]{:S(2)}, u32[]{:S(2)}) collective-permute-start(bf16[128,2048]{1,0:T(8,128)(2,1)S(1)} %constant_dynamic-update-slice_fusion), channel_id=1, source_target_pairs={{0,4},{1,5},{2,6},{3,7},{4,0},{5,1},{6,2},{7,3},{8,12},{9,13},{10,... | collective-permute-start | bytes 1572872 | tf_op jit(solution)/shard_map/ppermute | solution.py:103
  5.7 24.1 %collective-permute-start = (bf16[128,2048]{1,0:T(8,128)(2,1)S(1)}, bf16[128,2048]{1,0:T(8,128)(2,1)S(1)}, u32[]{:S(2)}, u32[]{:S(2)}) collective-permute-start(bf16[128,2048]{1,0:T(8,128)(2,1)S(1)} %constant_dynamic-update-slice_fusion), channel_id=1, source_target_pairs={{0,2},{1,3},{2,4},{3,5},{4,6},{5,7},{6,0},{7,1},{8,10},{9,11},{10,... | collective-permute-start | bytes 1572872 | tf_op jit(solution)/shard_map/ppermute | solution.py:103
  29.9 1.6 %copy-start.6 = (bf16[128,2048]{1,0:T(8,128)(2,1)}, bf16[128,2048]{1,0:T(8,128)(2,1)S(1)}, u32[]{:S(2)}) copy-start(bf16[128,2048]{1,0:T(8,128)(2,1)S(1)} %collective-permute-done.1) | copy-start | bytes 1572868
  29.9 1.6 %copy-start.8 = (bf16[128,2048]{1,0:T(8,128)(2,1)}, bf16[128,2048]{1,0:T(8,128)(2,1)S(1)}, u32[]{:S(2)}) copy-start(bf16[128,2048]{1,0:T(8,128)(2,1)S(1)} %collective-permute-done) | copy-start | bytes 1572868
  29.9 1.8 %copy-start.21 = (s32[256,2]{0,1:T(2,128)S(1)}, s32[256,2]{0,1:T(2,128)}, u32[]{:S(2)}) copy-start(s32[256,2]{0,1:T(2,128)} %param.12) | copy-start | bytes 6148
  29.9 2.3 %copy-start.13 = (bf16[128,1024]{1,0:T(8,128)(2,1)S(1)}, bf16[128,1024]{1,0:T(8,128)(2,1)}, u32[]{:S(2)}) copy-start(bf16[128,1024]{1,0:T(8,128)(2,1)} %param.11) | copy-start | bytes 786436
  31.5 4.5 %collective-permute-start.3 = (bf16[4,128,2048]{2,1,0:T(8,128)(2,1)}, bf16[4,128,2048]{2,1,0:T(8,128)(2,1)}, u32[]{:S(2)}, u32[]{:S(2)}) collective-permute-start(bf16[4,128,2048]{2,1,0:T(8,128)(2,1)} %pad_maximum_fusion), channel_id=1, source_target_pairs={{0,1},{1,0},{2,3},{3,2},{4,5},{5,4},{6,7},{7,6},{8,9},{9,8},{10,11... | collective-permute-start | bytes 6291464 | tf_op jit(solution)/shard_map/ppermute | solution.py:107
  34.2 2.9 %copy-start.9 = (bf16[128,2048]{1,0:T(8,128)(2,1)S(1)}, bf16[128,2048]{1,0:T(8,128)(2,1)}, u32[]{:S(2)}) copy-start(bf16[128,2048]{1,0:T(8,128)(2,1)} %copy-done.8) | copy-start | bytes 1572868
  34.3 4.0 %copy-start.7 = (bf16[128,2048]{1,0:T(8,128)(2,1)S(1)}, bf16[128,2048]{1,0:T(8,128)(2,1)}, u32[]{:S(2)}) copy-start(bf16[128,2048]{1,0:T(8,128)(2,1)} %copy-done.6) | copy-start | bytes 1572868
  38.3 2.4 %copy-start.22 = (bf16[512,1024]{1,0:T(8,128)(2,1)S(1)}, bf16[512,1024]{1,0:T(8,128)(2,1)}, u32[]{:S(2)}) copy-start(bf16[512,1024]{1,0:T(8,128)(2,1)} %param.10) | copy-start | bytes 3145732
  40.6 2.5 %copy-start.3 = (bf16[8,128,2048]{2,1,0:T(8,128)(2,1)}, bf16[8,128,2048]{2,1,0:T(8,128)(2,1)S(1)}, u32[]{:S(2)}) copy-start(bf16[8,128,2048]{2,1,0:T(8,128)(2,1)S(1)} %slice_dynamic-update-slice_fusion) | copy-start | bytes 12582916
  43.2 2.2 %copy-start.2 = (f32[512,2048]{0,1:T(8,128)}, f32[512,2048]{0,1:T(8,128)S(1)}, u32[]{:S(2)}) copy-start(f32[512,2048]{0,1:T(8,128)S(1)} %convolution_bitcast_fusion) | copy-start | bytes 12582916
  45.2 1.4 copy-start.1
  45.2 2.7 %copy-start.16 = (f32[1024]{0:T(1024)}, f32[1024]{0:T(1024)S(1)}, u32[]{:S(2)}) copy-start(f32[1024]{0:T(1024)S(1)} %get-tuple-element.83) | copy-start | bytes 12292
  48.5 16.9 %collective-permute-start.9 = (bf16[65,1024]{1,0:T(8,128)(2,1)}, bf16[65,1024]{1,0:T(8,128)(2,1)S(1)}, u32[]{:S(2)}, u32[]{:S(2)}) collective-permute-start(bf16[65,1024]{1,0:T(8,128)(2,1)} %fusion.21), channel_id=1, source_target_pairs={{3,0},{4,1},{5,2},{6,3},{7,4},{8,5},{9,6},{10,7},{11,8},{12,9},{13... | collective-permute-start | bytes 399368 | tf_op jit(solution)/shard_map/ppermute | solution.py:17
  51.8 27.0 %collective-permute-start.8 = (bf16[65,1024]{1,0:T(8,128)(2,1)}, bf16[65,1024]{1,0:T(8,128)(2,1)}, u32[]{:S(2)}, u32[]{:S(2)}) collective-permute-start(bf16[65,1024]{1,0:T(8,128)(2,1)} %fusion.21), channel_id=1, source_target_pairs={{0,3},{1,4},{2,5},{3,6},{4,7},{5,8},{6,9},{7,10},{8,11},{9,12},{10... | collective-permute-start | bytes 399368 | tf_op jit(solution)/shard_map/ppermute | solution.py:17
  55.3 23.4 %collective-permute-start.7 = (bf16[65,1024]{1,0:T(8,128)(2,1)}, bf16[65,1024]{1,0:T(8,128)(2,1)}, u32[]{:S(2)}, u32[]{:S(2)}) collective-permute-start(bf16[65,1024]{1,0:T(8,128)(2,1)} %fusion.21), channel_id=1, source_target_pairs={{2,0},{3,1},{4,2},{5,3},{6,4},{7,5},{8,6},{9,7},{10,8},{11,9},{12,... | collective-permute-start | bytes 399368 | tf_op jit(solution)/shard_map/ppermute | solution.py:17
  59.4 19.3 %collective-permute-start.6 = (bf16[65,1024]{1,0:T(8,128)(2,1)}, bf16[65,1024]{1,0:T(8,128)(2,1)}, u32[]{:S(2)}, u32[]{:S(2)}) collective-permute-start(bf16[65,1024]{1,0:T(8,128)(2,1)} %fusion.21), channel_id=1, source_target_pairs={{0,2},{1,3},{2,4},{3,5},{4,6},{5,7},{6,8},{7,9},{8,10},{9,11},{10,... | collective-permute-start | bytes 399368 | tf_op jit(solution)/shard_map/ppermute | solution.py:17
  61.3 17.4 %collective-permute-start.5 = (bf16[65,1024]{1,0:T(8,128)(2,1)}, bf16[65,1024]{1,0:T(8,128)(2,1)}, u32[]{:S(2)}, u32[]{:S(2)}) collective-permute-start(bf16[65,1024]{1,0:T(8,128)(2,1)} %fusion.21), channel_id=1, source_target_pairs={{1,0},{2,1},{3,2},{4,3},{5,4},{6,5},{7,6},{8,7},{9,8},{10,9},{11,1... | collective-permute-start | bytes 399368 | tf_op jit(solution)/shard_map/ppermute | solution.py:17
  65.4 13.4 %collective-permute-start.4 = (bf16[65,1024]{1,0:T(8,128)(2,1)}, bf16[65,1024]{1,0:T(8,128)(2,1)}, u32[]{:S(2)}, u32[]{:S(2)}) collective-permute-start(bf16[65,1024]{1,0:T(8,128)(2,1)} %fusion.21), channel_id=1, source_target_pairs={{0,1},{1,2},{2,3},{3,4},{4,5},{5,6},{6,7},{7,8},{8,9},{9,10},{10,1... | collective-permute-start | bytes 399368 | tf_op jit(solution)/shard_map/ppermute | solution.py:17
  82.5 6.7 %copy-start.18 = (s32[256,1]{0,1:T(1,128)S(1)}, s32[256,1]{0,1:T(1,128)}, u32[]{:S(2)}) copy-start(s32[256,1]{0,1:T(1,128)} %get-tuple-element.86) | copy-start | bytes 3076
  82.6 6.7 %copy-start.19 = (s32[256,1]{0,1:T(1,128)S(1)}, s32[256,1]{0,1:T(1,128)}, u32[]{:S(2)}) copy-start(s32[256,1]{0,1:T(1,128)} %get-tuple-element.87) | copy-start | bytes 3076
  82.6 7.5 %copy-start.17 = (f32[16,64]{1,0:T(8,128)S(1)}, f32[16,64]{1,0:T(8,128)}, u32[]{:S(2)}) copy-start(f32[16,64]{1,0:T(8,128)} %mul.68) | copy-start | bytes 12292
  89.3 3.6 %copy-start.12 = (f32[128,16,64]{0,2,1:T(8,128)S(1)}, f32[128,16,64]{0,2,1:T(8,128)}, u32[]{:S(2)}) copy-start(f32[128,16,64]{0,2,1:T(8,128)} %get-tuple-element.98) | copy-start | bytes 1572868
  89.3 3.9 %copy-start.11 = (f32[64,1024]{0,1:T(8,128)S(1)}, f32[64,1024]{0,1:T(8,128)}, u32[]{:S(2)}) copy-start(f32[64,1024]{0,1:T(8,128)} %copy.28) | copy-start | bytes 786436
  100.6 0.6 copy-start.14
  101.9 24.0 %collective-permute-start.15 = (bf16[65,1024]{1,0:T(8,128)(2,1)}, bf16[65,1024]{1,0:T(8,128)(2,1)S(1)}, u32[]{:S(2)}, u32[]{:S(2)}) collective-permute-start(bf16[65,1024]{1,0:T(8,128)(2,1)} %fusion.20), channel_id=1, source_target_pairs={{3,0},{4,1},{5,2},{6,3},{7,4},{8,5},{9,6},{10,7},{11,8},{12,9},{13... | collective-permute-start | bytes 399368 | tf_op jit(solution)/shard_map/ppermute | solution.py:17
  105.8 22.6 %collective-permute-start.14 = (bf16[65,1024]{1,0:T(8,128)(2,1)}, bf16[65,1024]{1,0:T(8,128)(2,1)}, u32[]{:S(2)}, u32[]{:S(2)}) collective-permute-start(bf16[65,1024]{1,0:T(8,128)(2,1)} %fusion.20), channel_id=1, source_target_pairs={{0,3},{1,4},{2,5},{3,6},{4,7},{5,8},{6,9},{7,10},{8,11},{9,12},{10... | collective-permute-start | bytes 399368 | tf_op jit(solution)/shard_map/ppermute | solution.py:17
  107.7 20.7 %collective-permute-start.13 = (bf16[65,1024]{1,0:T(8,128)(2,1)}, bf16[65,1024]{1,0:T(8,128)(2,1)}, u32[]{:S(2)}, u32[]{:S(2)}) collective-permute-start(bf16[65,1024]{1,0:T(8,128)(2,1)} %fusion.20), channel_id=1, source_target_pairs={{2,0},{3,1},{4,2},{5,3},{6,4},{7,5},{8,6},{9,7},{10,8},{11,9},{12,... | collective-permute-start | bytes 399368 | tf_op jit(solution)/shard_map/ppermute | solution.py:17
  113.6 14.9 %collective-permute-start.12 = (bf16[65,1024]{1,0:T(8,128)(2,1)}, bf16[65,1024]{1,0:T(8,128)(2,1)}, u32[]{:S(2)}, u32[]{:S(2)}) collective-permute-start(bf16[65,1024]{1,0:T(8,128)(2,1)} %fusion.20), channel_id=1, source_target_pairs={{0,2},{1,3},{2,4},{3,5},{4,6},{5,7},{6,8},{7,9},{8,10},{9,11},{10,... | collective-permute-start | bytes 399368 | tf_op jit(solution)/shard_map/ppermute | solution.py:17
  115.5 12.9 %collective-permute-start.11 = (bf16[65,1024]{1,0:T(8,128)(2,1)}, bf16[65,1024]{1,0:T(8,128)(2,1)}, u32[]{:S(2)}, u32[]{:S(2)}) collective-permute-start(bf16[65,1024]{1,0:T(8,128)(2,1)} %fusion.20), channel_id=1, source_target_pairs={{1,0},{2,1},{3,2},{4,3},{5,4},{6,5},{7,6},{8,7},{9,8},{10,9},{11,1... | collective-permute-start | bytes 399368 | tf_op jit(solution)/shard_map/ppermute | solution.py:17
  123.2 4.7 %copy-start.20 = (f32[256]{0:T(256)S(1)}, f32[256]{0:T(256)}, u32[]{:S(2)}) copy-start(f32[256]{0:T(256)} %get-tuple-element.82) | copy-start | bytes 3076
  123.2 11.2 %copy-start.15 = (f32[1024]{0:T(1024)S(1)}, f32[1024]{0:T(1024)}, u32[]{:S(2)}) copy-start(f32[1024]{0:T(1024)} %copy-done.14) | copy-start | bytes 12292
  125.9 8.5 %collective-permute-start.10 = (bf16[65,1024]{1,0:T(8,128)(2,1)}, bf16[65,1024]{1,0:T(8,128)(2,1)S(1)}, u32[]{:S(2)}, u32[]{:S(2)}) collective-permute-start(bf16[65,1024]{1,0:T(8,128)(2,1)} %fusion.20), channel_id=1, source_target_pairs={{0,1},{1,2},{2,3},{3,4},{4,5},{5,6},{6,7},{7,8},{8,9},{9,10},{10,1... | collective-permute-start | bytes 399368 | tf_op jit(solution)/shard_map/ppermute | solution.py:17
  138.7 1.0 copy-start.5
  139.7 2.8 %copy-start.4 = (bf16[8,128,2048]{2,1,0:T(8,128)(2,1)S(1)}, bf16[8,128,2048]{2,1,0:T(8,128)(2,1)}, u32[]{:S(2)}) copy-start(bf16[8,128,2048]{2,1,0:T(8,128)(2,1)} %copy-done.3) | copy-start | bytes 12582916
  139.7 3.1 %copy-start.10 = (bf16[16,64,512]{2,1,0:T(8,128)(2,1)S(1)}, bf16[16,64,512]{2,1,0:T(8,128)(2,1)}, u32[]{:S(2)}) copy-start(bf16[16,64,512]{2,1,0:T(8,128)(2,1)} %convolution_convert_fusion) | copy-start | bytes 3145732

commit v2 on v0

--- a/solution.py
+++ b/solution.py
@@ -63,15 +63,16 @@
     attended = numer / denom[:, :, None]
     weight_heads = score_weight.reshape(H, DH)
     scores = jnp.sum(attended * weight_heads[None], axis=(1, 2))
-    better = jnp.take(scores, pair_rows[:, 0])
-    worse = jnp.take(scores, pair_rows[:, 1])
+    slots = lax.broadcasted_iota(jnp.int32, (pair_rows.shape[0], count), 1)
+    is_better = slots == pair_rows[:, 0:1]
+    is_worse = slots == pair_rows[:, 1:2]
+    better = jnp.sum(jnp.where(is_better, scores[None, :], 0.0), axis=1)
+    worse = jnp.sum(jnp.where(is_worse, scores[None, :], 0.0), axis=1)
     delta = worse - better
     pair_loss = jax.nn.softplus(delta)
     push = jax.nn.sigmoid(delta)
-    slots = lax.broadcasted_iota(jnp.int32, (pair_rows.shape[0], count), 1)
     score_grad = jnp.sum(
-        jnp.where(slots == pair_rows[:, 1:2], push[:, None], 0.0)
-        - jnp.where(slots == pair_rows[:, 0:1], push[:, None], 0.0),
+        jnp.where(is_worse, push[:, None], 0.0) - jnp.where(is_better, push[:, None], 0.0),
         axis=0,
     )
     attended_grad = score_grad[:, None, None] * weight_heads[None]
@@ -93,16 +94,51 @@
     return (pair_loss, pose_grad.astype(jnp.bfloat16), pose_state)
 
 
+def gather_rows(shards):
+    count = lax.axis_size("blk")
+    rows = shards[0].shape[0]
+    if count > 16 or count % 2 or rows % 128:
+        full = tuple(lax.all_gather(part, "blk", axis=0, tiled=True) for part in shards)
+        return full, None
+    position = lax.axis_index("blk")
+    got = [shards] + [
+        lax.ppermute(shards, "blk", [(s, (s + 2 * k) % count) for s in range(count)])
+        for k in range(1, count // 2)
+    ]
+    sibling = lax.ppermute(got, "blk", [(s, s ^ 1) for s in range(count)])
+    pieces = got + sibling
+    full = tuple(
+        jnp.concatenate([piece[i] for piece in pieces], axis=0) for i in range(len(shards))
+    )
+    half = count // 2
+    source = [(position - 2 * k) % count for k in range(half)] + [
+        ((position ^ 1) - 2 * k) % count for k in range(half)
+    ]
+    slot = [
+        jnp.where(
+            (s - position) % 2 == 0,
+            ((position - s) % count) // 2,
+            half + (((position ^ 1) - s) % count) // 2,
+        )
+        for s in range(count)
+    ]
+    return full, (source, slot, rows)
+
+
+def reorder_columns(values, order, rows):
+    return jnp.concatenate(
+        [lax.dynamic_slice_in_dim(values, where * rows, rows, axis=1) for where in order], axis=1
+    )
+
+
 def shards(receptor, poses, pairs, block_complex, w_key, w_value, w_query, score_weight):
     rows = receptor.shape[0]
     width = receptor.shape[1]
     contract = (((1,), (1,)), ((), ()))
-    full_key, full_value = (
-        lax.all_gather(w_key, "blk", axis=0, tiled=True),
-        lax.all_gather(w_value, "blk", axis=0, tiled=True),
-    )
-    keys = jnp.dot(receptor, full_key, preferred_element_type=jnp.float32)
-    values = jnp.dot(receptor, full_value, preferred_element_type=jnp.float32)
+    (full_key, full_value), order = gather_rows((w_key, w_value))
+    moved = receptor if order is None else reorder_columns(receptor, order[0], order[2])
+    keys = jnp.dot(moved, full_key, preferred_element_type=jnp.float32)
+    values = jnp.dot(moved, full_value, preferred_element_type=jnp.float32)
     key_feat = features(keys).astype(jnp.bfloat16)
     val_round = values.astype(jnp.bfloat16)
     state = complex_total(local_state(key_feat, val_round), block_complex)
@@ -126,7 +162,10 @@
     total = total + lax.dot_general(
         value_grad, full_value, contract, preferred_element_type=jnp.float32
     )
-    return (pair_loss, pose_grad, total.astype(jnp.bfloat16))
+    total = total.astype(jnp.bfloat16)
+    if order is not None:
+        total = reorder_columns(total, order[1], order[2])
+    return (pair_loss, pose_grad, total)
 
 
 def solution(mesh):

time: 190 us -> 156 us (0.82)
  waiting for transfers between devices: 57.2 us -> 15.4 us
  local copies, waits for them, and re-layouts: 26.5 us -> 48.6 us
  between operations: 18.9 us -> 5.62 us
  other arithmetic: 11.4 us -> 7.48 us
  starting transfers between devices: 39.8 us -> 43.4 us
    all_gather x2 -> x0, waiting for transfers between devices: 50.1 us -> none  [the longest x1 25.9 us: shards(): lax.all_gather(w_value, 'blk', axis=0, tiled=True)]
    unnamed x26 -> x64, local copies, waits for them, and re-layouts: 0.64 us -> 24.4 us
    ppermute x0 -> x14, starting transfers between devices: none -> 9.18 us  [the longest x6 7.45 us: gather_rows(): lax.ppermute(shards, 'blk', [(s, (s + 2 * k) % count) for s in range(coun...]
    ppermute x0 -> x14, waiting for transfers between devices: none -> 6.42 us  [the longest x6 5.33 us: gather_rows(): lax.ppermute(shards, 'blk', [(s, (s + 2 * k) % count) for s in range(coun...]
    ppermute x12, starting transfers between devices: 39.7 us -> 34.2 us  [from_behind(): lax.ppermute(value, axis, [(source, source + steps) for source in range(i...]
    gather x2 -> x0, local copies, waits for them, and re-layouts: 4.01 us -> none  [the longest x1 2 us: pose_side(): worse = jnp.take(scores, pair_rows[:, 1])]
    ppermute x12, waiting for transfers between devices: 5.78 us -> 8.99 us  [from_behind(): lax.ppermute(value, axis, [(source, source + steps) for source in range(i...]
    concatenate x0 -> x4, local copies, waits for them, and re-layouts: none -> 2.46 us  [the longest x2 1.71 us: gather_rows(): jnp.concatenate([piece[i] for piece in pieces], axis=0)]
  transfers between devices with their start and end apart: 14 -> 26, of which waited for: 3 -> 5; matrix products, arithmetic and copies ran while one was open for 12% -> 28% of each run, Pallas kernels for 0% -> 0%
where the time goes in v2:
time: 156 us; the launch traced here: 154 us
  local copies, waits for them, and re-layouts  48.6 us (31%)
  starting transfers between devices  43.4 us (28%)
  matrix products  33.9 us (22%)
  waiting for transfers between devices  15.4 us (10%)
  other arithmetic  7.48 us (5%)
  between operations  5.62 us (4%)
    ppermute x12, starting transfers between devices, from_behind(): lax.ppermute(value, axis, [(source, source + steps) for source in range(i...  34.2 us
    unnamed x64, local copies, waits for them, and re-layouts  24.4 us
    ppermute x12, waiting for transfers between devices, from_behind(): lax.ppermute(value, axis, [(source, source + steps) for source in range(i...  8.99 us
    ppermute x6, starting transfers between devices, gather_rows(): lax.ppermute(shards, 'blk', [(s, (s + 2 * k) % count) for s in range(coun...  7.45 us
    ppermute x6, waiting for transfers between devices, gather_rows(): lax.ppermute(shards, 'blk', [(s, (s + 2 * k) % count) for s in range(coun...  5.33 us
    dot_general x1, matrix products, shards(): keys = jnp.dot(moved, full_key, preferred_element_type=jnp.float32)  5.04 us
    dot_general x1, matrix products, shards(): lax.dot_general(key_grad, full_key, contract, preferred_element_type=jnp....  4.76 us
    dot_general x1, matrix products, shards(): values = jnp.dot(moved, full_value, preferred_element_type=jnp.float32)  3.48 us
  transfers between devices with their start and end apart: 26, of which 5 were waited for; matrix products, arithmetic and copies ran while one was open for 28% of the time, Pallas kernels for 0%

profile of v2, /device:TPU:16, one launch (start us, length us, event | category | flops | bytes accessed | tf_op | source)
XLA Modules:
  0.0 154.4 jit_solution(16981529185463043625)
XLA Ops:
  0.7 2.5 %collective-permute-start.9 = (bf16[128,1024]{1,0:T(8,128)(2,1)}, bf16[128,1024]{1,0:T(8,128)(2,1)}, u32[]{:S(2)}, u32[]{:S(2)}) collective-permute-start(bf16[128,1024]{1,0:T(8,128)(2,1)} %param.12), channel_id=1, source_target_pairs={{0,6},{1,7},{2,0},{3,1},{4,2},{5,3},{6,4},{7,5},{8,14},{9,15},{10,... | collective-permute-start | bytes 786440 | tf_op jit(solution)/shard_map/ppermute | solution.py:105
  4.3 2.3 %collective-permute-start.2 = (bf16[128,1024]{1,0:T(8,128)(2,1)}, bf16[128,1024]{1,0:T(8,128)(2,1)}, u32[]{:S(2)}, u32[]{:S(2)}) collective-permute-start(bf16[128,1024]{1,0:T(8,128)(2,1)} %param.13), channel_id=1, source_target_pairs={{0,6},{1,7},{2,0},{3,1},{4,2},{5,3},{6,4},{7,5},{8,14},{9,15},{10,... | collective-permute-start | bytes 786440 | tf_op jit(solution)/shard_map/ppermute | solution.py:105
  6.6 1.7 %constant_dynamic-update-slice_fusion.15 = bf16[1024,1024]{1,0:T(8,128)(2,1)} fusion(bf16[128,1024]{1,0:T(8,128)(2,1)} %param.12), kind=kLoop, calls=%fused_computation.77 | loop fusion | bytes 524288
  8.3 1.7 %constant_dynamic-update-slice_fusion.7 = bf16[1024,1024]{1,0:T(8,128)(2,1)} fusion(bf16[128,1024]{1,0:T(8,128)(2,1)} %param.13), kind=kLoop, calls=%fused_computation.69 | loop fusion | bytes 524288
  9.9 1.6 %dynamic-slice_dynamic-update-slice_fusion.15 = bf16[512,1024]{1,0:T(8,128)(2,1)} fusion(bf16[512,1024]{1,0:T(8,128)(2,1)} %param.8, s32[]{:T(128)S(6)} %select_n.383), kind=kLoop, calls=%fused_computation.60 | loop fusion | bytes 262148
  11.5 1.6 %dynamic-slice_dynamic-update-slice_fusion.14 = bf16[512,1024]{1,0:T(8,128)(2,1)} fusion(bf16[512,1024]{1,0:T(8,128)(2,1)} %dynamic-slice_dynamic-update-slice_fusion.15, bf16[512,1024]{1,0:T(8,128)(2,1)} %param.8, s32[]{:T(128)S(6)} %select_n.385), kind=kLoop, calls=%fused_computation.59 | loop fusion | bytes 262148
  13.1 1.6 %dynamic-slice_dynamic-update-slice_fusion.13 = bf16[512,1024]{1,0:T(8,128)(2,1)} fusion(bf16[512,1024]{1,0:T(8,128)(2,1)} %dynamic-slice_dynamic-update-slice_fusion.14, bf16[512,1024]{1,0:T(8,128)(2,1)} %param.8, s32[]{:T(128)S(6)} %select_n.387), kind=kLoop, calls=%fused_computation.58 | loop fusion | bytes 262148
  18.1 1.5 collective-permute-start.1
  19.6 1.7 %constant_dynamic-update-slice_fusion.14 = bf16[1024,1024]{1,0:T(8,128)(2,1)} fusion(bf16[1024,1024]{1,0:T(8,128)(2,1)} %constant_dynamic-update-slice_fusion.15, bf16[128,1024]{1,0:T(8,128)(2,1)} %collective-permute-done.7), kind=kLoop, calls=%fused_computation.76 | loop fusion | bytes 524288
  21.3 1.7 %constant_dynamic-update-slice_fusion.13 = bf16[1024,1024]{1,0:T(8,128)(2,1)} fusion(bf16[1024,1024]{1,0:T(8,128)(2,1)} %constant_dynamic-update-slice_fusion.14, bf16[128,1024]{1,0:T(8,128)(2,1)} %collective-permute-done.8), kind=kLoop, calls=%fused_computation.75 | loop fusion | bytes 524288
  23.0 1.7 %constant_dynamic-update-slice_fusion.12 = bf16[1024,1024]{1,0:T(8,128)(2,1)} fusion(bf16[1024,1024]{1,0:T(8,128)(2,1)} %constant_dynamic-update-slice_fusion.13, bf16[128,1024]{1,0:T(8,128)(2,1)} %collective-permute-done.9), kind=kLoop, calls=%fused_computation.74 | loop fusion | bytes 524288
  25.2 1.7 %constant_dynamic-update-slice_fusion.11 = bf16[1024,1024]{1,0:T(8,128)(2,1)} fusion(bf16[1024,1024]{1,0:T(8,128)(2,1)} %constant_dynamic-update-slice_fusion.12, bf16[128,1024]{1,0:T(8,128)(2,1)} %collective-permute-done.10), kind=kLoop, calls=%fused_computation.73 | loop fusion | bytes 524288
  26.8 3.6 %collective-permute-done = bf16[128,1024]{1,0:T(8,128)(2,1)S(1)} collective-permute-done((bf16[128,1024]{1,0:T(8,128)(2,1)S(1)}, bf16[128,1024]{1,0:T(8,128)(2,1)S(1)}, u32[]{:S(2)}, u32[]{:S(2)}) %collective-permute-start) | collective-permute-done | bytes 262176 | tf_op jit(solution)/shard_map/ppermute | solution.py:105
  30.5 1.7 %collective-permute-done.1 = bf16[128,1024]{1,0:T(8,128)(2,1)S(1)} collective-permute-done((bf16[128,1024]{1,0:T(8,128)(2,1)S(1)}, bf16[128,1024]{1,0:T(8,128)(2,1)S(1)}, u32[]{:S(2)}, u32[]{:S(2)}) %collective-permute-start.1) | collective-permute-done | bytes 262176 | tf_op jit(solution)/shard_map/ppermute | solution.py:105
  36.9 3.5 %convolution_convert_fusion.1 = bf16[512,1024]{1,0:T(8,128)(2,1)} fusion(bf16[512,1024]{1,0:T(8,128)(2,1)} %dynamic-slice_dynamic-update-slice_fusion.8, bf16[1024,1024]{1,0:T(8,128)(2,1)S(1)} %constant_dynamic-update-slice_fusion), kind=kOutput, calls=%fused_computation.7 | convolution fusion | flops 1074266112 | bytes 4194304 | tf_op jit(solution)/shard_map/dot_general | solution.py:141
  42.6 1.7 %constant_dynamic-update-slice_fusion.9 = bf16[1024,1024]{1,0:T(8,128)(2,1)} fusion(bf16[1024,1024]{1,0:T(8,128)(2,1)} %constant_dynamic-update-slice_fusion.10, bf16[128,1024]{1,0:T(8,128)(2,1)} %collective-permute-done.12), kind=kLoop, calls=%fused_computation.71 | loop fusion | bytes 524288
  44.4 1.7 %constant_dynamic-update-slice_fusion.8 = bf16[1024,1024]{1,0:T(8,128)(2,1)} fusion(bf16[1024,1024]{1,0:T(8,128)(2,1)} %constant_dynamic-update-slice_fusion.9, bf16[128,1024]{1,0:T(8,128)(2,1)} %collective-permute-done.13), kind=kLoop, calls=%fused_computation.70 | loop fusion | bytes 524288 | tf_op jit(solution)/shard_map/concatenate | solution.py:111
  46.1 5.0 %convert_reduce_fusion = (f32[1024]{0:T(1024)S(1)}, bf16[512,1024]{1,0:T(8,128)(2,1)}, f32[512,1024]{1,0:T(8,128)}) fusion(bf16[512,1024]{1,0:T(8,128)(2,1)} %dynamic-slice_dynamic-update-slice_fusion.8, bf16[1024,1024]{1,0:T(8,128)(2,1)} %constant_dynamic-update-slice_fusion.8), kind=kOutput, calls=%fused_computation.2 | convolution fusion | flops 1077410816 | bytes 6295552 | tf_op jit(solution)/shard_map/dot_general | solution.py:140
  51.1 2.3 %copy.36 = bf16[512,1024]{0,1:T(8,128)(2,1)} copy(bf16[512,1024]{1,0:T(8,128)(2,1)} %get-tuple-element.83) | data formatting | bytes 2097152 | tf_op jit(solution)/shard_map/convert_element_type | solution.py:142
  53.4 2.4 %fusion.23 = f32[16,64,64]{2,1,0:T(8,128)} fusion(bf16[512,16,64]{0,2,1:T(8,128)(2,1)S(1)} %bitcast.65, bf16[512,16,64]{0,2,1:T(8,128)(2,1)} %bitcast.67), kind=kOutput, calls=%fused_computation.90 | convolution fusion | flops 67108864 | bytes 2359296 | tf_op jit(solution)/shard_map/thd,the->dhe/dot_general | solution.py:32
  57.7 3.0 %collective-permute-start.19 = (bf16[65,1024]{1,0:T(8,128)(2,1)}, bf16[65,1024]{1,0:T(8,128)(2,1)S(1)}, u32[]{:S(2)}, u32[]{:S(2)}) collective-permute-start(bf16[65,1024]{1,0:T(8,128)(2,1)} %fusion.15), channel_id=1, source_target_pairs={{3,0},{4,1},{5,2},{6,3},{7,4},{8,5},{9,6},{10,7},{11,8},{12,9},{13... | collective-permute-start | bytes 399368 | tf_op jit(solution)/shard_map/ppermute | solution.py:17
  60.8 2.4 %add_select_fusion = (f32[128,1024]{1,0:T(8,128)}, f32[128,1024]{1,0:T(8,128)}) fusion(bf16[128,1024]{1,0:T(8,128)(2,1)} %param.9, bf16[1024,1024]{1,0:T(8,128)(2,1)S(1)} %copy-done), kind=kOutput, calls=%fused_computation.24 | convolution fusion | flops 268959744 | bytes 3407872 | tf_op jit(solution)/shard_map/dot_general | solution.py:57
  63.2 1.6 %fusion.22 = (s32[1]{0:T(128)}, s32[1]{0:T(128)}, s32[1]{0:T(128)}, s32[1]{0:T(128)}, s32[1]{0:T(128)}, /*index=5*/s32[1]{0:T(128)}, s32[1]{0:T(128)}) fusion(s32[32]{0:T(128)} %param.11, s32[]{:T(128)S(6)} %max.20, s32[]{:T(128)S(6)} %select_n.411, s32[]{:T(128)S(6)} %max.21, s32[]{:T(128)S(6)} %select_n.404, s32[]{:T(128)S(6)} %select_n.400, ...), kind=kLoop, calls=%fused_computation.89 | loop fusion | bytes 84 | solution.py:47
  70.6 2.1 %copy.39 = f32[128,1024]{0,1:T(8,128)} copy(f32[128,1024]{1,0:T(8,128)} %get-tuple-element.96) | data formatting | bytes 1048576 | tf_op jit(solution)/shard_map/jit(_where)/select_n | solution.py:21
  72.6 2.5 %collective-permute-start.18 = (bf16[65,1024]{1,0:T(8,128)(2,1)}, bf16[65,1024]{1,0:T(8,128)(2,1)S(1)}, u32[]{:S(2)}, u32[]{:S(2)}) collective-permute-start(bf16[65,1024]{1,0:T(8,128)(2,1)} %fusion.15), channel_id=1, source_target_pairs={{0,3},{1,4},{2,5},{3,6},{4,7},{5,8},{6,9},{7,10},{8,11},{9,12},{10... | collective-permute-start | bytes 399368 | tf_op jit(solution)/shard_map/ppermute | solution.py:17
  75.1 3.7 %collective-permute-start.17 = (bf16[65,1024]{1,0:T(8,128)(2,1)}, bf16[65,1024]{1,0:T(8,128)(2,1)S(1)}, u32[]{:S(2)}, u32[]{:S(2)}) collective-permute-start(bf16[65,1024]{1,0:T(8,128)(2,1)} %fusion.15), channel_id=1, source_target_pairs={{2,0},{3,1},{4,2},{5,3},{6,4},{7,5},{8,6},{9,7},{10,8},{11,9},{12,... | collective-permute-start | bytes 399368 | tf_op jit(solution)/shard_map/ppermute | solution.py:17
  78.9 2.1 %collective-permute-start.16 = (bf16[65,1024]{1,0:T(8,128)(2,1)}, bf16[65,1024]{1,0:T(8,128)(2,1)S(1)}, u32[]{:S(2)}, u32[]{:S(2)}) collective-permute-start(bf16[65,1024]{1,0:T(8,128)(2,1)} %fusion.15), channel_id=1, source_target_pairs={{0,2},{1,3},{2,4},{3,5},{4,6},{5,7},{6,8},{7,9},{8,10},{9,11},{10,... | collective-permute-start | bytes 399368 | tf_op jit(solution)/shard_map/ppermute | solution.py:17
  81.0 4.0 %collective-permute-start.15 = (bf16[65,1024]{1,0:T(8,128)(2,1)}, bf16[65,1024]{1,0:T(8,128)(2,1)S(1)}, u32[]{:S(2)}, u32[]{:S(2)}) collective-permute-start(bf16[65,1024]{1,0:T(8,128)(2,1)} %fusion.15), channel_id=1, source_target_pairs={{1,0},{2,1},{3,2},{4,3},{5,4},{6,5},{7,6},{8,7},{9,8},{10,9},{11,1... | collective-permute-start | bytes 399368 | tf_op jit(solution)/shard_map/ppermute | solution.py:17
  85.0 1.9 %collective-permute-start.14 = (bf16[65,1024]{1,0:T(8,128)(2,1)}, bf16[65,1024]{1,0:T(8,128)(2,1)S(1)}, u32[]{:S(2)}, u32[]{:S(2)}) collective-permute-start(bf16[65,1024]{1,0:T(8,128)(2,1)} %fusion.15), channel_id=1, source_target_pairs={{0,1},{1,2},{2,3},{3,4},{4,5},{5,6},{6,7},{7,8},{8,9},{9,10},{10,1... | collective-permute-start | bytes 399368 | tf_op jit(solution)/shard_map/ppermute | solution.py:17
  88.3 5.2 %collective-permute-done.14 = bf16[65,1024]{1,0:T(8,128)(2,1)S(1)} collective-permute-done((bf16[65,1024]{1,0:T(8,128)(2,1)}, bf16[65,1024]{1,0:T(8,128)(2,1)S(1)}, u32[]{:S(2)}, u32[]{:S(2)}) %collective-permute-start.14) | collective-permute-done | bytes 133152 | tf_op jit(solution)/shard_map/ppermute | solution.py:17
  96.8 1.9 %multiply_reduce_fusion.1 = (f32[128]{0:T(128)S(1)}, f32[128,16,64]{0,2,1:T(8,128)S(1)}) fusion(f32[16,64]{1,0:T(8,128)} %mul.124, f32[128,16]{0,1:T(8,128)S(1)} %multiply_reduce_fusion.2, f32[64,16,64]{0,2,1:T(8,128)} %bitcast.77, f32[128,16,64]{0,2,1:T(8,128)} %bitcast.73), kind=kOutput, calls=%fused_computation.21 | convolution fusion | flops 101056384 | bytes 1323520 | tf_op jit(solution)/shard_map/phd,dhe->phe/dot_general | solution.py:61
  99.8 1.8 %fusion.5 = f32[16,64,64]{2,1,0:T(8,128)} fusion(f32[128,16,64]{0,2,1:T(8,128)S(1)} %bitcast.74, f32[128]{0:T(128)S(1)} %subtract_reduce_fusion, f32[16,64]{1,0:T(8,128)S(1)} %copy-done.8, f32[128,16]{0,1:T(8,128)S(1)} %multiply_reduce_fusion.2), kind=kOutput, calls=%fused_computation.25 | convolution fusion | flops 100925440 | bytes 799232 | tf_op jit(solution)/shard_map/phd,phe->dhe/dot_general | solution.py:81
  104.0 2.1 %copy.42 = f32[128,1024]{1,0:T(8,128)} copy(f32[128,1024]{0,1:T(8,128)} %bitcast.75) | data formatting | bytes 1048576 | tf_op jit(solution)/shard_map/mul | solution.py:88
  108.7 1.9 %collective-permute-start.25 = (bf16[65,1024]{1,0:T(8,128)(2,1)}, bf16[65,1024]{1,0:T(8,128)(2,1)S(1)}, u32[]{:S(2)}, u32[]{:S(2)}) collective-permute-start(bf16[65,1024]{1,0:T(8,128)(2,1)} %fusion.14), channel_id=1, source_target_pairs={{3,0},{4,1},{5,2},{6,3},{7,4},{8,5},{9,6},{10,7},{11,8},{12,9},{13... | collective-permute-start | bytes 399368 | tf_op jit(solution)/shard_map/ppermute | solution.py:17
  110.6 3.6 %collective-permute-start.24 = (bf16[65,1024]{1,0:T(8,128)(2,1)}, bf16[65,1024]{1,0:T(8,128)(2,1)}, u32[]{:S(2)}, u32[]{:S(2)}) collective-permute-start(bf16[65,1024]{1,0:T(8,128)(2,1)} %fusion.14), channel_id=1, source_target_pairs={{0,3},{1,4},{2,5},{3,6},{4,7},{5,8},{6,9},{7,10},{8,11},{9,12},{10... | collective-permute-start | bytes 399368 | tf_op jit(solution)/shard_map/ppermute | solution.py:17
  114.2 3.5 %collective-permute-start.23 = (bf16[65,1024]{1,0:T(8,128)(2,1)}, bf16[65,1024]{1,0:T(8,128)(2,1)}, u32[]{:S(2)}, u32[]{:S(2)}) collective-permute-start(bf16[65,1024]{1,0:T(8,128)(2,1)} %fusion.14), channel_id=1, source_target_pairs={{2,0},{3,1},{4,2},{5,3},{6,4},{7,5},{8,6},{9,7},{10,8},{11,9},{12,... | collective-permute-start | bytes 399368 | tf_op jit(solution)/shard_map/ppermute | solution.py:17
  117.7 2.4 %collective-permute-start.22 = (bf16[65,1024]{1,0:T(8,128)(2,1)}, bf16[65,1024]{1,0:T(8,128)(2,1)}, u32[]{:S(2)}, u32[]{:S(2)}) collective-permute-start(bf16[65,1024]{1,0:T(8,128)(2,1)} %fusion.14), channel_id=1, source_target_pairs={{0,2},{1,3},{2,4},{3,5},{4,6},{5,7},{6,8},{7,9},{8,10},{9,11},{10,... | collective-permute-start | bytes 399368 | tf_op jit(solution)/shard_map/ppermute | solution.py:17
  120.1 3.6 %collective-permute-start.21 = (bf16[65,1024]{1,0:T(8,128)(2,1)}, bf16[65,1024]{1,0:T(8,128)(2,1)}, u32[]{:S(2)}, u32[]{:S(2)}) collective-permute-start(bf16[65,1024]{1,0:T(8,128)(2,1)} %fusion.14), channel_id=1, source_target_pairs={{1,0},{2,1},{3,2},{4,3},{5,4},{6,5},{7,6},{8,7},{9,8},{10,9},{11,1... | collective-permute-start | bytes 399368 | tf_op jit(solution)/shard_map/ppermute | solution.py:17
  123.7 3.1 %fusion = f32[128,16,64]{0,2,1:T(8,128)} fusion(f32[64,16,64]{0,2,1:T(8,128)} %bitcast.78, f32[128,16]{0,1:T(8,128)} %copy-done.7, f32[128]{0:T(128)} %copy-done.17, f32[16,64]{1,0:T(8,128)} %mul.124, f32[128,16]{0,1:T(8,128)} %copy-done.6, f32[16,64]{1,0:T(8,128)} %copy-done.9), kind=kOutput, calls=%fused_computation.9 | convolution fusion | flops 101187584 | bytes 811520 | tf_op jit(solution)/shard_map/phe,dhe->phd/dot_general | solution.py:87
  126.8 2.0 %copy.41 = f32[128,1024]{1,0:T(8,128)} copy(f32[128,1024]{0,1:T(8,128)} %bitcast.80) | data formatting | bytes 1048576 | tf_op jit(solution)/shard_map/reshape | solution.py:90
  128.8 1.9 %collective-permute-start.20 = (bf16[65,1024]{1,0:T(8,128)(2,1)}, bf16[65,1024]{1,0:T(8,128)(2,1)S(1)}, u32[]{:S(2)}, u32[]{:S(2)}) collective-permute-start(bf16[65,1024]{1,0:T(8,128)(2,1)} %fusion.14), channel_id=1, source_target_pairs={{0,1},{1,2},{2,3},{3,4},{4,5},{5,6},{6,7},{7,8},{8,9},{9,10},{10,1... | collective-permute-start | bytes 399368 | tf_op jit(solution)/shard_map/ppermute | solution.py:17
  130.7 2.7 %convolution_convert_fusion.2 = bf16[128,1024]{1,0:T(8,128)(2,1)} fusion(bf16[1024,1024]{1,0:T(8,128)(2,1)S(1)} %copy-done, f32[128,1024]{1,0:T(8,128)} %copy.41, f32[128,1024]{1,0:T(8,128)} %get-tuple-element.97), kind=kOutput, calls=%fused_computation.12 | convolution fusion | flops 269221888 | bytes 3407872 | tf_op jit(solution)/shard_map/dot_general | solution.py:91
  133.5 3.8 %collective-permute-done.20 = bf16[65,1024]{1,0:T(8,128)(2,1)S(1)} collective-permute-done((bf16[65,1024]{1,0:T(8,128)(2,1)}, bf16[65,1024]{1,0:T(8,128)(2,1)S(1)}, u32[]{:S(2)}, u32[]{:S(2)}) %collective-permute-start.20) | collective-permute-done | bytes 133152 | tf_op jit(solution)/shard_map/ppermute | solution.py:17
  138.9 1.8 %convolution_convert_fusion = bf16[16,64,512]{2,1,0:T(8,128)(2,1)S(1)} fusion(bf16[64,16,64]{0,2,1:T(8,128)(2,1)S(1)} %bitcast.70, bf16[512,16,64]{0,2,1:T(8,128)(2,1)} %bitcast.68), kind=kOutput, calls=%fused_computation.6 | convolution fusion | flops 67633152 | bytes 2228224 | tf_op jit(solution)/shard_map/thd,dhe->the/dot_general | solution.py:157
  140.8 2.6 %fusion.24 = f32[512,1024]{1,0:T(8,128)} fusion(bf16[512,1024]{0,1:T(8,128)(2,1)S(1)} %bitcast.76, bf16[1024,1024]{1,0:T(8,128)(2,1)S(1)} %copy-done.12), kind=kOutput, calls=%fused_computation.91 | convolution fusion | flops 1073741824 | bytes 5242880 | tf_op jit(solution)/shard_map/dot_general | solution.py:162
  143.4 1.9 %convolution_add_fusion = f32[16,64,512]{2,1,0:T(8,128)} fusion(bf16[64,16,64]{0,2,1:T(8,128)(2,1)S(1)} %bitcast.71, bf16[512,16,64]{0,2,1:T(8,128)(2,1)S(1)} %bitcast.66, f32[16,64]{1,0:T(8,128)S(1)} %reshape.272), kind=kOutput, calls=%fused_computation.5 | convolution fusion | flops 67633152 | bytes 3280896 | tf_op jit(solution)/shard_map/the,dhe->thd/dot_general | solution.py:152
  145.3 2.9 %copy.45 = f32[512,1024]{1,0:T(8,128)} copy(f32[512,1024]{0,1:T(8,128)} %bitcast.69) | data formatting | bytes 4194304 | tf_op jit(solution)/shard_map/reshape | solution.py:155
  148.2 4.8 %add_convert_fusion = bf16[512,1024]{1,0:T(8,128)(2,1)S(1)} fusion(f32[512,1024]{1,0:T(8,128)} %fusion.24, bf16[1024,1024]{1,0:T(8,128)(2,1)} %constant_dynamic-update-slice_fusion.8, f32[512,1024]{1,0:T(8,128)} %copy.45, f32[512,1024]{1,0:T(8,128)} %get-tuple-element.95), kind=kOutput, calls=%fused_computation | convolution fusion | flops 1077411840 | bytes 9437184 | tf_op jit(solution)/shard_map/dot_general | solution.py:161
  (115 shorter events, 29.0 us)
Async XLA Ops:
  0.6 60.2 %copy-start = (bf16[1024,1024]{1,0:T(8,128)(2,1)S(1)}, bf16[1024,1024]{1,0:T(8,128)(2,1)}, u32[]{:S(2)}) copy-start(bf16[1024,1024]{1,0:T(8,128)(2,1)} %param.14) | copy-start | bytes 6291460
  0.6 17.5 %copy-start.3 = (bf16[128,1024]{1,0:T(8,128)(2,1)S(1)}, bf16[128,1024]{1,0:T(8,128)(2,1)}, u32[]{:S(2)}) copy-start(bf16[128,1024]{1,0:T(8,128)(2,1)} %param.13) | copy-start | bytes 786436
  0.7 14.0 %copy-start.2 = (bf16[512,1024]{1,0:T(8,128)(2,1)S(1)}, bf16[512,1024]{1,0:T(8,128)(2,1)}, u32[]{:S(2)}) copy-start(bf16[512,1024]{1,0:T(8,128)(2,1)} %param.8) | copy-start | bytes 3145732
  0.7 22.3 %collective-permute-start.9 = (bf16[128,1024]{1,0:T(8,128)(2,1)}, bf16[128,1024]{1,0:T(8,128)(2,1)}, u32[]{:S(2)}, u32[]{:S(2)}) collective-permute-start(bf16[128,1024]{1,0:T(8,128)(2,1)} %param.12), channel_id=1, source_target_pairs={{0,6},{1,7},{2,0},{3,1},{4,2},{5,3},{6,4},{7,5},{8,14},{9,15},{10,... | collective-permute-start | bytes 786440 | tf_op jit(solution)/shard_map/ppermute | solution.py:105
  3.2 18.1 %collective-permute-start.8 = (bf16[128,1024]{1,0:T(8,128)(2,1)}, bf16[128,1024]{1,0:T(8,128)(2,1)}, u32[]{:S(2)}, u32[]{:S(2)}) collective-permute-start(bf16[128,1024]{1,0:T(8,128)(2,1)} %param.12), channel_id=1, source_target_pairs={{0,4},{1,5},{2,6},{3,7},{4,0},{5,1},{6,2},{7,3},{8,12},{9,13},{10,... | collective-permute-start | bytes 786440 | tf_op jit(solution)/shard_map/ppermute | solution.py:105
  3.7 14.4 %collective-permute-start.7 = (bf16[128,1024]{1,0:T(8,128)(2,1)}, bf16[128,1024]{1,0:T(8,128)(2,1)}, u32[]{:S(2)}, u32[]{:S(2)}) collective-permute-start(bf16[128,1024]{1,0:T(8,128)(2,1)} %param.12), channel_id=1, source_target_pairs={{0,2},{1,3},{2,4},{3,5},{4,6},{5,7},{6,0},{7,1},{8,10},{9,11},{10,... | collective-permute-start | bytes 786440 | tf_op jit(solution)/shard_map/ppermute | solution.py:105
  4.3 20.4 %collective-permute-start.10 = (bf16[128,1024]{1,0:T(8,128)(2,1)}, bf16[128,1024]{1,0:T(8,128)(2,1)}, u32[]{:S(2)}, u32[]{:S(2)}) collective-permute-start(bf16[128,1024]{1,0:T(8,128)(2,1)} %param.12), channel_id=1, source_target_pairs={{0,1},{1,0},{2,3},{3,2},{4,5},{5,4},{6,7},{7,6},{8,9},{9,8},{10,11... | collective-permute-start | bytes 786440 | tf_op jit(solution)/shard_map/ppermute | solution.py:108
  4.3 27.9 %collective-permute-start.2 = (bf16[128,1024]{1,0:T(8,128)(2,1)}, bf16[128,1024]{1,0:T(8,128)(2,1)}, u32[]{:S(2)}, u32[]{:S(2)}) collective-permute-start(bf16[128,1024]{1,0:T(8,128)(2,1)} %param.13), channel_id=1, source_target_pairs={{0,6},{1,7},{2,0},{3,1},{4,2},{5,3},{6,4},{7,5},{8,14},{9,15},{10,... | collective-permute-start | bytes 786440 | tf_op jit(solution)/shard_map/ppermute | solution.py:105
  17.4 13.1 %copy-start.10 = (bf16[1024,1024]{1,0:T(8,128)(2,1)S(1)}, bf16[1024,1024]{1,0:T(8,128)(2,1)}, u32[]{:S(2)}) copy-start(bf16[1024,1024]{1,0:T(8,128)(2,1)} %constant_dynamic-update-slice_fusion.7) | copy-start | bytes 6291460
  18.1 14.1 %collective-permute-start.1 = (bf16[128,1024]{1,0:T(8,128)(2,1)S(1)}, bf16[128,1024]{1,0:T(8,128)(2,1)S(1)}, u32[]{:S(2)}, u32[]{:S(2)}) collective-permute-start(bf16[128,1024]{1,0:T(8,128)(2,1)S(1)} %copy-done.3), channel_id=1, source_target_pairs={{0,4},{1,5},{2,6},{3,7},{4,0},{5,1},{6,2},{7,3},{8,12},{9,13},{10,... | collective-permute-start | bytes 786440 | tf_op jit(solution)/shard_map/ppermute | solution.py:105
  21.3 9.2 %collective-permute-start = (bf16[128,1024]{1,0:T(8,128)(2,1)S(1)}, bf16[128,1024]{1,0:T(8,128)(2,1)S(1)}, u32[]{:S(2)}, u32[]{:S(2)}) collective-permute-start(bf16[128,1024]{1,0:T(8,128)(2,1)S(1)} %copy-done.3), channel_id=1, source_target_pairs={{0,2},{1,3},{2,4},{3,5},{4,6},{5,7},{6,0},{7,1},{8,10},{9,11},{10,... | collective-permute-start | bytes 786440 | tf_op jit(solution)/shard_map/ppermute | solution.py:105
  23.0 10.8 %collective-permute-start.3 = (bf16[128,1024]{1,0:T(8,128)(2,1)S(1)}, bf16[128,1024]{1,0:T(8,128)(2,1)S(1)}, u32[]{:S(2)}, u32[]{:S(2)}) collective-permute-start(bf16[128,1024]{1,0:T(8,128)(2,1)S(1)} %copy-done.3), channel_id=1, source_target_pairs={{0,1},{1,0},{2,3},{3,2},{4,5},{5,4},{6,7},{7,6},{8,9},{9,8},{10,11... | collective-permute-start | bytes 786440 | tf_op jit(solution)/shard_map/ppermute | solution.py:108
  24.7 19.7 %collective-permute-start.13 = (bf16[128,1024]{1,0:T(8,128)(2,1)}, bf16[128,1024]{1,0:T(8,128)(2,1)}, u32[]{:S(2)}, u32[]{:S(2)}) collective-permute-start(bf16[128,1024]{1,0:T(8,128)(2,1)} %collective-permute-done.9), channel_id=1, source_target_pairs={{0,1},{1,0},{2,3},{3,2},{4,5},{5,4},{6,7},{7,6},{8,9},{9,8},{10,11... | collective-permute-start | bytes 786440 | tf_op jit(solution)/shard_map/ppermute | solution.py:108
  30.5 12.2 %collective-permute-start.12 = (bf16[128,1024]{1,0:T(8,128)(2,1)}, bf16[128,1024]{1,0:T(8,128)(2,1)}, u32[]{:S(2)}, u32[]{:S(2)}) collective-permute-start(bf16[128,1024]{1,0:T(8,128)(2,1)} %collective-permute-done.8), channel_id=1, source_target_pairs={{0,1},{1,0},{2,3},{3,2},{4,5},{5,4},{6,7},{7,6},{8,9},{9,8},{10,11... | collective-permute-start | bytes 786440 | tf_op jit(solution)/shard_map/ppermute | solution.py:108
  32.2 1.7 %collective-permute-start.4 = (bf16[128,1024]{1,0:T(8,128)(2,1)S(1)}, bf16[128,1024]{1,0:T(8,128)(2,1)S(1)}, u32[]{:S(2)}, u32[]{:S(2)}) collective-permute-start(bf16[128,1024]{1,0:T(8,128)(2,1)S(1)} %collective-permute-done), channel_id=1, source_target_pairs={{0,1},{1,0},{2,3},{3,2},{4,5},{5,4},{6,7},{7,6},{8,9},{9,8},{10,11... | collective-permute-start | bytes 786440 | tf_op jit(solution)/shard_map/ppermute | solution.py:108
  32.2 2.2 %collective-permute-start.5 = (bf16[128,1024]{1,0:T(8,128)(2,1)S(1)}, bf16[128,1024]{1,0:T(8,128)(2,1)S(1)}, u32[]{:S(2)}, u32[]{:S(2)}) collective-permute-start(bf16[128,1024]{1,0:T(8,128)(2,1)S(1)} %collective-permute-done.1), channel_id=1, source_target_pairs={{0,1},{1,0},{2,3},{3,2},{4,5},{5,4},{6,7},{7,6},{8,9},{9,8},{10,11... | collective-permute-start | bytes 786440 | tf_op jit(solution)/shard_map/ppermute | solution.py:108
  33.8 1.8 %collective-permute-start.6 = (bf16[128,1024]{1,0:T(8,128)(2,1)}, bf16[128,1024]{1,0:T(8,128)(2,1)S(1)}, u32[]{:S(2)}, u32[]{:S(2)}) collective-permute-start(bf16[128,1024]{1,0:T(8,128)(2,1)} %collective-permute-done.2), channel_id=1, source_target_pairs={{0,1},{1,0},{2,3},{3,2},{4,5},{5,4},{6,7},{7,6},{8,9},{9,8},{10,11... | collective-permute-start | bytes 786440 | tf_op jit(solution)/shard_map/ppermute | solution.py:108
  33.9 8.0 %collective-permute-start.11 = (bf16[128,1024]{1,0:T(8,128)(2,1)}, bf16[128,1024]{1,0:T(8,128)(2,1)S(1)}, u32[]{:S(2)}, u32[]{:S(2)}) collective-permute-start(bf16[128,1024]{1,0:T(8,128)(2,1)} %collective-permute-done.7), channel_id=1, source_target_pairs={{0,1},{1,0},{2,3},{3,2},{4,5},{5,4},{6,7},{7,6},{8,9},{9,8},{10,11... | collective-permute-start | bytes 786440 | tf_op jit(solution)/shard_map/ppermute | solution.py:108
  35.6 1.3 copy-start.11
  51.1 5.9 %copy-start.13 = (f32[1024]{0:T(1024)}, f32[1024]{0:T(1024)S(1)}, u32[]{:S(2)}) copy-start(f32[1024]{0:T(1024)S(1)} %get-tuple-element.82) | copy-start | bytes 12292
  57.7 27.2 %collective-permute-start.19 = (bf16[65,1024]{1,0:T(8,128)(2,1)}, bf16[65,1024]{1,0:T(8,128)(2,1)S(1)}, u32[]{:S(2)}, u32[]{:S(2)}) collective-permute-start(bf16[65,1024]{1,0:T(8,128)(2,1)} %fusion.15), channel_id=1, source_target_pairs={{3,0},{4,1},{5,2},{6,3},{7,4},{8,5},{9,6},{10,7},{11,8},{12,9},{13... | collective-permute-start | bytes 399368 | tf_op jit(solution)/shard_map/ppermute | solution.py:17
  72.6 15.6 %collective-permute-start.18 = (bf16[65,1024]{1,0:T(8,128)(2,1)}, bf16[65,1024]{1,0:T(8,128)(2,1)S(1)}, u32[]{:S(2)}, u32[]{:S(2)}) collective-permute-start(bf16[65,1024]{1,0:T(8,128)(2,1)} %fusion.15), channel_id=1, source_target_pairs={{0,3},{1,4},{2,5},{3,6},{4,7},{5,8},{6,9},{7,10},{8,11},{9,12},{10... | collective-permute-start | bytes 399368 | tf_op jit(solution)/shard_map/ppermute | solution.py:17
  75.1 13.1 %collective-permute-start.17 = (bf16[65,1024]{1,0:T(8,128)(2,1)}, bf16[65,1024]{1,0:T(8,128)(2,1)S(1)}, u32[]{:S(2)}, u32[]{:S(2)}) collective-permute-start(bf16[65,1024]{1,0:T(8,128)(2,1)} %fusion.15), channel_id=1, source_target_pairs={{2,0},{3,1},{4,2},{5,3},{6,4},{7,5},{8,6},{9,7},{10,8},{11,9},{12,... | collective-permute-start | bytes 399368 | tf_op jit(solution)/shard_map/ppermute | solution.py:17
  78.9 9.4 %collective-permute-start.16 = (bf16[65,1024]{1,0:T(8,128)(2,1)}, bf16[65,1024]{1,0:T(8,128)(2,1)S(1)}, u32[]{:S(2)}, u32[]{:S(2)}) collective-permute-start(bf16[65,1024]{1,0:T(8,128)(2,1)} %fusion.15), channel_id=1, source_target_pairs={{0,2},{1,3},{2,4},{3,5},{4,6},{5,7},{6,8},{7,9},{8,10},{9,11},{10,... | collective-permute-start | bytes 399368 | tf_op jit(solution)/shard_map/ppermute | solution.py:17
  81.0 7.3 %collective-permute-start.15 = (bf16[65,1024]{1,0:T(8,128)(2,1)}, bf16[65,1024]{1,0:T(8,128)(2,1)S(1)}, u32[]{:S(2)}, u32[]{:S(2)}) collective-permute-start(bf16[65,1024]{1,0:T(8,128)(2,1)} %fusion.15), channel_id=1, source_target_pairs={{1,0},{2,1},{3,2},{4,3},{5,4},{6,5},{7,6},{8,7},{9,8},{10,9},{11,1... | collective-permute-start | bytes 399368 | tf_op jit(solution)/shard_map/ppermute | solution.py:17
  85.0 8.5 %collective-permute-start.14 = (bf16[65,1024]{1,0:T(8,128)(2,1)}, bf16[65,1024]{1,0:T(8,128)(2,1)S(1)}, u32[]{:S(2)}, u32[]{:S(2)}) collective-permute-start(bf16[65,1024]{1,0:T(8,128)(2,1)} %fusion.15), channel_id=1, source_target_pairs={{0,1},{1,2},{2,3},{3,4},{4,5},{5,6},{6,7},{7,8},{8,9},{9,10},{10,1... | collective-permute-start | bytes 399368 | tf_op jit(solution)/shard_map/ppermute | solution.py:17
  94.3 4.4 %copy-start.15 = (s32[256,1]{0,1:T(1,128)S(1)}, s32[256,1]{0,1:T(1,128)}, u32[]{:S(2)}) copy-start(s32[256,1]{0,1:T(1,128)} %get-tuple-element.86) | copy-start | bytes 3076
  94.4 4.4 %copy-start.16 = (s32[256,1]{0,1:T(1,128)S(1)}, s32[256,1]{0,1:T(1,128)}, u32[]{:S(2)}) copy-start(s32[256,1]{0,1:T(1,128)} %get-tuple-element.87) | copy-start | bytes 3076
  94.4 5.4 %copy-start.8 = (f32[16,64]{1,0:T(8,128)S(1)}, f32[16,64]{1,0:T(8,128)}, u32[]{:S(2)}) copy-start(f32[16,64]{1,0:T(8,128)} %mul.124) | copy-start | bytes 12292
  94.5 7.1 %copy-start.9 = (f32[16,64]{1,0:T(8,128)}, f32[16,64]{1,0:T(8,128)S(1)}, u32[]{:S(2)}) copy-start(f32[16,64]{1,0:T(8,128)S(1)} %mul.121) | copy-start | bytes 12292
  95.5 4.3 %copy-start.1 = (f32[128,1024]{0,1:T(8,128)S(1)}, f32[128,1024]{0,1:T(8,128)}, u32[]{:S(2)}) copy-start(f32[128,1024]{0,1:T(8,128)} %copy.39) | copy-start | bytes 1572868
  96.8 5.0 %copy-start.6 = (f32[128,16]{0,1:T(8,128)}, f32[128,16]{0,1:T(8,128)S(1)}, u32[]{:S(2)}) copy-start(f32[128,16]{0,1:T(8,128)S(1)} %multiply_reduce_fusion.2) | copy-start | bytes 24580
  99.8 2.1 %copy-start.17 = (f32[128]{0:T(128)}, f32[128]{0:T(128)S(1)}, u32[]{:S(2)}) copy-start(f32[128]{0:T(128)S(1)} %subtract_reduce_fusion) | copy-start | bytes 1540
  101.9 5.5 %copy-start.7 = (f32[128,16]{0,1:T(8,128)}, f32[128,16]{0,1:T(8,128)S(1)}, u32[]{:S(2)}) copy-start(f32[128,16]{0,1:T(8,128)S(1)} %negate_divide_fusion) | copy-start | bytes 24580
  107.4 0.6 copy-start.4
  108.7 20.1 %collective-permute-start.25 = (bf16[65,1024]{1,0:T(8,128)(2,1)}, bf16[65,1024]{1,0:T(8,128)(2,1)S(1)}, u32[]{:S(2)}, u32[]{:S(2)}) collective-permute-start(bf16[65,1024]{1,0:T(8,128)(2,1)} %fusion.14), channel_id=1, source_target_pairs={{3,0},{4,1},{5,2},{6,3},{7,4},{8,5},{9,6},{10,7},{11,8},{12,9},{13... | collective-permute-start | bytes 399368 | tf_op jit(solution)/shard_map/ppermute | solution.py:17
  110.6 22.9 %collective-permute-start.24 = (bf16[65,1024]{1,0:T(8,128)(2,1)}, bf16[65,1024]{1,0:T(8,128)(2,1)}, u32[]{:S(2)}, u32[]{:S(2)}) collective-permute-start(bf16[65,1024]{1,0:T(8,128)(2,1)} %fusion.14), channel_id=1, source_target_pairs={{0,3},{1,4},{2,5},{3,6},{4,7},{5,8},{6,9},{7,10},{8,11},{9,12},{10... | collective-permute-start | bytes 399368 | tf_op jit(solution)/shard_map/ppermute | solution.py:17
  114.2 19.2 %collective-permute-start.23 = (bf16[65,1024]{1,0:T(8,128)(2,1)}, bf16[65,1024]{1,0:T(8,128)(2,1)}, u32[]{:S(2)}, u32[]{:S(2)}) collective-permute-start(bf16[65,1024]{1,0:T(8,128)(2,1)} %fusion.14), channel_id=1, source_target_pairs={{2,0},{3,1},{4,2},{5,3},{6,4},{7,5},{8,6},{9,7},{10,8},{11,9},{12,... | collective-permute-start | bytes 399368 | tf_op jit(solution)/shard_map/ppermute | solution.py:17
  117.7 15.8 %collective-permute-start.22 = (bf16[65,1024]{1,0:T(8,128)(2,1)}, bf16[65,1024]{1,0:T(8,128)(2,1)}, u32[]{:S(2)}, u32[]{:S(2)}) collective-permute-start(bf16[65,1024]{1,0:T(8,128)(2,1)} %fusion.14), channel_id=1, source_target_pairs={{0,2},{1,3},{2,4},{3,5},{4,6},{5,7},{6,8},{7,9},{8,10},{9,11},{10,... | collective-permute-start | bytes 399368 | tf_op jit(solution)/shard_map/ppermute | solution.py:17
  120.1 13.4 %collective-permute-start.21 = (bf16[65,1024]{1,0:T(8,128)(2,1)}, bf16[65,1024]{1,0:T(8,128)(2,1)}, u32[]{:S(2)}, u32[]{:S(2)}) collective-permute-start(bf16[65,1024]{1,0:T(8,128)(2,1)} %fusion.14), channel_id=1, source_target_pairs={{1,0},{2,1},{3,2},{4,3},{5,4},{6,5},{7,6},{8,7},{9,8},{10,9},{11,1... | collective-permute-start | bytes 399368 | tf_op jit(solution)/shard_map/ppermute | solution.py:17
  128.8 8.5 %copy-start.5 = (f32[1024]{0:T(1024)S(1)}, f32[1024]{0:T(1024)}, u32[]{:S(2)}) copy-start(f32[1024]{0:T(1024)} %copy-done.4) | copy-start | bytes 12292
  128.8 8.5 %collective-permute-start.20 = (bf16[65,1024]{1,0:T(8,128)(2,1)}, bf16[65,1024]{1,0:T(8,128)(2,1)S(1)}, u32[]{:S(2)}, u32[]{:S(2)}) collective-permute-start(bf16[65,1024]{1,0:T(8,128)(2,1)} %fusion.14), channel_id=1, source_target_pairs={{0,1},{1,2},{2,3},{3,4},{4,5},{5,6},{6,7},{7,8},{8,9},{9,10},{10,1... | collective-permute-start | bytes 399368 | tf_op jit(solution)/shard_map/ppermute | solution.py:17
  138.9 1.9 %copy-start.12 = (bf16[1024,1024]{1,0:T(8,128)(2,1)S(1)}, bf16[1024,1024]{1,0:T(8,128)(2,1)}, u32[]{:S(2)}) copy-start(bf16[1024,1024]{1,0:T(8,128)(2,1)} %copy-done.11) | copy-start | bytes 6291460
  153.5 1.0 copy-start.14

commit v3 on v1

--- a/solution.py
+++ b/solution.py
@@ -63,15 +63,16 @@
     attended = numer / denom[:, :, None]
     weight_heads = score_weight.reshape(H, DH)
     scores = jnp.sum(attended * weight_heads[None], axis=(1, 2))
-    better = jnp.take(scores, pair_rows[:, 0])
-    worse = jnp.take(scores, pair_rows[:, 1])
+    slots = lax.broadcasted_iota(jnp.int32, (pair_rows.shape[0], count), 1)
+    is_better = slots == pair_rows[:, 0:1]
+    is_worse = slots == pair_rows[:, 1:2]
+    better = jnp.sum(jnp.where(is_better, scores[None, :], 0.0), axis=1)
+    worse = jnp.sum(jnp.where(is_worse, scores[None, :], 0.0), axis=1)
     delta = worse - better
     pair_loss = jax.nn.softplus(delta)
     push = jax.nn.sigmoid(delta)
-    slots = lax.broadcasted_iota(jnp.int32, (pair_rows.shape[0], count), 1)
     score_grad = jnp.sum(
-        jnp.where(slots == pair_rows[:, 1:2], push[:, None], 0.0)
-        - jnp.where(slots == pair_rows[:, 0:1], push[:, None], 0.0),
+        jnp.where(is_worse, push[:, None], 0.0) - jnp.where(is_better, push[:, None], 0.0),
         axis=0,
     )
     attended_grad = score_grad[:, None, None] * weight_heads[None]

time: 147 us -> 142 us (0.966)
  waiting for transfers between devices: 31.2 us -> 36.1 us
  starting transfers between devices: 42.2 us -> 38 us
  other arithmetic: 17.3 us -> 13.6 us
  local copies, waits for them, and re-layouts: 27.6 us -> 24.8 us
    ppermute x12, starting transfers between devices: 38.6 us -> 34.4 us  [from_behind(): lax.ppermute(value, axis, [(source, source + steps) for source in range(i...]
    gather x2 -> x0, local copies, waits for them, and re-layouts: 4.01 us -> none  [the longest x1 2 us: pose_side(): worse = jnp.take(scores, pair_rows[:, 1])]
    ppermute x12, waiting for transfers between devices: 5.96 us -> 8.82 us  [from_behind(): lax.ppermute(value, axis, [(source, source + steps) for source in range(i...]
    ppermute x1, waiting for transfers between devices: 1.69 us -> 3.74 us  [gather_rows(): sibling = lax.ppermute(mine, 'blk', [(s, s ^ 1) for s in range(count)])]
    gather x2 -> x0, other arithmetic: 1.82 us -> none
    select_n x2 -> x0, other arithmetic: 1.81 us -> none  [the longest x1 1.23 us: pose_side(): better = jnp.take(scores, pair_rows[:, 0])]
  transfers between devices with their start and end apart: 16 -> 16, of which waited for: 4 -> 5; matrix products, arithmetic and copies ran while one was open for 11% -> 12% of each run, Pallas kernels for 0% -> 0%
where the time goes in v3:
time: 142 us; the launch traced here: 141 us
  starting transfers between devices  38 us (27%)
  waiting for transfers between devices  36.1 us (25%)
  local copies, waits for them, and re-layouts  24.8 us (17%)
  matrix products  22.3 us (16%)
  other arithmetic  13.6 us (10%)
  between operations  5.72 us (4%)
    ppermute x12, starting transfers between devices, from_behind(): lax.ppermute(value, axis, [(source, source + steps) for source in range(i...  34.4 us
    ppermute x3, waiting for transfers between devices, gather_rows(): lax.ppermute(shard, 'blk', [(s, (s + 2 * k) % count) for s in range(count)])  23.5 us
    ppermute x12, waiting for transfers between devices, from_behind(): lax.ppermute(value, axis, [(source, source + steps) for source in range(i...  8.82 us
    dynamic_update_slice x4, local copies, waits for them, and re-layouts, gather_rows(): lax.dynamic_update_slice(full, sibling[k][None], (((position ^ 1) - 2 * k...  4.4 us
    ppermute x1, waiting for transfers between devices, gather_rows(): sibling = lax.ppermute(mine, 'blk', [(s, s ^ 1) for s in range(count)])  3.74 us
    ppermute x3, starting transfers between devices, gather_rows(): lax.ppermute(shard, 'blk', [(s, (s + 2 * k) % count) for s in range(count)])  3.6 us
    unnamed x47, local copies, waits for them, and re-layouts  3.54 us
    dot_general x1, matrix products, shards(): lax.dot_general(both_grad, full_both, contract, preferred_element_type=jn...  3.35 us
  transfers between devices with their start and end apart: 16, of which 5 were waited for; matrix products, arithmetic and copies ran while one was open for 12% of the time, Pallas kernels for 0%

profile of v3, /device:TPU:16, one launch (start us, length us, event | category | flops | bytes accessed | tf_op | source)
XLA Modules:
  0.0 140.6 jit_solution(13988683727473807610)
XLA Ops:
  0.6 1.1 constant_dynamic-update-slice_fusion.1
  1.8 1.0 constant_dynamic-update-slice_fusion
  2.7 2.5 %collective-permute-start.2 = (bf16[128,2048]{1,0:T(8,128)(2,1)S(1)}, bf16[128,2048]{1,0:T(8,128)(2,1)S(1)}, u32[]{:S(2)}, u32[]{:S(2)}) collective-permute-start(bf16[128,2048]{1,0:T(8,128)(2,1)S(1)} %constant_dynamic-update-slice_fusion), channel_id=1, source_target_pairs={{0,6},{1,7},{2,0},{3,1},{4,2},{5,3},{6,4},{7,5},{8,14},{9,15},{10,... | collective-permute-start | bytes 1572872 | tf_op jit(solution)/shard_map/ppermute | solution.py:104
  6.3 11.3 %collective-permute-done.2 = bf16[128,2048]{1,0:T(8,128)(2,1)S(1)} collective-permute-done((bf16[128,2048]{1,0:T(8,128)(2,1)S(1)}, bf16[128,2048]{1,0:T(8,128)(2,1)S(1)}, u32[]{:S(2)}, u32[]{:S(2)}) %collective-permute-start.2) | collective-permute-done | bytes 524320 | tf_op jit(solution)/shard_map/ppermute | solution.py:104
  17.6 12.3 %collective-permute-done.1 = bf16[128,2048]{1,0:T(8,128)(2,1)S(1)} collective-permute-done((bf16[128,2048]{1,0:T(8,128)(2,1)S(1)}, bf16[128,2048]{1,0:T(8,128)(2,1)S(1)}, u32[]{:S(2)}, u32[]{:S(2)}) %collective-permute-start.1) | collective-permute-done | bytes 524320 | tf_op jit(solution)/shard_map/ppermute | solution.py:104
  29.9 1.7 %pad_maximum_fusion = bf16[4,128,2048]{2,1,0:T(8,128)(2,1)} fusion(bf16[1,128,2048]{2,1,0:T(8,128)(2,1)S(1)} %bitcast.88, bf16[1,128,2048]{2,1,0:T(8,128)(2,1)S(1)} %bitcast.89, bf16[1,128,2048]{2,1,0:T(8,128)(2,1)S(1)} %bitcast.90, bf16[1,128,2048]{2,1,0:T(8,128)(2,1)S(1)} %bitcast.81), kind=kLoop, calls=%fused_computation.2 | loop fusion | flops 3145728 | bytes 4194304 | tf_op jit(solution)/shard_map/stack | solution.py:107
  32.3 3.7 %collective-permute-done.3 = bf16[4,128,2048]{2,1,0:T(8,128)(2,1)} collective-permute-done((bf16[4,128,2048]{2,1,0:T(8,128)(2,1)}, bf16[4,128,2048]{2,1,0:T(8,128)(2,1)}, u32[]{:S(2)}, u32[]{:S(2)}) %collective-permute-start.3) | collective-permute-done | bytes 2097184 | tf_op jit(solution)/shard_map/ppermute | solution.py:108
  36.0 1.1 slice_dynamic-update-slice_fusion.3
  37.2 1.1 slice_dynamic-update-slice_fusion.2
  38.4 1.2 slice_dynamic-update-slice_fusion.1
  39.6 1.1 slice_dynamic-update-slice_fusion
  40.7 2.5 %convolution_bitcast_fusion = f32[512,2048]{0,1:T(8,128)S(1)} fusion(bf16[1024,2048]{1,0:T(8,128)(2,1)S(1)} %bitcast.79, bf16[512,1024]{1,0:T(8,128)(2,1)S(1)} %copy-done.22), kind=kOutput, calls=%fused_computation | convolution fusion | flops 2147483648 | bytes 9437184 | tf_op jit(solution)/shard_map/dot_general | solution.py:123
  43.2 2.0 %convert_reduce_fusion = (f32[1024]{0:T(1024)S(1)}, bf16[512,1024]{0,1:T(8,128)(2,1)S(1)}, pred[512,1024]{0,1:T(8,128)(4,1)}) fusion(f32[512,2048]{0,1:T(8,128)S(1)} %convolution_bitcast_fusion), kind=kLoop, calls=%fused_computation.9 | loop fusion | flops 3668992 | bytes 3674112 | tf_op jit(solution)/shard_map/reduce_sum | solution.py:35
  45.3 1.3 fusion.28
  46.6 1.2 copy.27
  48.5 2.0 %collective-permute-start.9 = (bf16[65,1024]{1,0:T(8,128)(2,1)}, bf16[65,1024]{1,0:T(8,128)(2,1)S(1)}, u32[]{:S(2)}, u32[]{:S(2)}) collective-permute-start(bf16[65,1024]{1,0:T(8,128)(2,1)} %fusion.21), channel_id=1, source_target_pairs={{3,0},{4,1},{5,2},{6,3},{7,4},{8,5},{9,6},{10,7},{11,8},{12,9},{13... | collective-permute-start | bytes 399368 | tf_op jit(solution)/shard_map/ppermute | solution.py:17
  50.6 2.5 %add_select_fusion = (f32[128,1024]{1,0:T(8,128)}, f32[128,1024]{1,0:T(8,128)}) fusion(bf16[128,1024]{1,0:T(8,128)(2,1)} %param.9, bf16[1024,1024]{1,0:T(8,128)(2,1)S(1)} %copy-done), kind=kOutput, calls=%fused_computation.33 | convolution fusion | flops 268959744 | bytes 3407872 | tf_op jit(solution)/shard_map/dot_general | solution.py:57
  53.0 1.3 mul.68
  54.4 1.6 %fusion.27 = (s32[1]{0:T(128)}, s32[1]{0:T(128)}, s32[1]{0:T(128)}, s32[1]{0:T(128)}, s32[1]{0:T(128)}, /*index=5*/s32[1]{0:T(128)}, s32[1]{0:T(128)}) fusion(s32[32]{0:T(128)} %param.11, s32[]{:T(128)S(6)} %max.20, s32[]{:T(128)S(6)} %select_n.234, s32[]{:T(128)S(6)} %max.21, s32[]{:T(128)S(6)} %select_n.227, s32[]{:T(128)S(6)} %select_n.223, ...), kind=kLoop, calls=%fused_computation.71 | loop fusion | bytes 84 | solution.py:47
  60.4 2.1 %copy.29 = f32[128,1024]{0,1:T(8,128)} copy(f32[128,1024]{1,0:T(8,128)} %get-tuple-element.96) | data formatting | bytes 1048576 | tf_op jit(solution)/shard_map/jit(_where)/select_n | solution.py:21
  62.4 3.5 %collective-permute-start.8 = (bf16[65,1024]{1,0:T(8,128)(2,1)}, bf16[65,1024]{1,0:T(8,128)(2,1)S(1)}, u32[]{:S(2)}, u32[]{:S(2)}) collective-permute-start(bf16[65,1024]{1,0:T(8,128)(2,1)} %fusion.21), channel_id=1, source_target_pairs={{0,3},{1,4},{2,5},{3,6},{4,7},{5,8},{6,9},{7,10},{8,11},{9,12},{10... | collective-permute-start | bytes 399368 | tf_op jit(solution)/shard_map/ppermute | solution.py:17
  66.0 4.1 %collective-permute-start.7 = (bf16[65,1024]{1,0:T(8,128)(2,1)}, bf16[65,1024]{1,0:T(8,128)(2,1)S(1)}, u32[]{:S(2)}, u32[]{:S(2)}) collective-permute-start(bf16[65,1024]{1,0:T(8,128)(2,1)} %fusion.21), channel_id=1, source_target_pairs={{2,0},{3,1},{4,2},{5,3},{6,4},{7,5},{8,6},{9,7},{10,8},{11,9},{12,... | collective-permute-start | bytes 399368 | tf_op jit(solution)/shard_map/ppermute | solution.py:17
  70.1 1.9 %collective-permute-start.6 = (bf16[65,1024]{1,0:T(8,128)(2,1)}, bf16[65,1024]{1,0:T(8,128)(2,1)S(1)}, u32[]{:S(2)}, u32[]{:S(2)}) collective-permute-start(bf16[65,1024]{1,0:T(8,128)(2,1)} %fusion.21), channel_id=1, source_target_pairs={{0,2},{1,3},{2,4},{3,5},{4,6},{5,7},{6,8},{7,9},{8,10},{9,11},{10,... | collective-permute-start | bytes 399368 | tf_op jit(solution)/shard_map/ppermute | solution.py:17
  72.0 4.0 %collective-permute-start.5 = (bf16[65,1024]{1,0:T(8,128)(2,1)}, bf16[65,1024]{1,0:T(8,128)(2,1)S(1)}, u32[]{:S(2)}, u32[]{:S(2)}) collective-permute-start(bf16[65,1024]{1,0:T(8,128)(2,1)} %fusion.21), channel_id=1, source_target_pairs={{1,0},{2,1},{3,2},{4,3},{5,4},{6,5},{7,6},{8,7},{9,8},{10,9},{11,1... | collective-permute-start | bytes 399368 | tf_op jit(solution)/shard_map/ppermute | solution.py:17
  76.0 1.9 %collective-permute-start.4 = (bf16[65,1024]{1,0:T(8,128)(2,1)}, bf16[65,1024]{1,0:T(8,128)(2,1)S(1)}, u32[]{:S(2)}, u32[]{:S(2)}) collective-permute-start(bf16[65,1024]{1,0:T(8,128)(2,1)} %fusion.21), channel_id=1, source_target_pairs={{0,1},{1,2},{2,3},{3,4},{4,5},{5,6},{6,7},{7,8},{8,9},{9,10},{10,1... | collective-permute-start | bytes 399368 | tf_op jit(solution)/shard_map/ppermute | solution.py:17
  78.0 1.3 fusion.26
  79.3 5.2 %collective-permute-done.4 = bf16[65,1024]{1,0:T(8,128)(2,1)S(1)} collective-permute-done((bf16[65,1024]{1,0:T(8,128)(2,1)}, bf16[65,1024]{1,0:T(8,128)(2,1)S(1)}, u32[]{:S(2)}, u32[]{:S(2)}) %collective-permute-start.4) | collective-permute-done | bytes 133152 | tf_op jit(solution)/shard_map/ppermute | solution.py:17
  85.6 1.0 copy.28
  86.6 1.3 multiply_reduce_fusion.2
  87.9 1.9 %multiply_reduce_fusion.1 = (f32[128]{0:T(128)S(1)}, f32[128,16,64]{0,2,1:T(8,128)S(1)}) fusion(f32[16,64]{1,0:T(8,128)} %mul.68, f32[128,16]{0,1:T(8,128)S(1)} %multiply_reduce_fusion.2, f32[64,16,64]{0,2,1:T(8,128)} %bitcast.92, f32[128,16,64]{0,2,1:T(8,128)} %bitcast.85), kind=kOutput, calls=%fused_computation.30 | convolution fusion | flops 101056384 | bytes 1323520 | tf_op jit(solution)/shard_map/phd,dhe->phe/dot_general | solution.py:61
  90.9 1.8 %fusion.11 = f32[16,64,64]{2,1,0:T(8,128)} fusion(f32[128,16,64]{0,2,1:T(8,128)S(1)} %bitcast.86, f32[128]{0:T(128)S(1)} %subtract_reduce_fusion, f32[16,64]{1,0:T(8,128)S(1)} %copy-done.17, f32[128,16]{0,1:T(8,128)S(1)} %multiply_reduce_fusion.2), kind=kOutput, calls=%fused_computation.34 | convolution fusion | flops 100925440 | bytes 799232 | tf_op jit(solution)/shard_map/phd,phe->dhe/dot_general | solution.py:81
  94.4 2.0 %copy.32 = f32[128,1024]{1,0:T(8,128)} copy(f32[128,1024]{0,1:T(8,128)} %bitcast.87) | data formatting | bytes 1048576 | tf_op jit(solution)/shard_map/mul | solution.py:88
  96.5 1.2 copy.33
  97.7 1.4 multiply_reduce_fusion
  100.3 1.9 %collective-permute-start.15 = (bf16[65,1024]{1,0:T(8,128)(2,1)}, bf16[65,1024]{1,0:T(8,128)(2,1)S(1)}, u32[]{:S(2)}, u32[]{:S(2)}) collective-permute-start(bf16[65,1024]{1,0:T(8,128)(2,1)} %fusion.20), channel_id=1, source_target_pairs={{3,0},{4,1},{5,2},{6,3},{7,4},{8,5},{9,6},{10,7},{11,8},{12,9},{13... | collective-permute-start | bytes 399368 | tf_op jit(solution)/shard_map/ppermute | solution.py:17
  102.2 3.6 %collective-permute-start.14 = (bf16[65,1024]{1,0:T(8,128)(2,1)}, bf16[65,1024]{1,0:T(8,128)(2,1)}, u32[]{:S(2)}, u32[]{:S(2)}) collective-permute-start(bf16[65,1024]{1,0:T(8,128)(2,1)} %fusion.20), channel_id=1, source_target_pairs={{0,3},{1,4},{2,5},{3,6},{4,7},{5,8},{6,9},{7,10},{8,11},{9,12},{10... | collective-permute-start | bytes 399368 | tf_op jit(solution)/shard_map/ppermute | solution.py:17
  105.9 3.6 %collective-permute-start.13 = (bf16[65,1024]{1,0:T(8,128)(2,1)}, bf16[65,1024]{1,0:T(8,128)(2,1)}, u32[]{:S(2)}, u32[]{:S(2)}) collective-permute-start(bf16[65,1024]{1,0:T(8,128)(2,1)} %fusion.20), channel_id=1, source_target_pairs={{2,0},{3,1},{4,2},{5,3},{6,4},{7,5},{8,6},{9,7},{10,8},{11,9},{12,... | collective-permute-start | bytes 399368 | tf_op jit(solution)/shard_map/ppermute | solution.py:17
  109.5 2.2 %collective-permute-start.12 = (bf16[65,1024]{1,0:T(8,128)(2,1)}, bf16[65,1024]{1,0:T(8,128)(2,1)}, u32[]{:S(2)}, u32[]{:S(2)}) collective-permute-start(bf16[65,1024]{1,0:T(8,128)(2,1)} %fusion.20), channel_id=1, source_target_pairs={{0,2},{1,3},{2,4},{3,5},{4,6},{5,7},{6,8},{7,9},{8,10},{9,11},{10,... | collective-permute-start | bytes 399368 | tf_op jit(solution)/shard_map/ppermute | solution.py:17
  111.7 3.4 %collective-permute-start.11 = (bf16[65,1024]{1,0:T(8,128)(2,1)}, bf16[65,1024]{1,0:T(8,128)(2,1)}, u32[]{:S(2)}, u32[]{:S(2)}) collective-permute-start(bf16[65,1024]{1,0:T(8,128)(2,1)} %fusion.20), channel_id=1, source_target_pairs={{1,0},{2,1},{3,2},{4,3},{5,4},{6,5},{7,6},{8,7},{9,8},{10,9},{11,1... | collective-permute-start | bytes 399368 | tf_op jit(solution)/shard_map/ppermute | solution.py:17
  115.2 3.1 %fusion.8 = f32[128,16,64]{0,2,1:T(8,128)} fusion(f32[64,16,64]{0,2,1:T(8,128)} %bitcast.93, f32[128,16]{0,1:T(8,128)} %copy-done.16, f32[128]{0:T(128)} %copy-done.21, f32[16,64]{1,0:T(8,128)} %mul.68, f32[128,16]{0,1:T(8,128)} %copy-done.15, f32[16,64]{1,0:T(8,128)} %copy-done.18), kind=kOutput, calls=%fused_computation.17 | convolution fusion | flops 101187584 | bytes 811520 | tf_op jit(solution)/shard_map/phe,dhe->phd/dot_general | solution.py:87
  118.3 2.1 %copy.31 = f32[128,1024]{1,0:T(8,128)} copy(f32[128,1024]{0,1:T(8,128)} %bitcast.95) | data formatting | bytes 1048576 | tf_op jit(solution)/shard_map/reshape | solution.py:90
  120.3 2.1 %collective-permute-start.10 = (bf16[65,1024]{1,0:T(8,128)(2,1)}, bf16[65,1024]{1,0:T(8,128)(2,1)S(1)}, u32[]{:S(2)}, u32[]{:S(2)}) collective-permute-start(bf16[65,1024]{1,0:T(8,128)(2,1)} %fusion.20), channel_id=1, source_target_pairs={{0,1},{1,2},{2,3},{3,4},{4,5},{5,6},{6,7},{7,8},{8,9},{9,10},{10,1... | collective-permute-start | bytes 399368 | tf_op jit(solution)/shard_map/ppermute | solution.py:17
  122.4 2.7 %convolution_convert_fusion.1 = bf16[128,1024]{1,0:T(8,128)(2,1)} fusion(bf16[1024,1024]{1,0:T(8,128)(2,1)S(1)} %copy-done, f32[128,1024]{1,0:T(8,128)} %copy.31, f32[128,1024]{1,0:T(8,128)} %get-tuple-element.97), kind=kOutput, calls=%fused_computation.20 | convolution fusion | flops 269221888 | bytes 3407872 | tf_op jit(solution)/shard_map/dot_general | solution.py:91
  125.2 3.6 %collective-permute-done.10 = bf16[65,1024]{1,0:T(8,128)(2,1)S(1)} collective-permute-done((bf16[65,1024]{1,0:T(8,128)(2,1)}, bf16[65,1024]{1,0:T(8,128)(2,1)S(1)}, u32[]{:S(2)}, u32[]{:S(2)}) %collective-permute-start.10) | collective-permute-done | bytes 133152 | tf_op jit(solution)/shard_map/ppermute | solution.py:17
  128.8 1.3 add_convert_fusion
  130.3 2.7 %convolution_convert_fusion = bf16[16,64,512]{2,1,0:T(8,128)(2,1)} fusion(bf16[64,16,64]{0,2,1:T(8,128)(2,1)S(1)} %bitcast.82, bf16[512,16,64]{0,2,1:T(8,128)(2,1)} %bitcast.78), kind=kOutput, calls=%fused_computation.15 | convolution fusion | flops 67633152 | bytes 2228224 | tf_op jit(solution)/shard_map/thd,dhe->the/dot_general | solution.py:141
  134.1 2.5 %fusion.4 = bf16[512,1024]{0,1:T(8,128)(2,1)S(1)} fusion(f32[16,64,512]{2,1,0:T(8,128)S(1)} %convolution_add_fusion, pred[512,1024]{0,1:T(8,128)(4,1)S(1)} %copy-done.6, f32[512,2048]{0,1:T(8,128)} %copy-done.2), kind=kLoop, calls=%fused_computation.8 | loop fusion | flops 2097152 | bytes 5767168 | tf_op jit(solution)/shard_map/convert_element_type | solution.py:139
  137.3 3.4 %fusion.5 = bf16[512,1024]{1,0:T(8,128)(2,1)} fusion(bf16[1024,2048]{1,0:T(8,128)(2,1)S(1)} %bitcast.80, bf16[512,1024]{0,1:T(8,128)(2,1)S(1)} %bitcast.91, bf16[512,1024]{0,1:T(8,128)(2,1)S(1)} %fusion.4), kind=kOutput, calls=%fused_computation.14 | convolution fusion | flops 2152202240 | bytes 7340032 | tf_op jit(solution)/shard_map/dot_general | solution.py:146
  (83 shorter events, 9.5 us)
Async XLA Ops:
  0.6 49.9 %copy-start = (bf16[1024,1024]{1,0:T(8,128)(2,1)S(1)}, bf16[1024,1024]{1,0:T(8,128)(2,1)}, u32[]{:S(2)}) copy-start(bf16[1024,1024]{1,0:T(8,128)(2,1)} %param.14) | copy-start | bytes 6291460
  2.7 14.9 %collective-permute-start.2 = (bf16[128,2048]{1,0:T(8,128)(2,1)S(1)}, bf16[128,2048]{1,0:T(8,128)(2,1)S(1)}, u32[]{:S(2)}, u32[]{:S(2)}) collective-permute-start(bf16[128,2048]{1,0:T(8,128)(2,1)S(1)} %constant_dynamic-update-slice_fusion), channel_id=1, source_target_pairs={{0,6},{1,7},{2,0},{3,1},{4,2},{5,3},{6,4},{7,5},{8,14},{9,15},{10,... | collective-permute-start | bytes 1572872 | tf_op jit(solution)/shard_map/ppermute | solution.py:104
  5.2 24.6 %collective-permute-start.1 = (bf16[128,2048]{1,0:T(8,128)(2,1)S(1)}, bf16[128,2048]{1,0:T(8,128)(2,1)S(1)}, u32[]{:S(2)}, u32[]{:S(2)}) collective-permute-start(bf16[128,2048]{1,0:T(8,128)(2,1)S(1)} %constant_dynamic-update-slice_fusion), channel_id=1, source_target_pairs={{0,4},{1,5},{2,6},{3,7},{4,0},{5,1},{6,2},{7,3},{8,12},{9,13},{10,... | collective-permute-start | bytes 1572872 | tf_op jit(solution)/shard_map/ppermute | solution.py:104
  5.7 24.1 %collective-permute-start = (bf16[128,2048]{1,0:T(8,128)(2,1)S(1)}, bf16[128,2048]{1,0:T(8,128)(2,1)S(1)}, u32[]{:S(2)}, u32[]{:S(2)}) collective-permute-start(bf16[128,2048]{1,0:T(8,128)(2,1)S(1)} %constant_dynamic-update-slice_fusion), channel_id=1, source_target_pairs={{0,2},{1,3},{2,4},{3,5},{4,6},{5,7},{6,0},{7,1},{8,10},{9,11},{10,... | collective-permute-start | bytes 1572872 | tf_op jit(solution)/shard_map/ppermute | solution.py:104
  29.9 1.7 %copy-start.7 = (bf16[128,2048]{1,0:T(8,128)(2,1)}, bf16[128,2048]{1,0:T(8,128)(2,1)S(1)}, u32[]{:S(2)}) copy-start(bf16[128,2048]{1,0:T(8,128)(2,1)S(1)} %collective-permute-done.1) | copy-start | bytes 1572868
  29.9 1.7 %copy-start.9 = (bf16[128,2048]{1,0:T(8,128)(2,1)}, bf16[128,2048]{1,0:T(8,128)(2,1)S(1)}, u32[]{:S(2)}) copy-start(bf16[128,2048]{1,0:T(8,128)(2,1)S(1)} %collective-permute-done) | copy-start | bytes 1572868
  31.5 4.5 %collective-permute-start.3 = (bf16[4,128,2048]{2,1,0:T(8,128)(2,1)}, bf16[4,128,2048]{2,1,0:T(8,128)(2,1)}, u32[]{:S(2)}, u32[]{:S(2)}) collective-permute-start(bf16[4,128,2048]{2,1,0:T(8,128)(2,1)} %pad_maximum_fusion), channel_id=1, source_target_pairs={{0,1},{1,0},{2,3},{3,2},{4,5},{5,4},{6,7},{7,6},{8,9},{9,8},{10,11... | collective-permute-start | bytes 6291464 | tf_op jit(solution)/shard_map/ppermute | solution.py:108
  32.2 4.9 %copy-start.10 = (bf16[128,2048]{1,0:T(8,128)(2,1)S(1)}, bf16[128,2048]{1,0:T(8,128)(2,1)}, u32[]{:S(2)}) copy-start(bf16[128,2048]{1,0:T(8,128)(2,1)} %copy-done.9) | copy-start | bytes 1572868
  32.2 6.0 %copy-start.8 = (bf16[128,2048]{1,0:T(8,128)(2,1)S(1)}, bf16[128,2048]{1,0:T(8,128)(2,1)}, u32[]{:S(2)}) copy-start(bf16[128,2048]{1,0:T(8,128)(2,1)} %copy-done.7) | copy-start | bytes 1572868
  38.3 2.4 %copy-start.22 = (bf16[512,1024]{1,0:T(8,128)(2,1)S(1)}, bf16[512,1024]{1,0:T(8,128)(2,1)}, u32[]{:S(2)}) copy-start(bf16[512,1024]{1,0:T(8,128)(2,1)} %param.8) | copy-start | bytes 3145732
  40.7 2.5 %copy-start.3 = (bf16[8,128,2048]{2,1,0:T(8,128)(2,1)}, bf16[8,128,2048]{2,1,0:T(8,128)(2,1)S(1)}, u32[]{:S(2)}) copy-start(bf16[8,128,2048]{2,1,0:T(8,128)(2,1)S(1)} %slice_dynamic-update-slice_fusion) | copy-start | bytes 12582916
  43.2 2.2 %copy-start.2 = (f32[512,2048]{0,1:T(8,128)}, f32[512,2048]{0,1:T(8,128)S(1)}, u32[]{:S(2)}) copy-start(f32[512,2048]{0,1:T(8,128)S(1)} %convolution_bitcast_fusion) | copy-start | bytes 12582916
  45.2 1.4 %copy-start.1 = (bf16[512,1024]{0,1:T(8,128)(2,1)}, bf16[512,1024]{0,1:T(8,128)(2,1)S(1)}, u32[]{:S(2)}) copy-start(bf16[512,1024]{0,1:T(8,128)(2,1)S(1)} %get-tuple-element.83) | copy-start | bytes 3145732
  45.2 2.6 %copy-start.14 = (f32[1024]{0:T(1024)}, f32[1024]{0:T(1024)S(1)}, u32[]{:S(2)}) copy-start(f32[1024]{0:T(1024)S(1)} %get-tuple-element.82) | copy-start | bytes 12292
  48.5 27.5 %collective-permute-start.9 = (bf16[65,1024]{1,0:T(8,128)(2,1)}, bf16[65,1024]{1,0:T(8,128)(2,1)S(1)}, u32[]{:S(2)}, u32[]{:S(2)}) collective-permute-start(bf16[65,1024]{1,0:T(8,128)(2,1)} %fusion.21), channel_id=1, source_target_pairs={{3,0},{4,1},{5,2},{6,3},{7,4},{8,5},{9,6},{10,7},{11,8},{12,9},{13... | collective-permute-start | bytes 399368 | tf_op jit(solution)/shard_map/ppermute | solution.py:17
  62.4 16.9 %collective-permute-start.8 = (bf16[65,1024]{1,0:T(8,128)(2,1)}, bf16[65,1024]{1,0:T(8,128)(2,1)S(1)}, u32[]{:S(2)}, u32[]{:S(2)}) collective-permute-start(bf16[65,1024]{1,0:T(8,128)(2,1)} %fusion.21), channel_id=1, source_target_pairs={{0,3},{1,4},{2,5},{3,6},{4,7},{5,8},{6,9},{7,10},{8,11},{9,12},{10... | collective-permute-start | bytes 399368 | tf_op jit(solution)/shard_map/ppermute | solution.py:17
  66.0 13.3 %collective-permute-start.7 = (bf16[65,1024]{1,0:T(8,128)(2,1)}, bf16[65,1024]{1,0:T(8,128)(2,1)S(1)}, u32[]{:S(2)}, u32[]{:S(2)}) collective-permute-start(bf16[65,1024]{1,0:T(8,128)(2,1)} %fusion.21), channel_id=1, source_target_pairs={{2,0},{3,1},{4,2},{5,3},{6,4},{7,5},{8,6},{9,7},{10,8},{11,9},{12,... | collective-permute-start | bytes 399368 | tf_op jit(solution)/shard_map/ppermute | solution.py:17
  70.1 9.2 %collective-permute-start.6 = (bf16[65,1024]{1,0:T(8,128)(2,1)}, bf16[65,1024]{1,0:T(8,128)(2,1)S(1)}, u32[]{:S(2)}, u32[]{:S(2)}) collective-permute-start(bf16[65,1024]{1,0:T(8,128)(2,1)} %fusion.21), channel_id=1, source_target_pairs={{0,2},{1,3},{2,4},{3,5},{4,6},{5,7},{6,8},{7,9},{8,10},{9,11},{10,... | collective-permute-start | bytes 399368 | tf_op jit(solution)/shard_map/ppermute | solution.py:17
  72.0 7.3 %collective-permute-start.5 = (bf16[65,1024]{1,0:T(8,128)(2,1)}, bf16[65,1024]{1,0:T(8,128)(2,1)S(1)}, u32[]{:S(2)}, u32[]{:S(2)}) collective-permute-start(bf16[65,1024]{1,0:T(8,128)(2,1)} %fusion.21), channel_id=1, source_target_pairs={{1,0},{2,1},{3,2},{4,3},{5,4},{6,5},{7,6},{8,7},{9,8},{10,9},{11,1... | collective-permute-start | bytes 399368 | tf_op jit(solution)/shard_map/ppermute | solution.py:17
  76.0 8.5 %collective-permute-start.4 = (bf16[65,1024]{1,0:T(8,128)(2,1)}, bf16[65,1024]{1,0:T(8,128)(2,1)S(1)}, u32[]{:S(2)}, u32[]{:S(2)}) collective-permute-start(bf16[65,1024]{1,0:T(8,128)(2,1)} %fusion.21), channel_id=1, source_target_pairs={{0,1},{1,2},{2,3},{3,4},{4,5},{5,6},{6,7},{7,8},{8,9},{9,10},{10,1... | collective-permute-start | bytes 399368 | tf_op jit(solution)/shard_map/ppermute | solution.py:17
  85.4 4.5 %copy-start.19 = (s32[256,1]{0,1:T(1,128)S(1)}, s32[256,1]{0,1:T(1,128)}, u32[]{:S(2)}) copy-start(s32[256,1]{0,1:T(1,128)} %get-tuple-element.87) | copy-start | bytes 3076
  85.4 4.4 %copy-start.20 = (s32[256,1]{0,1:T(1,128)S(1)}, s32[256,1]{0,1:T(1,128)}, u32[]{:S(2)}) copy-start(s32[256,1]{0,1:T(1,128)} %get-tuple-element.88) | copy-start | bytes 3076
  85.4 5.5 %copy-start.17 = (f32[16,64]{1,0:T(8,128)S(1)}, f32[16,64]{1,0:T(8,128)}, u32[]{:S(2)}) copy-start(f32[16,64]{1,0:T(8,128)} %mul.68) | copy-start | bytes 12292
  85.5 7.2 %copy-start.18 = (f32[16,64]{1,0:T(8,128)}, f32[16,64]{1,0:T(8,128)S(1)}, u32[]{:S(2)}) copy-start(f32[16,64]{1,0:T(8,128)S(1)} %mul.65) | copy-start | bytes 12292
  86.6 4.3 %copy-start.5 = (f32[128,1024]{0,1:T(8,128)S(1)}, f32[128,1024]{0,1:T(8,128)}, u32[]{:S(2)}) copy-start(f32[128,1024]{0,1:T(8,128)} %copy.29) | copy-start | bytes 1572868
  87.9 5.1 %copy-start.15 = (f32[128,16]{0,1:T(8,128)}, f32[128,16]{0,1:T(8,128)S(1)}, u32[]{:S(2)}) copy-start(f32[128,16]{0,1:T(8,128)S(1)} %multiply_reduce_fusion.2) | copy-start | bytes 24580
  90.9 5.6 %copy-start.21 = (f32[128]{0:T(128)}, f32[128]{0:T(128)S(1)}, u32[]{:S(2)}) copy-start(f32[128]{0:T(128)S(1)} %subtract_reduce_fusion) | copy-start | bytes 1540
  93.0 0.6 copy-start.16
  99.0 0.6 copy-start.12
  100.3 20.0 %collective-permute-start.15 = (bf16[65,1024]{1,0:T(8,128)(2,1)}, bf16[65,1024]{1,0:T(8,128)(2,1)S(1)}, u32[]{:S(2)}, u32[]{:S(2)}) collective-permute-start(bf16[65,1024]{1,0:T(8,128)(2,1)} %fusion.20), channel_id=1, source_target_pairs={{3,0},{4,1},{5,2},{6,3},{7,4},{8,5},{9,6},{10,7},{11,8},{12,9},{13... | collective-permute-start | bytes 399368 | tf_op jit(solution)/shard_map/ppermute | solution.py:17
  102.2 22.9 %collective-permute-start.14 = (bf16[65,1024]{1,0:T(8,128)(2,1)}, bf16[65,1024]{1,0:T(8,128)(2,1)}, u32[]{:S(2)}, u32[]{:S(2)}) collective-permute-start(bf16[65,1024]{1,0:T(8,128)(2,1)} %fusion.20), channel_id=1, source_target_pairs={{0,3},{1,4},{2,5},{3,6},{4,7},{5,8},{6,9},{7,10},{8,11},{9,12},{10... | collective-permute-start | bytes 399368 | tf_op jit(solution)/shard_map/ppermute | solution.py:17
  105.9 19.3 %collective-permute-start.13 = (bf16[65,1024]{1,0:T(8,128)(2,1)}, bf16[65,1024]{1,0:T(8,128)(2,1)}, u32[]{:S(2)}, u32[]{:S(2)}) collective-permute-start(bf16[65,1024]{1,0:T(8,128)(2,1)} %fusion.20), channel_id=1, source_target_pairs={{2,0},{3,1},{4,2},{5,3},{6,4},{7,5},{8,6},{9,7},{10,8},{11,9},{12,... | collective-permute-start | bytes 399368 | tf_op jit(solution)/shard_map/ppermute | solution.py:17
  109.5 15.6 %collective-permute-start.12 = (bf16[65,1024]{1,0:T(8,128)(2,1)}, bf16[65,1024]{1,0:T(8,128)(2,1)}, u32[]{:S(2)}, u32[]{:S(2)}) collective-permute-start(bf16[65,1024]{1,0:T(8,128)(2,1)} %fusion.20), channel_id=1, source_target_pairs={{0,2},{1,3},{2,4},{3,5},{4,6},{5,7},{6,8},{7,9},{8,10},{9,11},{10,... | collective-permute-start | bytes 399368 | tf_op jit(solution)/shard_map/ppermute | solution.py:17
  111.7 13.4 %collective-permute-start.11 = (bf16[65,1024]{1,0:T(8,128)(2,1)}, bf16[65,1024]{1,0:T(8,128)(2,1)}, u32[]{:S(2)}, u32[]{:S(2)}) collective-permute-start(bf16[65,1024]{1,0:T(8,128)(2,1)} %fusion.20), channel_id=1, source_target_pairs={{1,0},{2,1},{3,2},{4,3},{5,4},{6,5},{7,6},{8,7},{9,8},{10,9},{11,1... | collective-permute-start | bytes 399368 | tf_op jit(solution)/shard_map/ppermute | solution.py:17
  120.3 8.5 %copy-start.13 = (f32[1024]{0:T(1024)S(1)}, f32[1024]{0:T(1024)}, u32[]{:S(2)}) copy-start(f32[1024]{0:T(1024)} %copy-done.12) | copy-start | bytes 12292
  120.3 8.5 %collective-permute-start.10 = (bf16[65,1024]{1,0:T(8,128)(2,1)}, bf16[65,1024]{1,0:T(8,128)(2,1)S(1)}, u32[]{:S(2)}, u32[]{:S(2)}) collective-permute-start(bf16[65,1024]{1,0:T(8,128)(2,1)} %fusion.20), channel_id=1, source_target_pairs={{0,1},{1,2},{2,3},{3,4},{4,5},{5,6},{6,7},{7,8},{8,9},{9,10},{10,1... | collective-permute-start | bytes 399368 | tf_op jit(solution)/shard_map/ppermute | solution.py:17
  133.1 1.0 copy-start.6
  134.1 2.8 %copy-start.4 = (bf16[8,128,2048]{2,1,0:T(8,128)(2,1)S(1)}, bf16[8,128,2048]{2,1,0:T(8,128)(2,1)}, u32[]{:S(2)}) copy-start(bf16[8,128,2048]{2,1,0:T(8,128)(2,1)} %copy-done.3) | copy-start | bytes 12582916
  134.1 3.1 %copy-start.11 = (bf16[16,64,512]{2,1,0:T(8,128)(2,1)S(1)}, bf16[16,64,512]{2,1,0:T(8,128)(2,1)}, u32[]{:S(2)}) copy-start(bf16[16,64,512]{2,1,0:T(8,128)(2,1)} %convolution_convert_fusion) | copy-start | bytes 3145732

commit v4 on v3

--- a/solution.py
+++ b/solution.py
@@ -96,22 +96,28 @@
 
 def gather_rows(shard):
     count = lax.axis_size("blk")
-    if count > 16 or count % 2:
+    if count != 8:
         return lax.all_gather(shard, "blk", axis=0, tiled=True)
     position = lax.axis_index("blk")
     rows = shard.shape[0]
-    got = [shard] + [
-        lax.ppermute(shard, "blk", [(s, (s + 2 * k) % count) for s in range(count)])
-        for k in range(1, count // 2)
+    odd = position % 2
+    first = jnp.where(odd == 1, 4, 2)
+    second = 6 - first
+    early = lax.ppermute(shard, "blk", [(s, s ^ (4 if s % 2 else 2)) for s in range(count)])
+    late = lax.ppermute(
+        jnp.stack([shard, early]), "blk", [(s, s ^ (2 if s % 2 else 4)) for s in range(count)]
+    )
+    mine = jnp.concatenate([jnp.stack([shard, early]), late], axis=0)
+    sibling = lax.ppermute(mine, "blk", [(s, s ^ 1) for s in range(count)])
+    twin = position ^ 1
+    sources = [
+        (mine, [position, position ^ first, position ^ second, position ^ 6]),
+        (sibling, [twin, twin ^ second, twin ^ first, twin ^ 6]),
     ]
-    mine = jnp.stack(got)
-    sibling = lax.ppermute(mine, "blk", [(s, s ^ 1) for s in range(count)])
     full = jnp.zeros((count,) + shard.shape, shard.dtype)
-    for k in range(count // 2):
-        full = lax.dynamic_update_slice(full, mine[k][None], ((position - 2 * k) % count, 0, 0))
-        full = lax.dynamic_update_slice(
-            full, sibling[k][None], (((position ^ 1) - 2 * k) % count, 0, 0)
-        )
+    for pieces, where in sources:
+        for k, at in enumerate(where):
+            full = lax.dynamic_update_slice(full, pieces[k][None], (at, 0, 0))
     return full.reshape(count * rows, shard.shape[1])
 
 

time: 142 us -> 141 us (level)
  waiting for transfers between devices: 36.1 us -> 32.4 us
  starting transfers between devices: 38 us -> 39.5 us
    ppermute x3 -> x2, waiting for transfers between devices: 23.5 us -> 21 us  [the longest x1 13.3 us: gather_rows(): lax.ppermute(jnp.stack([shard, early]), 'blk', [(s, s ^ (2 if s % 2 else...]
    ppermute x12, starting transfers between devices: 34.4 us -> 36.3 us  [from_behind(): lax.ppermute(value, axis, [(source, source + steps) for source in range(i...]
    concatenate x0 -> x1, other arithmetic: none -> 1.67 us  [gather_rows(): mine = jnp.concatenate([jnp.stack([shard, early]), late], axis=0)]
    another operation x1, other arithmetic: 1.67 us -> 0.1 us  [gather_rows(): jnp.stack([shard, early])]
    unnamed x47 -> x43, local copies, waits for them, and re-layouts: 3.54 us -> 4.63 us
    ppermute x3 -> x2, starting transfers between devices: 3.6 us -> 3.14 us  [the longest x1 1.58 us: gather_rows(): lax.ppermute(jnp.stack([shard, early]), 'blk', [(s, s ^ (2 if s % 2 else...]
  transfers between devices with their start and end apart: 16 -> 15, of which waited for: 5 -> 5; matrix products, arithmetic and copies ran while one was open for 12% -> 12% of each run, Pallas kernels for 0% -> 0%
where the time goes in v4:
time: 141 us; the launch traced here: 139 us
  starting transfers between devices  39.5 us (28%)
  waiting for transfers between devices  32.4 us (23%)
  local copies, waits for them, and re-layouts  25.8 us (18%)
  matrix products  22.3 us (16%)
  other arithmetic  13.7 us (10%)
  between operations  5.53 us (4%)
    ppermute x12, starting transfers between devices, from_behind(): lax.ppermute(value, axis, [(source, source + steps) for source in range(i...  36.3 us
    ppermute x1, waiting for transfers between devices, gather_rows(): lax.ppermute(jnp.stack([shard, early]), 'blk', [(s, s ^ (2 if s % 2 else...  13.3 us
    ppermute x12, waiting for transfers between devices, from_behind(): lax.ppermute(value, axis, [(source, source + steps) for source in range(i...  8.82 us
    ppermute x1, waiting for transfers between devices, gather_rows(): lax.ppermute(shard, 'blk', [(s, s ^ (4 if s % 2 else 2)) for s in range(c...  7.69 us
    unnamed x43, local copies, waits for them, and re-layouts  4.63 us
    dynamic_update_slice x8, local copies, waits for them, and re-layouts, gather_rows(): full = lax.dynamic_update_slice(full, pieces[k][None], (at, 0, 0))  4.51 us
    dot_general x1, matrix products, shards(): lax.dot_general(both_grad, full_both, contract, preferred_element_type=jn...  3.38 us
    dot_general x1, matrix products, pose_side(): jnp.einsum('phe,dhe->phd', numer_grad, state_heads, precision=highest)  3.06 us
  transfers between devices with their start and end apart: 15, of which 5 were waited for; matrix products, arithmetic and copies ran while one was open for 12% of the time, Pallas kernels for 0%

profile of v4, /device:TPU:16, one launch (start us, length us, event | category | flops | bytes accessed | tf_op | source)
XLA Modules:
  0.0 139.3 jit_solution(1884622370453275218)
XLA Ops:
  0.6 1.1 constant_dynamic-update-slice_fusion.1
  2.7 1.6 %collective-permute-start = (bf16[128,2048]{1,0:T(8,128)(2,1)S(1)}, bf16[128,2048]{1,0:T(8,128)(2,1)S(1)}, u32[]{:S(2)}, u32[]{:S(2)}) collective-permute-start(bf16[128,2048]{1,0:T(8,128)(2,1)S(1)} %constant_dynamic-update-slice_fusion), channel_id=1, source_target_pairs={{0,2},{1,5},{2,0},{3,7},{4,6},{5,1},{6,4},{7,3},{8,10},{9,13},{10,... | collective-permute-start | bytes 1572872 | tf_op jit(solution)/shard_map/ppermute | solution.py:106
  4.3 7.7 %collective-permute-done = bf16[128,2048]{1,0:T(8,128)(2,1)S(1)} collective-permute-done((bf16[128,2048]{1,0:T(8,128)(2,1)S(1)}, bf16[128,2048]{1,0:T(8,128)(2,1)S(1)}, u32[]{:S(2)}, u32[]{:S(2)}) %collective-permute-start) | collective-permute-done | bytes 524320 | tf_op jit(solution)/shard_map/ppermute | solution.py:106
  12.1 1.6 %collective-permute-start.1 = (bf16[2,128,2048]{2,1,0:T(8,128)(2,1)S(1)}, bf16[2,128,2048]{2,1,0:T(8,128)(2,1)S(1)}, u32[]{:S(2)}, u32[]{:S(2)}) collective-permute-start(bf16[2,128,2048]{2,1,0:T(8,128)(2,1)S(1)} %pad_maximum_fusion.1), channel_id=1, source_target_pairs={{0,4},{1,3},{2,6},{3,1},{4,0},{5,7},{6,2},{7,5},{8,12},{9,11},{10,... | collective-permute-start | bytes 3145736 | tf_op jit(solution)/shard_map/ppermute | solution.py:107
  13.7 13.3 %collective-permute-done.1 = bf16[2,128,2048]{2,1,0:T(8,128)(2,1)S(1)} collective-permute-done((bf16[2,128,2048]{2,1,0:T(8,128)(2,1)S(1)}, bf16[2,128,2048]{2,1,0:T(8,128)(2,1)S(1)}, u32[]{:S(2)}, u32[]{:S(2)}) %collective-permute-start.1) | collective-permute-done | bytes 1048608 | tf_op jit(solution)/shard_map/ppermute | solution.py:107
  27.0 1.7 %pad_maximum_fusion = bf16[4,128,2048]{2,1,0:T(8,128)(2,1)} fusion(bf16[2,128,2048]{2,1,0:T(8,128)(2,1)S(1)} %collective-permute-done.1, bf16[1,128,2048]{2,1,0:T(8,128)(2,1)S(1)} %bitcast.78, bf16[1,128,2048]{2,1,0:T(8,128)(2,1)S(1)} %bitcast.76), kind=kLoop, calls=%fused_computation.2 | loop fusion | flops 2097152 | bytes 4194304 | tf_op jit(solution)/shard_map/concatenate | solution.py:110
  29.3 1.1 copy-done.6
  30.5 2.6 %collective-permute-done.2 = bf16[4,128,2048]{2,1,0:T(8,128)(2,1)} collective-permute-done((bf16[4,128,2048]{2,1,0:T(8,128)(2,1)}, bf16[4,128,2048]{2,1,0:T(8,128)(2,1)}, u32[]{:S(2)}, u32[]{:S(2)}) %collective-permute-start.2) | collective-permute-done | bytes 2097184 | tf_op jit(solution)/shard_map/ppermute | solution.py:111
  33.1 1.1 slice_dynamic-update-slice_fusion.3
  34.2 1.1 slice_dynamic-update-slice_fusion.2
  35.3 1.1 slice_dynamic-update-slice_fusion.1
  36.4 1.1 slice_dynamic-update-slice_fusion
  37.5 2.5 %convolution_bitcast_fusion = f32[512,2048]{0,1:T(8,128)S(1)} fusion(bf16[1024,2048]{1,0:T(8,128)(2,1)S(1)} %bitcast.79, bf16[512,1024]{1,0:T(8,128)(2,1)S(1)} %copy-done.20), kind=kOutput, calls=%fused_computation | convolution fusion | flops 2147483648 | bytes 9437184 | tf_op jit(solution)/shard_map/dot_general | solution.py:129
  40.0 2.0 %convert_reduce_fusion = (f32[1024]{0:T(1024)S(1)}, bf16[512,1024]{0,1:T(8,128)(2,1)S(1)}, pred[512,1024]{0,1:T(8,128)(4,1)}) fusion(f32[512,2048]{0,1:T(8,128)S(1)} %convolution_bitcast_fusion), kind=kLoop, calls=%fused_computation.9 | loop fusion | flops 3668992 | bytes 3674112 | tf_op jit(solution)/shard_map/reduce_sum | solution.py:35
  42.1 1.3 fusion.28
  43.4 1.2 copy.27
  45.3 3.0 %collective-permute-start.8 = (bf16[65,1024]{1,0:T(8,128)(2,1)}, bf16[65,1024]{1,0:T(8,128)(2,1)S(1)}, u32[]{:S(2)}, u32[]{:S(2)}) collective-permute-start(bf16[65,1024]{1,0:T(8,128)(2,1)} %fusion.21), channel_id=1, source_target_pairs={{3,0},{4,1},{5,2},{6,3},{7,4},{8,5},{9,6},{10,7},{11,8},{12,9},{13... | collective-permute-start | bytes 399368 | tf_op jit(solution)/shard_map/ppermute | solution.py:17
  48.4 2.5 %add_select_fusion = (f32[128,1024]{1,0:T(8,128)}, f32[128,1024]{1,0:T(8,128)}) fusion(bf16[128,1024]{1,0:T(8,128)(2,1)} %param.9, bf16[1024,1024]{1,0:T(8,128)(2,1)S(1)} %copy-done), kind=kOutput, calls=%fused_computation.36 | convolution fusion | flops 268959744 | bytes 3407872 | tf_op jit(solution)/shard_map/dot_general | solution.py:57
  50.8 1.4 mul.68
  52.2 1.6 %fusion.27 = (s32[1]{0:T(128)}, s32[1]{0:T(128)}, s32[1]{0:T(128)}, s32[1]{0:T(128)}, s32[1]{0:T(128)}, /*index=5*/s32[1]{0:T(128)}, s32[1]{0:T(128)}) fusion(s32[32]{0:T(128)} %param.11, s32[]{:T(128)S(6)} %max.20, s32[]{:T(128)S(6)} %select_n.204, s32[]{:T(128)S(6)} %max.21, s32[]{:T(128)S(6)} %select_n.197, s32[]{:T(128)S(6)} %select_n.193, ...), kind=kLoop, calls=%fused_computation.72 | loop fusion | bytes 84 | solution.py:47
  58.2 2.0 %copy.29 = f32[128,1024]{0,1:T(8,128)} copy(f32[128,1024]{1,0:T(8,128)} %get-tuple-element.96) | data formatting | bytes 1048576 | tf_op jit(solution)/shard_map/jit(_where)/select_n | solution.py:21
  60.2 2.5 %collective-permute-start.7 = (bf16[65,1024]{1,0:T(8,128)(2,1)}, bf16[65,1024]{1,0:T(8,128)(2,1)S(1)}, u32[]{:S(2)}, u32[]{:S(2)}) collective-permute-start(bf16[65,1024]{1,0:T(8,128)(2,1)} %fusion.21), channel_id=1, source_target_pairs={{0,3},{1,4},{2,5},{3,6},{4,7},{5,8},{6,9},{7,10},{8,11},{9,12},{10... | collective-permute-start | bytes 399368 | tf_op jit(solution)/shard_map/ppermute | solution.py:17
  62.7 6.0 %collective-permute-start.6 = (bf16[65,1024]{1,0:T(8,128)(2,1)}, bf16[65,1024]{1,0:T(8,128)(2,1)S(1)}, u32[]{:S(2)}, u32[]{:S(2)}) collective-permute-start(bf16[65,1024]{1,0:T(8,128)(2,1)} %fusion.21), channel_id=1, source_target_pairs={{2,0},{3,1},{4,2},{5,3},{6,4},{7,5},{8,6},{9,7},{10,8},{11,9},{12,... | collective-permute-start | bytes 399368 | tf_op jit(solution)/shard_map/ppermute | solution.py:17
  68.8 1.9 %collective-permute-start.5 = (bf16[65,1024]{1,0:T(8,128)(2,1)}, bf16[65,1024]{1,0:T(8,128)(2,1)S(1)}, u32[]{:S(2)}, u32[]{:S(2)}) collective-permute-start(bf16[65,1024]{1,0:T(8,128)(2,1)} %fusion.21), channel_id=1, source_target_pairs={{0,2},{1,3},{2,4},{3,5},{4,6},{5,7},{6,8},{7,9},{8,10},{9,11},{10,... | collective-permute-start | bytes 399368 | tf_op jit(solution)/shard_map/ppermute | solution.py:17
  70.7 4.0 %collective-permute-start.4 = (bf16[65,1024]{1,0:T(8,128)(2,1)}, bf16[65,1024]{1,0:T(8,128)(2,1)S(1)}, u32[]{:S(2)}, u32[]{:S(2)}) collective-permute-start(bf16[65,1024]{1,0:T(8,128)(2,1)} %fusion.21), channel_id=1, source_target_pairs={{1,0},{2,1},{3,2},{4,3},{5,4},{6,5},{7,6},{8,7},{9,8},{10,9},{11,1... | collective-permute-start | bytes 399368 | tf_op jit(solution)/shard_map/ppermute | solution.py:17
  74.7 1.9 %collective-permute-start.3 = (bf16[65,1024]{1,0:T(8,128)(2,1)}, bf16[65,1024]{1,0:T(8,128)(2,1)S(1)}, u32[]{:S(2)}, u32[]{:S(2)}) collective-permute-start(bf16[65,1024]{1,0:T(8,128)(2,1)} %fusion.21), channel_id=1, source_target_pairs={{0,1},{1,2},{2,3},{3,4},{4,5},{5,6},{6,7},{7,8},{8,9},{9,10},{10,1... | collective-permute-start | bytes 399368 | tf_op jit(solution)/shard_map/ppermute | solution.py:17
  76.7 1.3 fusion.26
  78.0 5.2 %collective-permute-done.3 = bf16[65,1024]{1,0:T(8,128)(2,1)S(1)} collective-permute-done((bf16[65,1024]{1,0:T(8,128)(2,1)}, bf16[65,1024]{1,0:T(8,128)(2,1)S(1)}, u32[]{:S(2)}, u32[]{:S(2)}) %collective-permute-start.3) | collective-permute-done | bytes 133152 | tf_op jit(solution)/shard_map/ppermute | solution.py:17
  85.3 1.3 multiply_reduce_fusion.2
  86.6 1.9 %multiply_reduce_fusion.1 = (f32[128]{0:T(128)S(1)}, f32[128,16,64]{0,2,1:T(8,128)S(1)}) fusion(f32[16,64]{1,0:T(8,128)} %mul.68, f32[128,16]{0,1:T(8,128)S(1)} %multiply_reduce_fusion.2, f32[64,16,64]{0,2,1:T(8,128)} %bitcast.88, f32[128,16,64]{0,2,1:T(8,128)} %bitcast.84), kind=kOutput, calls=%fused_computation.33 | convolution fusion | flops 101056384 | bytes 1323520 | tf_op jit(solution)/shard_map/phd,dhe->phe/dot_general | solution.py:61
  89.6 1.8 %fusion.11 = f32[16,64,64]{2,1,0:T(8,128)} fusion(f32[128,16,64]{0,2,1:T(8,128)S(1)} %bitcast.85, f32[128]{0:T(128)S(1)} %subtract_reduce_fusion, f32[16,64]{1,0:T(8,128)S(1)} %copy-done.15, f32[128,16]{0,1:T(8,128)S(1)} %multiply_reduce_fusion.2), kind=kOutput, calls=%fused_computation.37 | convolution fusion | flops 100925440 | bytes 799232 | tf_op jit(solution)/shard_map/phd,phe->dhe/dot_general | solution.py:81
  93.1 2.0 %copy.32 = f32[128,1024]{1,0:T(8,128)} copy(f32[128,1024]{0,1:T(8,128)} %bitcast.86) | data formatting | bytes 1048576 | tf_op jit(solution)/shard_map/mul | solution.py:88
  95.1 1.2 copy.33
  96.3 1.4 multiply_reduce_fusion
  99.0 1.9 %collective-permute-start.14 = (bf16[65,1024]{1,0:T(8,128)(2,1)}, bf16[65,1024]{1,0:T(8,128)(2,1)S(1)}, u32[]{:S(2)}, u32[]{:S(2)}) collective-permute-start(bf16[65,1024]{1,0:T(8,128)(2,1)} %fusion.20), channel_id=1, source_target_pairs={{3,0},{4,1},{5,2},{6,3},{7,4},{8,5},{9,6},{10,7},{11,8},{12,9},{13... | collective-permute-start | bytes 399368 | tf_op jit(solution)/shard_map/ppermute | solution.py:17
  100.9 3.6 %collective-permute-start.13 = (bf16[65,1024]{1,0:T(8,128)(2,1)}, bf16[65,1024]{1,0:T(8,128)(2,1)}, u32[]{:S(2)}, u32[]{:S(2)}) collective-permute-start(bf16[65,1024]{1,0:T(8,128)(2,1)} %fusion.20), channel_id=1, source_target_pairs={{0,3},{1,4},{2,5},{3,6},{4,7},{5,8},{6,9},{7,10},{8,11},{9,12},{10... | collective-permute-start | bytes 399368 | tf_op jit(solution)/shard_map/ppermute | solution.py:17
  104.5 3.6 %collective-permute-start.12 = (bf16[65,1024]{1,0:T(8,128)(2,1)}, bf16[65,1024]{1,0:T(8,128)(2,1)}, u32[]{:S(2)}, u32[]{:S(2)}) collective-permute-start(bf16[65,1024]{1,0:T(8,128)(2,1)} %fusion.20), channel_id=1, source_target_pairs={{2,0},{3,1},{4,2},{5,3},{6,4},{7,5},{8,6},{9,7},{10,8},{11,9},{12,... | collective-permute-start | bytes 399368 | tf_op jit(solution)/shard_map/ppermute | solution.py:17
  108.2 2.2 %collective-permute-start.11 = (bf16[65,1024]{1,0:T(8,128)(2,1)}, bf16[65,1024]{1,0:T(8,128)(2,1)}, u32[]{:S(2)}, u32[]{:S(2)}) collective-permute-start(bf16[65,1024]{1,0:T(8,128)(2,1)} %fusion.20), channel_id=1, source_target_pairs={{0,2},{1,3},{2,4},{3,5},{4,6},{5,7},{6,8},{7,9},{8,10},{9,11},{10,... | collective-permute-start | bytes 399368 | tf_op jit(solution)/shard_map/ppermute | solution.py:17
  110.4 3.4 %collective-permute-start.10 = (bf16[65,1024]{1,0:T(8,128)(2,1)}, bf16[65,1024]{1,0:T(8,128)(2,1)}, u32[]{:S(2)}, u32[]{:S(2)}) collective-permute-start(bf16[65,1024]{1,0:T(8,128)(2,1)} %fusion.20), channel_id=1, source_target_pairs={{1,0},{2,1},{3,2},{4,3},{5,4},{6,5},{7,6},{8,7},{9,8},{10,9},{11,1... | collective-permute-start | bytes 399368 | tf_op jit(solution)/shard_map/ppermute | solution.py:17
  113.8 3.1 %fusion.8 = f32[128,16,64]{0,2,1:T(8,128)} fusion(f32[64,16,64]{0,2,1:T(8,128)} %bitcast.89, f32[128,16]{0,1:T(8,128)} %copy-done.14, f32[128]{0:T(128)} %copy-done.19, f32[16,64]{1,0:T(8,128)} %mul.68, f32[128,16]{0,1:T(8,128)} %copy-done.13, f32[16,64]{1,0:T(8,128)} %copy-done.16), kind=kOutput, calls=%fused_computation.17 | convolution fusion | flops 101187584 | bytes 811520 | tf_op jit(solution)/shard_map/phe,dhe->phd/dot_general | solution.py:87
  116.9 2.1 %copy.31 = f32[128,1024]{1,0:T(8,128)} copy(f32[128,1024]{0,1:T(8,128)} %bitcast.91) | data formatting | bytes 1048576 | tf_op jit(solution)/shard_map/reshape | solution.py:90
  119.0 2.1 %collective-permute-start.9 = (bf16[65,1024]{1,0:T(8,128)(2,1)}, bf16[65,1024]{1,0:T(8,128)(2,1)S(1)}, u32[]{:S(2)}, u32[]{:S(2)}) collective-permute-start(bf16[65,1024]{1,0:T(8,128)(2,1)} %fusion.20), channel_id=1, source_target_pairs={{0,1},{1,2},{2,3},{3,4},{4,5},{5,6},{6,7},{7,8},{8,9},{9,10},{10,1... | collective-permute-start | bytes 399368 | tf_op jit(solution)/shard_map/ppermute | solution.py:17
  121.1 2.7 %convolution_convert_fusion.1 = bf16[128,1024]{1,0:T(8,128)(2,1)} fusion(bf16[1024,1024]{1,0:T(8,128)(2,1)S(1)} %copy-done, f32[128,1024]{1,0:T(8,128)} %copy.31, f32[128,1024]{1,0:T(8,128)} %get-tuple-element.97), kind=kOutput, calls=%fused_computation.20 | convolution fusion | flops 269221888 | bytes 3407872 | tf_op jit(solution)/shard_map/dot_general | solution.py:91
  123.8 3.6 %collective-permute-done.9 = bf16[65,1024]{1,0:T(8,128)(2,1)S(1)} collective-permute-done((bf16[65,1024]{1,0:T(8,128)(2,1)}, bf16[65,1024]{1,0:T(8,128)(2,1)S(1)}, u32[]{:S(2)}, u32[]{:S(2)}) %collective-permute-start.9) | collective-permute-done | bytes 133152 | tf_op jit(solution)/shard_map/ppermute | solution.py:17
  127.4 1.3 add_convert_fusion
  129.0 2.7 %convolution_convert_fusion = bf16[16,64,512]{2,1,0:T(8,128)(2,1)} fusion(bf16[64,16,64]{0,2,1:T(8,128)(2,1)S(1)} %bitcast.81, bf16[512,16,64]{0,2,1:T(8,128)(2,1)} %bitcast.74), kind=kOutput, calls=%fused_computation.15 | convolution fusion | flops 67633152 | bytes 2228224 | tf_op jit(solution)/shard_map/thd,dhe->the/dot_general | solution.py:147
  132.8 2.5 %fusion.4 = bf16[512,1024]{0,1:T(8,128)(2,1)S(1)} fusion(f32[16,64,512]{2,1,0:T(8,128)S(1)} %convolution_add_fusion, pred[512,1024]{0,1:T(8,128)(4,1)S(1)} %copy-done.8, f32[512,2048]{0,1:T(8,128)} %copy-done.2), kind=kLoop, calls=%fused_computation.8 | loop fusion | flops 2097152 | bytes 5767168 | tf_op jit(solution)/shard_map/convert_element_type | solution.py:145
  135.9 3.4 %fusion.5 = bf16[512,1024]{1,0:T(8,128)(2,1)} fusion(bf16[1024,2048]{1,0:T(8,128)(2,1)S(1)} %bitcast.80, bf16[512,1024]{0,1:T(8,128)(2,1)S(1)} %bitcast.87, bf16[512,1024]{0,1:T(8,128)(2,1)S(1)} %fusion.4), kind=kOutput, calls=%fused_computation.14 | convolution fusion | flops 2152202240 | bytes 7340032 | tf_op jit(solution)/shard_map/dot_general | solution.py:152
  (78 shorter events, 10.5 us)
Async XLA Ops:
  0.6 47.7 %copy-start = (bf16[1024,1024]{1,0:T(8,128)(2,1)S(1)}, bf16[1024,1024]{1,0:T(8,128)(2,1)}, u32[]{:S(2)}) copy-start(bf16[1024,1024]{1,0:T(8,128)(2,1)} %param.14) | copy-start | bytes 6291460
  2.7 9.2 %collective-permute-start = (bf16[128,2048]{1,0:T(8,128)(2,1)S(1)}, bf16[128,2048]{1,0:T(8,128)(2,1)S(1)}, u32[]{:S(2)}, u32[]{:S(2)}) collective-permute-start(bf16[128,2048]{1,0:T(8,128)(2,1)S(1)} %constant_dynamic-update-slice_fusion), channel_id=1, source_target_pairs={{0,2},{1,5},{2,0},{3,7},{4,6},{5,1},{6,4},{7,3},{8,10},{9,13},{10,... | collective-permute-start | bytes 1572872 | tf_op jit(solution)/shard_map/ppermute | solution.py:106
  12.1 14.9 %collective-permute-start.1 = (bf16[2,128,2048]{2,1,0:T(8,128)(2,1)S(1)}, bf16[2,128,2048]{2,1,0:T(8,128)(2,1)S(1)}, u32[]{:S(2)}, u32[]{:S(2)}) collective-permute-start(bf16[2,128,2048]{2,1,0:T(8,128)(2,1)S(1)} %pad_maximum_fusion.1), channel_id=1, source_target_pairs={{0,4},{1,3},{2,6},{3,1},{4,0},{5,7},{6,2},{7,5},{8,12},{9,11},{10,... | collective-permute-start | bytes 3145736 | tf_op jit(solution)/shard_map/ppermute | solution.py:107
  27.0 1.7 %copy-start.5 = (bf16[2,128,2048]{2,1,0:T(8,128)(2,1)}, bf16[2,128,2048]{2,1,0:T(8,128)(2,1)S(1)}, u32[]{:S(2)}) copy-start(bf16[2,128,2048]{2,1,0:T(8,128)(2,1)S(1)} %collective-permute-done.1) | copy-start | bytes 3145732
  28.6 4.5 %collective-permute-start.2 = (bf16[4,128,2048]{2,1,0:T(8,128)(2,1)}, bf16[4,128,2048]{2,1,0:T(8,128)(2,1)}, u32[]{:S(2)}, u32[]{:S(2)}) collective-permute-start(bf16[4,128,2048]{2,1,0:T(8,128)(2,1)} %pad_maximum_fusion), channel_id=1, source_target_pairs={{0,1},{1,0},{2,3},{3,2},{4,5},{5,4},{6,7},{7,6},{8,9},{9,8},{10,11... | collective-permute-start | bytes 6291464 | tf_op jit(solution)/shard_map/ppermute | solution.py:111
  29.1 1.2 copy-start.6
  30.5 7.0 %copy-start.20 = (bf16[512,1024]{1,0:T(8,128)(2,1)S(1)}, bf16[512,1024]{1,0:T(8,128)(2,1)}, u32[]{:S(2)}) copy-start(bf16[512,1024]{1,0:T(8,128)(2,1)} %param.8) | copy-start | bytes 3145732
  37.5 2.5 %copy-start.3 = (bf16[8,128,2048]{2,1,0:T(8,128)(2,1)}, bf16[8,128,2048]{2,1,0:T(8,128)(2,1)S(1)}, u32[]{:S(2)}) copy-start(bf16[8,128,2048]{2,1,0:T(8,128)(2,1)S(1)} %slice_dynamic-update-slice_fusion) | copy-start | bytes 12582916
  40.0 2.1 %copy-start.2 = (f32[512,2048]{0,1:T(8,128)}, f32[512,2048]{0,1:T(8,128)S(1)}, u32[]{:S(2)}) copy-start(f32[512,2048]{0,1:T(8,128)S(1)} %convolution_bitcast_fusion) | copy-start | bytes 12582916
  42.0 1.4 %copy-start.1 = (bf16[512,1024]{0,1:T(8,128)(2,1)}, bf16[512,1024]{0,1:T(8,128)(2,1)S(1)}, u32[]{:S(2)}) copy-start(bf16[512,1024]{0,1:T(8,128)(2,1)S(1)} %get-tuple-element.83) | copy-start | bytes 3145732
  42.0 2.6 %copy-start.12 = (f32[1024]{0:T(1024)}, f32[1024]{0:T(1024)S(1)}, u32[]{:S(2)}) copy-start(f32[1024]{0:T(1024)S(1)} %get-tuple-element.82) | copy-start | bytes 12292
  45.3 29.4 %collective-permute-start.8 = (bf16[65,1024]{1,0:T(8,128)(2,1)}, bf16[65,1024]{1,0:T(8,128)(2,1)S(1)}, u32[]{:S(2)}, u32[]{:S(2)}) collective-permute-start(bf16[65,1024]{1,0:T(8,128)(2,1)} %fusion.21), channel_id=1, source_target_pairs={{3,0},{4,1},{5,2},{6,3},{7,4},{8,5},{9,6},{10,7},{11,8},{12,9},{13... | collective-permute-start | bytes 399368 | tf_op jit(solution)/shard_map/ppermute | solution.py:17
  60.2 17.8 %collective-permute-start.7 = (bf16[65,1024]{1,0:T(8,128)(2,1)}, bf16[65,1024]{1,0:T(8,128)(2,1)S(1)}, u32[]{:S(2)}, u32[]{:S(2)}) collective-permute-start(bf16[65,1024]{1,0:T(8,128)(2,1)} %fusion.21), channel_id=1, source_target_pairs={{0,3},{1,4},{2,5},{3,6},{4,7},{5,8},{6,9},{7,10},{8,11},{9,12},{10... | collective-permute-start | bytes 399368 | tf_op jit(solution)/shard_map/ppermute | solution.py:17
  62.7 15.3 %collective-permute-start.6 = (bf16[65,1024]{1,0:T(8,128)(2,1)}, bf16[65,1024]{1,0:T(8,128)(2,1)S(1)}, u32[]{:S(2)}, u32[]{:S(2)}) collective-permute-start(bf16[65,1024]{1,0:T(8,128)(2,1)} %fusion.21), channel_id=1, source_target_pairs={{2,0},{3,1},{4,2},{5,3},{6,4},{7,5},{8,6},{9,7},{10,8},{11,9},{12,... | collective-permute-start | bytes 399368 | tf_op jit(solution)/shard_map/ppermute | solution.py:17
  68.8 9.2 %collective-permute-start.5 = (bf16[65,1024]{1,0:T(8,128)(2,1)}, bf16[65,1024]{1,0:T(8,128)(2,1)S(1)}, u32[]{:S(2)}, u32[]{:S(2)}) collective-permute-start(bf16[65,1024]{1,0:T(8,128)(2,1)} %fusion.21), channel_id=1, source_target_pairs={{0,2},{1,3},{2,4},{3,5},{4,6},{5,7},{6,8},{7,9},{8,10},{9,11},{10,... | collective-permute-start | bytes 399368 | tf_op jit(solution)/shard_map/ppermute | solution.py:17
  70.7 7.3 %collective-permute-start.4 = (bf16[65,1024]{1,0:T(8,128)(2,1)}, bf16[65,1024]{1,0:T(8,128)(2,1)S(1)}, u32[]{:S(2)}, u32[]{:S(2)}) collective-permute-start(bf16[65,1024]{1,0:T(8,128)(2,1)} %fusion.21), channel_id=1, source_target_pairs={{1,0},{2,1},{3,2},{4,3},{5,4},{6,5},{7,6},{8,7},{9,8},{10,9},{11,1... | collective-permute-start | bytes 399368 | tf_op jit(solution)/shard_map/ppermute | solution.py:17
  74.7 8.5 %collective-permute-start.3 = (bf16[65,1024]{1,0:T(8,128)(2,1)}, bf16[65,1024]{1,0:T(8,128)(2,1)S(1)}, u32[]{:S(2)}, u32[]{:S(2)}) collective-permute-start(bf16[65,1024]{1,0:T(8,128)(2,1)} %fusion.21), channel_id=1, source_target_pairs={{0,1},{1,2},{2,3},{3,4},{4,5},{5,6},{6,7},{7,8},{8,9},{9,10},{10,1... | collective-permute-start | bytes 399368 | tf_op jit(solution)/shard_map/ppermute | solution.py:17
  84.1 4.5 %copy-start.17 = (s32[256,1]{0,1:T(1,128)S(1)}, s32[256,1]{0,1:T(1,128)}, u32[]{:S(2)}) copy-start(s32[256,1]{0,1:T(1,128)} %get-tuple-element.87) | copy-start | bytes 3076
  84.1 4.5 %copy-start.18 = (s32[256,1]{0,1:T(1,128)S(1)}, s32[256,1]{0,1:T(1,128)}, u32[]{:S(2)}) copy-start(s32[256,1]{0,1:T(1,128)} %get-tuple-element.88) | copy-start | bytes 3076
  84.1 5.5 %copy-start.15 = (f32[16,64]{1,0:T(8,128)S(1)}, f32[16,64]{1,0:T(8,128)}, u32[]{:S(2)}) copy-start(f32[16,64]{1,0:T(8,128)} %mul.68) | copy-start | bytes 12292
  84.2 7.2 %copy-start.16 = (f32[16,64]{1,0:T(8,128)}, f32[16,64]{1,0:T(8,128)S(1)}, u32[]{:S(2)}) copy-start(f32[16,64]{1,0:T(8,128)S(1)} %mul.65) | copy-start | bytes 12292
  85.3 4.3 %copy-start.7 = (f32[128,1024]{0,1:T(8,128)S(1)}, f32[128,1024]{0,1:T(8,128)}, u32[]{:S(2)}) copy-start(f32[128,1024]{0,1:T(8,128)} %copy.29) | copy-start | bytes 1572868
  86.6 5.0 %copy-start.13 = (f32[128,16]{0,1:T(8,128)}, f32[128,16]{0,1:T(8,128)S(1)}, u32[]{:S(2)}) copy-start(f32[128,16]{0,1:T(8,128)S(1)} %multiply_reduce_fusion.2) | copy-start | bytes 24580
  89.6 3.5 %copy-start.19 = (f32[128]{0:T(128)}, f32[128]{0:T(128)S(1)}, u32[]{:S(2)}) copy-start(f32[128]{0:T(128)S(1)} %subtract_reduce_fusion) | copy-start | bytes 1540
  91.6 0.6 copy-start.14
  97.7 0.6 copy-start.10
  99.0 20.0 %collective-permute-start.14 = (bf16[65,1024]{1,0:T(8,128)(2,1)}, bf16[65,1024]{1,0:T(8,128)(2,1)S(1)}, u32[]{:S(2)}, u32[]{:S(2)}) collective-permute-start(bf16[65,1024]{1,0:T(8,128)(2,1)} %fusion.20), channel_id=1, source_target_pairs={{3,0},{4,1},{5,2},{6,3},{7,4},{8,5},{9,6},{10,7},{11,8},{12,9},{13... | collective-permute-start | bytes 399368 | tf_op jit(solution)/shard_map/ppermute | solution.py:17
  100.9 22.9 %collective-permute-start.13 = (bf16[65,1024]{1,0:T(8,128)(2,1)}, bf16[65,1024]{1,0:T(8,128)(2,1)}, u32[]{:S(2)}, u32[]{:S(2)}) collective-permute-start(bf16[65,1024]{1,0:T(8,128)(2,1)} %fusion.20), channel_id=1, source_target_pairs={{0,3},{1,4},{2,5},{3,6},{4,7},{5,8},{6,9},{7,10},{8,11},{9,12},{10... | collective-permute-start | bytes 399368 | tf_op jit(solution)/shard_map/ppermute | solution.py:17
  104.5 19.3 %collective-permute-start.12 = (bf16[65,1024]{1,0:T(8,128)(2,1)}, bf16[65,1024]{1,0:T(8,128)(2,1)}, u32[]{:S(2)}, u32[]{:S(2)}) collective-permute-start(bf16[65,1024]{1,0:T(8,128)(2,1)} %fusion.20), channel_id=1, source_target_pairs={{2,0},{3,1},{4,2},{5,3},{6,4},{7,5},{8,6},{9,7},{10,8},{11,9},{12,... | collective-permute-start | bytes 399368 | tf_op jit(solution)/shard_map/ppermute | solution.py:17
  108.2 15.6 %collective-permute-start.11 = (bf16[65,1024]{1,0:T(8,128)(2,1)}, bf16[65,1024]{1,0:T(8,128)(2,1)}, u32[]{:S(2)}, u32[]{:S(2)}) collective-permute-start(bf16[65,1024]{1,0:T(8,128)(2,1)} %fusion.20), channel_id=1, source_target_pairs={{0,2},{1,3},{2,4},{3,5},{4,6},{5,7},{6,8},{7,9},{8,10},{9,11},{10,... | collective-permute-start | bytes 399368 | tf_op jit(solution)/shard_map/ppermute | solution.py:17
  110.4 13.4 %collective-permute-start.10 = (bf16[65,1024]{1,0:T(8,128)(2,1)}, bf16[65,1024]{1,0:T(8,128)(2,1)}, u32[]{:S(2)}, u32[]{:S(2)}) collective-permute-start(bf16[65,1024]{1,0:T(8,128)(2,1)} %fusion.20), channel_id=1, source_target_pairs={{1,0},{2,1},{3,2},{4,3},{5,4},{6,5},{7,6},{8,7},{9,8},{10,9},{11,1... | collective-permute-start | bytes 399368 | tf_op jit(solution)/shard_map/ppermute | solution.py:17
  119.0 8.5 %copy-start.11 = (f32[1024]{0:T(1024)S(1)}, f32[1024]{0:T(1024)}, u32[]{:S(2)}) copy-start(f32[1024]{0:T(1024)} %copy-done.10) | copy-start | bytes 12292
  119.0 8.5 %collective-permute-start.9 = (bf16[65,1024]{1,0:T(8,128)(2,1)}, bf16[65,1024]{1,0:T(8,128)(2,1)S(1)}, u32[]{:S(2)}, u32[]{:S(2)}) collective-permute-start(bf16[65,1024]{1,0:T(8,128)(2,1)} %fusion.20), channel_id=1, source_target_pairs={{0,1},{1,2},{2,3},{3,4},{4,5},{5,6},{6,7},{7,8},{8,9},{9,10},{10,1... | collective-permute-start | bytes 399368 | tf_op jit(solution)/shard_map/ppermute | solution.py:17
  131.7 1.0 copy-start.8
  132.8 2.8 %copy-start.4 = (bf16[8,128,2048]{2,1,0:T(8,128)(2,1)S(1)}, bf16[8,128,2048]{2,1,0:T(8,128)(2,1)}, u32[]{:S(2)}) copy-start(bf16[8,128,2048]{2,1,0:T(8,128)(2,1)} %copy-done.3) | copy-start | bytes 12582916
  132.8 3.1 %copy-start.9 = (bf16[16,64,512]{2,1,0:T(8,128)(2,1)S(1)}, bf16[16,64,512]{2,1,0:T(8,128)(2,1)}, u32[]{:S(2)}) copy-start(bf16[16,64,512]{2,1,0:T(8,128)(2,1)} %convolution_convert_fusion) | copy-start | bytes 3145732

commit v5 on v4

--- a/solution.py
+++ b/solution.py
@@ -103,16 +103,24 @@
     odd = position % 2
     first = jnp.where(odd == 1, 4, 2)
     second = 6 - first
-    early = lax.ppermute(shard, "blk", [(s, s ^ (4 if s % 2 else 2)) for s in range(count)])
-    late = lax.ppermute(
-        jnp.stack([shard, early]), "blk", [(s, s ^ (2 if s % 2 else 4)) for s in range(count)]
-    )
-    mine = jnp.concatenate([jnp.stack([shard, early]), late], axis=0)
-    sibling = lax.ppermute(mine, "blk", [(s, s ^ 1) for s in range(count)])
+    along_first = [(s, s ^ (4 if s % 2 else 2)) for s in range(count)]
+    along_second = [(s, s ^ (2 if s % 2 else 4)) for s in range(count)]
+    near = lax.ppermute(shard, "blk", along_first)
+    across = lax.ppermute(shard, "blk", along_second)
+    corner = lax.ppermute(near, "blk", along_second)
+    swap = [(s, s ^ 1) for s in range(count)]
+    sibling = lax.ppermute(jnp.stack([shard, near, across]), "blk", swap)
+    sibling_corner = lax.ppermute(corner, "blk", swap)
     twin = position ^ 1
     sources = [
-        (mine, [position, position ^ first, position ^ second, position ^ 6]),
-        (sibling, [twin, twin ^ second, twin ^ first, twin ^ 6]),
+        (
+            [shard, near, across, corner],
+            [position, position ^ first, position ^ second, position ^ 6],
+        ),
+        (
+            [sibling[0], sibling[1], sibling[2], sibling_corner],
+            [twin, twin ^ second, twin ^ first, twin ^ 6],
+        ),
     ]
     full = jnp.zeros((count,) + shard.shape, shard.dtype)
     for pieces, where in sources:

time: 141 us -> 146 us (1.035)
  local copies, waits for them, and re-layouts: 25.8 us -> 32.7 us
  waiting for transfers between devices: 32.4 us -> 26.3 us
  matrix products: 22.3 us -> 26.6 us
    dynamic_update_slice x8, local copies, waits for them, and re-layouts: 4.51 us -> 11.1 us  [gather_rows(): full = lax.dynamic_update_slice(full, pieces[k][None], (at, 0, 0))]
    ppermute x3 -> x5, waiting for transfers between devices: 23.6 us -> 17.5 us  [the longest x1 11.7 us: gather_rows(): near = lax.ppermute(shard, 'blk', along_first)]
    another operation x1, other arithmetic: 0.1 us -> 2.37 us  [gather_rows(): sibling = lax.ppermute(jnp.stack([shard, near, across]), 'blk', swap)]
    dot_general x1, matrix products: 3.38 us -> 5.56 us  [shards(): lax.dot_general(both_grad, full_both, contract, preferred_element_type=jn...]
    dot_general x1, matrix products: 2.48 us -> 4.66 us  [shards(): both = jnp.dot(receptor, full_both, preferred_element_type=jnp.float32)]
    broadcast_in_dim x1, local copies, waits for them, and re-layouts: 0.51 us -> 2.49 us  [gather_rows(): full = jnp.zeros((count,) + shard.shape, shard.dtype)]
    unnamed x43 -> x35, local copies, waits for them, and re-layouts: 4.63 us -> 2.91 us
    concatenate x1 -> x0, other arithmetic: 1.67 us -> none  [gather_rows(): mine = jnp.concatenate([jnp.stack([shard, early]), late], axis=0)]
  transfers between devices with their start and end apart: 15 -> 17, of which waited for: 5 -> 4; matrix products, arithmetic and copies ran while one was open for 12% -> 20% of each run, Pallas kernels for 0% -> 0%
where the time goes in v5:
time: 146 us; the launch traced here: 145 us
  starting transfers between devices  39.6 us (27%)
  local copies, waits for them, and re-layouts  32.7 us (22%)
  matrix products  26.6 us (18%)
  waiting for transfers between devices  26.3 us (18%)
  other arithmetic  14.3 us (10%)
  between operations  5.48 us (4%)
    ppermute x12, starting transfers between devices, from_behind(): lax.ppermute(value, axis, [(source, source + steps) for source in range(i...  35.8 us
    ppermute x1, waiting for transfers between devices, gather_rows(): near = lax.ppermute(shard, 'blk', along_first)  11.7 us
    dynamic_update_slice x8, local copies, waits for them, and re-layouts, gather_rows(): full = lax.dynamic_update_slice(full, pieces[k][None], (at, 0, 0))  11.1 us
    ppermute x12, waiting for transfers between devices, from_behind(): lax.ppermute(value, axis, [(source, source + steps) for source in range(i...  8.82 us
    ppermute x1, waiting for transfers between devices, gather_rows(): corner = lax.ppermute(near, 'blk', along_second)  5.77 us
    dot_general x1, matrix products, shards(): lax.dot_general(both_grad, full_both, contract, preferred_element_type=jn...  5.56 us
    dot_general x1, matrix products, shards(): both = jnp.dot(receptor, full_both, preferred_element_type=jnp.float32)  4.66 us
    dot_general x1, matrix products, pose_side(): jnp.einsum('phe,dhe->phd', numer_grad, state_heads, precision=highest)  3.05 us
  transfers between devices with their start and end apart: 17, of which 4 were waited for; matrix products, arithmetic and copies ran while one was open for 20% of the time, Pallas kernels for 0%

profile of v5, /device:TPU:16, one launch (start us, length us, event | category | flops | bytes accessed | tf_op | source)
XLA Modules:
  0.0 144.9 jit_solution(5615790987900801336)
XLA Ops:
  0.6 1.1 constant_dynamic-update-slice_fusion.1
  2.7 1.6 %collective-permute-start = (bf16[128,2048]{1,0:T(8,128)(2,1)S(1)}, bf16[128,2048]{1,0:T(8,128)(2,1)S(1)}, u32[]{:S(2)}, u32[]{:S(2)}) collective-permute-start(bf16[128,2048]{1,0:T(8,128)(2,1)S(1)} %constant_dynamic-update-slice_fusion), channel_id=1, source_target_pairs={{0,2},{1,5},{2,0},{3,7},{4,6},{5,1},{6,4},{7,3},{8,10},{9,13},{10,... | collective-permute-start | bytes 1572872 | tf_op jit(solution)/shard_map/ppermute | solution.py:108
  4.3 1.5 %collective-permute-start.1 = (bf16[128,2048]{1,0:T(8,128)(2,1)S(1)}, bf16[128,2048]{1,0:T(8,128)(2,1)}, u32[]{:S(2)}, u32[]{:S(2)}) collective-permute-start(bf16[128,2048]{1,0:T(8,128)(2,1)S(1)} %constant_dynamic-update-slice_fusion), channel_id=1, source_target_pairs={{0,4},{1,3},{2,6},{3,1},{4,0},{5,7},{6,2},{7,5},{8,12},{9,11},{10,... | collective-permute-start | bytes 1572872 | tf_op jit(solution)/shard_map/ppermute | solution.py:109
  5.8 11.7 %collective-permute-done = bf16[128,2048]{1,0:T(8,128)(2,1)S(1)} collective-permute-done((bf16[128,2048]{1,0:T(8,128)(2,1)S(1)}, bf16[128,2048]{1,0:T(8,128)(2,1)S(1)}, u32[]{:S(2)}, u32[]{:S(2)}) %collective-permute-start) | collective-permute-done | bytes 524320 | tf_op jit(solution)/shard_map/ppermute | solution.py:108
  17.5 2.4 %pad_maximum_fusion = bf16[3,128,2048]{2,1,0:T(8,128)(2,1)} fusion(bf16[1,128,2048]{2,1,0:T(8,128)(2,1)} %bitcast.3, bf16[1,128,2048]{2,1,0:T(8,128)(2,1)S(1)} %bitcast.88, bf16[1,128,2048]{2,1,0:T(8,128)(2,1)S(1)} %bitcast.81), kind=kLoop, calls=%fused_computation.13 | loop fusion | flops 1572864 | bytes 3145728 | tf_op jit(solution)/shard_map/stack | solution.py:112
  20.0 2.5 %broadcast_in_dim.104 = bf16[8,128,2048]{2,1,0:T(8,128)(2,1)} broadcast(bf16[]{:T(256)} %constant.129.clone.1), dimensions={} | broadcast | bytes 4194306 | tf_op jit(solution)/shard_map/broadcast_in_dim | solution.py:125
  24.8 1.9 %constant_dynamic-update-slice_fusion.2 = bf16[8,128,2048]{2,1,0:T(8,128)(2,1)} fusion(bf16[8,128,2048]{2,1,0:T(8,128)(2,1)} %constant_dynamic-update-slice_fusion.3, s32[]{:T(128)S(6)} %select_n.185, bf16[128,2048]{1,0:T(8,128)(2,1)} %collective-permute-done.1), kind=kLoop, calls=%fused_computation.63 | loop fusion | bytes 1048580 | tf_op jit(solution)/shard_map/dynamic_update_slice | solution.py:128
  26.7 5.8 %collective-permute-done.2 = bf16[128,2048]{1,0:T(8,128)(2,1)S(1)} collective-permute-done((bf16[128,2048]{1,0:T(8,128)(2,1)S(1)}, bf16[128,2048]{1,0:T(8,128)(2,1)S(1)}, u32[]{:S(2)}, u32[]{:S(2)}) %collective-permute-start.2) | collective-permute-done | bytes 524320 | tf_op jit(solution)/shard_map/ppermute | solution.py:110
  33.3 2.0 %slice_dynamic-update-slice_fusion.2 = bf16[8,128,2048]{2,1,0:T(8,128)(2,1)} fusion(bf16[8,128,2048]{2,1,0:T(8,128)(2,1)} %bitcast_dynamic-update-slice_fusion.1, s32[]{:T(128)S(6)} %select_n.187, bf16[3,128,2048]{2,1,0:T(8,128)(2,1)} %collective-permute-done.3), kind=kLoop, calls=%fused_computation.26 | loop fusion | bytes 1048580 | tf_op jit(solution)/shard_map/dynamic_update_slice | solution.py:128
  35.3 1.9 %slice_dynamic-update-slice_fusion.1 = bf16[8,128,2048]{2,1,0:T(8,128)(2,1)} fusion(bf16[8,128,2048]{2,1,0:T(8,128)(2,1)} %slice_dynamic-update-slice_fusion.2, s32[]{:T(128)S(6)} %select_n.188, bf16[3,128,2048]{2,1,0:T(8,128)(2,1)} %collective-permute-done.3), kind=kLoop, calls=%fused_computation.25 | loop fusion | bytes 1048580 | tf_op jit(solution)/shard_map/dynamic_update_slice | solution.py:128
  37.2 1.9 %slice_dynamic-update-slice_fusion = bf16[8,128,2048]{2,1,0:T(8,128)(2,1)} fusion(bf16[8,128,2048]{2,1,0:T(8,128)(2,1)} %slice_dynamic-update-slice_fusion.1, s32[]{:T(128)S(6)} %select_n.189, bf16[3,128,2048]{2,1,0:T(8,128)(2,1)} %collective-permute-done.3), kind=kLoop, calls=%fused_computation.24 | loop fusion | bytes 1048580 | tf_op jit(solution)/shard_map/dynamic_update_slice | solution.py:128
  40.0 4.7 %convolution_bitcast_fusion = f32[512,2048]{0,1:T(8,128)S(1)} fusion(bf16[1024,2048]{1,0:T(8,128)(2,1)} %bitcast.6, bf16[512,1024]{1,0:T(8,128)(2,1)S(1)} %copy-done.16), kind=kOutput, calls=%fused_computation | convolution fusion | flops 2147483648 | bytes 9437184 | tf_op jit(solution)/shard_map/dot_general | solution.py:137
  44.6 2.0 %convert_reduce_fusion = (f32[1024]{0:T(1024)S(1)}, bf16[512,1024]{0,1:T(8,128)(2,1)S(1)}, pred[512,1024]{0,1:T(8,128)(4,1)}) fusion(f32[512,2048]{0,1:T(8,128)S(1)} %convolution_bitcast_fusion), kind=kLoop, calls=%fused_computation.8 | loop fusion | flops 3668992 | bytes 3674112 | tf_op jit(solution)/shard_map/reduce_sum | solution.py:35
  46.8 1.2 fusion.28
  48.1 1.2 copy.27
  50.0 2.5 %collective-permute-start.10 = (bf16[65,1024]{1,0:T(8,128)(2,1)}, bf16[65,1024]{1,0:T(8,128)(2,1)S(1)}, u32[]{:S(2)}, u32[]{:S(2)}) collective-permute-start(bf16[65,1024]{1,0:T(8,128)(2,1)} %fusion.21), channel_id=1, source_target_pairs={{3,0},{4,1},{5,2},{6,3},{7,4},{8,5},{9,6},{10,7},{11,8},{12,9},{13... | collective-permute-start | bytes 399368 | tf_op jit(solution)/shard_map/ppermute | solution.py:17
  52.5 2.5 %add_select_fusion = (f32[128,1024]{1,0:T(8,128)}, f32[128,1024]{1,0:T(8,128)}) fusion(bf16[128,1024]{1,0:T(8,128)(2,1)} %param.9, bf16[1024,1024]{1,0:T(8,128)(2,1)S(1)} %copy-done), kind=kOutput, calls=%fused_computation.34 | convolution fusion | flops 268959744 | bytes 3407872 | tf_op jit(solution)/shard_map/dot_general | solution.py:57
  55.0 1.3 mul.68
  56.3 1.6 %fusion.27 = (s32[1]{0:T(128)}, s32[1]{0:T(128)}, s32[1]{0:T(128)}, s32[1]{0:T(128)}, s32[1]{0:T(128)}, /*index=5*/s32[1]{0:T(128)}, s32[1]{0:T(128)}) fusion(s32[32]{0:T(128)} %param.11, s32[]{:T(128)S(6)} %max.20, s32[]{:T(128)S(6)} %select_n.204, s32[]{:T(128)S(6)} %max.21, s32[]{:T(128)S(6)} %select_n.197, s32[]{:T(128)S(6)} %select_n.193, ...), kind=kLoop, calls=%fused_computation.71 | loop fusion | bytes 84 | solution.py:47
  62.4 2.0 %copy.29 = f32[128,1024]{0,1:T(8,128)} copy(f32[128,1024]{1,0:T(8,128)} %get-tuple-element.96) | data formatting | bytes 1048576 | tf_op jit(solution)/shard_map/jit(_where)/select_n | solution.py:21
  64.4 3.0 %collective-permute-start.9 = (bf16[65,1024]{1,0:T(8,128)(2,1)}, bf16[65,1024]{1,0:T(8,128)(2,1)S(1)}, u32[]{:S(2)}, u32[]{:S(2)}) collective-permute-start(bf16[65,1024]{1,0:T(8,128)(2,1)} %fusion.21), channel_id=1, source_target_pairs={{0,3},{1,4},{2,5},{3,6},{4,7},{5,8},{6,9},{7,10},{8,11},{9,12},{10... | collective-permute-start | bytes 399368 | tf_op jit(solution)/shard_map/ppermute | solution.py:17
  67.4 5.1 %collective-permute-start.8 = (bf16[65,1024]{1,0:T(8,128)(2,1)}, bf16[65,1024]{1,0:T(8,128)(2,1)S(1)}, u32[]{:S(2)}, u32[]{:S(2)}) collective-permute-start(bf16[65,1024]{1,0:T(8,128)(2,1)} %fusion.21), channel_id=1, source_target_pairs={{2,0},{3,1},{4,2},{5,3},{6,4},{7,5},{8,6},{9,7},{10,8},{11,9},{12,... | collective-permute-start | bytes 399368 | tf_op jit(solution)/shard_map/ppermute | solution.py:17
  72.6 1.9 %collective-permute-start.7 = (bf16[65,1024]{1,0:T(8,128)(2,1)}, bf16[65,1024]{1,0:T(8,128)(2,1)S(1)}, u32[]{:S(2)}, u32[]{:S(2)}) collective-permute-start(bf16[65,1024]{1,0:T(8,128)(2,1)} %fusion.21), channel_id=1, source_target_pairs={{0,2},{1,3},{2,4},{3,5},{4,6},{5,7},{6,8},{7,9},{8,10},{9,11},{10,... | collective-permute-start | bytes 399368 | tf_op jit(solution)/shard_map/ppermute | solution.py:17
  74.5 4.4 %collective-permute-start.6 = (bf16[65,1024]{1,0:T(8,128)(2,1)}, bf16[65,1024]{1,0:T(8,128)(2,1)S(1)}, u32[]{:S(2)}, u32[]{:S(2)}) collective-permute-start(bf16[65,1024]{1,0:T(8,128)(2,1)} %fusion.21), channel_id=1, source_target_pairs={{1,0},{2,1},{3,2},{4,3},{5,4},{6,5},{7,6},{8,7},{9,8},{10,9},{11,1... | collective-permute-start | bytes 399368 | tf_op jit(solution)/shard_map/ppermute | solution.py:17
  78.9 1.9 %collective-permute-start.5 = (bf16[65,1024]{1,0:T(8,128)(2,1)}, bf16[65,1024]{1,0:T(8,128)(2,1)S(1)}, u32[]{:S(2)}, u32[]{:S(2)}) collective-permute-start(bf16[65,1024]{1,0:T(8,128)(2,1)} %fusion.21), channel_id=1, source_target_pairs={{0,1},{1,2},{2,3},{3,4},{4,5},{5,6},{6,7},{7,8},{8,9},{9,10},{10,1... | collective-permute-start | bytes 399368 | tf_op jit(solution)/shard_map/ppermute | solution.py:17
  80.8 1.3 fusion.26
  82.2 5.2 %collective-permute-done.5 = bf16[65,1024]{1,0:T(8,128)(2,1)S(1)} collective-permute-done((bf16[65,1024]{1,0:T(8,128)(2,1)}, bf16[65,1024]{1,0:T(8,128)(2,1)S(1)}, u32[]{:S(2)}, u32[]{:S(2)}) %collective-permute-start.5) | collective-permute-done | bytes 133152 | tf_op jit(solution)/shard_map/ppermute | solution.py:17
  88.4 1.0 copy.28
  89.4 1.3 multiply_reduce_fusion.2
  90.8 1.9 %multiply_reduce_fusion.1 = (f32[128]{0:T(128)S(1)}, f32[128,16,64]{0,2,1:T(8,128)S(1)}) fusion(f32[16,64]{1,0:T(8,128)} %mul.68, f32[128,16]{0,1:T(8,128)S(1)} %multiply_reduce_fusion.2, f32[64,16,64]{0,2,1:T(8,128)} %bitcast.90, f32[128,16,64]{0,2,1:T(8,128)} %bitcast.85), kind=kOutput, calls=%fused_computation.31 | convolution fusion | flops 101056384 | bytes 1323520 | tf_op jit(solution)/shard_map/phd,dhe->phe/dot_general | solution.py:61
  93.8 1.8 %fusion.11 = f32[16,64,64]{2,1,0:T(8,128)} fusion(f32[128,16,64]{0,2,1:T(8,128)S(1)} %bitcast.86, f32[128]{0:T(128)S(1)} %subtract_reduce_fusion, f32[16,64]{1,0:T(8,128)S(1)} %copy-done.11, f32[128,16]{0,1:T(8,128)S(1)} %multiply_reduce_fusion.2), kind=kOutput, calls=%fused_computation.35 | convolution fusion | flops 100925440 | bytes 799232 | tf_op jit(solution)/shard_map/phd,phe->dhe/dot_general | solution.py:81
  97.2 2.0 %copy.32 = f32[128,1024]{1,0:T(8,128)} copy(f32[128,1024]{0,1:T(8,128)} %bitcast.87) | data formatting | bytes 1048576 | tf_op jit(solution)/shard_map/mul | solution.py:88
  99.3 1.2 copy.33
  100.5 1.4 multiply_reduce_fusion
  103.1 1.9 %collective-permute-start.16 = (bf16[65,1024]{1,0:T(8,128)(2,1)}, bf16[65,1024]{1,0:T(8,128)(2,1)S(1)}, u32[]{:S(2)}, u32[]{:S(2)}) collective-permute-start(bf16[65,1024]{1,0:T(8,128)(2,1)} %fusion.20), channel_id=1, source_target_pairs={{3,0},{4,1},{5,2},{6,3},{7,4},{8,5},{9,6},{10,7},{11,8},{12,9},{13... | collective-permute-start | bytes 399368 | tf_op jit(solution)/shard_map/ppermute | solution.py:17
  105.0 3.6 %collective-permute-start.15 = (bf16[65,1024]{1,0:T(8,128)(2,1)}, bf16[65,1024]{1,0:T(8,128)(2,1)}, u32[]{:S(2)}, u32[]{:S(2)}) collective-permute-start(bf16[65,1024]{1,0:T(8,128)(2,1)} %fusion.20), channel_id=1, source_target_pairs={{0,3},{1,4},{2,5},{3,6},{4,7},{5,8},{6,9},{7,10},{8,11},{9,12},{10... | collective-permute-start | bytes 399368 | tf_op jit(solution)/shard_map/ppermute | solution.py:17
  108.7 3.3 %collective-permute-start.14 = (bf16[65,1024]{1,0:T(8,128)(2,1)}, bf16[65,1024]{1,0:T(8,128)(2,1)}, u32[]{:S(2)}, u32[]{:S(2)}) collective-permute-start(bf16[65,1024]{1,0:T(8,128)(2,1)} %fusion.20), channel_id=1, source_target_pairs={{2,0},{3,1},{4,2},{5,3},{6,4},{7,5},{8,6},{9,7},{10,8},{11,9},{12,... | collective-permute-start | bytes 399368 | tf_op jit(solution)/shard_map/ppermute | solution.py:17
  111.9 2.6 %collective-permute-start.13 = (bf16[65,1024]{1,0:T(8,128)(2,1)}, bf16[65,1024]{1,0:T(8,128)(2,1)}, u32[]{:S(2)}, u32[]{:S(2)}) collective-permute-start(bf16[65,1024]{1,0:T(8,128)(2,1)} %fusion.20), channel_id=1, source_target_pairs={{0,2},{1,3},{2,4},{3,5},{4,6},{5,7},{6,8},{7,9},{8,10},{9,11},{10,... | collective-permute-start | bytes 399368 | tf_op jit(solution)/shard_map/ppermute | solution.py:17
  114.5 3.4 %collective-permute-start.12 = (bf16[65,1024]{1,0:T(8,128)(2,1)}, bf16[65,1024]{1,0:T(8,128)(2,1)}, u32[]{:S(2)}, u32[]{:S(2)}) collective-permute-start(bf16[65,1024]{1,0:T(8,128)(2,1)} %fusion.20), channel_id=1, source_target_pairs={{1,0},{2,1},{3,2},{4,3},{5,4},{6,5},{7,6},{8,7},{9,8},{10,9},{11,1... | collective-permute-start | bytes 399368 | tf_op jit(solution)/shard_map/ppermute | solution.py:17
  118.0 3.0 %fusion.8 = f32[128,16,64]{0,2,1:T(8,128)} fusion(f32[64,16,64]{0,2,1:T(8,128)} %bitcast.91, f32[128,16]{0,1:T(8,128)} %copy-done.10, f32[128]{0:T(128)} %copy-done.15, f32[16,64]{1,0:T(8,128)} %mul.68, f32[128,16]{0,1:T(8,128)} %copy-done.9, f32[16,64]{1,0:T(8,128)} %copy-done.12), kind=kOutput, calls=%fused_computation.17 | convolution fusion | flops 101187584 | bytes 811520 | tf_op jit(solution)/shard_map/phe,dhe->phd/dot_general | solution.py:87
  121.0 2.1 %copy.31 = f32[128,1024]{1,0:T(8,128)} copy(f32[128,1024]{0,1:T(8,128)} %bitcast.93) | data formatting | bytes 1048576 | tf_op jit(solution)/shard_map/reshape | solution.py:90
  123.1 2.1 %collective-permute-start.11 = (bf16[65,1024]{1,0:T(8,128)(2,1)}, bf16[65,1024]{1,0:T(8,128)(2,1)S(1)}, u32[]{:S(2)}, u32[]{:S(2)}) collective-permute-start(bf16[65,1024]{1,0:T(8,128)(2,1)} %fusion.20), channel_id=1, source_target_pairs={{0,1},{1,2},{2,3},{3,4},{4,5},{5,6},{6,7},{7,8},{8,9},{9,10},{10,1... | collective-permute-start | bytes 399368 | tf_op jit(solution)/shard_map/ppermute | solution.py:17
  125.2 2.7 %convolution_convert_fusion.1 = bf16[128,1024]{1,0:T(8,128)(2,1)} fusion(bf16[1024,1024]{1,0:T(8,128)(2,1)S(1)} %copy-done, f32[128,1024]{1,0:T(8,128)} %copy.31, f32[128,1024]{1,0:T(8,128)} %get-tuple-element.97), kind=kOutput, calls=%fused_computation.20 | convolution fusion | flops 269221888 | bytes 3407872 | tf_op jit(solution)/shard_map/dot_general | solution.py:91
  127.9 3.6 %collective-permute-done.11 = bf16[65,1024]{1,0:T(8,128)(2,1)S(1)} collective-permute-done((bf16[65,1024]{1,0:T(8,128)(2,1)}, bf16[65,1024]{1,0:T(8,128)(2,1)S(1)}, u32[]{:S(2)}, u32[]{:S(2)}) %collective-permute-start.11) | collective-permute-done | bytes 133152 | tf_op jit(solution)/shard_map/ppermute | solution.py:17
  131.6 1.3 add_convert_fusion
  133.1 2.7 %convolution_convert_fusion = bf16[16,64,512]{2,1,0:T(8,128)(2,1)} fusion(bf16[64,16,64]{0,2,1:T(8,128)(2,1)S(1)} %bitcast.82, bf16[512,16,64]{0,2,1:T(8,128)(2,1)} %bitcast.80), kind=kOutput, calls=%fused_computation.15 | convolution fusion | flops 67633152 | bytes 2228224 | tf_op jit(solution)/shard_map/thd,dhe->the/dot_general | solution.py:155
  136.9 2.4 %fusion.4 = bf16[512,1024]{0,1:T(8,128)(2,1)S(1)} fusion(f32[16,64,512]{2,1,0:T(8,128)S(1)} %convolution_add_fusion, pred[512,1024]{0,1:T(8,128)(4,1)S(1)} %copy-done.4, f32[512,2048]{0,1:T(8,128)} %copy-done.2), kind=kLoop, calls=%fused_computation.7 | loop fusion | flops 2097152 | bytes 5767168 | tf_op jit(solution)/shard_map/convert_element_type | solution.py:153
  139.4 5.6 %fusion.5 = bf16[512,1024]{1,0:T(8,128)(2,1)} fusion(bf16[1024,2048]{1,0:T(8,128)(2,1)} %bitcast.6, bf16[512,1024]{0,1:T(8,128)(2,1)S(1)} %bitcast.89, bf16[512,1024]{0,1:T(8,128)(2,1)S(1)} %fusion.4), kind=kOutput, calls=%fused_computation.14 | convolution fusion | flops 2152202240 | bytes 7340032 | tf_op jit(solution)/shard_map/dot_general | solution.py:160
  (73 shorter events, 12.2 us)
Async XLA Ops:
  0.6 51.9 %copy-start = (bf16[1024,1024]{1,0:T(8,128)(2,1)S(1)}, bf16[1024,1024]{1,0:T(8,128)(2,1)}, u32[]{:S(2)}) copy-start(bf16[1024,1024]{1,0:T(8,128)(2,1)} %param.14) | copy-start | bytes 6291460
  2.7 14.8 %collective-permute-start = (bf16[128,2048]{1,0:T(8,128)(2,1)S(1)}, bf16[128,2048]{1,0:T(8,128)(2,1)S(1)}, u32[]{:S(2)}, u32[]{:S(2)}) collective-permute-start(bf16[128,2048]{1,0:T(8,128)(2,1)S(1)} %constant_dynamic-update-slice_fusion), channel_id=1, source_target_pairs={{0,2},{1,5},{2,0},{3,7},{4,6},{5,1},{6,4},{7,3},{8,10},{9,13},{10,... | collective-permute-start | bytes 1572872 | tf_op jit(solution)/shard_map/ppermute | solution.py:108
  4.3 13.2 %collective-permute-start.1 = (bf16[128,2048]{1,0:T(8,128)(2,1)S(1)}, bf16[128,2048]{1,0:T(8,128)(2,1)}, u32[]{:S(2)}, u32[]{:S(2)}) collective-permute-start(bf16[128,2048]{1,0:T(8,128)(2,1)S(1)} %constant_dynamic-update-slice_fusion), channel_id=1, source_target_pairs={{0,4},{1,3},{2,6},{3,1},{4,0},{5,7},{6,2},{7,5},{8,12},{9,11},{10,... | collective-permute-start | bytes 1572872 | tf_op jit(solution)/shard_map/ppermute | solution.py:109
  19.9 13.5 %collective-permute-start.3 = (bf16[3,128,2048]{2,1,0:T(8,128)(2,1)}, bf16[3,128,2048]{2,1,0:T(8,128)(2,1)}, u32[]{:S(2)}, u32[]{:S(2)}) collective-permute-start(bf16[3,128,2048]{2,1,0:T(8,128)(2,1)} %pad_maximum_fusion), channel_id=1, source_target_pairs={{0,1},{1,0},{2,3},{3,2},{4,5},{5,4},{6,7},{7,6},{8,9},{9,8},{10,11... | collective-permute-start | bytes 4718600 | tf_op jit(solution)/shard_map/ppermute | solution.py:112
  23.3 9.2 %collective-permute-start.2 = (bf16[128,2048]{1,0:T(8,128)(2,1)S(1)}, bf16[128,2048]{1,0:T(8,128)(2,1)S(1)}, u32[]{:S(2)}, u32[]{:S(2)}) collective-permute-start(bf16[128,2048]{1,0:T(8,128)(2,1)S(1)} %collective-permute-done), channel_id=1, source_target_pairs={{0,4},{1,3},{2,6},{3,1},{4,0},{5,7},{6,2},{7,5},{8,12},{9,11},{10,... | collective-permute-start | bytes 1572872 | tf_op jit(solution)/shard_map/ppermute | solution.py:110
  32.5 6.6 %collective-permute-start.4 = (bf16[128,2048]{1,0:T(8,128)(2,1)S(1)}, bf16[128,2048]{1,0:T(8,128)(2,1)S(1)}, u32[]{:S(2)}, u32[]{:S(2)}) collective-permute-start(bf16[128,2048]{1,0:T(8,128)(2,1)S(1)} %collective-permute-done.2), channel_id=1, source_target_pairs={{0,1},{1,0},{2,3},{3,2},{4,5},{5,4},{6,7},{7,6},{8,9},{9,8},{10,11... | collective-permute-start | bytes 1572872 | tf_op jit(solution)/shard_map/ppermute | solution.py:113
  33.3 6.6 %copy-start.16 = (bf16[512,1024]{1,0:T(8,128)(2,1)S(1)}, bf16[512,1024]{1,0:T(8,128)(2,1)}, u32[]{:S(2)}) copy-start(bf16[512,1024]{1,0:T(8,128)(2,1)} %param.8) | copy-start | bytes 3145732
  44.6 2.2 %copy-start.2 = (f32[512,2048]{0,1:T(8,128)}, f32[512,2048]{0,1:T(8,128)S(1)}, u32[]{:S(2)}) copy-start(f32[512,2048]{0,1:T(8,128)S(1)} %convolution_bitcast_fusion) | copy-start | bytes 12582916
  46.7 1.4 copy-start.1
  46.7 2.6 %copy-start.8 = (f32[1024]{0:T(1024)}, f32[1024]{0:T(1024)S(1)}, u32[]{:S(2)}) copy-start(f32[1024]{0:T(1024)S(1)} %get-tuple-element.82) | copy-start | bytes 12292
  50.0 28.9 %collective-permute-start.10 = (bf16[65,1024]{1,0:T(8,128)(2,1)}, bf16[65,1024]{1,0:T(8,128)(2,1)S(1)}, u32[]{:S(2)}, u32[]{:S(2)}) collective-permute-start(bf16[65,1024]{1,0:T(8,128)(2,1)} %fusion.21), channel_id=1, source_target_pairs={{3,0},{4,1},{5,2},{6,3},{7,4},{8,5},{9,6},{10,7},{11,8},{12,9},{13... | collective-permute-start | bytes 399368 | tf_op jit(solution)/shard_map/ppermute | solution.py:17
  64.4 17.7 %collective-permute-start.9 = (bf16[65,1024]{1,0:T(8,128)(2,1)}, bf16[65,1024]{1,0:T(8,128)(2,1)S(1)}, u32[]{:S(2)}, u32[]{:S(2)}) collective-permute-start(bf16[65,1024]{1,0:T(8,128)(2,1)} %fusion.21), channel_id=1, source_target_pairs={{0,3},{1,4},{2,5},{3,6},{4,7},{5,8},{6,9},{7,10},{8,11},{9,12},{10... | collective-permute-start | bytes 399368 | tf_op jit(solution)/shard_map/ppermute | solution.py:17
  67.4 14.7 %collective-permute-start.8 = (bf16[65,1024]{1,0:T(8,128)(2,1)}, bf16[65,1024]{1,0:T(8,128)(2,1)S(1)}, u32[]{:S(2)}, u32[]{:S(2)}) collective-permute-start(bf16[65,1024]{1,0:T(8,128)(2,1)} %fusion.21), channel_id=1, source_target_pairs={{2,0},{3,1},{4,2},{5,3},{6,4},{7,5},{8,6},{9,7},{10,8},{11,9},{12,... | collective-permute-start | bytes 399368 | tf_op jit(solution)/shard_map/ppermute | solution.py:17
  72.6 9.6 %collective-permute-start.7 = (bf16[65,1024]{1,0:T(8,128)(2,1)}, bf16[65,1024]{1,0:T(8,128)(2,1)S(1)}, u32[]{:S(2)}, u32[]{:S(2)}) collective-permute-start(bf16[65,1024]{1,0:T(8,128)(2,1)} %fusion.21), channel_id=1, source_target_pairs={{0,2},{1,3},{2,4},{3,5},{4,6},{5,7},{6,8},{7,9},{8,10},{9,11},{10,... | collective-permute-start | bytes 399368 | tf_op jit(solution)/shard_map/ppermute | solution.py:17
  74.5 7.7 %collective-permute-start.6 = (bf16[65,1024]{1,0:T(8,128)(2,1)}, bf16[65,1024]{1,0:T(8,128)(2,1)S(1)}, u32[]{:S(2)}, u32[]{:S(2)}) collective-permute-start(bf16[65,1024]{1,0:T(8,128)(2,1)} %fusion.21), channel_id=1, source_target_pairs={{1,0},{2,1},{3,2},{4,3},{5,4},{6,5},{7,6},{8,7},{9,8},{10,9},{11,1... | collective-permute-start | bytes 399368 | tf_op jit(solution)/shard_map/ppermute | solution.py:17
  78.9 8.5 %collective-permute-start.5 = (bf16[65,1024]{1,0:T(8,128)(2,1)}, bf16[65,1024]{1,0:T(8,128)(2,1)S(1)}, u32[]{:S(2)}, u32[]{:S(2)}) collective-permute-start(bf16[65,1024]{1,0:T(8,128)(2,1)} %fusion.21), channel_id=1, source_target_pairs={{0,1},{1,2},{2,3},{3,4},{4,5},{5,6},{6,7},{7,8},{8,9},{9,10},{10,1... | collective-permute-start | bytes 399368 | tf_op jit(solution)/shard_map/ppermute | solution.py:17
  88.2 4.5 %copy-start.13 = (s32[256,1]{0,1:T(1,128)S(1)}, s32[256,1]{0,1:T(1,128)}, u32[]{:S(2)}) copy-start(s32[256,1]{0,1:T(1,128)} %get-tuple-element.87) | copy-start | bytes 3076
  88.2 4.5 %copy-start.14 = (s32[256,1]{0,1:T(1,128)S(1)}, s32[256,1]{0,1:T(1,128)}, u32[]{:S(2)}) copy-start(s32[256,1]{0,1:T(1,128)} %get-tuple-element.88) | copy-start | bytes 3076
  88.3 5.5 %copy-start.11 = (f32[16,64]{1,0:T(8,128)S(1)}, f32[16,64]{1,0:T(8,128)}, u32[]{:S(2)}) copy-start(f32[16,64]{1,0:T(8,128)} %mul.68) | copy-start | bytes 12292
  88.4 7.2 %copy-start.12 = (f32[16,64]{1,0:T(8,128)}, f32[16,64]{1,0:T(8,128)S(1)}, u32[]{:S(2)}) copy-start(f32[16,64]{1,0:T(8,128)S(1)} %mul.65) | copy-start | bytes 12292
  89.4 4.3 %copy-start.3 = (f32[128,1024]{0,1:T(8,128)S(1)}, f32[128,1024]{0,1:T(8,128)}, u32[]{:S(2)}) copy-start(f32[128,1024]{0,1:T(8,128)} %copy.29) | copy-start | bytes 1572868
  90.8 5.0 %copy-start.9 = (f32[128,16]{0,1:T(8,128)}, f32[128,16]{0,1:T(8,128)S(1)}, u32[]{:S(2)}) copy-start(f32[128,16]{0,1:T(8,128)S(1)} %multiply_reduce_fusion.2) | copy-start | bytes 24580
  93.7 3.5 %copy-start.15 = (f32[128]{0:T(128)}, f32[128]{0:T(128)S(1)}, u32[]{:S(2)}) copy-start(f32[128]{0:T(128)S(1)} %subtract_reduce_fusion) | copy-start | bytes 1540
  95.8 0.6 copy-start.10
  101.8 0.6 copy-start.6
  103.1 20.0 %collective-permute-start.16 = (bf16[65,1024]{1,0:T(8,128)(2,1)}, bf16[65,1024]{1,0:T(8,128)(2,1)S(1)}, u32[]{:S(2)}, u32[]{:S(2)}) collective-permute-start(bf16[65,1024]{1,0:T(8,128)(2,1)} %fusion.20), channel_id=1, source_target_pairs={{3,0},{4,1},{5,2},{6,3},{7,4},{8,5},{9,6},{10,7},{11,8},{12,9},{13... | collective-permute-start | bytes 399368 | tf_op jit(solution)/shard_map/ppermute | solution.py:17
  105.0 22.9 %collective-permute-start.15 = (bf16[65,1024]{1,0:T(8,128)(2,1)}, bf16[65,1024]{1,0:T(8,128)(2,1)}, u32[]{:S(2)}, u32[]{:S(2)}) collective-permute-start(bf16[65,1024]{1,0:T(8,128)(2,1)} %fusion.20), channel_id=1, source_target_pairs={{0,3},{1,4},{2,5},{3,6},{4,7},{5,8},{6,9},{7,10},{8,11},{9,12},{10... | collective-permute-start | bytes 399368 | tf_op jit(solution)/shard_map/ppermute | solution.py:17
  108.7 19.3 %collective-permute-start.14 = (bf16[65,1024]{1,0:T(8,128)(2,1)}, bf16[65,1024]{1,0:T(8,128)(2,1)}, u32[]{:S(2)}, u32[]{:S(2)}) collective-permute-start(bf16[65,1024]{1,0:T(8,128)(2,1)} %fusion.20), channel_id=1, source_target_pairs={{2,0},{3,1},{4,2},{5,3},{6,4},{7,5},{8,6},{9,7},{10,8},{11,9},{12,... | collective-permute-start | bytes 399368 | tf_op jit(solution)/shard_map/ppermute | solution.py:17
  111.9 16.0 %collective-permute-start.13 = (bf16[65,1024]{1,0:T(8,128)(2,1)}, bf16[65,1024]{1,0:T(8,128)(2,1)}, u32[]{:S(2)}, u32[]{:S(2)}) collective-permute-start(bf16[65,1024]{1,0:T(8,128)(2,1)} %fusion.20), channel_id=1, source_target_pairs={{0,2},{1,3},{2,4},{3,5},{4,6},{5,7},{6,8},{7,9},{8,10},{9,11},{10,... | collective-permute-start | bytes 399368 | tf_op jit(solution)/shard_map/ppermute | solution.py:17
  114.5 13.4 %collective-permute-start.12 = (bf16[65,1024]{1,0:T(8,128)(2,1)}, bf16[65,1024]{1,0:T(8,128)(2,1)}, u32[]{:S(2)}, u32[]{:S(2)}) collective-permute-start(bf16[65,1024]{1,0:T(8,128)(2,1)} %fusion.20), channel_id=1, source_target_pairs={{1,0},{2,1},{3,2},{4,3},{5,4},{6,5},{7,6},{8,7},{9,8},{10,9},{11,1... | collective-permute-start | bytes 399368 | tf_op jit(solution)/shard_map/ppermute | solution.py:17
  123.1 8.5 %copy-start.7 = (f32[1024]{0:T(1024)S(1)}, f32[1024]{0:T(1024)}, u32[]{:S(2)}) copy-start(f32[1024]{0:T(1024)} %copy-done.6) | copy-start | bytes 12292
  123.1 8.5 %collective-permute-start.11 = (bf16[65,1024]{1,0:T(8,128)(2,1)}, bf16[65,1024]{1,0:T(8,128)(2,1)S(1)}, u32[]{:S(2)}, u32[]{:S(2)}) collective-permute-start(bf16[65,1024]{1,0:T(8,128)(2,1)} %fusion.20), channel_id=1, source_target_pairs={{0,1},{1,2},{2,3},{3,4},{4,5},{5,6},{6,7},{7,8},{8,9},{9,10},{10,1... | collective-permute-start | bytes 399368 | tf_op jit(solution)/shard_map/ppermute | solution.py:17
  135.9 1.0 copy-start.4
  136.9 2.5 %copy-start.5 = (bf16[16,64,512]{2,1,0:T(8,128)(2,1)S(1)}, bf16[16,64,512]{2,1,0:T(8,128)(2,1)}, u32[]{:S(2)}) copy-start(bf16[16,64,512]{2,1,0:T(8,128)(2,1)} %convolution_convert_fusion) | copy-start | bytes 3145732

commit v6 on v4

--- a/solution.py
+++ b/solution.py
@@ -2,6 +2,8 @@
 import jax.numpy as jnp
 from jax import lax
 from jax.sharding import PartitionSpec as P
+from jax.experimental import pallas as pl
+from jax.experimental.pallas import tpu as pltpu
 
 H = 16
 DH = 64
@@ -94,6 +96,86 @@
     return (pair_loss, pose_grad.astype(jnp.bfloat16), pose_state)
 
 
+def pose_kernel(pose_ref, pair_ref, state_ref, query_ref, weight_ref, loss_ref, grad_ref, back_ref, feat_ref):
+    count, width = pose_ref.shape
+    lanes = 2 * DH
+    queries = jnp.dot(pose_ref[...], query_ref[...], preferred_element_type=jnp.float32)
+    query_feat = features(queries)
+    norm = state_ref[DH : DH + 1, :]
+    weight = weight_ref[...]
+    head_row = lax.broadcasted_iota(jnp.int32, (lanes, lanes), 0) // DH
+    head_col = lax.broadcasted_iota(jnp.int32, (lanes, lanes), 1) // DH
+    same = head_row == head_col
+    ones = same.astype(jnp.float32)
+    blocks, numers, denoms = [], [], []
+    scores = jnp.zeros((count, 1), jnp.float32)
+    for g in range(width // lanes):
+        cols = slice(g * lanes, (g + 1) * lanes)
+        part = state_ref[0:DH, cols]
+        block = jnp.where(same, jnp.concatenate([part, part], axis=0), 0.0)
+        feat = query_feat[:, cols]
+        numer = jnp.dot(feat, block, precision=highest, preferred_element_type=jnp.float32)
+        denom = jnp.dot(
+            feat * norm[:, cols], ones, precision=highest, preferred_element_type=jnp.float32
+        )
+        attended = numer / denom
+        scores = scores + jnp.sum(attended * weight[:, cols], axis=1, keepdims=True)
+        blocks.append(block)
+        numers.append(attended)
+        denoms.append(denom)
+    slots = lax.broadcasted_iota(jnp.int32, (count, pair_ref.shape[1]), 0)
+    is_better = slots == pair_ref[0:1, :]
+    is_worse = slots == pair_ref[1:2, :]
+    better = jnp.sum(jnp.where(is_better, scores, 0.0), axis=0, keepdims=True)
+    worse = jnp.sum(jnp.where(is_worse, scores, 0.0), axis=0, keepdims=True)
+    delta = worse - better
+    loss_ref[...] = jnp.maximum(delta, 0.0) + jnp.log1p(jnp.exp(-jnp.abs(delta)))
+    push = 1.0 / (1.0 + jnp.exp(-delta))
+    score_grad = jnp.sum(
+        jnp.where(is_worse, push, 0.0) - jnp.where(is_better, push, 0.0), axis=1, keepdims=True
+    )
+    low = lax.broadcasted_iota(jnp.int32, (DH, lanes), 1) < DH
+    for g in range(width // lanes):
+        cols = slice(g * lanes, (g + 1) * lanes)
+        feat = query_feat[:, cols]
+        attended_grad = score_grad * weight[:, cols]
+        numer_grad = attended_grad / denoms[g]
+        denom_grad = -jnp.dot(
+            attended_grad * numers[g], ones, precision=highest, preferred_element_type=jnp.float32
+        ) / denoms[g]
+        outer = jnp.dot(feat.T, numer_grad, precision=highest, preferred_element_type=jnp.float32)
+        back_ref[0:DH, cols] = jnp.where(low, outer[:DH], outer[DH:])
+        back_ref[DH : DH + 1, cols] = jnp.sum(feat * denom_grad, axis=0, keepdims=True)
+        feat_grad = lax.dot_general(
+            numer_grad,
+            blocks[g],
+            (((1,), (1,)), ((), ())),
+            precision=highest,
+            preferred_element_type=jnp.float32,
+        ) + denom_grad * norm[:, cols]
+        feat_ref[:, cols] = (feat_grad * slope(queries[:, cols])).astype(feat_ref.dtype)
+    grad = lax.dot_general(
+        feat_ref[...], query_ref[...], (((1,), (1,)), ((), ())), preferred_element_type=jnp.float32
+    )
+    grad_ref[...] = grad.astype(grad_ref.dtype)
+
+
+def pose_fused(pose_rows, pair_rows, state, w_query, score_weight, interpret=False):
+    count, width = pose_rows.shape
+    pairs_t = pair_rows.T
+    loss, grad, back = pl.pallas_call(
+        pose_kernel,
+        out_shape=(
+            jax.ShapeDtypeStruct((1, pair_rows.shape[0]), jnp.float32),
+            jax.ShapeDtypeStruct((count, width), jnp.bfloat16),
+            jax.ShapeDtypeStruct(state.shape, jnp.float32),
+        ),
+        scratch_shapes=[pltpu.VMEM((count, width), jnp.bfloat16)],
+        interpret=interpret,
+    )(pose_rows, pairs_t, state, w_query, score_weight.reshape(1, width))
+    return (loss.reshape(pair_rows.shape[0]), grad, back)
+
+
 def gather_rows(shard):
     count = lax.axis_size("blk")
     if count != 8:
@@ -132,7 +214,7 @@
     key_feat = features(keys).astype(jnp.bfloat16)
     val_round = values.astype(jnp.bfloat16)
     state = complex_total(local_state(key_feat, val_round), block_complex)
-    pair_loss, pose_grad, pose_state = pose_side(poses, pairs, state, w_query, score_weight)
+    pair_loss, pose_grad, pose_state = pose_fused(poses, pairs, state, w_query, score_weight)
     state_grad = complex_total(pose_state, block_complex).astype(jnp.bfloat16)
     key_heads = key_feat.reshape(rows, H, DH)
     val_heads = val_round.reshape(rows, H, DH)

time: 141 us -> 117 us (0.83)
  matrix products: 22.3 us -> 8.01 us
  local copies, waits for them, and re-layouts: 25.8 us -> 12.4 us
  Pallas kernels: 0 us -> 6.8 us
  other arithmetic: 13.7 us -> 9.26 us
  starting transfers between devices: 39.5 us -> 43.1 us
    dot_general x5 -> x0, matrix products: 12 us -> none  [the longest x1 3.06 us: pose_side(): jnp.einsum('phe,dhe->phd', numer_grad, state_heads, precision=highest)]
    pallas_call x0 -> x1, Pallas kernels: none -> 6.8 us  [pose_fused(): pl.pallas_call(pose_kernel, out_shape=(jax.ShapeDtypeStruct((1, pair_rows...]
    mul x4 -> x0, local copies, waits for them, and re-layouts: 4.29 us -> none  [the longest x2 2.87 us: pose_side(): denom_grad[:, :, None] * norm_heads[None]]
    ppermute x12, starting transfers between devices: 36.3 us -> 40 us  [from_behind(): lax.ppermute(value, axis, [(source, source + steps) for source in range(i...]
    reduce_sum x5 -> x0, other arithmetic: 3.31 us -> none  [the longest x1 1.35 us: pose_side(): jnp.sum(query_heads * denom_grad[:, :, None], axis=0).reshape(H * DH)]
    reshape x2 -> x0, local copies, waits for them, and re-layouts: 3.29 us -> none  [the longest x1 2.07 us: pose_side(): feat_grad.reshape(count, H * DH) * slope(queries)]
    slice x4 -> x0, local copies, waits for them, and re-layouts: 2.4 us -> none  [the longest x1 1.33 us: pose_side(): is_worse = slots == pair_rows[:, 1:2]]
    dot_general x1, matrix products: 2.71 us -> 0.4 us  [shards(): jnp.einsum('thd,dhe->the', key_heads, grad_heads, preferred_element_type=...]
  transfers between devices with their start and end apart: 15 -> 15, of which waited for: 5 -> 7; matrix products, arithmetic and copies ran while one was open for 12% -> 2% of each run, Pallas kernels for 0% -> 0%
where the time goes in v6:
time: 117 us
  starting transfers between devices  43.1 us (37%)
  waiting for transfers between devices  31.4 us (27%)
  local copies, waits for them, and re-layouts  12.4 us (11%)
  other arithmetic  9.26 us (8%)
  matrix products  8.01 us (7%)
  Pallas kernels  6.8 us (6%)
  between operations  5.46 us (5%)
    ppermute x12, starting transfers between devices, from_behind(): lax.ppermute(value, axis, [(source, source + steps) for source in range(i...  40 us
    ppermute x1, waiting for transfers between devices, gather_rows(): lax.ppermute(jnp.stack([shard, early]), 'blk', [(s, s ^ (2 if s % 2 else...  13.3 us
    ppermute x1, waiting for transfers between devices, gather_rows(): lax.ppermute(shard, 'blk', [(s, s ^ (4 if s % 2 else 2)) for s in range(c...  7.69 us
    pallas_call x1, Pallas kernels, pose_fused(): pl.pallas_call(pose_kernel, out_shape=(jax.ShapeDtypeStruct((1, pair_rows...  6.8 us
    ppermute x12, waiting for transfers between devices, from_behind(): lax.ppermute(value, axis, [(source, source + steps) for source in range(i...  6.69 us
    dynamic_update_slice x8, local copies, waits for them, and re-layouts, gather_rows(): full = lax.dynamic_update_slice(full, pieces[k][None], (at, 0, 0))  4.52 us
    ppermute x1, waiting for transfers between devices, gather_rows(): sibling = lax.ppermute(mine, 'blk', [(s, s ^ 1) for s in range(count)])  3.75 us
    dot_general x1, matrix products, shards(): lax.dot_general(both_grad, full_both, contract, preferred_element_type=jn...  3.38 us
  transfers between devices with their start and end apart: 15, of which 7 were waited for; matrix products, arithmetic and copies ran while one was open for 2% of the time, Pallas kernels for 0%

profile of v6, /device:TPU:16, one launch (start us, length us, event | category | flops | bytes accessed | tf_op | source)
XLA Modules:
  0.0 116.5 jit_solution(17552396993342851630)
XLA Ops:
  0.6 1.1 constant_dynamic-update-slice_fusion.1
  1.7 1.0 constant_dynamic-update-slice_fusion
  2.7 1.6 %collective-permute-start = (bf16[128,2048]{1,0:T(8,128)(2,1)S(1)}, bf16[128,2048]{1,0:T(8,128)(2,1)S(1)}, u32[]{:S(2)}, u32[]{:S(2)}) collective-permute-start(bf16[128,2048]{1,0:T(8,128)(2,1)S(1)} %constant_dynamic-update-slice_fusion), channel_id=1, source_target_pairs={{0,2},{1,5},{2,0},{3,7},{4,6},{5,1},{6,4},{7,3},{8,10},{9,13},{10,... | collective-permute-start | bytes 1572872 | tf_op jit(solution)/shard_map/ppermute | solution.py:188
  4.2 7.7 %collective-permute-done = bf16[128,2048]{1,0:T(8,128)(2,1)S(1)} collective-permute-done((bf16[128,2048]{1,0:T(8,128)(2,1)S(1)}, bf16[128,2048]{1,0:T(8,128)(2,1)S(1)}, u32[]{:S(2)}, u32[]{:S(2)}) %collective-permute-start) | collective-permute-done | bytes 524320 | tf_op jit(solution)/shard_map/ppermute | solution.py:188
  12.0 1.6 %collective-permute-start.1 = (bf16[2,128,2048]{2,1,0:T(8,128)(2,1)S(1)}, bf16[2,128,2048]{2,1,0:T(8,128)(2,1)S(1)}, u32[]{:S(2)}, u32[]{:S(2)}) collective-permute-start(bf16[2,128,2048]{2,1,0:T(8,128)(2,1)S(1)} %pad_maximum_fusion.1), channel_id=1, source_target_pairs={{0,4},{1,3},{2,6},{3,1},{4,0},{5,7},{6,2},{7,5},{8,12},{9,11},{10,... | collective-permute-start | bytes 3145736 | tf_op jit(solution)/shard_map/ppermute | solution.py:189
  13.6 13.3 %collective-permute-done.1 = bf16[2,128,2048]{2,1,0:T(8,128)(2,1)S(1)} collective-permute-done((bf16[2,128,2048]{2,1,0:T(8,128)(2,1)S(1)}, bf16[2,128,2048]{2,1,0:T(8,128)(2,1)S(1)}, u32[]{:S(2)}, u32[]{:S(2)}) %collective-permute-start.1) | collective-permute-done | bytes 1048608 | tf_op jit(solution)/shard_map/ppermute | solution.py:189
  26.9 1.5 %pad_maximum_fusion = bf16[4,128,2048]{2,1,0:T(8,128)(2,1)} fusion(bf16[2,128,2048]{2,1,0:T(8,128)(2,1)S(1)} %collective-permute-done.1, bf16[1,128,2048]{2,1,0:T(8,128)(2,1)S(1)} %bitcast.55, bf16[1,128,2048]{2,1,0:T(8,128)(2,1)S(1)} %bitcast.53), kind=kLoop, calls=%fused_computation.2 | loop fusion | flops 2097152 | bytes 4194304 | tf_op jit(solution)/shard_map/concatenate | solution.py:192
  28.4 0.5 broadcast_in_dim.50
  29.2 3.8 %collective-permute-done.2 = bf16[4,128,2048]{2,1,0:T(8,128)(2,1)} collective-permute-done((bf16[4,128,2048]{2,1,0:T(8,128)(2,1)}, bf16[4,128,2048]{2,1,0:T(8,128)(2,1)}, u32[]{:S(2)}, u32[]{:S(2)}) %collective-permute-start.2) | collective-permute-done | bytes 2097184 | tf_op jit(solution)/shard_map/ppermute | solution.py:193
  32.9 1.1 slice_dynamic-update-slice_fusion.3
  34.0 1.1 slice_dynamic-update-slice_fusion.2
  35.1 1.1 slice_dynamic-update-slice_fusion.1
  36.2 1.1 slice_dynamic-update-slice_fusion
  37.3 2.5 %convolution_bitcast_fusion = f32[512,2048]{0,1:T(8,128)S(1)} fusion(bf16[1024,2048]{1,0:T(8,128)(2,1)S(1)} %bitcast.56, bf16[512,1024]{1,0:T(8,128)(2,1)S(1)} %copy-done), kind=kOutput, calls=%fused_computation | convolution fusion | flops 2147483648 | bytes 9437184 | tf_op jit(solution)/shard_map/dot_general | solution.py:211
  39.8 0.1 slice.99
  40.0 2.0 %convert_reduce_fusion = (f32[1024]{0:T(1024)S(1)}, bf16[512,1024]{0,1:T(8,128)(2,1)S(1)}, pred[512,1024]{0,1:T(8,128)(4,1)}) fusion(f32[512,2048]{0,1:T(8,128)S(1)} %convolution_bitcast_fusion), kind=kLoop, calls=%fused_computation.9 | loop fusion | flops 3668992 | bytes 3674112 | tf_op jit(solution)/shard_map/reduce_sum | solution.py:37
  42.0 1.3 %fusion.12 = f32[16,64,64]{2,1,0:T(8,128)} fusion(bf16[512,16,64]{0,2,1:T(8,128)(2,1)S(1)} %bitcast.48, bf16[512,16,64]{0,2,1:T(8,128)(2,1)S(1)} %bitcast.50), kind=kOutput, calls=%fused_computation.35 | convolution fusion | flops 67108864 | bytes 2359296 | tf_op jit(solution)/shard_map/thd,the->dhe/dot_general | solution.py:34
  43.2 1.2 %copy.14 = f32[64,1024]{1,0:T(8,128)S(1)} copy(f32[64,1024]{0,1:T(8,128)} %bitcast.60) | data formatting | bytes 524288 | tf_op jit(solution)/shard_map/reshape | solution.py:36
  44.5 0.7 fusion.8
  45.2 3.0 %collective-permute-start.8 = (bf16[65,1024]{1,0:T(8,128)(2,1)}, bf16[65,1024]{1,0:T(8,128)(2,1)S(1)}, u32[]{:S(2)}, u32[]{:S(2)}) collective-permute-start(bf16[65,1024]{1,0:T(8,128)(2,1)} %fusion.8), channel_id=1, source_target_pairs={{3,0},{4,1},{5,2},{6,3},{7,4},{8,5},{9,6},{10,7},{11,8},{12,9},{13... | collective-permute-start | bytes 399368 | tf_op jit(solution)/shard_map/ppermute | solution.py:19
  48.2 2.5 %collective-permute-start.7 = (bf16[65,1024]{1,0:T(8,128)(2,1)}, bf16[65,1024]{1,0:T(8,128)(2,1)}, u32[]{:S(2)}, u32[]{:S(2)}) collective-permute-start(bf16[65,1024]{1,0:T(8,128)(2,1)} %fusion.8), channel_id=1, source_target_pairs={{0,3},{1,4},{2,5},{3,6},{4,7},{5,8},{6,9},{7,10},{8,11},{9,12},{10... | collective-permute-start | bytes 399368 | tf_op jit(solution)/shard_map/ppermute | solution.py:19
  50.7 6.0 %collective-permute-start.6 = (bf16[65,1024]{1,0:T(8,128)(2,1)}, bf16[65,1024]{1,0:T(8,128)(2,1)}, u32[]{:S(2)}, u32[]{:S(2)}) collective-permute-start(bf16[65,1024]{1,0:T(8,128)(2,1)} %fusion.8), channel_id=1, source_target_pairs={{2,0},{3,1},{4,2},{5,3},{6,4},{7,5},{8,6},{9,7},{10,8},{11,9},{12,... | collective-permute-start | bytes 399368 | tf_op jit(solution)/shard_map/ppermute | solution.py:19
  56.8 1.9 %collective-permute-start.5 = (bf16[65,1024]{1,0:T(8,128)(2,1)}, bf16[65,1024]{1,0:T(8,128)(2,1)}, u32[]{:S(2)}, u32[]{:S(2)}) collective-permute-start(bf16[65,1024]{1,0:T(8,128)(2,1)} %fusion.8), channel_id=1, source_target_pairs={{0,2},{1,3},{2,4},{3,5},{4,6},{5,7},{6,8},{7,9},{8,10},{9,11},{10,... | collective-permute-start | bytes 399368 | tf_op jit(solution)/shard_map/ppermute | solution.py:19
  58.7 4.0 %collective-permute-start.4 = (bf16[65,1024]{1,0:T(8,128)(2,1)}, bf16[65,1024]{1,0:T(8,128)(2,1)}, u32[]{:S(2)}, u32[]{:S(2)}) collective-permute-start(bf16[65,1024]{1,0:T(8,128)(2,1)} %fusion.8), channel_id=1, source_target_pairs={{1,0},{2,1},{3,2},{4,3},{5,4},{6,5},{7,6},{8,7},{9,8},{10,9},{11,1... | collective-permute-start | bytes 399368 | tf_op jit(solution)/shard_map/ppermute | solution.py:19
  62.7 1.9 %collective-permute-start.3 = (bf16[65,1024]{1,0:T(8,128)(2,1)}, bf16[65,1024]{1,0:T(8,128)(2,1)}, u32[]{:S(2)}, u32[]{:S(2)}) collective-permute-start(bf16[65,1024]{1,0:T(8,128)(2,1)} %fusion.8), channel_id=1, source_target_pairs={{0,1},{1,2},{2,3},{3,4},{4,5},{5,6},{6,7},{7,8},{8,9},{9,10},{10,1... | collective-permute-start | bytes 399368 | tf_op jit(solution)/shard_map/ppermute | solution.py:19
  64.7 1.6 %fusion.11 = (s32[1]{0:T(128)}, s32[1]{0:T(128)}, s32[1]{0:T(128)}, s32[1]{0:T(128)}, s32[1]{0:T(128)}, /*index=5*/s32[1]{0:T(128)}, s32[1]{0:T(128)}) fusion(s32[32]{0:T(128)} %param.11, s32[]{:T(128)S(6)} %max.12, s32[]{:T(128)S(6)} %select_n.179, s32[]{:T(128)S(6)} %max.13, s32[]{:T(128)S(6)} %select_n.172, s32[]{:T(128)S(6)} %select_n.168, ...), kind=kLoop, calls=%fused_computation.34 | loop fusion | bytes 84 | solution.py:49
  70.8 0.5 collective-permute-done.3
  71.3 2.1 %select_add_fusion.state_ref = f32[65,1024]{1,0:T(8,128)} fusion(bf16[65,1024]{1,0:T(8,128)(2,1)S(1)} %collective-permute-done.8, bf16[65,1024]{1,0:T(8,128)(2,1)} %collective-permute-done.7, bf16[65,1024]{1,0:T(8,128)(2,1)} %collective-permute-done.6, bf16[65,1024]{1,0:T(8,128)(2,1)} %collective-permute-done.5, bf16[65,1024]{1,0:T(8,128)(2,1)} %collective-permute-done.4, ...), kind=kLoop, calls=%fused_computation.25 | loop fusion | flops 1264640 | bytes 1331206 | tf_op jit(solution)/shard_map/add | solution.py:53
  73.4 6.8 %shard_map.103 = (f32[1,256]{1,0:T(1,128)}, bf16[128,1024]{1,0:T(8,128)(2,1)}, f32[65,1024]{1,0:T(8,128)}) custom-call(bf16[128,1024]{1,0:T(8,128)(2,1)} %pose_ref.1, s32[2,256]{1,0:T(2,128)} %bitcast.65, f32[65,1024]{1,0:T(8,128)} %select_add_fusion.state_ref, bf16[1024,1024]{1,0:T(8,128)(2,1)} %query_ref.1, f32[1,1024]{1,0:T(1,128)} %bitcast.64), custom_call_target="tpu_custom_call" | custom-call | tf_op jit(solution)/shard_map/pallas_call | solution.py:166
  80.2 1.0 convert_element_type.96
  81.2 3.4 %collective-permute-start.14 = (bf16[65,1024]{1,0:T(8,128)(2,1)S(1)}, bf16[65,1024]{1,0:T(8,128)(2,1)S(1)}, u32[]{:S(2)}, u32[]{:S(2)}) collective-permute-start(bf16[65,1024]{1,0:T(8,128)(2,1)S(1)} %convert_element_type.96), channel_id=1, source_target_pairs={{3,0},{4,1},{5,2},{6,3},{7,4},{8,5},{9,6},{10,7},{11,8},{12,9},{13... | collective-permute-start | bytes 399368 | tf_op jit(solution)/shard_map/ppermute | solution.py:19
  84.6 2.2 %collective-permute-start.13 = (bf16[65,1024]{1,0:T(8,128)(2,1)S(1)}, bf16[65,1024]{1,0:T(8,128)(2,1)S(1)}, u32[]{:S(2)}, u32[]{:S(2)}) collective-permute-start(bf16[65,1024]{1,0:T(8,128)(2,1)S(1)} %convert_element_type.96), channel_id=1, source_target_pairs={{0,3},{1,4},{2,5},{3,6},{4,7},{5,8},{6,9},{7,10},{8,11},{9,12},{10... | collective-permute-start | bytes 399368 | tf_op jit(solution)/shard_map/ppermute | solution.py:19
  86.8 5.4 %collective-permute-start.12 = (bf16[65,1024]{1,0:T(8,128)(2,1)S(1)}, bf16[65,1024]{1,0:T(8,128)(2,1)S(1)}, u32[]{:S(2)}, u32[]{:S(2)}) collective-permute-start(bf16[65,1024]{1,0:T(8,128)(2,1)S(1)} %convert_element_type.96), channel_id=1, source_target_pairs={{2,0},{3,1},{4,2},{5,3},{6,4},{7,5},{8,6},{9,7},{10,8},{11,9},{12,... | collective-permute-start | bytes 399368 | tf_op jit(solution)/shard_map/ppermute | solution.py:19
  92.2 1.9 %collective-permute-start.11 = (bf16[65,1024]{1,0:T(8,128)(2,1)S(1)}, bf16[65,1024]{1,0:T(8,128)(2,1)S(1)}, u32[]{:S(2)}, u32[]{:S(2)}) collective-permute-start(bf16[65,1024]{1,0:T(8,128)(2,1)S(1)} %convert_element_type.96), channel_id=1, source_target_pairs={{0,2},{1,3},{2,4},{3,5},{4,6},{5,7},{6,8},{7,9},{8,10},{9,11},{10,... | collective-permute-start | bytes 399368 | tf_op jit(solution)/shard_map/ppermute | solution.py:19
  94.1 5.6 %collective-permute-start.10 = (bf16[65,1024]{1,0:T(8,128)(2,1)S(1)}, bf16[65,1024]{1,0:T(8,128)(2,1)S(1)}, u32[]{:S(2)}, u32[]{:S(2)}) collective-permute-start(bf16[65,1024]{1,0:T(8,128)(2,1)S(1)} %convert_element_type.96), channel_id=1, source_target_pairs={{1,0},{2,1},{3,2},{4,3},{5,4},{6,5},{7,6},{8,7},{9,8},{10,9},{11,1... | collective-permute-start | bytes 399368 | tf_op jit(solution)/shard_map/ppermute | solution.py:19
  99.7 2.1 %collective-permute-start.9 = (bf16[65,1024]{1,0:T(8,128)(2,1)S(1)}, bf16[65,1024]{1,0:T(8,128)(2,1)S(1)}, u32[]{:S(2)}, u32[]{:S(2)}) collective-permute-start(bf16[65,1024]{1,0:T(8,128)(2,1)S(1)} %convert_element_type.96), channel_id=1, source_target_pairs={{0,1},{1,2},{2,3},{3,4},{4,5},{5,6},{6,7},{7,8},{8,9},{9,10},{10,1... | collective-permute-start | bytes 399368 | tf_op jit(solution)/shard_map/ppermute | solution.py:19
  101.8 0.4 collective-permute-done.11
  102.2 0.1 collective-permute-done.10
  102.4 5.6 %collective-permute-done.9 = bf16[65,1024]{1,0:T(8,128)(2,1)S(1)} collective-permute-done((bf16[65,1024]{1,0:T(8,128)(2,1)S(1)}, bf16[65,1024]{1,0:T(8,128)(2,1)S(1)}, u32[]{:S(2)}, u32[]{:S(2)}) %collective-permute-start.9) | collective-permute-done | bytes 133152 | tf_op jit(solution)/shard_map/ppermute | solution.py:19
  108.0 1.2 add_convert_fusion
  109.2 0.2 copy.15
  109.4 0.4 convolution_convert_fusion
  109.9 0.5 convolution_add_fusion
  110.4 1.3 %copy-done.2 = f32[512,2048]{0,1:T(8,128)S(1)} copy-done((f32[512,2048]{0,1:T(8,128)S(1)}, f32[512,2048]{0,1:T(8,128)}, u32[]{:S(2)}) %copy-start.2) | copy-done | bytes 4194328
  111.6 0.1 copy-done.5
  111.7 0.6 fusion.4
  112.4 0.8 copy-done.4
  113.2 3.4 %fusion.5 = bf16[512,1024]{1,0:T(8,128)(2,1)} fusion(bf16[1024,2048]{1,0:T(8,128)(2,1)S(1)} %bitcast.57, bf16[512,1024]{0,1:T(8,128)(2,1)S(1)} %bitcast.61, bf16[512,1024]{0,1:T(8,128)(2,1)S(1)} %fusion.4), kind=kOutput, calls=%fused_computation.14 | convolution fusion | flops 2152202240 | bytes 7340032 | tf_op jit(solution)/shard_map/dot_general | solution.py:234
  (28 shorter events, 0.4 us)
Async XLA Ops:
  0.6 36.7 %copy-start = (bf16[512,1024]{1,0:T(8,128)(2,1)S(1)}, bf16[512,1024]{1,0:T(8,128)(2,1)}, u32[]{:S(2)}) copy-start(bf16[512,1024]{1,0:T(8,128)(2,1)} %param.8) | copy-start | bytes 3145732
  2.7 9.2 %collective-permute-start = (bf16[128,2048]{1,0:T(8,128)(2,1)S(1)}, bf16[128,2048]{1,0:T(8,128)(2,1)S(1)}, u32[]{:S(2)}, u32[]{:S(2)}) collective-permute-start(bf16[128,2048]{1,0:T(8,128)(2,1)S(1)} %constant_dynamic-update-slice_fusion), channel_id=1, source_target_pairs={{0,2},{1,5},{2,0},{3,7},{4,6},{5,1},{6,4},{7,3},{8,10},{9,13},{10,... | collective-permute-start | bytes 1572872 | tf_op jit(solution)/shard_map/ppermute | solution.py:188
  12.0 14.9 %collective-permute-start.1 = (bf16[2,128,2048]{2,1,0:T(8,128)(2,1)S(1)}, bf16[2,128,2048]{2,1,0:T(8,128)(2,1)S(1)}, u32[]{:S(2)}, u32[]{:S(2)}) collective-permute-start(bf16[2,128,2048]{2,1,0:T(8,128)(2,1)S(1)} %pad_maximum_fusion.1), channel_id=1, source_target_pairs={{0,4},{1,3},{2,6},{3,1},{4,0},{5,7},{6,2},{7,5},{8,12},{9,11},{10,... | collective-permute-start | bytes 3145736 | tf_op jit(solution)/shard_map/ppermute | solution.py:189
  28.4 4.5 %collective-permute-start.2 = (bf16[4,128,2048]{2,1,0:T(8,128)(2,1)}, bf16[4,128,2048]{2,1,0:T(8,128)(2,1)}, u32[]{:S(2)}, u32[]{:S(2)}) collective-permute-start(bf16[4,128,2048]{2,1,0:T(8,128)(2,1)} %pad_maximum_fusion), channel_id=1, source_target_pairs={{0,1},{1,0},{2,3},{3,2},{4,5},{5,4},{6,7},{7,6},{8,9},{9,8},{10,11... | collective-permute-start | bytes 6291464 | tf_op jit(solution)/shard_map/ppermute | solution.py:193
  37.3 2.5 %copy-start.3 = (bf16[8,128,2048]{2,1,0:T(8,128)(2,1)}, bf16[8,128,2048]{2,1,0:T(8,128)(2,1)S(1)}, u32[]{:S(2)}) copy-start(bf16[8,128,2048]{2,1,0:T(8,128)(2,1)S(1)} %slice_dynamic-update-slice_fusion) | copy-start | bytes 12582916
  39.8 3.4 %copy-start.1 = (f32[512,2048]{0,1:T(8,128)}, f32[512,2048]{0,1:T(8,128)S(1)}, u32[]{:S(2)}) copy-start(f32[512,2048]{0,1:T(8,128)S(1)} %convolution_bitcast_fusion) | copy-start | bytes 12582916
  42.0 2.5 %copy-start.6 = (f32[1024]{0:T(1024)}, f32[1024]{0:T(1024)S(1)}, u32[]{:S(2)}) copy-start(f32[1024]{0:T(1024)S(1)} %get-tuple-element.86) | copy-start | bytes 12292
  45.2 17.6 %collective-permute-start.8 = (bf16[65,1024]{1,0:T(8,128)(2,1)}, bf16[65,1024]{1,0:T(8,128)(2,1)S(1)}, u32[]{:S(2)}, u32[]{:S(2)}) collective-permute-start(bf16[65,1024]{1,0:T(8,128)(2,1)} %fusion.8), channel_id=1, source_target_pairs={{3,0},{4,1},{5,2},{6,3},{7,4},{8,5},{9,6},{10,7},{11,8},{12,9},{13... | collective-permute-start | bytes 399368 | tf_op jit(solution)/shard_map/ppermute | solution.py:19
  48.2 22.5 %collective-permute-start.7 = (bf16[65,1024]{1,0:T(8,128)(2,1)}, bf16[65,1024]{1,0:T(8,128)(2,1)}, u32[]{:S(2)}, u32[]{:S(2)}) collective-permute-start(bf16[65,1024]{1,0:T(8,128)(2,1)} %fusion.8), channel_id=1, source_target_pairs={{0,3},{1,4},{2,5},{3,6},{4,7},{5,8},{6,9},{7,10},{8,11},{9,12},{10... | collective-permute-start | bytes 399368 | tf_op jit(solution)/shard_map/ppermute | solution.py:19
  50.7 20.0 %collective-permute-start.6 = (bf16[65,1024]{1,0:T(8,128)(2,1)}, bf16[65,1024]{1,0:T(8,128)(2,1)}, u32[]{:S(2)}, u32[]{:S(2)}) collective-permute-start(bf16[65,1024]{1,0:T(8,128)(2,1)} %fusion.8), channel_id=1, source_target_pairs={{2,0},{3,1},{4,2},{5,3},{6,4},{7,5},{8,6},{9,7},{10,8},{11,9},{12,... | collective-permute-start | bytes 399368 | tf_op jit(solution)/shard_map/ppermute | solution.py:19
  56.8 14.0 %collective-permute-start.5 = (bf16[65,1024]{1,0:T(8,128)(2,1)}, bf16[65,1024]{1,0:T(8,128)(2,1)}, u32[]{:S(2)}, u32[]{:S(2)}) collective-permute-start(bf16[65,1024]{1,0:T(8,128)(2,1)} %fusion.8), channel_id=1, source_target_pairs={{0,2},{1,3},{2,4},{3,5},{4,6},{5,7},{6,8},{7,9},{8,10},{9,11},{10,... | collective-permute-start | bytes 399368 | tf_op jit(solution)/shard_map/ppermute | solution.py:19
  58.7 12.1 %collective-permute-start.4 = (bf16[65,1024]{1,0:T(8,128)(2,1)}, bf16[65,1024]{1,0:T(8,128)(2,1)}, u32[]{:S(2)}, u32[]{:S(2)}) collective-permute-start(bf16[65,1024]{1,0:T(8,128)(2,1)} %fusion.8), channel_id=1, source_target_pairs={{1,0},{2,1},{3,2},{4,3},{5,4},{6,5},{7,6},{8,7},{9,8},{10,9},{11,1... | collective-permute-start | bytes 399368 | tf_op jit(solution)/shard_map/ppermute | solution.py:19
  62.7 8.6 %collective-permute-start.3 = (bf16[65,1024]{1,0:T(8,128)(2,1)}, bf16[65,1024]{1,0:T(8,128)(2,1)}, u32[]{:S(2)}, u32[]{:S(2)}) collective-permute-start(bf16[65,1024]{1,0:T(8,128)(2,1)} %fusion.8), channel_id=1, source_target_pairs={{0,1},{1,2},{2,3},{3,4},{4,5},{5,6},{6,7},{7,8},{8,9},{9,10},{10,1... | collective-permute-start | bytes 399368 | tf_op jit(solution)/shard_map/ppermute | solution.py:19
  81.2 18.5 %collective-permute-start.14 = (bf16[65,1024]{1,0:T(8,128)(2,1)S(1)}, bf16[65,1024]{1,0:T(8,128)(2,1)S(1)}, u32[]{:S(2)}, u32[]{:S(2)}) collective-permute-start(bf16[65,1024]{1,0:T(8,128)(2,1)S(1)} %convert_element_type.96), channel_id=1, source_target_pairs={{3,0},{4,1},{5,2},{6,3},{7,4},{8,5},{9,6},{10,7},{11,8},{12,9},{13... | collective-permute-start | bytes 399368 | tf_op jit(solution)/shard_map/ppermute | solution.py:19
  84.6 17.2 %collective-permute-start.13 = (bf16[65,1024]{1,0:T(8,128)(2,1)S(1)}, bf16[65,1024]{1,0:T(8,128)(2,1)S(1)}, u32[]{:S(2)}, u32[]{:S(2)}) collective-permute-start(bf16[65,1024]{1,0:T(8,128)(2,1)S(1)} %convert_element_type.96), channel_id=1, source_target_pairs={{0,3},{1,4},{2,5},{3,6},{4,7},{5,8},{6,9},{7,10},{8,11},{9,12},{10... | collective-permute-start | bytes 399368 | tf_op jit(solution)/shard_map/ppermute | solution.py:19
  86.8 15.0 %collective-permute-start.12 = (bf16[65,1024]{1,0:T(8,128)(2,1)S(1)}, bf16[65,1024]{1,0:T(8,128)(2,1)S(1)}, u32[]{:S(2)}, u32[]{:S(2)}) collective-permute-start(bf16[65,1024]{1,0:T(8,128)(2,1)S(1)} %convert_element_type.96), channel_id=1, source_target_pairs={{2,0},{3,1},{4,2},{5,3},{6,4},{7,5},{8,6},{9,7},{10,8},{11,9},{12,... | collective-permute-start | bytes 399368 | tf_op jit(solution)/shard_map/ppermute | solution.py:19
  92.2 10.1 %collective-permute-start.11 = (bf16[65,1024]{1,0:T(8,128)(2,1)S(1)}, bf16[65,1024]{1,0:T(8,128)(2,1)S(1)}, u32[]{:S(2)}, u32[]{:S(2)}) collective-permute-start(bf16[65,1024]{1,0:T(8,128)(2,1)S(1)} %convert_element_type.96), channel_id=1, source_target_pairs={{0,2},{1,3},{2,4},{3,5},{4,6},{5,7},{6,8},{7,9},{8,10},{9,11},{10,... | collective-permute-start | bytes 399368 | tf_op jit(solution)/shard_map/ppermute | solution.py:19
  94.1 8.3 %collective-permute-start.10 = (bf16[65,1024]{1,0:T(8,128)(2,1)S(1)}, bf16[65,1024]{1,0:T(8,128)(2,1)S(1)}, u32[]{:S(2)}, u32[]{:S(2)}) collective-permute-start(bf16[65,1024]{1,0:T(8,128)(2,1)S(1)} %convert_element_type.96), channel_id=1, source_target_pairs={{1,0},{2,1},{3,2},{4,3},{5,4},{6,5},{7,6},{8,7},{9,8},{10,9},{11,1... | collective-permute-start | bytes 399368 | tf_op jit(solution)/shard_map/ppermute | solution.py:19
  99.7 8.3 %collective-permute-start.9 = (bf16[65,1024]{1,0:T(8,128)(2,1)S(1)}, bf16[65,1024]{1,0:T(8,128)(2,1)S(1)}, u32[]{:S(2)}, u32[]{:S(2)}) collective-permute-start(bf16[65,1024]{1,0:T(8,128)(2,1)S(1)} %convert_element_type.96), channel_id=1, source_target_pairs={{0,1},{1,2},{2,3},{3,4},{4,5},{5,6},{6,7},{7,8},{8,9},{9,10},{10,1... | collective-permute-start | bytes 399368 | tf_op jit(solution)/shard_map/ppermute | solution.py:19
  109.4 2.2 %copy-start.2 = (f32[512,2048]{0,1:T(8,128)S(1)}, f32[512,2048]{0,1:T(8,128)}, u32[]{:S(2)}) copy-start(f32[512,2048]{0,1:T(8,128)} %copy-done.1) | copy-start | bytes 12582916
  109.4 2.3 %copy-start.5 = (pred[512,1024]{0,1:T(8,128)(4,1)S(1)}, pred[512,1024]{0,1:T(8,128)(4,1)}, u32[]{:S(2)}) copy-start(pred[512,1024]{0,1:T(8,128)(4,1)} %get-tuple-element.88) | copy-start | bytes 1572868
  109.8 3.3 %copy-start.4 = (bf16[8,128,2048]{2,1,0:T(8,128)(2,1)S(1)}, bf16[8,128,2048]{2,1,0:T(8,128)(2,1)}, u32[]{:S(2)}) copy-start(bf16[8,128,2048]{2,1,0:T(8,128)(2,1)} %copy-done.3) | copy-start | bytes 12582916

commit v7 on v6

--- a/solution.py
+++ b/solution.py
@@ -52,6 +52,46 @@
         take_upper = jnp.logical_and(position + reach < blocks, above == mine)
         total = total + jnp.where(take_lower, lower, 0.0) + jnp.where(take_upper, upper, 0.0)
     return total
+
+
+def send(value, axis, pairs):
+    return lax.ppermute(value, axis, pairs)
+
+
+def complex_sum(own, block_complex):
+    axis = ("sec", "blk")
+    count = lax.axis_size(axis)
+    position = lax.axis_index(axis)
+    last = block_complex.shape[0] - 1
+
+    def complex_of(block):
+        return jnp.take(block_complex, jnp.clip(block, 0, last))
+
+    def kept(value, block, target):
+        inside = jnp.logical_and(target >= 0, target <= last)
+        return jnp.where(jnp.logical_and(inside, complex_of(block) == complex_of(target)), value, 0.0)
+
+    narrow = own.astype(jnp.bfloat16)
+    twin = position ^ 1
+    sibling = send(narrow, axis, [(s, s ^ 1) for s in range(count)]).astype(own.dtype)
+    odd = position % 2 == 1
+    far_target = jnp.where(odd, position + 3, position - 3)
+    far = send(
+        kept(own, position, far_target).astype(jnp.bfloat16),
+        axis,
+        [(s, s + 3) for s in range(1, count - 3, 2)] + [(s, s - 3) for s in range(4, count, 2)],
+    )
+    low = jnp.where(odd, sibling, own)
+    high = jnp.where(odd, own, sibling)
+    first = position - position % 2
+
+    def chip_part(target):
+        return (kept(low, first, target) + kept(high, first + 1, target)).astype(jnp.bfloat16)
+
+    up = send(chip_part(position + 2), axis, [(s, s + 2) for s in range(count - 2)])
+    down = send(chip_part(position - 2), axis, [(s, s - 2) for s in range(2, count)])
+    total = own + kept(sibling, twin, position)
+    return total + up.astype(own.dtype) + down.astype(own.dtype) + far.astype(own.dtype)
 
 
 def pose_side(pose_rows, pair_rows, state, w_query, score_weight):
@@ -213,9 +253,9 @@
     values = both[:, width:]
     key_feat = features(keys).astype(jnp.bfloat16)
     val_round = values.astype(jnp.bfloat16)
-    state = complex_total(local_state(key_feat, val_round), block_complex)
+    state = complex_sum(local_state(key_feat, val_round), block_complex)
     pair_loss, pose_grad, pose_state = pose_fused(poses, pairs, state, w_query, score_weight)
-    state_grad = complex_total(pose_state, block_complex).astype(jnp.bfloat16)
+    state_grad = complex_sum(pose_state, block_complex).astype(jnp.bfloat16)
     key_heads = key_feat.reshape(rows, H, DH)
     val_heads = val_round.reshape(rows, H, DH)
     grad_heads = state_grad[:DH].reshape(DH, H, DH)

time: 117 us -> 101 us (0.86)
  starting transfers between devices: 43.1 us -> 25.6 us
  other arithmetic: 9.26 us -> 11.6 us
    ppermute x12 -> x8, starting transfers between devices: 40 us -> 22.4 us  [send(): return lax.ppermute(value, axis, pairs)]
    convert_element_type x3 -> x6, other arithmetic: 2.81 us -> 5.41 us  [the longest x2 2.58 us: chip_part(): (kept(low, first, target) + kept(high, first + 1, target)).astype(jnp.bfl...]
    ppermute x1, waiting for transfers between devices: 3.75 us -> 1.76 us  [gather_rows(): sibling = lax.ppermute(mine, 'blk', [(s, s ^ 1) for s in range(count)])]
    ppermute x12 -> x8, waiting for transfers between devices: 6.69 us -> 7.85 us  [send(): return lax.ppermute(value, axis, pairs)]
    unnamed x15 -> x17, local copies, waits for them, and re-layouts: 3.23 us -> 3.24 us
  transfers between devices with their start and end apart: 15 -> 11, of which waited for: 7 -> 7; matrix products, arithmetic and copies ran while one was open for 2% -> 4% of each run, Pallas kernels for 0% -> 0%
where the time goes in v7:
time: 101 us; the launch traced here: 99.5 us
  waiting for transfers between devices  30.6 us (30%)
  starting transfers between devices  25.6 us (25%)
  other arithmetic  11.6 us (11%)
  local copies, waits for them, and re-layouts  11.5 us (11%)
  matrix products  7.98 us (8%)
  Pallas kernels  6.8 us (7%)
  between operations  5.4 us (5%)
    ppermute x8, starting transfers between devices, send(): return lax.ppermute(value, axis, pairs)  22.4 us
    ppermute x1, waiting for transfers between devices, gather_rows(): lax.ppermute(jnp.stack([shard, early]), 'blk', [(s, s ^ (2 if s % 2 else...  13.3 us
    ppermute x8, waiting for transfers between devices, send(): return lax.ppermute(value, axis, pairs)  7.85 us
    ppermute x1, waiting for transfers between devices, gather_rows(): lax.ppermute(shard, 'blk', [(s, s ^ (4 if s % 2 else 2)) for s in range(c...  7.69 us
    pallas_call x1, Pallas kernels, pose_fused(): pl.pallas_call(pose_kernel, out_shape=(jax.ShapeDtypeStruct((1, pair_rows...  6.8 us
    dynamic_update_slice x8, local copies, waits for them, and re-layouts, gather_rows(): full = lax.dynamic_update_slice(full, pieces[k][None], (at, 0, 0))  4.53 us
    dot_general x1, matrix products, shards(): lax.dot_general(both_grad, full_both, contract, preferred_element_type=jn...  3.35 us
    unnamed x17, local copies, waits for them, and re-layouts  3.24 us
  transfers between devices with their start and end apart: 11, of which 7 were waited for; matrix products, arithmetic and copies ran while one was open for 4% of the time, Pallas kernels for 0%

profile of v7, /device:TPU:16, one launch (start us, length us, event | category | flops | bytes accessed | tf_op | source)
XLA Modules:
  0.0 99.5 jit_solution(15719405835449646038)
XLA Ops:
  0.7 1.1 %constant_dynamic-update-slice_fusion.1 = bf16[128,2048]{1,0:T(8,128)(2,1)S(1)} fusion(bf16[128,1024]{1,0:T(8,128)(2,1)} %param.12), kind=kLoop, calls=%fused_computation.47 | loop fusion | bytes 524288
  1.7 1.0 constant_dynamic-update-slice_fusion
  2.7 1.6 %collective-permute-start = (bf16[128,2048]{1,0:T(8,128)(2,1)S(1)}, bf16[128,2048]{1,0:T(8,128)(2,1)S(1)}, u32[]{:S(2)}, u32[]{:S(2)}) collective-permute-start(bf16[128,2048]{1,0:T(8,128)(2,1)S(1)} %constant_dynamic-update-slice_fusion), channel_id=1, source_target_pairs={{0,2},{1,5},{2,0},{3,7},{4,6},{5,1},{6,4},{7,3},{8,10},{9,13},{10,... | collective-permute-start | bytes 1572872 | tf_op jit(solution)/shard_map/ppermute | solution.py:228
  4.2 7.7 %collective-permute-done = bf16[128,2048]{1,0:T(8,128)(2,1)S(1)} collective-permute-done((bf16[128,2048]{1,0:T(8,128)(2,1)S(1)}, bf16[128,2048]{1,0:T(8,128)(2,1)S(1)}, u32[]{:S(2)}, u32[]{:S(2)}) %collective-permute-start) | collective-permute-done | bytes 524320 | tf_op jit(solution)/shard_map/ppermute | solution.py:228
  11.9 0.1 pad_maximum_fusion.1
  12.0 1.6 %collective-permute-start.1 = (bf16[2,128,2048]{2,1,0:T(8,128)(2,1)S(1)}, bf16[2,128,2048]{2,1,0:T(8,128)(2,1)S(1)}, u32[]{:S(2)}, u32[]{:S(2)}) collective-permute-start(bf16[2,128,2048]{2,1,0:T(8,128)(2,1)S(1)} %pad_maximum_fusion.1), channel_id=1, source_target_pairs={{0,4},{1,3},{2,6},{3,1},{4,0},{5,7},{6,2},{7,5},{8,12},{9,11},{10,... | collective-permute-start | bytes 3145736 | tf_op jit(solution)/shard_map/ppermute | solution.py:229
  13.6 13.3 %collective-permute-done.1 = bf16[2,128,2048]{2,1,0:T(8,128)(2,1)S(1)} collective-permute-done((bf16[2,128,2048]{2,1,0:T(8,128)(2,1)S(1)}, bf16[2,128,2048]{2,1,0:T(8,128)(2,1)S(1)}, u32[]{:S(2)}, u32[]{:S(2)}) %collective-permute-start.1) | collective-permute-done | bytes 1048608 | tf_op jit(solution)/shard_map/ppermute | solution.py:229
  26.9 1.5 %pad_maximum_fusion = bf16[4,128,2048]{2,1,0:T(8,128)(2,1)} fusion(bf16[2,128,2048]{2,1,0:T(8,128)(2,1)S(1)} %collective-permute-done.1, bf16[1,128,2048]{2,1,0:T(8,128)(2,1)S(1)} %bitcast.55, bf16[1,128,2048]{2,1,0:T(8,128)(2,1)S(1)} %bitcast.53), kind=kLoop, calls=%fused_computation.2 | loop fusion | flops 2097152 | bytes 4194304 | tf_op jit(solution)/shard_map/concatenate | solution.py:232
  28.5 0.7 fusion.20
  30.4 0.5 broadcast_in_dim.60
  31.2 1.8 %collective-permute-done.2 = bf16[4,128,2048]{2,1,0:T(8,128)(2,1)} collective-permute-done((bf16[4,128,2048]{2,1,0:T(8,128)(2,1)}, bf16[4,128,2048]{2,1,0:T(8,128)(2,1)}, u32[]{:S(2)}, u32[]{:S(2)}) %collective-permute-start.2) | collective-permute-done | bytes 2097184 | tf_op jit(solution)/shard_map/ppermute | solution.py:233
  33.0 1.1 %slice_dynamic-update-slice_fusion.3 = bf16[8,128,2048]{2,1,0:T(8,128)(2,1)S(1)} fusion(bf16[8,128,2048]{2,1,0:T(8,128)(2,1)S(1)} %slice_dynamic-update-slice_fusion.4, s32[]{:T(128)S(6)} %select_n.208, bf16[4,128,2048]{2,1,0:T(8,128)(2,1)} %collective-permute-done.2), kind=kLoop, calls=%fused_computation.20 | loop fusion | bytes 1048580 | tf_op jit(solution)/shard_map/dynamic_update_slice | solution.py:242
  34.0 1.1 %slice_dynamic-update-slice_fusion.2 = bf16[8,128,2048]{2,1,0:T(8,128)(2,1)S(1)} fusion(bf16[8,128,2048]{2,1,0:T(8,128)(2,1)S(1)} %slice_dynamic-update-slice_fusion.3, s32[]{:T(128)S(6)} %select_n.209, bf16[4,128,2048]{2,1,0:T(8,128)(2,1)} %collective-permute-done.2), kind=kLoop, calls=%fused_computation.19 | loop fusion | bytes 1048580 | tf_op jit(solution)/shard_map/dynamic_update_slice | solution.py:242
  35.1 1.1 %slice_dynamic-update-slice_fusion.1 = bf16[8,128,2048]{2,1,0:T(8,128)(2,1)S(1)} fusion(bf16[8,128,2048]{2,1,0:T(8,128)(2,1)S(1)} %slice_dynamic-update-slice_fusion.2, s32[]{:T(128)S(6)} %select_n.210, bf16[4,128,2048]{2,1,0:T(8,128)(2,1)} %collective-permute-done.2), kind=kLoop, calls=%fused_computation.18 | loop fusion | bytes 1048580 | tf_op jit(solution)/shard_map/dynamic_update_slice | solution.py:242
  36.2 1.1 %slice_dynamic-update-slice_fusion = bf16[8,128,2048]{2,1,0:T(8,128)(2,1)S(1)} fusion(bf16[8,128,2048]{2,1,0:T(8,128)(2,1)S(1)} %slice_dynamic-update-slice_fusion.1, s32[]{:T(128)S(6)} %select_n.211, bf16[4,128,2048]{2,1,0:T(8,128)(2,1)} %collective-permute-done.2), kind=kLoop, calls=%fused_computation.17 | loop fusion | bytes 1048580 | tf_op jit(solution)/shard_map/dynamic_update_slice | solution.py:242
  37.3 2.5 %convolution_bitcast_fusion = f32[512,2048]{0,1:T(8,128)S(1)} fusion(bf16[1024,2048]{1,0:T(8,128)(2,1)S(1)} %bitcast.56, bf16[512,1024]{1,0:T(8,128)(2,1)S(1)} %copy-done), kind=kOutput, calls=%fused_computation | convolution fusion | flops 2147483648 | bytes 9437184 | tf_op jit(solution)/shard_map/dot_general | solution.py:251
  39.8 0.1 slice.99
  40.0 2.0 %convert_reduce_fusion = (f32[1024]{0:T(1024)S(1)}, bf16[512,1024]{0,1:T(8,128)(2,1)S(1)}, pred[512,1024]{0,1:T(8,128)(4,1)}) fusion(f32[512,2048]{0,1:T(8,128)S(1)} %convolution_bitcast_fusion), kind=kLoop, calls=%fused_computation.9 | loop fusion | flops 3668992 | bytes 3674112 | tf_op jit(solution)/shard_map/reduce_sum | solution.py:37
  42.0 1.3 %fusion.21 = f32[16,64,64]{2,1,0:T(8,128)} fusion(bf16[512,16,64]{0,2,1:T(8,128)(2,1)S(1)} %bitcast.48, bf16[512,16,64]{0,2,1:T(8,128)(2,1)S(1)} %bitcast.50), kind=kOutput, calls=%fused_computation.54 | convolution fusion | flops 67108864 | bytes 2359296 | tf_op jit(solution)/shard_map/thd,the->dhe/dot_general | solution.py:34
  43.3 1.2 %copy.14 = f32[64,1024]{1,0:T(8,128)S(1)} copy(f32[64,1024]{0,1:T(8,128)} %bitcast.60) | data formatting | bytes 524288 | tf_op jit(solution)/shard_map/reshape | solution.py:36
  44.5 0.8 select_convert_fusion.2
  45.2 0.1 collective-permute-start.3
  47.9 3.3 %collective-permute-start.6 = (bf16[65,1024]{1,0:T(8,128)(2,1)}, bf16[65,1024]{1,0:T(8,128)(2,1)}, u32[]{:S(2)}, u32[]{:S(2)}) collective-permute-start(bf16[65,1024]{1,0:T(8,128)(2,1)} %get-tuple-element.93), channel_id=1, source_target_pairs={{1,4},{3,6},{5,8},{7,10},{9,12},{11,14},{13,16},{15,18},{17,20},{1... | collective-permute-start | bytes 399368 | tf_op jit(solution)/shard_map/ppermute | solution.py:58
  51.2 1.5 %add_convert_fusion.3 = (bf16[65,1024]{1,0:T(8,128)(2,1)}, bf16[65,1024]{1,0:T(8,128)(2,1)}) fusion(bf16[65,1024]{1,0:T(8,128)(2,1)S(1)} %collective-permute-done.3, pred[]{:T(512)S(6)} %and.108, pred[]{:T(512)S(6)} %eq.40, pred[]{:T(512)S(6)} %and.106, f32[1,1024]{1,0:T(1,128)} %bitcast.63, f32[64,1024]{1,0:T(8,128)S(1)} %copy.14, pred[]{:T(512)S(6)} %and.112, ...), kind=kLoop, calls=%fused_computation.44 | loop fusion | flops 798720 | bytes 665605 | tf_op jit(solution)/shard_map/convert_element_type | solution.py:89
  52.7 3.4 %collective-permute-start.4 = (bf16[65,1024]{1,0:T(8,128)(2,1)}, bf16[65,1024]{1,0:T(8,128)(2,1)}, u32[]{:S(2)}, u32[]{:S(2)}) collective-permute-start(bf16[65,1024]{1,0:T(8,128)(2,1)} %get-tuple-element.91), channel_id=1, source_target_pairs={{0,2},{1,3},{2,4},{3,5},{4,6},{5,7},{6,8},{7,9},{8,10},{9,11},{10,... | collective-permute-start | bytes 399368 | tf_op jit(solution)/shard_map/ppermute | solution.py:58
  56.1 4.2 %collective-permute-start.5 = (bf16[65,1024]{1,0:T(8,128)(2,1)}, bf16[65,1024]{1,0:T(8,128)(2,1)}, u32[]{:S(2)}, u32[]{:S(2)}) collective-permute-start(bf16[65,1024]{1,0:T(8,128)(2,1)} %get-tuple-element.92), channel_id=1, source_target_pairs={{2,0},{3,1},{4,2},{5,3},{6,4},{7,5},{8,6},{9,7},{10,8},{11,9},{12,... | collective-permute-start | bytes 399368 | tf_op jit(solution)/shard_map/ppermute | solution.py:58
  61.0 1.8 %collective-permute-done.4 = bf16[65,1024]{1,0:T(8,128)(2,1)} collective-permute-done((bf16[65,1024]{1,0:T(8,128)(2,1)}, bf16[65,1024]{1,0:T(8,128)(2,1)}, u32[]{:S(2)}, u32[]{:S(2)}) %collective-permute-start.4) | collective-permute-done | bytes 133152 | tf_op jit(solution)/shard_map/ppermute | solution.py:58
  62.8 2.0 %collective-permute-done.5 = bf16[65,1024]{1,0:T(8,128)(2,1)} collective-permute-done((bf16[65,1024]{1,0:T(8,128)(2,1)}, bf16[65,1024]{1,0:T(8,128)(2,1)}, u32[]{:S(2)}, u32[]{:S(2)}) %collective-permute-start.5) | collective-permute-done | bytes 133152 | tf_op jit(solution)/shard_map/ppermute | solution.py:58
  64.8 1.9 %fusion.11.state_ref = f32[65,1024]{1,0:T(8,128)} fusion(bf16[65,1024]{1,0:T(8,128)(2,1)S(1)} %collective-permute-done.3, bf16[65,1024]{1,0:T(8,128)(2,1)} %collective-permute-done.6, bf16[65,1024]{1,0:T(8,128)(2,1)} %collective-permute-done.5, bf16[65,1024]{1,0:T(8,128)(2,1)} %collective-permute-done.4, pred[]{:T(512)S(6)} %and.101, f32[1,1024]{1,0:T(1,128)} %bitcast.64, ...), kind=kLoop, calls=%fused_computation.32 | loop fusion | flops 665600 | bytes 1064961 | tf_op jit(solution)/shard_map/add | solution.py:94
  66.7 6.8 %shard_map.103 = (f32[1,256]{1,0:T(1,128)}, bf16[128,1024]{1,0:T(8,128)(2,1)}, f32[65,1024]{1,0:T(8,128)}) custom-call(bf16[128,1024]{1,0:T(8,128)(2,1)} %pose_ref.1, s32[2,256]{1,0:T(2,128)} %bitcast.66, f32[65,1024]{1,0:T(8,128)} %fusion.11.state_ref, bf16[1024,1024]{1,0:T(8,128)(2,1)} %query_ref.1, f32[1,1024]{1,0:T(1,128)} %bitcast.65), custom_call_target="tpu_custom_call" | custom-call | tf_op jit(solution)/shard_map/pallas_call | solution.py:206
  73.5 1.0 convert_element_type.93
  74.5 0.1 collective-permute-start.7
  74.6 3.5 %collective-permute-start.10 = (bf16[65,1024]{1,0:T(8,128)(2,1)S(1)}, bf16[65,1024]{1,0:T(8,128)(2,1)S(1)}, u32[]{:S(2)}, u32[]{:S(2)}) collective-permute-start(bf16[65,1024]{1,0:T(8,128)(2,1)S(1)} %select_convert_fusion.1), channel_id=1, source_target_pairs={{1,4},{3,6},{5,8},{7,10},{9,12},{11,14},{13,16},{15,18},{17,20},{1... | collective-permute-start | bytes 399368 | tf_op jit(solution)/shard_map/ppermute | solution.py:58
  78.1 1.1 %add_convert_fusion.1 = (bf16[65,1024]{1,0:T(8,128)(2,1)S(1)}, bf16[65,1024]{1,0:T(8,128)(2,1)S(1)}) fusion(f32[65,1024]{1,0:T(8,128)} %get-tuple-element.8, bf16[65,1024]{1,0:T(8,128)(2,1)S(1)} %collective-permute-done.7, pred[]{:T(512)S(6)} %and.108, pred[]{:T(512)S(6)} %eq.40, pred[]{:T(512)S(6)} %and.106, pred[]{:T(512)S(6)} %and.112, pred[]{:T(512)S(6)} %and.111), kind=kLoop, calls=%fused_computation.41 | loop fusion | flops 732160 | bytes 665605 | tf_op jit(solution)/shard_map/convert_element_type | solution.py:89
  79.2 4.3 %collective-permute-start.8 = (bf16[65,1024]{1,0:T(8,128)(2,1)S(1)}, bf16[65,1024]{1,0:T(8,128)(2,1)S(1)}, u32[]{:S(2)}, u32[]{:S(2)}) collective-permute-start(bf16[65,1024]{1,0:T(8,128)(2,1)S(1)} %get-tuple-element.89), channel_id=1, source_target_pairs={{0,2},{1,3},{2,4},{3,5},{4,6},{5,7},{6,8},{7,9},{8,10},{9,11},{10,... | collective-permute-start | bytes 399368 | tf_op jit(solution)/shard_map/ppermute | solution.py:58
  83.5 3.5 %collective-permute-start.9 = (bf16[65,1024]{1,0:T(8,128)(2,1)S(1)}, bf16[65,1024]{1,0:T(8,128)(2,1)S(1)}, u32[]{:S(2)}, u32[]{:S(2)}) collective-permute-start(bf16[65,1024]{1,0:T(8,128)(2,1)S(1)} %get-tuple-element.90), channel_id=1, source_target_pairs={{2,0},{3,1},{4,2},{5,3},{6,4},{7,5},{8,6},{9,7},{10,8},{11,9},{12,... | collective-permute-start | bytes 399368 | tf_op jit(solution)/shard_map/ppermute | solution.py:58
  87.0 1.8 %collective-permute-done.8 = bf16[65,1024]{1,0:T(8,128)(2,1)S(1)} collective-permute-done((bf16[65,1024]{1,0:T(8,128)(2,1)S(1)}, bf16[65,1024]{1,0:T(8,128)(2,1)S(1)}, u32[]{:S(2)}, u32[]{:S(2)}) %collective-permute-start.8) | collective-permute-done | bytes 133152 | tf_op jit(solution)/shard_map/ppermute | solution.py:58
  88.8 2.2 %collective-permute-done.9 = bf16[65,1024]{1,0:T(8,128)(2,1)S(1)} collective-permute-done((bf16[65,1024]{1,0:T(8,128)(2,1)S(1)}, bf16[65,1024]{1,0:T(8,128)(2,1)S(1)}, u32[]{:S(2)}, u32[]{:S(2)}) %collective-permute-start.9) | collective-permute-done | bytes 133152 | tf_op jit(solution)/shard_map/ppermute | solution.py:58
  91.0 1.1 %fusion.16 = bf16[65,1024]{1,0:T(8,128)(2,1)S(1)} fusion(f32[65,1024]{1,0:T(8,128)} %get-tuple-element.8, bf16[65,1024]{1,0:T(8,128)(2,1)S(1)} %collective-permute-done.7, bf16[65,1024]{1,0:T(8,128)(2,1)S(1)} %collective-permute-done.10, bf16[65,1024]{1,0:T(8,128)(2,1)S(1)} %collective-permute-done.9, bf16[65,1024]{1,0:T(8,128)(2,1)S(1)} %collective-permute-done.8, ...), kind=kLoop, calls=%fused_computation.37 | loop fusion | flops 665600 | bytes 931841 | tf_op jit(solution)/shard_map/convert_element_type | solution.py:258
  92.1 0.1 reshape.245
  92.2 0.2 copy.15
  92.4 0.4 convolution_convert_fusion
  92.8 0.5 convolution_add_fusion
  93.3 1.3 %copy-done.2 = f32[512,2048]{0,1:T(8,128)S(1)} copy-done((f32[512,2048]{0,1:T(8,128)S(1)}, f32[512,2048]{0,1:T(8,128)}, u32[]{:S(2)}) %copy-start.2) | copy-done | bytes 4194328
  94.6 0.1 copy-done.5
  94.7 0.6 fusion.4
  95.3 0.8 copy-done.4
  96.1 3.3 %fusion.5 = bf16[512,1024]{1,0:T(8,128)(2,1)} fusion(bf16[1024,2048]{1,0:T(8,128)(2,1)S(1)} %bitcast.57, bf16[512,1024]{0,1:T(8,128)(2,1)S(1)} %bitcast.61, bf16[512,1024]{0,1:T(8,128)(2,1)S(1)} %fusion.4), kind=kOutput, calls=%fused_computation.14 | convolution fusion | flops 2152202240 | bytes 7340032 | tf_op jit(solution)/shard_map/dot_general | solution.py:274
  (25 shorter events, 0.3 us)
Async XLA Ops:
  0.6 36.7 %copy-start = (bf16[512,1024]{1,0:T(8,128)(2,1)S(1)}, bf16[512,1024]{1,0:T(8,128)(2,1)}, u32[]{:S(2)}) copy-start(bf16[512,1024]{1,0:T(8,128)(2,1)} %param.8) | copy-start | bytes 3145732
  0.6 27.8 %copy-start.7 = (s32[32]{0:T(128)S(1)}, s32[32]{0:T(128)}, u32[]{:S(2)}) copy-start(s32[32]{0:T(128)} %param.11) | copy-start | bytes 388
  2.7 9.2 %collective-permute-start = (bf16[128,2048]{1,0:T(8,128)(2,1)S(1)}, bf16[128,2048]{1,0:T(8,128)(2,1)S(1)}, u32[]{:S(2)}, u32[]{:S(2)}) collective-permute-start(bf16[128,2048]{1,0:T(8,128)(2,1)S(1)} %constant_dynamic-update-slice_fusion), channel_id=1, source_target_pairs={{0,2},{1,5},{2,0},{3,7},{4,6},{5,1},{6,4},{7,3},{8,10},{9,13},{10,... | collective-permute-start | bytes 1572872 | tf_op jit(solution)/shard_map/ppermute | solution.py:228
  12.0 14.9 %collective-permute-start.1 = (bf16[2,128,2048]{2,1,0:T(8,128)(2,1)S(1)}, bf16[2,128,2048]{2,1,0:T(8,128)(2,1)S(1)}, u32[]{:S(2)}, u32[]{:S(2)}) collective-permute-start(bf16[2,128,2048]{2,1,0:T(8,128)(2,1)S(1)} %pad_maximum_fusion.1), channel_id=1, source_target_pairs={{0,4},{1,3},{2,6},{3,1},{4,0},{5,7},{6,2},{7,5},{8,12},{9,11},{10,... | collective-permute-start | bytes 3145736 | tf_op jit(solution)/shard_map/ppermute | solution.py:229
  28.5 4.5 %collective-permute-start.2 = (bf16[4,128,2048]{2,1,0:T(8,128)(2,1)}, bf16[4,128,2048]{2,1,0:T(8,128)(2,1)}, u32[]{:S(2)}, u32[]{:S(2)}) collective-permute-start(bf16[4,128,2048]{2,1,0:T(8,128)(2,1)} %pad_maximum_fusion), channel_id=1, source_target_pairs={{0,1},{1,0},{2,3},{3,2},{4,5},{5,4},{6,7},{7,6},{8,9},{9,8},{10,11... | collective-permute-start | bytes 6291464 | tf_op jit(solution)/shard_map/ppermute | solution.py:233
  37.3 2.5 %copy-start.3 = (bf16[8,128,2048]{2,1,0:T(8,128)(2,1)}, bf16[8,128,2048]{2,1,0:T(8,128)(2,1)S(1)}, u32[]{:S(2)}) copy-start(bf16[8,128,2048]{2,1,0:T(8,128)(2,1)S(1)} %slice_dynamic-update-slice_fusion) | copy-start | bytes 12582916
  39.8 3.4 %copy-start.1 = (f32[512,2048]{0,1:T(8,128)}, f32[512,2048]{0,1:T(8,128)S(1)}, u32[]{:S(2)}) copy-start(f32[512,2048]{0,1:T(8,128)S(1)} %convolution_bitcast_fusion) | copy-start | bytes 12582916
  42.0 3.2 %copy-start.6 = (f32[1024]{0:T(1024)}, f32[1024]{0:T(1024)S(1)}, u32[]{:S(2)}) copy-start(f32[1024]{0:T(1024)S(1)} %get-tuple-element.86) | copy-start | bytes 12292
  45.2 5.9 %collective-permute-start.3 = (bf16[65,1024]{1,0:T(8,128)(2,1)}, bf16[65,1024]{1,0:T(8,128)(2,1)S(1)}, u32[]{:S(2)}, u32[]{:S(2)}) collective-permute-start(bf16[65,1024]{1,0:T(8,128)(2,1)} %get-tuple-element.94), channel_id=1, source_target_pairs={{0,1},{1,0},{2,3},{3,2},{4,5},{5,4},{6,7},{7,6},{8,9},{9,8},{10,11... | collective-permute-start | bytes 399368 | tf_op jit(solution)/shard_map/ppermute | solution.py:58
  47.9 13.1 %collective-permute-start.6 = (bf16[65,1024]{1,0:T(8,128)(2,1)}, bf16[65,1024]{1,0:T(8,128)(2,1)}, u32[]{:S(2)}, u32[]{:S(2)}) collective-permute-start(bf16[65,1024]{1,0:T(8,128)(2,1)} %get-tuple-element.93), channel_id=1, source_target_pairs={{1,4},{3,6},{5,8},{7,10},{9,12},{11,14},{13,16},{15,18},{17,20},{1... | collective-permute-start | bytes 399368 | tf_op jit(solution)/shard_map/ppermute | solution.py:58
  52.7 10.1 %collective-permute-start.4 = (bf16[65,1024]{1,0:T(8,128)(2,1)}, bf16[65,1024]{1,0:T(8,128)(2,1)}, u32[]{:S(2)}, u32[]{:S(2)}) collective-permute-start(bf16[65,1024]{1,0:T(8,128)(2,1)} %get-tuple-element.91), channel_id=1, source_target_pairs={{0,2},{1,3},{2,4},{3,5},{4,6},{5,7},{6,8},{7,9},{8,10},{9,11},{10,... | collective-permute-start | bytes 399368 | tf_op jit(solution)/shard_map/ppermute | solution.py:58
  56.1 8.7 %collective-permute-start.5 = (bf16[65,1024]{1,0:T(8,128)(2,1)}, bf16[65,1024]{1,0:T(8,128)(2,1)}, u32[]{:S(2)}, u32[]{:S(2)}) collective-permute-start(bf16[65,1024]{1,0:T(8,128)(2,1)} %get-tuple-element.92), channel_id=1, source_target_pairs={{2,0},{3,1},{4,2},{5,3},{6,4},{7,5},{8,6},{9,7},{10,8},{11,9},{12,... | collective-permute-start | bytes 399368 | tf_op jit(solution)/shard_map/ppermute | solution.py:58
  74.5 3.6 %collective-permute-start.7 = (bf16[65,1024]{1,0:T(8,128)(2,1)S(1)}, bf16[65,1024]{1,0:T(8,128)(2,1)S(1)}, u32[]{:S(2)}, u32[]{:S(2)}) collective-permute-start(bf16[65,1024]{1,0:T(8,128)(2,1)S(1)} %convert_element_type.93), channel_id=1, source_target_pairs={{0,1},{1,0},{2,3},{3,2},{4,5},{5,4},{6,7},{7,6},{8,9},{9,8},{10,11... | collective-permute-start | bytes 399368 | tf_op jit(solution)/shard_map/ppermute | solution.py:58
  74.6 12.4 %collective-permute-start.10 = (bf16[65,1024]{1,0:T(8,128)(2,1)S(1)}, bf16[65,1024]{1,0:T(8,128)(2,1)S(1)}, u32[]{:S(2)}, u32[]{:S(2)}) collective-permute-start(bf16[65,1024]{1,0:T(8,128)(2,1)S(1)} %select_convert_fusion.1), channel_id=1, source_target_pairs={{1,4},{3,6},{5,8},{7,10},{9,12},{11,14},{13,16},{15,18},{17,20},{1... | collective-permute-start | bytes 399368 | tf_op jit(solution)/shard_map/ppermute | solution.py:58
  79.2 9.7 %collective-permute-start.8 = (bf16[65,1024]{1,0:T(8,128)(2,1)S(1)}, bf16[65,1024]{1,0:T(8,128)(2,1)S(1)}, u32[]{:S(2)}, u32[]{:S(2)}) collective-permute-start(bf16[65,1024]{1,0:T(8,128)(2,1)S(1)} %get-tuple-element.89), channel_id=1, source_target_pairs={{0,2},{1,3},{2,4},{3,5},{4,6},{5,7},{6,8},{7,9},{8,10},{9,11},{10,... | collective-permute-start | bytes 399368 | tf_op jit(solution)/shard_map/ppermute | solution.py:58
  83.5 7.5 %collective-permute-start.9 = (bf16[65,1024]{1,0:T(8,128)(2,1)S(1)}, bf16[65,1024]{1,0:T(8,128)(2,1)S(1)}, u32[]{:S(2)}, u32[]{:S(2)}) collective-permute-start(bf16[65,1024]{1,0:T(8,128)(2,1)S(1)} %get-tuple-element.90), channel_id=1, source_target_pairs={{2,0},{3,1},{4,2},{5,3},{6,4},{7,5},{8,6},{9,7},{10,8},{11,9},{12,... | collective-permute-start | bytes 399368 | tf_op jit(solution)/shard_map/ppermute | solution.py:58
  92.4 2.2 %copy-start.2 = (f32[512,2048]{0,1:T(8,128)S(1)}, f32[512,2048]{0,1:T(8,128)}, u32[]{:S(2)}) copy-start(f32[512,2048]{0,1:T(8,128)} %copy-done.1) | copy-start | bytes 12582916
  92.4 2.3 %copy-start.5 = (pred[512,1024]{0,1:T(8,128)(4,1)S(1)}, pred[512,1024]{0,1:T(8,128)(4,1)}, u32[]{:S(2)}) copy-start(pred[512,1024]{0,1:T(8,128)(4,1)} %get-tuple-element.88) | copy-start | bytes 1572868
  92.8 3.3 %copy-start.4 = (bf16[8,128,2048]{2,1,0:T(8,128)(2,1)S(1)}, bf16[8,128,2048]{2,1,0:T(8,128)(2,1)}, u32[]{:S(2)}) copy-start(bf16[8,128,2048]{2,1,0:T(8,128)(2,1)} %copy-done.3) | copy-start | bytes 12582916

commit v8 on v7

--- a/solution.py
+++ b/solution.py
@@ -216,10 +216,66 @@
     return (loss.reshape(pair_rows.shape[0]), grad, back)
 
 
+def project_kernel(
+    order_ref, rec_ref, own_ref, early_ref, late_ref, twin_ref, feat_ref, val_ref, keys_ref, state_ref
+):
+    width = feat_ref.shape[1]
+    lanes = 2 * DH
+    pieces = [own_ref[...], early_ref[...], late_ref[0], late_ref[1]] + [
+        twin_ref[k] for k in range(twin_ref.shape[0])
+    ]
+    both = jnp.dot(rec_ref[order_ref[0]], pieces[0], preferred_element_type=jnp.float32)
+    for m in range(1, len(pieces)):
+        both = both + jnp.dot(rec_ref[order_ref[m]], pieces[m], preferred_element_type=jnp.float32)
+    keys = both[:, :width]
+    keys_ref[...] = keys
+    key_feat = features(keys).astype(jnp.bfloat16)
+    val_round = both[:, width:].astype(jnp.bfloat16)
+    feat_ref[...] = key_feat
+    val_ref[...] = val_round
+    wide_feat = key_feat.astype(jnp.float32)
+    wide_val = val_round.astype(jnp.float32)
+    low = lax.broadcasted_iota(jnp.int32, (DH, lanes), 1) < DH
+    for g in range(width // lanes):
+        cols = slice(g * lanes, (g + 1) * lanes)
+        outer = jnp.dot(
+            wide_feat[:, cols].T, wide_val[:, cols], precision=highest,
+            preferred_element_type=jnp.float32,
+        )
+        state_ref[0:DH, cols] = jnp.where(low, outer[:DH], outer[DH:])
+    state_ref[DH : DH + 1, :] = jnp.sum(wide_feat, axis=0, keepdims=True)
+
+
+def project_fused(receptor, parts, interpret=False):
+    own, early, late, twin, order = parts
+    rows, width = receptor.shape
+    count = order.shape[0]
+    split = receptor.reshape(rows, count, width // count).transpose(1, 0, 2)
+    whole = lambda shape: pl.BlockSpec(shape, lambda i, order: (0,) * len(shape))
+    return pl.pallas_call(
+        project_kernel,
+        grid_spec=pltpu.PrefetchScalarGridSpec(
+            num_scalar_prefetch=1,
+            grid=(1,),
+            in_specs=[whole(split.shape), whole(own.shape), whole(early.shape),
+                      whole(late.shape), whole(twin.shape)],
+            out_specs=[whole((rows, width)), whole((rows, width)), whole((rows, width)),
+                       whole((DH + 1, width))],
+        ),
+        out_shape=(
+            jax.ShapeDtypeStruct((rows, width), jnp.bfloat16),
+            jax.ShapeDtypeStruct((rows, width), jnp.bfloat16),
+            jax.ShapeDtypeStruct((rows, width), jnp.float32),
+            jax.ShapeDtypeStruct((DH + 1, width), jnp.float32),
+        ),
+        interpret=interpret,
+    )(order, split, own, early, late, twin)
+
+
 def gather_rows(shard):
     count = lax.axis_size("blk")
     if count != 8:
-        return lax.all_gather(shard, "blk", axis=0, tiled=True)
+        return lax.all_gather(shard, "blk", axis=0, tiled=True), None
     position = lax.axis_index("blk")
     rows = shard.shape[0]
     odd = position % 2
@@ -240,20 +296,24 @@
     for pieces, where in sources:
         for k, at in enumerate(where):
             full = lax.dynamic_update_slice(full, pieces[k][None], (at, 0, 0))
-    return full.reshape(count * rows, shard.shape[1])
+    order = jnp.stack(sources[0][1] + sources[1][1]).astype(jnp.int32)
+    return full.reshape(count * rows, shard.shape[1]), (shard, early, late, sibling, order)
 
 
 def shards(receptor, poses, pairs, block_complex, w_key, w_value, w_query, score_weight):
     rows = receptor.shape[0]
     width = receptor.shape[1]
     contract = (((1,), (1,)), ((), ()))
-    full_both = gather_rows(jnp.concatenate([w_key, w_value], axis=1))
-    both = jnp.dot(receptor, full_both, preferred_element_type=jnp.float32)
-    keys = both[:, :width]
-    values = both[:, width:]
-    key_feat = features(keys).astype(jnp.bfloat16)
-    val_round = values.astype(jnp.bfloat16)
-    state = complex_sum(local_state(key_feat, val_round), block_complex)
+    full_both, parts = gather_rows(jnp.concatenate([w_key, w_value], axis=1))
+    if parts is None:
+        both = jnp.dot(receptor, full_both, preferred_element_type=jnp.float32)
+        keys = both[:, :width]
+        key_feat = features(keys).astype(jnp.bfloat16)
+        val_round = both[:, width:].astype(jnp.bfloat16)
+        own_state = local_state(key_feat, val_round)
+    else:
+        key_feat, val_round, keys, own_state = project_fused(receptor, parts)
+    state = complex_sum(own_state, block_complex)
     pair_loss, pose_grad, pose_state = pose_fused(poses, pairs, state, w_query, score_weight)
     state_grad = complex_sum(pose_state, block_complex).astype(jnp.bfloat16)
     key_heads = key_feat.reshape(rows, H, DH)

time: 101 us -> 114 us (1.13)
  Pallas kernels: 6.8 us -> 17.8 us
  local copies, waits for them, and re-layouts: 11.5 us -> 21.6 us
  waiting for transfers between devices: 30.6 us -> 24.6 us
  matrix products: 7.98 us -> 6.59 us
    pallas_call x0 -> x1, Pallas kernels: none -> 10.9 us  [project_fused(): pl.pallas_call(project_kernel, grid_spec=pltpu.PrefetchScalarGridSpec(num...]
    ppermute x8, waiting for transfers between devices: 7.85 us -> 3.59 us  [send(): return lax.ppermute(value, axis, pairs)]
    dot_general x2 -> x0, matrix products: 3.74 us -> none  [the longest x1 2.48 us: shards(): both = jnp.dot(receptor, full_both, preferred_element_type=jnp.float32)]
    dynamic_update_slice x8, local copies, waits for them, and re-layouts: 4.53 us -> 7.77 us  [gather_rows(): full = lax.dynamic_update_slice(full, pieces[k][None], (at, 0, 0))]
    reduce_sum x1 -> x0, other arithmetic: 2.02 us -> none  [local_state(): norm_row = jnp.sum(key_feat, axis=0, dtype=jnp.float32)]
    reshape x1 -> x2, local copies, waits for them, and re-layouts: 1.22 us -> 3.23 us  [the longest x1 1.92 us: shards(): feat_grad.reshape(rows, width) * slope(keys)]
    ppermute x1, waiting for transfers between devices: 1.76 us -> 0.01 us  [gather_rows(): sibling = lax.ppermute(mine, 'blk', [(s, s ^ 1) for s in range(count)])]
    unnamed x17 -> x24, local copies, waits for them, and re-layouts: 3.24 us -> 4.99 us
  transfers between devices with their start and end apart: 11 -> 11, of which waited for: 7 -> 5; matrix products, arithmetic and copies ran while one was open for 4% -> 14% of each run, Pallas kernels for 0% -> 0%
where the time goes in v8:
time: 114 us; the launch traced here: 112 us
  starting transfers between devices  26 us (23%)
  waiting for transfers between devices  24.6 us (22%)
  local copies, waits for them, and re-layouts  21.6 us (19%)
  Pallas kernels  17.8 us (16%)
  other arithmetic  10.8 us (9%)
  matrix products  6.59 us (6%)
  between operations  5.21 us (5%)
    ppermute x8, starting transfers between devices, send(): return lax.ppermute(value, axis, pairs)  22.8 us
    ppermute x1, waiting for transfers between devices, gather_rows(): lax.ppermute(jnp.stack([shard, early]), 'blk', [(s, s ^ (2 if s % 2 else...  13.3 us
    pallas_call x1, Pallas kernels, project_fused(): pl.pallas_call(project_kernel, grid_spec=pltpu.PrefetchScalarGridSpec(num...  10.9 us
    dynamic_update_slice x8, local copies, waits for them, and re-layouts, gather_rows(): full = lax.dynamic_update_slice(full, pieces[k][None], (at, 0, 0))  7.77 us
    ppermute x1, waiting for transfers between devices, gather_rows(): lax.ppermute(shard, 'blk', [(s, s ^ (4 if s % 2 else 2)) for s in range(c...  7.69 us
    pallas_call x1, Pallas kernels, pose_fused(): pl.pallas_call(pose_kernel, out_shape=(jax.ShapeDtypeStruct((1, pair_rows...  6.87 us
    unnamed x24, local copies, waits for them, and re-layouts  4.99 us
    ppermute x8, waiting for transfers between devices, send(): return lax.ppermute(value, axis, pairs)  3.59 us
  transfers between devices with their start and end apart: 11, of which 5 were waited for; matrix products, arithmetic and copies ran while one was open for 14% of the time, Pallas kernels for 0%

profile of v8, /device:TPU:16, one launch (start us, length us, event | category | flops | bytes accessed | tf_op | source)
XLA Modules:
  0.0 112.5 jit_solution(14087136423216499063)
XLA Ops:
  0.6 1.0 constant_dynamic-update-slice_fusion.1
  1.6 1.0 constant_dynamic-update-slice_fusion.own_ref
  2.6 1.6 %collective-permute-start = (bf16[128,2048]{1,0:T(8,128)(2,1)S(1)}, bf16[128,2048]{1,0:T(8,128)(2,1)S(1)}, u32[]{:S(2)}, u32[]{:S(2)}) collective-permute-start(bf16[128,2048]{1,0:T(8,128)(2,1)S(1)} %constant_dynamic-update-slice_fusion.own_ref), channel_id=1, source_target_pairs={{0,2},{1,5},{2,0},{3,7},{4,6},{5,1},{6,4},{7,3},{8,10},{9,13},{10,... | collective-permute-start | bytes 1572872 | tf_op jit(solution)/shard_map/ppermute | solution.py:284
  4.1 7.7 %collective-permute-done.early_ref = bf16[128,2048]{1,0:T(8,128)(2,1)S(1)} collective-permute-done((bf16[128,2048]{1,0:T(8,128)(2,1)S(1)}, bf16[128,2048]{1,0:T(8,128)(2,1)S(1)}, u32[]{:S(2)}, u32[]{:S(2)}) %collective-permute-start) | collective-permute-done | bytes 524320 | tf_op jit(solution)/shard_map/ppermute | solution.py:284
  11.8 0.1 pad_maximum_fusion.1
  11.9 1.6 %collective-permute-start.1 = (bf16[2,128,2048]{2,1,0:T(8,128)(2,1)S(1)}, bf16[2,128,2048]{2,1,0:T(8,128)(2,1)S(1)}, u32[]{:S(2)}, u32[]{:S(2)}) collective-permute-start(bf16[2,128,2048]{2,1,0:T(8,128)(2,1)S(1)} %pad_maximum_fusion.1), channel_id=1, source_target_pairs={{0,4},{1,3},{2,6},{3,1},{4,0},{5,7},{6,2},{7,5},{8,12},{9,11},{10,... | collective-permute-start | bytes 3145736 | tf_op jit(solution)/shard_map/ppermute | solution.py:285
  13.5 13.3 %collective-permute-done.1.late_ref = bf16[2,128,2048]{2,1,0:T(8,128)(2,1)S(1)} collective-permute-done((bf16[2,128,2048]{2,1,0:T(8,128)(2,1)S(1)}, bf16[2,128,2048]{2,1,0:T(8,128)(2,1)S(1)}, u32[]{:S(2)}, u32[]{:S(2)}) %collective-permute-start.1) | collective-permute-done | bytes 1048608 | tf_op jit(solution)/shard_map/ppermute | solution.py:285
  26.8 1.7 %pad_maximum_fusion = bf16[4,128,2048]{2,1,0:T(8,128)(2,1)} fusion(bf16[2,128,2048]{2,1,0:T(8,128)(2,1)S(1)} %collective-permute-done.1.late_ref, bf16[1,128,2048]{2,1,0:T(8,128)(2,1)S(1)} %bitcast.49, bf16[1,128,2048]{2,1,0:T(8,128)(2,1)S(1)} %bitcast.46), kind=kLoop, calls=%fused_computation | loop fusion | flops 2097152 | bytes 4194304 | tf_op jit(solution)/shard_map/concatenate | solution.py:288
  28.5 0.7 fusion.18
  33.5 1.5 %copy.17 = bf16[512,1024]{0,1:T(8,128)(2,1)S(1)} copy(bf16[512,1024]{1,0:T(8,128)(2,1)} %param.8) | data formatting | bytes 2097152 | tf_op args[0]
  35.0 1.3 %copy.18 = bf16[512,8,128]{2,0,1:T(8,128)(2,1)} copy(bf16[512,8,128]{0,2,1:T(8,128)(2,1)S(1)} %bitcast.54) | data formatting | bytes 2097152 | tf_op jit(solution)/shard_map/reshape | solution.py:253
  36.3 0.6 stack.46.order_ref
  36.9 0.5 broadcast_in_dim.69
  37.7 1.9 %copy-done.5 = bf16[8,128,2048]{2,1,0:T(8,128)(2,1)} copy-done((bf16[8,128,2048]{2,1,0:T(8,128)(2,1)}, bf16[8,128,2048]{2,1,0:T(8,128)(2,1)S(1)}, u32[]{:S(2)}) %copy-start.5) | copy-done | bytes 4194328
  39.6 10.9 %shard_map.103 = (bf16[512,1024]{1,0:T(8,128)(2,1)}, bf16[512,1024]{1,0:T(8,128)(2,1)}, f32[512,1024]{1,0:T(8,128)}, f32[65,1024]{1,0:T(8,128)}) custom-call(s32[8]{0:T(128)} %stack.46.order_ref, bf16[8,512,128]{2,1,0:T(8,128)(2,1)} %bitcast.55, bf16[128,2048]{1,0:T(8,128)(2,1)} %copy-done, bf16[128,2048]{1,0:T(8,128)(2,1)} %copy-done.2, ...), custom_call_target="tpu_custom_call" | custom-call | tf_op jit(solution)/shard_map/pallas_call | solution.py:255
  50.5 1.0 convert_element_type.76
  51.6 0.6 collective-permute-start.3
  52.2 2.9 %collective-permute-start.6 = (bf16[65,1024]{1,0:T(8,128)(2,1)S(1)}, bf16[65,1024]{1,0:T(8,128)(2,1)S(1)}, u32[]{:S(2)}, u32[]{:S(2)}) collective-permute-start(bf16[65,1024]{1,0:T(8,128)(2,1)S(1)} %select_convert_fusion.1), channel_id=1, source_target_pairs={{1,4},{3,6},{5,8},{7,10},{9,12},{11,14},{13,16},{15,18},{17,20},{1... | collective-permute-start | bytes 399368 | tf_op jit(solution)/shard_map/ppermute | solution.py:58
  55.1 1.9 %slice_dynamic-update-slice_fusion.3 = bf16[8,128,2048]{2,1,0:T(8,128)(2,1)} fusion(bf16[8,128,2048]{2,1,0:T(8,128)(2,1)} %copy-done.5, s32[]{:T(128)S(6)} %select_n.238, bf16[4,128,2048]{2,1,0:T(8,128)(2,1)} %collective-permute-done.2.twin_ref), kind=kLoop, calls=%fused_computation.13 | loop fusion | bytes 1048580 | tf_op jit(solution)/shard_map/dynamic_update_slice | solution.py:298
  57.0 1.9 %slice_dynamic-update-slice_fusion.2 = bf16[8,128,2048]{2,1,0:T(8,128)(2,1)} fusion(bf16[8,128,2048]{2,1,0:T(8,128)(2,1)} %slice_dynamic-update-slice_fusion.3, s32[]{:T(128)S(6)} %select_n.239, bf16[4,128,2048]{2,1,0:T(8,128)(2,1)} %collective-permute-done.2.twin_ref), kind=kLoop, calls=%fused_computation.12 | loop fusion | bytes 1048580 | tf_op jit(solution)/shard_map/dynamic_update_slice | solution.py:298
  58.9 0.1 add_convert_fusion.3
  59.0 3.4 %collective-permute-start.4 = (bf16[65,1024]{1,0:T(8,128)(2,1)S(1)}, bf16[65,1024]{1,0:T(8,128)(2,1)S(1)}, u32[]{:S(2)}, u32[]{:S(2)}) collective-permute-start(bf16[65,1024]{1,0:T(8,128)(2,1)S(1)} %get-tuple-element.96), channel_id=1, source_target_pairs={{0,2},{1,3},{2,4},{3,5},{4,6},{5,7},{6,8},{7,9},{8,10},{9,11},{10,... | collective-permute-start | bytes 399368 | tf_op jit(solution)/shard_map/ppermute | solution.py:58
  62.4 4.4 %collective-permute-start.5 = (bf16[65,1024]{1,0:T(8,128)(2,1)S(1)}, bf16[65,1024]{1,0:T(8,128)(2,1)S(1)}, u32[]{:S(2)}, u32[]{:S(2)}) collective-permute-start(bf16[65,1024]{1,0:T(8,128)(2,1)S(1)} %get-tuple-element.97), channel_id=1, source_target_pairs={{2,0},{3,1},{4,2},{5,3},{6,4},{7,5},{8,6},{9,7},{10,8},{11,9},{12,... | collective-permute-start | bytes 399368 | tf_op jit(solution)/shard_map/ppermute | solution.py:58
  66.9 1.9 %slice_dynamic-update-slice_fusion.1 = bf16[8,128,2048]{2,1,0:T(8,128)(2,1)} fusion(bf16[8,128,2048]{2,1,0:T(8,128)(2,1)} %slice_dynamic-update-slice_fusion.2, s32[]{:T(128)S(6)} %select_n.240, bf16[4,128,2048]{2,1,0:T(8,128)(2,1)} %collective-permute-done.2.twin_ref), kind=kLoop, calls=%fused_computation.11 | loop fusion | bytes 1048580 | tf_op jit(solution)/shard_map/dynamic_update_slice | solution.py:298
  68.8 0.4 collective-permute-done.4
  69.2 1.7 %collective-permute-done.5 = bf16[65,1024]{1,0:T(8,128)(2,1)S(1)} collective-permute-done((bf16[65,1024]{1,0:T(8,128)(2,1)S(1)}, bf16[65,1024]{1,0:T(8,128)(2,1)S(1)}, u32[]{:S(2)}, u32[]{:S(2)}) %collective-permute-start.5) | collective-permute-done | bytes 133152 | tf_op jit(solution)/shard_map/ppermute | solution.py:58
  70.9 0.8 fusion.10.state_ref
  71.7 6.9 %shard_map.104 = (f32[1,256]{1,0:T(1,128)}, bf16[128,1024]{1,0:T(8,128)(2,1)}, f32[65,1024]{1,0:T(8,128)}) custom-call(bf16[128,1024]{1,0:T(8,128)(2,1)} %pose_ref.1, s32[2,256]{1,0:T(2,128)} %bitcast.59, f32[65,1024]{1,0:T(8,128)} %fusion.10.state_ref, bf16[1024,1024]{1,0:T(8,128)(2,1)} %query_ref.1, f32[1,1024]{1,0:T(1,128)} %bitcast.58), custom_call_target="tpu_custom_call" | custom-call | tf_op jit(solution)/shard_map/pallas_call | solution.py:206
  78.6 1.0 convert_element_type.84
  79.5 0.1 collective-permute-start.7
  79.6 0.7 select_convert_fusion
  80.3 3.8 %collective-permute-start.10 = (bf16[65,1024]{1,0:T(8,128)(2,1)}, bf16[65,1024]{1,0:T(8,128)(2,1)}, u32[]{:S(2)}, u32[]{:S(2)}) collective-permute-start(bf16[65,1024]{1,0:T(8,128)(2,1)} %select_convert_fusion), channel_id=1, source_target_pairs={{1,4},{3,6},{5,8},{7,10},{9,12},{11,14},{13,16},{15,18},{17,20},{1... | collective-permute-start | bytes 399368 | tf_op jit(solution)/shard_map/ppermute | solution.py:58
  84.2 1.8 %add_convert_fusion.1 = (bf16[65,1024]{1,0:T(8,128)(2,1)}, bf16[65,1024]{1,0:T(8,128)(2,1)}) fusion(f32[65,1024]{1,0:T(8,128)} %get-tuple-element.13, bf16[65,1024]{1,0:T(8,128)(2,1)S(1)} %collective-permute-done.7, pred[]{:T(512)S(6)} %and.108, pred[]{:T(512)S(6)} %eq.40, pred[]{:T(512)S(6)} %and.106, pred[]{:T(512)S(6)} %and.112, pred[]{:T(512)S(6)} %and.111), kind=kLoop, calls=%fused_computation.33 | loop fusion | flops 732160 | bytes 665605 | tf_op jit(solution)/shard_map/convert_element_type | solution.py:89
  86.0 4.3 %collective-permute-start.8 = (bf16[65,1024]{1,0:T(8,128)(2,1)}, bf16[65,1024]{1,0:T(8,128)(2,1)}, u32[]{:S(2)}, u32[]{:S(2)}) collective-permute-start(bf16[65,1024]{1,0:T(8,128)(2,1)} %get-tuple-element.94), channel_id=1, source_target_pairs={{0,2},{1,3},{2,4},{3,5},{4,6},{5,7},{6,8},{7,9},{8,10},{9,11},{10,... | collective-permute-start | bytes 399368 | tf_op jit(solution)/shard_map/ppermute | solution.py:58
  90.3 3.3 %collective-permute-start.9 = (bf16[65,1024]{1,0:T(8,128)(2,1)}, bf16[65,1024]{1,0:T(8,128)(2,1)}, u32[]{:S(2)}, u32[]{:S(2)}) collective-permute-start(bf16[65,1024]{1,0:T(8,128)(2,1)} %get-tuple-element.95), channel_id=1, source_target_pairs={{2,0},{3,1},{4,2},{5,3},{6,4},{7,5},{8,6},{9,7},{10,8},{11,9},{12,... | collective-permute-start | bytes 399368 | tf_op jit(solution)/shard_map/ppermute | solution.py:58
  93.6 1.9 %slice_dynamic-update-slice_fusion = bf16[8,128,2048]{2,1,0:T(8,128)(2,1)} fusion(bf16[8,128,2048]{2,1,0:T(8,128)(2,1)} %slice_dynamic-update-slice_fusion.1, s32[]{:T(128)S(6)} %select_n.241, bf16[4,128,2048]{2,1,0:T(8,128)(2,1)} %collective-permute-done.2.twin_ref), kind=kLoop, calls=%fused_computation.10 | loop fusion | bytes 1048580 | tf_op jit(solution)/shard_map/dynamic_update_slice | solution.py:298
  95.5 0.5 copy.19
  96.1 0.5 copy.22
  96.7 1.5 %collective-permute-done.9 = bf16[65,1024]{1,0:T(8,128)(2,1)} collective-permute-done((bf16[65,1024]{1,0:T(8,128)(2,1)}, bf16[65,1024]{1,0:T(8,128)(2,1)}, u32[]{:S(2)}, u32[]{:S(2)}) %collective-permute-start.9) | collective-permute-done | bytes 133152 | tf_op jit(solution)/shard_map/ppermute | solution.py:58
  98.1 1.2 %fusion.15 = bf16[65,1024]{1,0:T(8,128)(2,1)S(1)} fusion(f32[65,1024]{1,0:T(8,128)S(1)} %copy-done.3, bf16[65,1024]{1,0:T(8,128)(2,1)} %copy-done.9, bf16[65,1024]{1,0:T(8,128)(2,1)} %collective-permute-done.10, bf16[65,1024]{1,0:T(8,128)(2,1)} %collective-permute-done.9, bf16[65,1024]{1,0:T(8,128)(2,1)} %collective-permute-done.8, pred[]{:T(512)S(6)} %and.101), kind=kLoop, calls=%fused_computation.30 | loop fusion | flops 665600 | bytes 931841 | tf_op jit(solution)/shard_map/convert_element_type | solution.py:318
  99.5 0.2 copy.25
  99.7 1.8 %convolution_add_fusion = f32[16,64,512]{2,1,0:T(8,128)} fusion(bf16[64,16,64]{0,2,1:T(8,128)(2,1)S(1)} %bitcast.56, bf16[512,16,64]{0,2,1:T(8,128)(2,1)S(1)} %bitcast.52, f32[16,64]{1,0:T(8,128)S(1)} %reshape.243), kind=kOutput, calls=%fused_computation.6 | convolution fusion | flops 67633152 | bytes 3280896 | tf_op jit(solution)/shard_map/the,dhe->thd/dot_general | solution.py:324
  101.5 1.9 %copy.21 = f32[512,1024]{1,0:T(8,128)S(1)} copy(f32[512,1024]{0,1:T(8,128)} %bitcast.47) | data formatting | bytes 4194304 | tf_op jit(solution)/shard_map/reshape | solution.py:327
  103.4 1.4 %convolution_convert_fusion = bf16[16,64,512]{2,1,0:T(8,128)(2,1)} fusion(bf16[64,16,64]{0,2,1:T(8,128)(2,1)S(1)} %bitcast.57, bf16[512,16,64]{0,2,1:T(8,128)(2,1)S(1)} %bitcast.51), kind=kOutput, calls=%fused_computation.8 | convolution fusion | flops 67633152 | bytes 2228224 | tf_op jit(solution)/shard_map/thd,dhe->the/dot_general | solution.py:329
  104.8 1.5 %copy.24 = bf16[512,1024]{1,0:T(8,128)(2,1)S(1)} copy(bf16[512,1024]{0,1:T(8,128)(2,1)} %bitcast.53) | data formatting | bytes 2097152 | tf_op jit(solution)/shard_map/convert_element_type | solution.py:331
  106.3 2.3 %multiply_convert_fusion = bf16[512,1024]{1,0:T(8,128)(2,1)S(1)} fusion(f32[512,1024]{1,0:T(8,128)S(1)} %copy.21, f32[512,1024]{1,0:T(8,128)} %get-tuple-element.15), kind=kLoop, calls=%fused_computation.5 | loop fusion | flops 2621440 | bytes 5242880 | tf_op jit(solution)/shard_map/convert_element_type | solution.py:327
  108.6 0.5 copy-done.6
  109.1 3.4 %fusion.4 = bf16[512,1024]{1,0:T(8,128)(2,1)} fusion(bf16[1024,2048]{1,0:T(8,128)(2,1)S(1)} %bitcast.50, bf16[512,1024]{1,0:T(8,128)(2,1)S(1)} %copy.24, bf16[512,1024]{1,0:T(8,128)(2,1)S(1)} %multiply_convert_fusion), kind=kOutput, calls=%fused_computation.7 | convolution fusion | flops 2152202240 | bytes 7340032 | tf_op jit(solution)/shard_map/dot_general | solution.py:334
  (35 shorter events, 0.4 us)
Async XLA Ops:
  2.6 34.8 %copy-start = (bf16[128,2048]{1,0:T(8,128)(2,1)}, bf16[128,2048]{1,0:T(8,128)(2,1)S(1)}, u32[]{:S(2)}) copy-start(bf16[128,2048]{1,0:T(8,128)(2,1)S(1)} %constant_dynamic-update-slice_fusion.own_ref) | copy-start | bytes 1572868
  2.6 9.2 %collective-permute-start = (bf16[128,2048]{1,0:T(8,128)(2,1)S(1)}, bf16[128,2048]{1,0:T(8,128)(2,1)S(1)}, u32[]{:S(2)}, u32[]{:S(2)}) collective-permute-start(bf16[128,2048]{1,0:T(8,128)(2,1)S(1)} %constant_dynamic-update-slice_fusion.own_ref), channel_id=1, source_target_pairs={{0,2},{1,5},{2,0},{3,7},{4,6},{5,1},{6,4},{7,3},{8,10},{9,13},{10,... | collective-permute-start | bytes 1572872 | tf_op jit(solution)/shard_map/ppermute | solution.py:284
  11.8 25.6 %copy-start.2 = (bf16[128,2048]{1,0:T(8,128)(2,1)}, bf16[128,2048]{1,0:T(8,128)(2,1)S(1)}, u32[]{:S(2)}) copy-start(bf16[128,2048]{1,0:T(8,128)(2,1)S(1)} %collective-permute-done.early_ref) | copy-start | bytes 1572868
  11.9 16.6 %copy-start.10 = (s32[32]{0:T(128)S(1)}, s32[32]{0:T(128)}, u32[]{:S(2)}) copy-start(s32[32]{0:T(128)} %param.11) | copy-start | bytes 388
  11.9 14.9 %collective-permute-start.1 = (bf16[2,128,2048]{2,1,0:T(8,128)(2,1)S(1)}, bf16[2,128,2048]{2,1,0:T(8,128)(2,1)S(1)}, u32[]{:S(2)}, u32[]{:S(2)}) collective-permute-start(bf16[2,128,2048]{2,1,0:T(8,128)(2,1)S(1)} %pad_maximum_fusion.1), channel_id=1, source_target_pairs={{0,4},{1,3},{2,6},{3,1},{4,0},{5,7},{6,2},{7,5},{8,12},{9,11},{10,... | collective-permute-start | bytes 3145736 | tf_op jit(solution)/shard_map/ppermute | solution.py:285
  26.8 10.8 %copy-start.1 = (bf16[2,128,2048]{2,1,0:T(8,128)(2,1)}, bf16[2,128,2048]{2,1,0:T(8,128)(2,1)S(1)}, u32[]{:S(2)}) copy-start(bf16[2,128,2048]{2,1,0:T(8,128)(2,1)S(1)} %collective-permute-done.1.late_ref) | copy-start | bytes 3145732
  28.5 11.1 %collective-permute-start.2 = (bf16[4,128,2048]{2,1,0:T(8,128)(2,1)}, bf16[4,128,2048]{2,1,0:T(8,128)(2,1)}, u32[]{:S(2)}, u32[]{:S(2)}) collective-permute-start(bf16[4,128,2048]{2,1,0:T(8,128)(2,1)} %pad_maximum_fusion), channel_id=1, source_target_pairs={{0,1},{1,0},{2,3},{3,2},{4,5},{5,4},{6,7},{7,6},{8,9},{9,8},{10,11... | collective-permute-start | bytes 6291464 | tf_op jit(solution)/shard_map/ppermute | solution.py:289
  37.7 1.9 %copy-start.5 = (bf16[8,128,2048]{2,1,0:T(8,128)(2,1)}, bf16[8,128,2048]{2,1,0:T(8,128)(2,1)S(1)}, u32[]{:S(2)}) copy-start(bf16[8,128,2048]{2,1,0:T(8,128)(2,1)S(1)} %slice_dynamic-update-slice_fusion.4) | copy-start | bytes 12582916
  50.5 8.4 %copy-start.4 = (f32[65,1024]{1,0:T(8,128)S(1)}, f32[65,1024]{1,0:T(8,128)}, u32[]{:S(2)}) copy-start(f32[65,1024]{1,0:T(8,128)} %get-tuple-element.10) | copy-start | bytes 798724
  51.6 7.3 %collective-permute-start.3 = (bf16[65,1024]{1,0:T(8,128)(2,1)S(1)}, bf16[65,1024]{1,0:T(8,128)(2,1)S(1)}, u32[]{:S(2)}, u32[]{:S(2)}) collective-permute-start(bf16[65,1024]{1,0:T(8,128)(2,1)S(1)} %convert_element_type.76), channel_id=1, source_target_pairs={{0,1},{1,0},{2,3},{3,2},{4,5},{5,4},{6,7},{7,6},{8,9},{9,8},{10,11... | collective-permute-start | bytes 399368 | tf_op jit(solution)/shard_map/ppermute | solution.py:58
  52.2 16.6 %collective-permute-start.6 = (bf16[65,1024]{1,0:T(8,128)(2,1)S(1)}, bf16[65,1024]{1,0:T(8,128)(2,1)S(1)}, u32[]{:S(2)}, u32[]{:S(2)}) collective-permute-start(bf16[65,1024]{1,0:T(8,128)(2,1)S(1)} %select_convert_fusion.1), channel_id=1, source_target_pairs={{1,4},{3,6},{5,8},{7,10},{9,12},{11,14},{13,16},{15,18},{17,20},{1... | collective-permute-start | bytes 399368 | tf_op jit(solution)/shard_map/ppermute | solution.py:58
  59.0 10.1 %collective-permute-start.4 = (bf16[65,1024]{1,0:T(8,128)(2,1)S(1)}, bf16[65,1024]{1,0:T(8,128)(2,1)S(1)}, u32[]{:S(2)}, u32[]{:S(2)}) collective-permute-start(bf16[65,1024]{1,0:T(8,128)(2,1)S(1)} %get-tuple-element.96), channel_id=1, source_target_pairs={{0,2},{1,3},{2,4},{3,5},{4,6},{5,7},{6,8},{7,9},{8,10},{9,11},{10,... | collective-permute-start | bytes 399368 | tf_op jit(solution)/shard_map/ppermute | solution.py:58
  62.4 8.4 %collective-permute-start.5 = (bf16[65,1024]{1,0:T(8,128)(2,1)S(1)}, bf16[65,1024]{1,0:T(8,128)(2,1)S(1)}, u32[]{:S(2)}, u32[]{:S(2)}) collective-permute-start(bf16[65,1024]{1,0:T(8,128)(2,1)S(1)} %get-tuple-element.97), channel_id=1, source_target_pairs={{2,0},{3,1},{4,2},{5,3},{6,4},{7,5},{8,6},{9,7},{10,8},{11,9},{12,... | collective-permute-start | bytes 399368 | tf_op jit(solution)/shard_map/ppermute | solution.py:58
  71.7 23.8 %copy-start.8 = (bf16[512,1024]{1,0:T(8,128)(2,1)S(1)}, bf16[512,1024]{1,0:T(8,128)(2,1)}, u32[]{:S(2)}) copy-start(bf16[512,1024]{1,0:T(8,128)(2,1)} %get-tuple-element.14) | copy-start | bytes 3145732
  79.5 16.5 %copy-start.7 = (bf16[512,1024]{1,0:T(8,128)(2,1)S(1)}, bf16[512,1024]{1,0:T(8,128)(2,1)}, u32[]{:S(2)}) copy-start(bf16[512,1024]{1,0:T(8,128)(2,1)} %get-tuple-element.16) | copy-start | bytes 3145732
  79.5 4.6 %collective-permute-start.7 = (bf16[65,1024]{1,0:T(8,128)(2,1)S(1)}, bf16[65,1024]{1,0:T(8,128)(2,1)S(1)}, u32[]{:S(2)}, u32[]{:S(2)}) collective-permute-start(bf16[65,1024]{1,0:T(8,128)(2,1)S(1)} %convert_element_type.84), channel_id=1, source_target_pairs={{0,1},{1,0},{2,3},{3,2},{4,5},{5,4},{6,7},{7,6},{8,9},{9,8},{10,11... | collective-permute-start | bytes 399368 | tf_op jit(solution)/shard_map/ppermute | solution.py:58
  80.3 16.3 %collective-permute-start.10 = (bf16[65,1024]{1,0:T(8,128)(2,1)}, bf16[65,1024]{1,0:T(8,128)(2,1)}, u32[]{:S(2)}, u32[]{:S(2)}) collective-permute-start(bf16[65,1024]{1,0:T(8,128)(2,1)} %select_convert_fusion), channel_id=1, source_target_pairs={{1,4},{3,6},{5,8},{7,10},{9,12},{11,14},{13,16},{15,18},{17,20},{1... | collective-permute-start | bytes 399368 | tf_op jit(solution)/shard_map/ppermute | solution.py:58
  84.1 11.4 %copy-start.9 = (bf16[65,1024]{1,0:T(8,128)(2,1)}, bf16[65,1024]{1,0:T(8,128)(2,1)S(1)}, u32[]{:S(2)}) copy-start(bf16[65,1024]{1,0:T(8,128)(2,1)S(1)} %collective-permute-done.7) | copy-start | bytes 399364
  86.0 10.7 %collective-permute-start.8 = (bf16[65,1024]{1,0:T(8,128)(2,1)}, bf16[65,1024]{1,0:T(8,128)(2,1)}, u32[]{:S(2)}, u32[]{:S(2)}) collective-permute-start(bf16[65,1024]{1,0:T(8,128)(2,1)} %get-tuple-element.94), channel_id=1, source_target_pairs={{0,2},{1,3},{2,4},{3,5},{4,6},{5,7},{6,8},{7,9},{8,10},{9,11},{10,... | collective-permute-start | bytes 399368 | tf_op jit(solution)/shard_map/ppermute | solution.py:58
  90.3 7.8 %collective-permute-start.9 = (bf16[65,1024]{1,0:T(8,128)(2,1)}, bf16[65,1024]{1,0:T(8,128)(2,1)}, u32[]{:S(2)}, u32[]{:S(2)}) collective-permute-start(bf16[65,1024]{1,0:T(8,128)(2,1)} %get-tuple-element.95), channel_id=1, source_target_pairs={{2,0},{3,1},{4,2},{5,3},{6,4},{7,5},{8,6},{9,7},{10,8},{11,9},{12,... | collective-permute-start | bytes 399368 | tf_op jit(solution)/shard_map/ppermute | solution.py:58
  95.5 2.6 %copy-start.3 = (f32[65,1024]{1,0:T(8,128)S(1)}, f32[65,1024]{1,0:T(8,128)}, u32[]{:S(2)}) copy-start(f32[65,1024]{1,0:T(8,128)} %get-tuple-element.13) | copy-start | bytes 798724
  106.3 2.8 %copy-start.6 = (bf16[8,128,2048]{2,1,0:T(8,128)(2,1)S(1)}, bf16[8,128,2048]{2,1,0:T(8,128)(2,1)}, u32[]{:S(2)}) copy-start(bf16[8,128,2048]{2,1,0:T(8,128)(2,1)} %slice_dynamic-update-slice_fusion) | copy-start | bytes 12582916

commit v9 on v7

--- a/solution.py
+++ b/solution.py
@@ -216,6 +216,38 @@
     return (loss.reshape(pair_rows.shape[0]), grad, back)
 
 
+def back_kernel(feat_ref, val_ref, keys_ref, grad_ref, full_ref, out_ref, both_ref):
+    width = feat_ref.shape[1]
+    lanes = 2 * DH
+    head_row = lax.broadcasted_iota(jnp.int32, (lanes, lanes), 0) // DH
+    head_col = lax.broadcasted_iota(jnp.int32, (lanes, lanes), 1) // DH
+    same = head_row == head_col
+    for g in range(width // lanes):
+        cols = slice(g * lanes, (g + 1) * lanes)
+        part = grad_ref[0:DH, cols].astype(jnp.float32)
+        block = jnp.where(same, jnp.concatenate([part, part], axis=0), 0.0).astype(jnp.bfloat16)
+        feat_grad = lax.dot_general(
+            val_ref[:, cols], block, (((1,), (1,)), ((), ())), preferred_element_type=jnp.float32
+        ) + grad_ref[DH : DH + 1, cols].astype(jnp.float32)
+        both_ref[:, cols] = (feat_grad * slope(keys_ref[:, cols])).astype(both_ref.dtype)
+        value_grad = jnp.dot(feat_ref[:, cols], block, preferred_element_type=jnp.float32)
+        both_ref[:, width + g * lanes : width + (g + 1) * lanes] = value_grad.astype(both_ref.dtype)
+    total = lax.dot_general(
+        both_ref[...], full_ref[...], (((1,), (1,)), ((), ())), preferred_element_type=jnp.float32
+    )
+    out_ref[...] = total.astype(out_ref.dtype)
+
+
+def back_fused(key_feat, val_round, keys, state_grad, full_both, interpret=False):
+    rows, width = key_feat.shape
+    return pl.pallas_call(
+        back_kernel,
+        out_shape=jax.ShapeDtypeStruct((rows, width), jnp.bfloat16),
+        scratch_shapes=[pltpu.VMEM((rows, 2 * width), jnp.bfloat16)],
+        interpret=interpret,
+    )(key_feat, val_round, keys, state_grad, full_both)
+
+
 def gather_rows(shard):
     count = lax.axis_size("blk")
     if count != 8:
@@ -256,23 +288,8 @@
     state = complex_sum(local_state(key_feat, val_round), block_complex)
     pair_loss, pose_grad, pose_state = pose_fused(poses, pairs, state, w_query, score_weight)
     state_grad = complex_sum(pose_state, block_complex).astype(jnp.bfloat16)
-    key_heads = key_feat.reshape(rows, H, DH)
-    val_heads = val_round.reshape(rows, H, DH)
-    grad_heads = state_grad[:DH].reshape(DH, H, DH)
-    norm_back = state_grad[DH].astype(jnp.float32).reshape(H, DH)
-    feat_grad = (
-        jnp.einsum("the,dhe->thd", val_heads, grad_heads, preferred_element_type=jnp.float32)
-        + norm_back[None]
-    )
-    key_grad = (feat_grad.reshape(rows, width) * slope(keys)).astype(jnp.bfloat16)
-    value_grad = (
-        jnp.einsum("thd,dhe->the", key_heads, grad_heads, preferred_element_type=jnp.float32)
-        .reshape(rows, width)
-        .astype(jnp.bfloat16)
-    )
-    both_grad = jnp.concatenate([key_grad, value_grad], axis=1)
-    total = lax.dot_general(both_grad, full_both, contract, preferred_element_type=jnp.float32)
-    return (pair_loss, pose_grad, total.astype(jnp.bfloat16))
+    total = back_fused(key_feat, val_round, keys, state_grad, full_both)
+    return (pair_loss, pose_grad, total)
 
 
 def solution(mesh):

time: 101 us -> 101 us (level)
  Pallas kernels: 6.8 us -> 14.4 us
  matrix products: 7.98 us -> 4.29 us
  other arithmetic: 11.6 us -> 8.27 us
    pallas_call x0 -> x1, Pallas kernels: none -> 7.63 us  [back_fused(): pl.pallas_call(back_kernel, out_shape=jax.ShapeDtypeStruct((rows, width),...]
    dot_general x3 -> x0, matrix products: 4.25 us -> none  [the longest x1 3.35 us: shards(): lax.dot_general(both_grad, full_both, contract, preferred_element_type=jn...]
    unnamed x17 -> x11, local copies, waits for them, and re-layouts: 3.24 us -> 1.09 us
    convert_element_type x2, other arithmetic: 2.58 us -> 1.18 us  [chip_part(): (kept(low, first, target) + kept(high, first + 1, target)).astype(jnp.bfl...]
    convert_element_type x1, local copies, waits for them, and re-layouts: 0.07 us -> 1.41 us  [shards(): key_feat = features(keys).astype(jnp.bfloat16)]
    slice x1 -> x2, local copies, waits for them, and re-layouts: 0.13 us -> 1.47 us  [shards(): values = both[:, width:]]
    add x1, other arithmetic: 1.88 us -> 0.81 us  [complex_sum(): total + up.astype(own.dtype) + down.astype(own.dtype)]
    reshape x1, local copies, waits for them, and re-layouts: 1.22 us -> 0.18 us  [local_state(): outer = jnp.einsum('thd,the->dhe', key_heads, val_heads, preferred_elemen...]
  transfers between devices with their start and end apart: 11 -> 11, of which waited for: 7 -> 7; matrix products, arithmetic and copies ran while one was open for 4% -> 3% of each run, Pallas kernels for 0% -> 0%
where the time goes in v9:
time: 101 us; the launch traced here: 99 us
  waiting for transfers between devices  30.3 us (30%)
  starting transfers between devices  25.6 us (25%)
  Pallas kernels  14.4 us (14%)
  local copies, waits for them, and re-layouts  10.8 us (11%)
  other arithmetic  8.27 us (8%)
  between operations  5.36 us (5%)
  matrix products  4.29 us (4%)
    ppermute x8, starting transfers between devices, send(): return lax.ppermute(value, axis, pairs)  22.5 us
    ppermute x1, waiting for transfers between devices, gather_rows(): lax.ppermute(jnp.stack([shard, early]), 'blk', [(s, s ^ (2 if s % 2 else...  13.3 us
    ppermute x1, waiting for transfers between devices, gather_rows(): lax.ppermute(shard, 'blk', [(s, s ^ (4 if s % 2 else 2)) for s in range(c...  7.69 us
    pallas_call x1, Pallas kernels, back_fused(): pl.pallas_call(back_kernel, out_shape=jax.ShapeDtypeStruct((rows, width),...  7.63 us
    ppermute x8, waiting for transfers between devices, send(): return lax.ppermute(value, axis, pairs)  7.52 us
    pallas_call x1, Pallas kernels, pose_fused(): pl.pallas_call(pose_kernel, out_shape=(jax.ShapeDtypeStruct((1, pair_rows...  6.79 us
    dynamic_update_slice x8, local copies, waits for them, and re-layouts, gather_rows(): full = lax.dynamic_update_slice(full, pieces[k][None], (at, 0, 0))  4.53 us
    dot_general x1, matrix products, shards(): both = jnp.dot(receptor, full_both, preferred_element_type=jnp.float32)  2.33 us
  transfers between devices with their start and end apart: 11, of which 7 were waited for; matrix products, arithmetic and copies ran while one was open for 3% of the time, Pallas kernels for 0%

profile of v9, /device:TPU:16, one launch (start us, length us, event | category | flops | bytes accessed | tf_op | source)
XLA Modules:
  0.0 99.0 jit_solution(8007384923593808358)
XLA Ops:
  0.6 0.0 copy-start
  0.7 1.1 %constant_dynamic-update-slice_fusion.1 = bf16[128,2048]{1,0:T(8,128)(2,1)S(1)} fusion(bf16[128,1024]{1,0:T(8,128)(2,1)} %param.12), kind=kLoop, calls=%fused_computation.36 | loop fusion | bytes 524288
  1.7 1.0 constant_dynamic-update-slice_fusion
  2.7 1.6 %collective-permute-start = (bf16[128,2048]{1,0:T(8,128)(2,1)S(1)}, bf16[128,2048]{1,0:T(8,128)(2,1)S(1)}, u32[]{:S(2)}, u32[]{:S(2)}) collective-permute-start(bf16[128,2048]{1,0:T(8,128)(2,1)S(1)} %constant_dynamic-update-slice_fusion), channel_id=1, source_target_pairs={{0,2},{1,5},{2,0},{3,7},{4,6},{5,1},{6,4},{7,3},{8,10},{9,13},{10,... | collective-permute-start | bytes 1572872 | tf_op jit(solution)/shard_map/ppermute | solution.py:260
  4.2 7.7 %collective-permute-done = bf16[128,2048]{1,0:T(8,128)(2,1)S(1)} collective-permute-done((bf16[128,2048]{1,0:T(8,128)(2,1)S(1)}, bf16[128,2048]{1,0:T(8,128)(2,1)S(1)}, u32[]{:S(2)}, u32[]{:S(2)}) %collective-permute-start) | collective-permute-done | bytes 524320 | tf_op jit(solution)/shard_map/ppermute | solution.py:260
  11.9 0.1 pad_maximum_fusion.1
  12.0 1.6 %collective-permute-start.1 = (bf16[2,128,2048]{2,1,0:T(8,128)(2,1)S(1)}, bf16[2,128,2048]{2,1,0:T(8,128)(2,1)S(1)}, u32[]{:S(2)}, u32[]{:S(2)}) collective-permute-start(bf16[2,128,2048]{2,1,0:T(8,128)(2,1)S(1)} %pad_maximum_fusion.1), channel_id=1, source_target_pairs={{0,4},{1,3},{2,6},{3,1},{4,0},{5,7},{6,2},{7,5},{8,12},{9,11},{10,... | collective-permute-start | bytes 3145736 | tf_op jit(solution)/shard_map/ppermute | solution.py:261
  13.6 13.3 %collective-permute-done.1 = bf16[2,128,2048]{2,1,0:T(8,128)(2,1)S(1)} collective-permute-done((bf16[2,128,2048]{2,1,0:T(8,128)(2,1)S(1)}, bf16[2,128,2048]{2,1,0:T(8,128)(2,1)S(1)}, u32[]{:S(2)}, u32[]{:S(2)}) %collective-permute-start.1) | collective-permute-done | bytes 1048608 | tf_op jit(solution)/shard_map/ppermute | solution.py:261
  26.9 1.5 %pad_maximum_fusion = bf16[4,128,2048]{2,1,0:T(8,128)(2,1)} fusion(bf16[2,128,2048]{2,1,0:T(8,128)(2,1)S(1)} %collective-permute-done.1, bf16[1,128,2048]{2,1,0:T(8,128)(2,1)S(1)} %bitcast.38, bf16[1,128,2048]{2,1,0:T(8,128)(2,1)S(1)} %bitcast.36), kind=kLoop, calls=%fused_computation.2 | loop fusion | flops 2097152 | bytes 4194304 | tf_op jit(solution)/shard_map/concatenate | solution.py:264
  28.5 0.7 fusion.10
  30.4 0.5 broadcast_in_dim.60
  30.9 0.1 constant_dynamic-update-slice_fusion.3
  31.0 0.1 constant_dynamic-update-slice_fusion.2
  31.1 0.1 slice_dynamic-update-slice_fusion.5
  31.1 0.1 slice_dynamic-update-slice_fusion.4
  31.2 1.8 %collective-permute-done.2 = bf16[4,128,2048]{2,1,0:T(8,128)(2,1)} collective-permute-done((bf16[4,128,2048]{2,1,0:T(8,128)(2,1)}, bf16[4,128,2048]{2,1,0:T(8,128)(2,1)}, u32[]{:S(2)}, u32[]{:S(2)}) %collective-permute-start.2) | collective-permute-done | bytes 2097184 | tf_op jit(solution)/shard_map/ppermute | solution.py:265
  33.0 1.1 %slice_dynamic-update-slice_fusion.3 = bf16[8,128,2048]{2,1,0:T(8,128)(2,1)S(1)} fusion(bf16[8,128,2048]{2,1,0:T(8,128)(2,1)S(1)} %slice_dynamic-update-slice_fusion.4, s32[]{:T(128)S(6)} %select_n.205, bf16[4,128,2048]{2,1,0:T(8,128)(2,1)} %collective-permute-done.2), kind=kLoop, calls=%fused_computation.9 | loop fusion | bytes 1048580 | tf_op jit(solution)/shard_map/dynamic_update_slice | solution.py:274
  34.0 1.1 %slice_dynamic-update-slice_fusion.2 = bf16[8,128,2048]{2,1,0:T(8,128)(2,1)S(1)} fusion(bf16[8,128,2048]{2,1,0:T(8,128)(2,1)S(1)} %slice_dynamic-update-slice_fusion.3, s32[]{:T(128)S(6)} %select_n.206, bf16[4,128,2048]{2,1,0:T(8,128)(2,1)} %collective-permute-done.2), kind=kLoop, calls=%fused_computation.8 | loop fusion | bytes 1048580 | tf_op jit(solution)/shard_map/dynamic_update_slice | solution.py:274
  35.1 1.1 %slice_dynamic-update-slice_fusion.1 = bf16[8,128,2048]{2,1,0:T(8,128)(2,1)S(1)} fusion(bf16[8,128,2048]{2,1,0:T(8,128)(2,1)S(1)} %slice_dynamic-update-slice_fusion.2, s32[]{:T(128)S(6)} %select_n.207, bf16[4,128,2048]{2,1,0:T(8,128)(2,1)} %collective-permute-done.2), kind=kLoop, calls=%fused_computation.7 | loop fusion | bytes 1048580 | tf_op jit(solution)/shard_map/dynamic_update_slice | solution.py:274
  36.2 1.1 %slice_dynamic-update-slice_fusion = bf16[8,128,2048]{2,1,0:T(8,128)(2,1)S(1)} fusion(bf16[8,128,2048]{2,1,0:T(8,128)(2,1)S(1)} %slice_dynamic-update-slice_fusion.1, s32[]{:T(128)S(6)} %select_n.208, bf16[4,128,2048]{2,1,0:T(8,128)(2,1)} %collective-permute-done.2), kind=kLoop, calls=%fused_computation.6 | loop fusion | bytes 1048580 | tf_op jit(solution)/shard_map/dynamic_update_slice | solution.py:274
  37.3 2.3 %convolution_bitcast_fusion = f32[512,2048]{1,0:T(8,128)S(1)} fusion(bf16[512,1024]{1,0:T(8,128)(2,1)S(1)} %copy-done, bf16[1024,2048]{1,0:T(8,128)(2,1)S(1)} %bitcast.33), kind=kOutput, calls=%fused_computation | convolution fusion | flops 2147483648 | bytes 9437184 | tf_op jit(solution)/shard_map/dot_general | solution.py:283
  39.7 0.2 slice.84.val_ref
  39.8 1.9 %convert_reduce_fusion = (f32[1024]{0:T(1024)S(1)}, bf16[512,1024]{1,0:T(8,128)(2,1)S(1)}, f32[512,1024]{1,0:T(8,128)}) fusion(f32[512,2048]{1,0:T(8,128)S(1)} %convolution_bitcast_fusion), kind=kLoop, calls=%fused_computation.3 | loop fusion | flops 3668992 | bytes 5246976 | tf_op jit(solution)/shard_map/reduce_sum | solution.py:37
  41.7 1.4 %copy.17 = bf16[512,1024]{0,1:T(8,128)(2,1)} copy(bf16[512,1024]{1,0:T(8,128)(2,1)S(1)} %get-tuple-element.87.feat_ref) | data formatting | bytes 2097152 | tf_op jit(solution)/shard_map/convert_element_type | solution.py:286
  43.1 1.3 %copy.16 = bf16[512,1024]{0,1:T(8,128)(2,1)} copy(bf16[512,1024]{1,0:T(8,128)(2,1)S(1)} %slice.84.val_ref) | data formatting | bytes 2097152 | tf_op jit(solution)/shard_map/slice | solution.py:285
  44.4 2.0 %fusion.11 = f32[16,64,64]{2,1,0:T(8,128)S(1)} fusion(bf16[512,16,64]{0,2,1:T(8,128)(2,1)} %bitcast.40, bf16[512,16,64]{0,2,1:T(8,128)(2,1)} %bitcast.39), kind=kOutput, calls=%fused_computation.40 | convolution fusion | flops 67108864 | bytes 2359296 | tf_op jit(solution)/shard_map/thd,the->dhe/dot_general | solution.py:34
  46.4 0.2 copy.20
  46.6 0.2 collective-permute-start.3
  49.3 3.3 %collective-permute-start.6 = (bf16[65,1024]{1,0:T(8,128)(2,1)S(1)}, bf16[65,1024]{1,0:T(8,128)(2,1)S(1)}, u32[]{:S(2)}, u32[]{:S(2)}) collective-permute-start(bf16[65,1024]{1,0:T(8,128)(2,1)S(1)} %get-tuple-element.93), channel_id=1, source_target_pairs={{1,4},{3,6},{5,8},{7,10},{9,12},{11,14},{13,16},{15,18},{17,20},{1... | collective-permute-start | bytes 399368 | tf_op jit(solution)/shard_map/ppermute | solution.py:58
  52.6 0.0 collective-permute-done.3
  52.6 0.1 add_convert_fusion.3
  52.7 3.4 %collective-permute-start.4 = (bf16[65,1024]{1,0:T(8,128)(2,1)S(1)}, bf16[65,1024]{1,0:T(8,128)(2,1)S(1)}, u32[]{:S(2)}, u32[]{:S(2)}) collective-permute-start(bf16[65,1024]{1,0:T(8,128)(2,1)S(1)} %get-tuple-element.91), channel_id=1, source_target_pairs={{0,2},{1,3},{2,4},{3,5},{4,6},{5,7},{6,8},{7,9},{8,10},{9,11},{10,... | collective-permute-start | bytes 399368 | tf_op jit(solution)/shard_map/ppermute | solution.py:58
  56.2 4.2 %collective-permute-start.5 = (bf16[65,1024]{1,0:T(8,128)(2,1)S(1)}, bf16[65,1024]{1,0:T(8,128)(2,1)S(1)}, u32[]{:S(2)}, u32[]{:S(2)}) collective-permute-start(bf16[65,1024]{1,0:T(8,128)(2,1)S(1)} %get-tuple-element.92), channel_id=1, source_target_pairs={{2,0},{3,1},{4,2},{5,3},{6,4},{7,5},{8,6},{9,7},{10,8},{11,9},{12,... | collective-permute-start | bytes 399368 | tf_op jit(solution)/shard_map/ppermute | solution.py:58
  61.1 0.0 collective-permute-done.6
  61.1 1.5 %collective-permute-done.4 = bf16[65,1024]{1,0:T(8,128)(2,1)S(1)} collective-permute-done((bf16[65,1024]{1,0:T(8,128)(2,1)S(1)}, bf16[65,1024]{1,0:T(8,128)(2,1)S(1)}, u32[]{:S(2)}, u32[]{:S(2)}) %collective-permute-start.4) | collective-permute-done | bytes 133152 | tf_op jit(solution)/shard_map/ppermute | solution.py:58
  62.5 2.0 %collective-permute-done.5 = bf16[65,1024]{1,0:T(8,128)(2,1)S(1)} collective-permute-done((bf16[65,1024]{1,0:T(8,128)(2,1)S(1)}, bf16[65,1024]{1,0:T(8,128)(2,1)S(1)}, u32[]{:S(2)}, u32[]{:S(2)}) %collective-permute-start.5) | collective-permute-done | bytes 133152 | tf_op jit(solution)/shard_map/ppermute | solution.py:58
  64.6 0.8 fusion.3.state_ref
  65.4 6.8 %shard_map.103 = (f32[1,256]{1,0:T(1,128)}, bf16[128,1024]{1,0:T(8,128)(2,1)}, f32[65,1024]{1,0:T(8,128)}) custom-call(bf16[128,1024]{1,0:T(8,128)(2,1)} %pose_ref.1, s32[2,256]{1,0:T(2,128)} %bitcast.46, f32[65,1024]{1,0:T(8,128)} %fusion.3.state_ref, bf16[1024,1024]{1,0:T(8,128)(2,1)} %query_ref.1, f32[1,1024]{1,0:T(1,128)} %bitcast.45), custom_call_target="tpu_custom_call" | custom-call | tf_op jit(solution)/shard_map/pallas_call | solution.py:206
  72.2 1.0 convert_element_type.68
  73.2 0.1 collective-permute-start.7
  73.3 3.5 %collective-permute-start.10 = (bf16[65,1024]{1,0:T(8,128)(2,1)S(1)}, bf16[65,1024]{1,0:T(8,128)(2,1)S(1)}, u32[]{:S(2)}, u32[]{:S(2)}) collective-permute-start(bf16[65,1024]{1,0:T(8,128)(2,1)S(1)} %select_convert_fusion.1), channel_id=1, source_target_pairs={{1,4},{3,6},{5,8},{7,10},{9,12},{11,14},{13,16},{15,18},{17,20},{1... | collective-permute-start | bytes 399368 | tf_op jit(solution)/shard_map/ppermute | solution.py:58
  76.8 1.1 %add_convert_fusion.1 = (bf16[65,1024]{1,0:T(8,128)(2,1)S(1)}, bf16[65,1024]{1,0:T(8,128)(2,1)S(1)}) fusion(f32[65,1024]{1,0:T(8,128)} %get-tuple-element.8, bf16[65,1024]{1,0:T(8,128)(2,1)S(1)} %collective-permute-done.7, pred[]{:T(512)S(6)} %and.108, pred[]{:T(512)S(6)} %eq.40, pred[]{:T(512)S(6)} %and.106, pred[]{:T(512)S(6)} %and.112, pred[]{:T(512)S(6)} %and.111), kind=kLoop, calls=%fused_computation.30 | loop fusion | flops 732160 | bytes 665605 | tf_op jit(solution)/shard_map/convert_element_type | solution.py:89
  77.8 4.3 %collective-permute-start.8 = (bf16[65,1024]{1,0:T(8,128)(2,1)S(1)}, bf16[65,1024]{1,0:T(8,128)(2,1)S(1)}, u32[]{:S(2)}, u32[]{:S(2)}) collective-permute-start(bf16[65,1024]{1,0:T(8,128)(2,1)S(1)} %get-tuple-element.89), channel_id=1, source_target_pairs={{0,2},{1,3},{2,4},{3,5},{4,6},{5,7},{6,8},{7,9},{8,10},{9,11},{10,... | collective-permute-start | bytes 399368 | tf_op jit(solution)/shard_map/ppermute | solution.py:58
  82.2 3.5 %collective-permute-start.9 = (bf16[65,1024]{1,0:T(8,128)(2,1)S(1)}, bf16[65,1024]{1,0:T(8,128)(2,1)S(1)}, u32[]{:S(2)}, u32[]{:S(2)}) collective-permute-start(bf16[65,1024]{1,0:T(8,128)(2,1)S(1)} %get-tuple-element.90), channel_id=1, source_target_pairs={{2,0},{3,1},{4,2},{5,3},{6,4},{7,5},{8,6},{9,7},{10,8},{11,9},{12,... | collective-permute-start | bytes 399368 | tf_op jit(solution)/shard_map/ppermute | solution.py:58
  85.7 1.9 %collective-permute-done.8 = bf16[65,1024]{1,0:T(8,128)(2,1)S(1)} collective-permute-done((bf16[65,1024]{1,0:T(8,128)(2,1)S(1)}, bf16[65,1024]{1,0:T(8,128)(2,1)S(1)}, u32[]{:S(2)}, u32[]{:S(2)}) %collective-permute-start.8) | collective-permute-done | bytes 133152 | tf_op jit(solution)/shard_map/ppermute | solution.py:58
  87.6 2.1 %collective-permute-done.9 = bf16[65,1024]{1,0:T(8,128)(2,1)S(1)} collective-permute-done((bf16[65,1024]{1,0:T(8,128)(2,1)S(1)}, bf16[65,1024]{1,0:T(8,128)(2,1)S(1)}, u32[]{:S(2)}, u32[]{:S(2)}) %collective-permute-start.9) | collective-permute-done | bytes 133152 | tf_op jit(solution)/shard_map/ppermute | solution.py:58
  89.7 1.7 %fusion.8.grad_ref = bf16[65,1024]{1,0:T(8,128)(2,1)} fusion(f32[65,1024]{1,0:T(8,128)} %get-tuple-element.8, bf16[65,1024]{1,0:T(8,128)(2,1)S(1)} %collective-permute-done.7, bf16[65,1024]{1,0:T(8,128)(2,1)S(1)} %collective-permute-done.10, bf16[65,1024]{1,0:T(8,128)(2,1)S(1)} %collective-permute-done.9, bf16[65,1024]{1,0:T(8,128)(2,1)S(1)} %collective-permute-done.8, ...), kind=kLoop, calls=%fused_computation.26 | loop fusion | flops 665600 | bytes 931841 | tf_op jit(solution)/shard_map/convert_element_type | solution.py:290
  91.4 7.6 %shard_map.104 = bf16[512,1024]{1,0:T(8,128)(2,1)} custom-call(bf16[512,1024]{1,0:T(8,128)(2,1)} %copy-done.3, bf16[512,1024]{1,0:T(8,128)(2,1)} %copy-done.2, f32[512,1024]{1,0:T(8,128)} %get-tuple-element.88.keys_ref, bf16[65,1024]{1,0:T(8,128)(2,1)} %fusion.8.grad_ref, bf16[1024,2048]{1,0:T(8,128)(2,1)} %bitcast.34), custom_call_target="tpu_custom_call" | custom-call | tf_op jit(solution)/shard_map/pallas_call | solution.py:243
  (14 shorter events, 0.1 us)
Async XLA Ops:
  0.6 36.7 %copy-start = (bf16[512,1024]{1,0:T(8,128)(2,1)S(1)}, bf16[512,1024]{1,0:T(8,128)(2,1)}, u32[]{:S(2)}) copy-start(bf16[512,1024]{1,0:T(8,128)(2,1)} %param.8) | copy-start | bytes 3145732
  0.6 27.8 %copy-start.4 = (s32[32]{0:T(128)S(1)}, s32[32]{0:T(128)}, u32[]{:S(2)}) copy-start(s32[32]{0:T(128)} %param.11) | copy-start | bytes 388
  2.7 9.2 %collective-permute-start = (bf16[128,2048]{1,0:T(8,128)(2,1)S(1)}, bf16[128,2048]{1,0:T(8,128)(2,1)S(1)}, u32[]{:S(2)}, u32[]{:S(2)}) collective-permute-start(bf16[128,2048]{1,0:T(8,128)(2,1)S(1)} %constant_dynamic-update-slice_fusion), channel_id=1, source_target_pairs={{0,2},{1,5},{2,0},{3,7},{4,6},{5,1},{6,4},{7,3},{8,10},{9,13},{10,... | collective-permute-start | bytes 1572872 | tf_op jit(solution)/shard_map/ppermute | solution.py:260
  12.0 14.9 %collective-permute-start.1 = (bf16[2,128,2048]{2,1,0:T(8,128)(2,1)S(1)}, bf16[2,128,2048]{2,1,0:T(8,128)(2,1)S(1)}, u32[]{:S(2)}, u32[]{:S(2)}) collective-permute-start(bf16[2,128,2048]{2,1,0:T(8,128)(2,1)S(1)} %pad_maximum_fusion.1), channel_id=1, source_target_pairs={{0,4},{1,3},{2,6},{3,1},{4,0},{5,7},{6,2},{7,5},{8,12},{9,11},{10,... | collective-permute-start | bytes 3145736 | tf_op jit(solution)/shard_map/ppermute | solution.py:261
  28.5 4.5 %collective-permute-start.2 = (bf16[4,128,2048]{2,1,0:T(8,128)(2,1)}, bf16[4,128,2048]{2,1,0:T(8,128)(2,1)}, u32[]{:S(2)}, u32[]{:S(2)}) collective-permute-start(bf16[4,128,2048]{2,1,0:T(8,128)(2,1)} %pad_maximum_fusion), channel_id=1, source_target_pairs={{0,1},{1,0},{2,3},{3,2},{4,5},{5,4},{6,7},{7,6},{8,9},{9,8},{10,11... | collective-permute-start | bytes 6291464 | tf_op jit(solution)/shard_map/ppermute | solution.py:265
  37.3 2.4 %copy-start.1 = (bf16[8,128,2048]{2,1,0:T(8,128)(2,1)}, bf16[8,128,2048]{2,1,0:T(8,128)(2,1)S(1)}, u32[]{:S(2)}) copy-start(bf16[8,128,2048]{2,1,0:T(8,128)(2,1)S(1)} %slice_dynamic-update-slice_fusion) | copy-start | bytes 12582916
  39.8 4.6 %copy-start.2 = (bf16[512,1024]{1,0:T(8,128)(2,1)}, bf16[512,1024]{1,0:T(8,128)(2,1)S(1)}, u32[]{:S(2)}) copy-start(bf16[512,1024]{1,0:T(8,128)(2,1)S(1)} %slice.84.val_ref) | copy-start | bytes 3145732
  41.7 11.0 %copy-start.3 = (bf16[512,1024]{1,0:T(8,128)(2,1)}, bf16[512,1024]{1,0:T(8,128)(2,1)S(1)}, u32[]{:S(2)}) copy-start(bf16[512,1024]{1,0:T(8,128)(2,1)S(1)} %get-tuple-element.87.feat_ref) | copy-start | bytes 3145732
  46.6 6.0 %collective-permute-start.3 = (bf16[65,1024]{1,0:T(8,128)(2,1)S(1)}, bf16[65,1024]{1,0:T(8,128)(2,1)S(1)}, u32[]{:S(2)}, u32[]{:S(2)}) collective-permute-start(bf16[65,1024]{1,0:T(8,128)(2,1)S(1)} %get-tuple-element.94), channel_id=1, source_target_pairs={{0,1},{1,0},{2,3},{3,2},{4,5},{5,4},{6,7},{7,6},{8,9},{9,8},{10,11... | collective-permute-start | bytes 399368 | tf_op jit(solution)/shard_map/ppermute | solution.py:58
  49.3 11.7 %collective-permute-start.6 = (bf16[65,1024]{1,0:T(8,128)(2,1)S(1)}, bf16[65,1024]{1,0:T(8,128)(2,1)S(1)}, u32[]{:S(2)}, u32[]{:S(2)}) collective-permute-start(bf16[65,1024]{1,0:T(8,128)(2,1)S(1)} %get-tuple-element.93), channel_id=1, source_target_pairs={{1,4},{3,6},{5,8},{7,10},{9,12},{11,14},{13,16},{15,18},{17,20},{1... | collective-permute-start | bytes 399368 | tf_op jit(solution)/shard_map/ppermute | solution.py:58
  52.7 9.8 %collective-permute-start.4 = (bf16[65,1024]{1,0:T(8,128)(2,1)S(1)}, bf16[65,1024]{1,0:T(8,128)(2,1)S(1)}, u32[]{:S(2)}, u32[]{:S(2)}) collective-permute-start(bf16[65,1024]{1,0:T(8,128)(2,1)S(1)} %get-tuple-element.91), channel_id=1, source_target_pairs={{0,2},{1,3},{2,4},{3,5},{4,6},{5,7},{6,8},{7,9},{8,10},{9,11},{10,... | collective-permute-start | bytes 399368 | tf_op jit(solution)/shard_map/ppermute | solution.py:58
  56.2 8.4 %collective-permute-start.5 = (bf16[65,1024]{1,0:T(8,128)(2,1)S(1)}, bf16[65,1024]{1,0:T(8,128)(2,1)S(1)}, u32[]{:S(2)}, u32[]{:S(2)}) collective-permute-start(bf16[65,1024]{1,0:T(8,128)(2,1)S(1)} %get-tuple-element.92), channel_id=1, source_target_pairs={{2,0},{3,1},{4,2},{5,3},{6,4},{7,5},{8,6},{9,7},{10,8},{11,9},{12,... | collective-permute-start | bytes 399368 | tf_op jit(solution)/shard_map/ppermute | solution.py:58
  73.2 3.6 %collective-permute-start.7 = (bf16[65,1024]{1,0:T(8,128)(2,1)S(1)}, bf16[65,1024]{1,0:T(8,128)(2,1)S(1)}, u32[]{:S(2)}, u32[]{:S(2)}) collective-permute-start(bf16[65,1024]{1,0:T(8,128)(2,1)S(1)} %convert_element_type.68), channel_id=1, source_target_pairs={{0,1},{1,0},{2,3},{3,2},{4,5},{5,4},{6,7},{7,6},{8,9},{9,8},{10,11... | collective-permute-start | bytes 399368 | tf_op jit(solution)/shard_map/ppermute | solution.py:58
  73.3 12.4 %collective-permute-start.10 = (bf16[65,1024]{1,0:T(8,128)(2,1)S(1)}, bf16[65,1024]{1,0:T(8,128)(2,1)S(1)}, u32[]{:S(2)}, u32[]{:S(2)}) collective-permute-start(bf16[65,1024]{1,0:T(8,128)(2,1)S(1)} %select_convert_fusion.1), channel_id=1, source_target_pairs={{1,4},{3,6},{5,8},{7,10},{9,12},{11,14},{13,16},{15,18},{17,20},{1... | collective-permute-start | bytes 399368 | tf_op jit(solution)/shard_map/ppermute | solution.py:58
  77.8 9.7 %collective-permute-start.8 = (bf16[65,1024]{1,0:T(8,128)(2,1)S(1)}, bf16[65,1024]{1,0:T(8,128)(2,1)S(1)}, u32[]{:S(2)}, u32[]{:S(2)}) collective-permute-start(bf16[65,1024]{1,0:T(8,128)(2,1)S(1)} %get-tuple-element.89), channel_id=1, source_target_pairs={{0,2},{1,3},{2,4},{3,5},{4,6},{5,7},{6,8},{7,9},{8,10},{9,11},{10,... | collective-permute-start | bytes 399368 | tf_op jit(solution)/shard_map/ppermute | solution.py:58
  82.2 7.5 %collective-permute-start.9 = (bf16[65,1024]{1,0:T(8,128)(2,1)S(1)}, bf16[65,1024]{1,0:T(8,128)(2,1)S(1)}, u32[]{:S(2)}, u32[]{:S(2)}) collective-permute-start(bf16[65,1024]{1,0:T(8,128)(2,1)S(1)} %get-tuple-element.90), channel_id=1, source_target_pairs={{2,0},{3,1},{4,2},{5,3},{6,4},{7,5},{8,6},{9,7},{10,8},{11,9},{12,... | collective-permute-start | bytes 399368 | tf_op jit(solution)/shard_map/ppermute | solution.py:58

commit v10 on v9

--- a/solution.py
+++ b/solution.py
@@ -257,16 +257,21 @@
     odd = position % 2
     first = jnp.where(odd == 1, 4, 2)
     second = 6 - first
+    swap = [(s, s ^ 1) for s in range(count)]
+    twin_own = lax.ppermute(shard, "blk", swap)
     early = lax.ppermute(shard, "blk", [(s, s ^ (4 if s % 2 else 2)) for s in range(count)])
+    twin_early = lax.ppermute(early, "blk", swap)
     late = lax.ppermute(
         jnp.stack([shard, early]), "blk", [(s, s ^ (2 if s % 2 else 4)) for s in range(count)]
     )
-    mine = jnp.concatenate([jnp.stack([shard, early]), late], axis=0)
-    sibling = lax.ppermute(mine, "blk", [(s, s ^ 1) for s in range(count)])
+    twin_late = lax.ppermute(late, "blk", swap)
     twin = position ^ 1
     sources = [
-        (mine, [position, position ^ first, position ^ second, position ^ 6]),
-        (sibling, [twin, twin ^ second, twin ^ first, twin ^ 6]),
+        ([shard, twin_own, early, twin_early], [position, twin, position ^ first, twin ^ second]),
+        (
+            [late[0], late[1], twin_late[0], twin_late[1]],
+            [position ^ second, position ^ 6, twin ^ first, twin ^ 6],
+        ),
     ]
     full = jnp.zeros((count,) + shard.shape, shard.dtype)
     for pieces, where in sources:

time: 101 us -> 99.5 us (0.985)
  waiting for transfers between devices: 30.3 us -> 20.5 us
  local copies, waits for them, and re-layouts: 10.8 us -> 18.1 us
  matrix products: 4.29 us -> 6.47 us
  other arithmetic: 8.27 us -> 6.71 us
    ppermute x1, waiting for transfers between devices: 13.3 us -> 5.33 us  [gather_rows(): lax.ppermute(jnp.stack([shard, early]), 'blk', [(s, s ^ (2 if s % 2 else...]
    dynamic_update_slice x8, local copies, waits for them, and re-layouts: 4.53 us -> 9.84 us  [gather_rows(): full = lax.dynamic_update_slice(full, pieces[k][None], (at, 0, 0))]
    dot_general x1, matrix products: 2.33 us -> 4.52 us  [shards(): both = jnp.dot(receptor, full_both, preferred_element_type=jnp.float32)]
    broadcast_in_dim x1, local copies, waits for them, and re-layouts: 0.51 us -> 2.47 us  [gather_rows(): full = jnp.zeros((count,) + shard.shape, shard.dtype)]
    ppermute x1 -> x3, waiting for transfers between devices: 1.78 us -> 0.01 us  [the longest x1 0.01 us: gather_rows(): twin_own = lax.ppermute(shard, 'blk', swap)]
    concatenate x1 -> x0, other arithmetic: 1.55 us -> none  [gather_rows(): mine = jnp.concatenate([jnp.stack([shard, early]), late], axis=0)]
  transfers between devices with their start and end apart: 11 -> 13, of which waited for: 7 -> 6; matrix products, arithmetic and copies ran while one was open for 3% -> 13% of each run, Pallas kernels for 0% -> 0%
where the time goes in v10:
time: 99.5 us; the launch traced here: 97.5 us
  starting transfers between devices  26.1 us (26%)
  waiting for transfers between devices  20.5 us (21%)
  local copies, waits for them, and re-layouts  18.1 us (18%)
  Pallas kernels  14.4 us (14%)
  other arithmetic  6.71 us (7%)
  matrix products  6.47 us (7%)
  between operations  5.18 us (5%)
    ppermute x8, starting transfers between devices, send(): return lax.ppermute(value, axis, pairs)  22.9 us
    dynamic_update_slice x8, local copies, waits for them, and re-layouts, gather_rows(): full = lax.dynamic_update_slice(full, pieces[k][None], (at, 0, 0))  9.84 us
    ppermute x1, waiting for transfers between devices, gather_rows(): lax.ppermute(shard, 'blk', [(s, s ^ (4 if s % 2 else 2)) for s in range(c...  7.69 us
    pallas_call x1, Pallas kernels, back_fused(): pl.pallas_call(back_kernel, out_shape=jax.ShapeDtypeStruct((rows, width),...  7.63 us
    ppermute x8, waiting for transfers between devices, send(): return lax.ppermute(value, axis, pairs)  7.52 us
    pallas_call x1, Pallas kernels, pose_fused(): pl.pallas_call(pose_kernel, out_shape=(jax.ShapeDtypeStruct((1, pair_rows...  6.8 us
    ppermute x1, waiting for transfers between devices, gather_rows(): lax.ppermute(jnp.stack([shard, early]), 'blk', [(s, s ^ (2 if s % 2 else...  5.33 us
    dot_general x1, matrix products, shards(): both = jnp.dot(receptor, full_both, preferred_element_type=jnp.float32)  4.52 us
  transfers between devices with their start and end apart: 13, of which 6 were waited for; matrix products, arithmetic and copies ran while one was open for 13% of the time, Pallas kernels for 0%

profile of v10, /device:TPU:16, one launch (start us, length us, event | category | flops | bytes accessed | tf_op | source)
XLA Modules:
  0.0 97.5 jit_solution(17972607208988377792)
XLA Ops:
  0.6 0.0 copy-start
  0.7 1.1 %constant_dynamic-update-slice_fusion.1 = bf16[128,2048]{1,0:T(8,128)(2,1)S(1)} fusion(bf16[128,1024]{1,0:T(8,128)(2,1)} %param.12), kind=kLoop, calls=%fused_computation.35 | loop fusion | bytes 524288
  1.7 1.0 constant_dynamic-update-slice_fusion
  2.7 1.6 %collective-permute-start.1 = (bf16[128,2048]{1,0:T(8,128)(2,1)S(1)}, bf16[128,2048]{1,0:T(8,128)(2,1)S(1)}, u32[]{:S(2)}, u32[]{:S(2)}) collective-permute-start(bf16[128,2048]{1,0:T(8,128)(2,1)S(1)} %constant_dynamic-update-slice_fusion), channel_id=1, source_target_pairs={{0,2},{1,5},{2,0},{3,7},{4,6},{5,1},{6,4},{7,3},{8,10},{9,13},{10,... | collective-permute-start | bytes 1572872 | tf_op jit(solution)/shard_map/ppermute | solution.py:262
  4.2 0.0 collective-permute-start
  4.3 7.7 %collective-permute-done.1 = bf16[128,2048]{1,0:T(8,128)(2,1)S(1)} collective-permute-done((bf16[128,2048]{1,0:T(8,128)(2,1)S(1)}, bf16[128,2048]{1,0:T(8,128)(2,1)S(1)}, u32[]{:S(2)}, u32[]{:S(2)}) %collective-permute-start.1) | collective-permute-done | bytes 524320 | tf_op jit(solution)/shard_map/ppermute | solution.py:262
  11.9 0.1 pad_maximum_fusion
  12.0 1.6 %collective-permute-start.3 = (bf16[2,128,2048]{2,1,0:T(8,128)(2,1)S(1)}, bf16[2,128,2048]{2,1,0:T(8,128)(2,1)}, u32[]{:S(2)}, u32[]{:S(2)}) collective-permute-start(bf16[2,128,2048]{2,1,0:T(8,128)(2,1)S(1)} %pad_maximum_fusion), channel_id=1, source_target_pairs={{0,4},{1,3},{2,6},{3,1},{4,0},{5,7},{6,2},{7,5},{8,12},{9,11},{10,... | collective-permute-start | bytes 3145736 | tf_op jit(solution)/shard_map/ppermute | solution.py:264
  13.6 2.5 %broadcast_in_dim.72 = bf16[8,128,2048]{2,1,0:T(8,128)(2,1)} broadcast(bf16[]{:T(256)} %constant.196.clone.1), dimensions={} | broadcast | bytes 4194306 | tf_op jit(solution)/shard_map/broadcast_in_dim | solution.py:276
  16.1 0.8 constant_dynamic-update-slice_fusion.3
  16.9 0.6 fusion.10
  18.8 0.1 collective-permute-start.2
  18.9 0.0 collective-permute-done
  18.9 1.9 %bitcast_dynamic-update-slice_fusion.1 = bf16[8,128,2048]{2,1,0:T(8,128)(2,1)} fusion(bf16[8,128,2048]{2,1,0:T(8,128)(2,1)} %constant_dynamic-update-slice_fusion.3, s32[]{:T(128)S(6)} %select_n.200, bf16[128,2048]{1,0:T(8,128)(2,1)} %collective-permute-done), kind=kLoop, calls=%fused_computation.10 | loop fusion | bytes 1048580 | tf_op jit(solution)/shard_map/dynamic_update_slice | solution.py:279
  20.8 0.8 constant_dynamic-update-slice_fusion.2
  21.7 5.3 %collective-permute-done.3 = bf16[2,128,2048]{2,1,0:T(8,128)(2,1)} collective-permute-done((bf16[2,128,2048]{2,1,0:T(8,128)(2,1)S(1)}, bf16[2,128,2048]{2,1,0:T(8,128)(2,1)}, u32[]{:S(2)}, u32[]{:S(2)}) %collective-permute-start.3) | collective-permute-done | bytes 1048608 | tf_op jit(solution)/shard_map/ppermute | solution.py:264
  27.0 0.0 collective-permute-done.2
  27.0 0.8 bitcast_dynamic-update-slice_fusion
  27.9 1.9 %slice_dynamic-update-slice_fusion.3 = bf16[8,128,2048]{2,1,0:T(8,128)(2,1)} fusion(bf16[8,128,2048]{2,1,0:T(8,128)(2,1)} %bitcast_dynamic-update-slice_fusion, s32[]{:T(128)S(6)} %select_n.205, bf16[2,128,2048]{2,1,0:T(8,128)(2,1)} %collective-permute-done.3), kind=kLoop, calls=%fused_computation.8 | loop fusion | bytes 1048580 | tf_op jit(solution)/shard_map/dynamic_update_slice | solution.py:279
  29.7 1.9 %slice_dynamic-update-slice_fusion.2 = bf16[8,128,2048]{2,1,0:T(8,128)(2,1)} fusion(bf16[8,128,2048]{2,1,0:T(8,128)(2,1)} %slice_dynamic-update-slice_fusion.3, s32[]{:T(128)S(6)} %select_n.206, bf16[2,128,2048]{2,1,0:T(8,128)(2,1)} %collective-permute-done.3), kind=kLoop, calls=%fused_computation.7 | loop fusion | bytes 1048580 | tf_op jit(solution)/shard_map/dynamic_update_slice | solution.py:279
  31.6 0.9 slice_dynamic-update-slice_fusion.1
  32.5 0.8 slice_dynamic-update-slice_fusion
  33.3 4.5 %convolution_bitcast_fusion = f32[512,2048]{1,0:T(8,128)S(1)} fusion(bf16[512,1024]{1,0:T(8,128)(2,1)S(1)} %copy-done, bf16[1024,2048]{1,0:T(8,128)(2,1)} %bitcast.5.full_ref), kind=kOutput, calls=%fused_computation | convolution fusion | flops 2147483648 | bytes 9437184 | tf_op jit(solution)/shard_map/dot_general | solution.py:288
  37.8 0.2 slice.72.val_ref
  38.0 1.8 %convert_reduce_fusion = (f32[1024]{0:T(1024)S(1)}, bf16[512,1024]{1,0:T(8,128)(2,1)S(1)}, f32[512,1024]{1,0:T(8,128)}) fusion(f32[512,2048]{1,0:T(8,128)S(1)} %convolution_bitcast_fusion), kind=kLoop, calls=%fused_computation.2 | loop fusion | flops 3668992 | bytes 5246976 | tf_op jit(solution)/shard_map/reduce_sum | solution.py:37
  39.8 1.4 %copy.17 = bf16[512,1024]{0,1:T(8,128)(2,1)} copy(bf16[512,1024]{1,0:T(8,128)(2,1)S(1)} %get-tuple-element.87.feat_ref) | data formatting | bytes 2097152 | tf_op jit(solution)/shard_map/convert_element_type | solution.py:291
  41.3 1.3 %copy.16 = bf16[512,1024]{0,1:T(8,128)(2,1)} copy(bf16[512,1024]{1,0:T(8,128)(2,1)S(1)} %slice.72.val_ref) | data formatting | bytes 2097152 | tf_op jit(solution)/shard_map/slice | solution.py:290
  42.6 2.0 %fusion.11 = f32[16,64,64]{2,1,0:T(8,128)S(1)} fusion(bf16[512,16,64]{0,2,1:T(8,128)(2,1)} %bitcast.38, bf16[512,16,64]{0,2,1:T(8,128)(2,1)} %bitcast.37), kind=kOutput, calls=%fused_computation.39 | convolution fusion | flops 67108864 | bytes 2359296 | tf_op jit(solution)/shard_map/thd,the->dhe/dot_general | solution.py:34
  44.5 0.2 copy.20
  44.8 0.6 collective-permute-start.5
  47.8 2.9 %collective-permute-start.8 = (bf16[65,1024]{1,0:T(8,128)(2,1)S(1)}, bf16[65,1024]{1,0:T(8,128)(2,1)S(1)}, u32[]{:S(2)}, u32[]{:S(2)}) collective-permute-start(bf16[65,1024]{1,0:T(8,128)(2,1)S(1)} %get-tuple-element.93), channel_id=1, source_target_pairs={{1,4},{3,6},{5,8},{7,10},{9,12},{11,14},{13,16},{15,18},{17,20},{1... | collective-permute-start | bytes 399368 | tf_op jit(solution)/shard_map/ppermute | solution.py:58
  50.7 0.1 add_convert_fusion.3
  50.8 3.4 %collective-permute-start.6 = (bf16[65,1024]{1,0:T(8,128)(2,1)S(1)}, bf16[65,1024]{1,0:T(8,128)(2,1)S(1)}, u32[]{:S(2)}, u32[]{:S(2)}) collective-permute-start(bf16[65,1024]{1,0:T(8,128)(2,1)S(1)} %get-tuple-element.91), channel_id=1, source_target_pairs={{0,2},{1,3},{2,4},{3,5},{4,6},{5,7},{6,8},{7,9},{8,10},{9,11},{10,... | collective-permute-start | bytes 399368 | tf_op jit(solution)/shard_map/ppermute | solution.py:58
  54.2 4.2 %collective-permute-start.7 = (bf16[65,1024]{1,0:T(8,128)(2,1)S(1)}, bf16[65,1024]{1,0:T(8,128)(2,1)S(1)}, u32[]{:S(2)}, u32[]{:S(2)}) collective-permute-start(bf16[65,1024]{1,0:T(8,128)(2,1)S(1)} %get-tuple-element.92), channel_id=1, source_target_pairs={{2,0},{3,1},{4,2},{5,3},{6,4},{7,5},{8,6},{9,7},{10,8},{11,9},{12,... | collective-permute-start | bytes 399368 | tf_op jit(solution)/shard_map/ppermute | solution.py:58
  59.2 1.8 %collective-permute-done.6 = bf16[65,1024]{1,0:T(8,128)(2,1)S(1)} collective-permute-done((bf16[65,1024]{1,0:T(8,128)(2,1)S(1)}, bf16[65,1024]{1,0:T(8,128)(2,1)S(1)}, u32[]{:S(2)}, u32[]{:S(2)}) %collective-permute-start.6) | collective-permute-done | bytes 133152 | tf_op jit(solution)/shard_map/ppermute | solution.py:58
  61.0 1.7 %collective-permute-done.7 = bf16[65,1024]{1,0:T(8,128)(2,1)S(1)} collective-permute-done((bf16[65,1024]{1,0:T(8,128)(2,1)S(1)}, bf16[65,1024]{1,0:T(8,128)(2,1)S(1)}, u32[]{:S(2)}, u32[]{:S(2)}) %collective-permute-start.7) | collective-permute-done | bytes 133152 | tf_op jit(solution)/shard_map/ppermute | solution.py:58
  62.7 0.8 fusion.3.state_ref
  63.5 6.8 %shard_map.103 = (f32[1,256]{1,0:T(1,128)}, bf16[128,1024]{1,0:T(8,128)(2,1)}, f32[65,1024]{1,0:T(8,128)}) custom-call(bf16[128,1024]{1,0:T(8,128)(2,1)} %pose_ref.1, s32[2,256]{1,0:T(2,128)} %bitcast.46, f32[65,1024]{1,0:T(8,128)} %fusion.3.state_ref, bf16[1024,1024]{1,0:T(8,128)(2,1)} %query_ref.1, f32[1,1024]{1,0:T(1,128)} %bitcast.45), custom_call_target="tpu_custom_call" | custom-call | tf_op jit(solution)/shard_map/pallas_call | solution.py:206
  70.3 1.0 %convert_element_type.68 = bf16[65,1024]{1,0:T(8,128)(2,1)S(1)} convert(f32[65,1024]{1,0:T(8,128)} %get-tuple-element.8) | non-fusion elementwise | flops 66560 | bytes 399360 | tf_op jit(solution)/shard_map/convert_element_type | solution.py:74
  71.3 0.1 collective-permute-start.9
  71.4 3.8 %collective-permute-start.12 = (bf16[65,1024]{1,0:T(8,128)(2,1)S(1)}, bf16[65,1024]{1,0:T(8,128)(2,1)S(1)}, u32[]{:S(2)}, u32[]{:S(2)}) collective-permute-start(bf16[65,1024]{1,0:T(8,128)(2,1)S(1)} %select_convert_fusion.1), channel_id=1, source_target_pairs={{1,4},{3,6},{5,8},{7,10},{9,12},{11,14},{13,16},{15,18},{17,20},{1... | collective-permute-start | bytes 399368 | tf_op jit(solution)/shard_map/ppermute | solution.py:58
  75.2 1.1 %add_convert_fusion.1 = (bf16[65,1024]{1,0:T(8,128)(2,1)S(1)}, bf16[65,1024]{1,0:T(8,128)(2,1)S(1)}) fusion(f32[65,1024]{1,0:T(8,128)} %get-tuple-element.8, bf16[65,1024]{1,0:T(8,128)(2,1)S(1)} %collective-permute-done.9, pred[]{:T(512)S(6)} %and.108, pred[]{:T(512)S(6)} %eq.40, pred[]{:T(512)S(6)} %and.106, pred[]{:T(512)S(6)} %and.112, pred[]{:T(512)S(6)} %and.111), kind=kLoop, calls=%fused_computation.29 | loop fusion | flops 732160 | bytes 665605 | tf_op jit(solution)/shard_map/convert_element_type | solution.py:89
  76.3 4.3 %collective-permute-start.10 = (bf16[65,1024]{1,0:T(8,128)(2,1)S(1)}, bf16[65,1024]{1,0:T(8,128)(2,1)S(1)}, u32[]{:S(2)}, u32[]{:S(2)}) collective-permute-start(bf16[65,1024]{1,0:T(8,128)(2,1)S(1)} %get-tuple-element.89), channel_id=1, source_target_pairs={{0,2},{1,3},{2,4},{3,5},{4,6},{5,7},{6,8},{7,9},{8,10},{9,11},{10,... | collective-permute-start | bytes 399368 | tf_op jit(solution)/shard_map/ppermute | solution.py:58
  80.6 3.5 %collective-permute-start.11 = (bf16[65,1024]{1,0:T(8,128)(2,1)S(1)}, bf16[65,1024]{1,0:T(8,128)(2,1)S(1)}, u32[]{:S(2)}, u32[]{:S(2)}) collective-permute-start(bf16[65,1024]{1,0:T(8,128)(2,1)S(1)} %get-tuple-element.90), channel_id=1, source_target_pairs={{2,0},{3,1},{4,2},{5,3},{6,4},{7,5},{8,6},{9,7},{10,8},{11,9},{12,... | collective-permute-start | bytes 399368 | tf_op jit(solution)/shard_map/ppermute | solution.py:58
  84.1 1.9 %collective-permute-done.10 = bf16[65,1024]{1,0:T(8,128)(2,1)S(1)} collective-permute-done((bf16[65,1024]{1,0:T(8,128)(2,1)S(1)}, bf16[65,1024]{1,0:T(8,128)(2,1)S(1)}, u32[]{:S(2)}, u32[]{:S(2)}) %collective-permute-start.10) | collective-permute-done | bytes 133152 | tf_op jit(solution)/shard_map/ppermute | solution.py:58
  86.0 2.1 %collective-permute-done.11 = bf16[65,1024]{1,0:T(8,128)(2,1)S(1)} collective-permute-done((bf16[65,1024]{1,0:T(8,128)(2,1)S(1)}, bf16[65,1024]{1,0:T(8,128)(2,1)S(1)}, u32[]{:S(2)}, u32[]{:S(2)}) %collective-permute-start.11) | collective-permute-done | bytes 133152 | tf_op jit(solution)/shard_map/ppermute | solution.py:58
  88.1 1.7 %fusion.8.grad_ref = bf16[65,1024]{1,0:T(8,128)(2,1)} fusion(f32[65,1024]{1,0:T(8,128)} %get-tuple-element.8, bf16[65,1024]{1,0:T(8,128)(2,1)S(1)} %collective-permute-done.9, bf16[65,1024]{1,0:T(8,128)(2,1)S(1)} %collective-permute-done.12, bf16[65,1024]{1,0:T(8,128)(2,1)S(1)} %collective-permute-done.11, bf16[65,1024]{1,0:T(8,128)(2,1)S(1)} %collective-permute-done.10, ...), kind=kLoop, calls=%fused_computation.25 | loop fusion | flops 665600 | bytes 931841 | tf_op jit(solution)/shard_map/convert_element_type | solution.py:295
  89.9 7.6 %shard_map.104 = bf16[512,1024]{1,0:T(8,128)(2,1)} custom-call(bf16[512,1024]{1,0:T(8,128)(2,1)} %copy-done.2, bf16[512,1024]{1,0:T(8,128)(2,1)} %copy-done.1, f32[512,1024]{1,0:T(8,128)} %get-tuple-element.88.keys_ref, bf16[65,1024]{1,0:T(8,128)(2,1)} %fusion.8.grad_ref, bf16[1024,2048]{1,0:T(8,128)(2,1)} %bitcast.5.full_ref), custom_call_target="tpu_custom_call" | custom-call | tf_op jit(solution)/shard_map/pallas_call | solution.py:243
  (15 shorter events, 0.1 us)
Async XLA Ops:
  0.6 32.7 %copy-start = (bf16[512,1024]{1,0:T(8,128)(2,1)S(1)}, bf16[512,1024]{1,0:T(8,128)(2,1)}, u32[]{:S(2)}) copy-start(bf16[512,1024]{1,0:T(8,128)(2,1)} %param.8) | copy-start | bytes 3145732
  0.6 16.3 %copy-start.3 = (s32[32]{0:T(128)S(1)}, s32[32]{0:T(128)}, u32[]{:S(2)}) copy-start(s32[32]{0:T(128)} %param.11) | copy-start | bytes 388
  2.7 9.2 %collective-permute-start.1 = (bf16[128,2048]{1,0:T(8,128)(2,1)S(1)}, bf16[128,2048]{1,0:T(8,128)(2,1)S(1)}, u32[]{:S(2)}, u32[]{:S(2)}) collective-permute-start(bf16[128,2048]{1,0:T(8,128)(2,1)S(1)} %constant_dynamic-update-slice_fusion), channel_id=1, source_target_pairs={{0,2},{1,5},{2,0},{3,7},{4,6},{5,1},{6,4},{7,3},{8,10},{9,13},{10,... | collective-permute-start | bytes 1572872 | tf_op jit(solution)/shard_map/ppermute | solution.py:262
  4.2 14.7 %collective-permute-start = (bf16[128,2048]{1,0:T(8,128)(2,1)S(1)}, bf16[128,2048]{1,0:T(8,128)(2,1)}, u32[]{:S(2)}, u32[]{:S(2)}) collective-permute-start(bf16[128,2048]{1,0:T(8,128)(2,1)S(1)} %constant_dynamic-update-slice_fusion), channel_id=1, source_target_pairs={{0,1},{1,0},{2,3},{3,2},{4,5},{5,4},{6,7},{7,6},{8,9},{9,8},{10,11... | collective-permute-start | bytes 1572872 | tf_op jit(solution)/shard_map/ppermute | solution.py:261
  12.0 15.0 %collective-permute-start.3 = (bf16[2,128,2048]{2,1,0:T(8,128)(2,1)S(1)}, bf16[2,128,2048]{2,1,0:T(8,128)(2,1)}, u32[]{:S(2)}, u32[]{:S(2)}) collective-permute-start(bf16[2,128,2048]{2,1,0:T(8,128)(2,1)S(1)} %pad_maximum_fusion), channel_id=1, source_target_pairs={{0,4},{1,3},{2,6},{3,1},{4,0},{5,7},{6,2},{7,5},{8,12},{9,11},{10,... | collective-permute-start | bytes 3145736 | tf_op jit(solution)/shard_map/ppermute | solution.py:264
  18.8 8.2 %collective-permute-start.2 = (bf16[128,2048]{1,0:T(8,128)(2,1)S(1)}, bf16[128,2048]{1,0:T(8,128)(2,1)S(1)}, u32[]{:S(2)}, u32[]{:S(2)}) collective-permute-start(bf16[128,2048]{1,0:T(8,128)(2,1)S(1)} %collective-permute-done.1), channel_id=1, source_target_pairs={{0,1},{1,0},{2,3},{3,2},{4,5},{5,4},{6,7},{7,6},{8,9},{9,8},{10,11... | collective-permute-start | bytes 1572872 | tf_op jit(solution)/shard_map/ppermute | solution.py:263
  27.0 4.6 %collective-permute-start.4 = (bf16[2,128,2048]{2,1,0:T(8,128)(2,1)}, bf16[2,128,2048]{2,1,0:T(8,128)(2,1)S(1)}, u32[]{:S(2)}, u32[]{:S(2)}) collective-permute-start(bf16[2,128,2048]{2,1,0:T(8,128)(2,1)} %collective-permute-done.3), channel_id=1, source_target_pairs={{0,1},{1,0},{2,3},{3,2},{4,5},{5,4},{6,7},{7,6},{8,9},{9,8},{10,11... | collective-permute-start | bytes 3145736 | tf_op jit(solution)/shard_map/ppermute | solution.py:267
  38.0 4.6 %copy-start.1 = (bf16[512,1024]{1,0:T(8,128)(2,1)}, bf16[512,1024]{1,0:T(8,128)(2,1)S(1)}, u32[]{:S(2)}) copy-start(bf16[512,1024]{1,0:T(8,128)(2,1)S(1)} %slice.72.val_ref) | copy-start | bytes 3145732
  39.8 11.0 %copy-start.2 = (bf16[512,1024]{1,0:T(8,128)(2,1)}, bf16[512,1024]{1,0:T(8,128)(2,1)S(1)}, u32[]{:S(2)}) copy-start(bf16[512,1024]{1,0:T(8,128)(2,1)S(1)} %get-tuple-element.87.feat_ref) | copy-start | bytes 3145732
  44.8 5.9 %collective-permute-start.5 = (bf16[65,1024]{1,0:T(8,128)(2,1)S(1)}, bf16[65,1024]{1,0:T(8,128)(2,1)S(1)}, u32[]{:S(2)}, u32[]{:S(2)}) collective-permute-start(bf16[65,1024]{1,0:T(8,128)(2,1)S(1)} %get-tuple-element.94), channel_id=1, source_target_pairs={{0,1},{1,0},{2,3},{3,2},{4,5},{5,4},{6,7},{7,6},{8,9},{9,8},{10,11... | collective-permute-start | bytes 399368 | tf_op jit(solution)/shard_map/ppermute | solution.py:58
  47.8 11.4 %collective-permute-start.8 = (bf16[65,1024]{1,0:T(8,128)(2,1)S(1)}, bf16[65,1024]{1,0:T(8,128)(2,1)S(1)}, u32[]{:S(2)}, u32[]{:S(2)}) collective-permute-start(bf16[65,1024]{1,0:T(8,128)(2,1)S(1)} %get-tuple-element.93), channel_id=1, source_target_pairs={{1,4},{3,6},{5,8},{7,10},{9,12},{11,14},{13,16},{15,18},{17,20},{1... | collective-permute-start | bytes 399368 | tf_op jit(solution)/shard_map/ppermute | solution.py:58
  50.8 10.1 %collective-permute-start.6 = (bf16[65,1024]{1,0:T(8,128)(2,1)S(1)}, bf16[65,1024]{1,0:T(8,128)(2,1)S(1)}, u32[]{:S(2)}, u32[]{:S(2)}) collective-permute-start(bf16[65,1024]{1,0:T(8,128)(2,1)S(1)} %get-tuple-element.91), channel_id=1, source_target_pairs={{0,2},{1,3},{2,4},{3,5},{4,6},{5,7},{6,8},{7,9},{8,10},{9,11},{10,... | collective-permute-start | bytes 399368 | tf_op jit(solution)/shard_map/ppermute | solution.py:58
  54.2 8.4 %collective-permute-start.7 = (bf16[65,1024]{1,0:T(8,128)(2,1)S(1)}, bf16[65,1024]{1,0:T(8,128)(2,1)S(1)}, u32[]{:S(2)}, u32[]{:S(2)}) collective-permute-start(bf16[65,1024]{1,0:T(8,128)(2,1)S(1)} %get-tuple-element.92), channel_id=1, source_target_pairs={{2,0},{3,1},{4,2},{5,3},{6,4},{7,5},{8,6},{9,7},{10,8},{11,9},{12,... | collective-permute-start | bytes 399368 | tf_op jit(solution)/shard_map/ppermute | solution.py:58
  71.3 3.9 %collective-permute-start.9 = (bf16[65,1024]{1,0:T(8,128)(2,1)S(1)}, bf16[65,1024]{1,0:T(8,128)(2,1)S(1)}, u32[]{:S(2)}, u32[]{:S(2)}) collective-permute-start(bf16[65,1024]{1,0:T(8,128)(2,1)S(1)} %convert_element_type.68), channel_id=1, source_target_pairs={{0,1},{1,0},{2,3},{3,2},{4,5},{5,4},{6,7},{7,6},{8,9},{9,8},{10,11... | collective-permute-start | bytes 399368 | tf_op jit(solution)/shard_map/ppermute | solution.py:58
  71.4 12.7 %collective-permute-start.12 = (bf16[65,1024]{1,0:T(8,128)(2,1)S(1)}, bf16[65,1024]{1,0:T(8,128)(2,1)S(1)}, u32[]{:S(2)}, u32[]{:S(2)}) collective-permute-start(bf16[65,1024]{1,0:T(8,128)(2,1)S(1)} %select_convert_fusion.1), channel_id=1, source_target_pairs={{1,4},{3,6},{5,8},{7,10},{9,12},{11,14},{13,16},{15,18},{17,20},{1... | collective-permute-start | bytes 399368 | tf_op jit(solution)/shard_map/ppermute | solution.py:58
  76.3 9.7 %collective-permute-start.10 = (bf16[65,1024]{1,0:T(8,128)(2,1)S(1)}, bf16[65,1024]{1,0:T(8,128)(2,1)S(1)}, u32[]{:S(2)}, u32[]{:S(2)}) collective-permute-start(bf16[65,1024]{1,0:T(8,128)(2,1)S(1)} %get-tuple-element.89), channel_id=1, source_target_pairs={{0,2},{1,3},{2,4},{3,5},{4,6},{5,7},{6,8},{7,9},{8,10},{9,11},{10,... | collective-permute-start | bytes 399368 | tf_op jit(solution)/shard_map/ppermute | solution.py:58
  80.6 7.5 %collective-permute-start.11 = (bf16[65,1024]{1,0:T(8,128)(2,1)S(1)}, bf16[65,1024]{1,0:T(8,128)(2,1)S(1)}, u32[]{:S(2)}, u32[]{:S(2)}) collective-permute-start(bf16[65,1024]{1,0:T(8,128)(2,1)S(1)} %get-tuple-element.90), channel_id=1, source_target_pairs={{2,0},{3,1},{4,2},{5,3},{6,4},{7,5},{8,6},{9,7},{10,8},{11,9},{12,... | collective-permute-start | bytes 399368 | tf_op jit(solution)/shard_map/ppermute | solution.py:58

commit v11 on v10

--- a/solution.py
+++ b/solution.py
@@ -251,7 +251,7 @@
 def gather_rows(shard):
     count = lax.axis_size("blk")
     if count != 8:
-        return lax.all_gather(shard, "blk", axis=0, tiled=True)
+        return lax.all_gather(shard, "blk", axis=0, tiled=True), None
     position = lax.axis_index("blk")
     rows = shard.shape[0]
     odd = position % 2
@@ -268,24 +268,36 @@
     twin = position ^ 1
     sources = [
         ([shard, twin_own, early, twin_early], [position, twin, position ^ first, twin ^ second]),
-        (
-            [late[0], late[1], twin_late[0], twin_late[1]],
-            [position ^ second, position ^ 6, twin ^ first, twin ^ 6],
-        ),
+        ([late[0], late[1]], [position ^ second, position ^ 6]),
     ]
     full = jnp.zeros((count,) + shard.shape, shard.dtype)
     for pieces, where in sources:
         for k, at in enumerate(where):
             full = lax.dynamic_update_slice(full, pieces[k][None], (at, 0, 0))
-    return full.reshape(count * rows, shard.shape[1])
+    return full, (twin_late, [twin ^ first, twin ^ 6])
 
 
 def shards(receptor, poses, pairs, block_complex, w_key, w_value, w_query, score_weight):
     rows = receptor.shape[0]
     width = receptor.shape[1]
-    contract = (((1,), (1,)), ((), ()))
-    full_both = gather_rows(jnp.concatenate([w_key, w_value], axis=1))
-    both = jnp.dot(receptor, full_both, preferred_element_type=jnp.float32)
+    full_both, rest = gather_rows(jnp.concatenate([w_key, w_value], axis=1))
+    if rest is None:
+        both = jnp.dot(receptor, full_both, preferred_element_type=jnp.float32)
+    else:
+        pieces, where = rest
+        part = full_both.shape[1]
+        both = jnp.dot(
+            receptor, full_both.reshape(-1, full_both.shape[2]), preferred_element_type=jnp.float32
+        )
+        picked = jnp.concatenate(
+            [lax.dynamic_slice_in_dim(receptor, at * part, part, axis=1) for at in where], axis=1
+        )
+        both = both + jnp.dot(
+            picked, pieces.reshape(-1, pieces.shape[2]), preferred_element_type=jnp.float32
+        )
+        for k, at in enumerate(where):
+            full_both = lax.dynamic_update_slice(full_both, pieces[k][None], (at, 0, 0))
+        full_both = full_both.reshape(-1, full_both.shape[2])
     keys = both[:, :width]
     values = both[:, width:]
     key_feat = features(keys).astype(jnp.bfloat16)

time: 99.5 us -> 95.9 us (0.964)
  local copies, waits for them, and re-layouts: 18.1 us -> 15 us
    ppermute x1, waiting for transfers between devices: 7.69 us -> 2.29 us  [gather_rows(): lax.ppermute(shard, 'blk', [(s, s ^ (4 if s % 2 else 2)) for s in range(c...]
    ppermute x1, waiting for transfers between devices: 5.33 us -> 10.5 us  [gather_rows(): lax.ppermute(jnp.stack([shard, early]), 'blk', [(s, s ^ (2 if s % 2 else...]
    dynamic_update_slice x8 -> x6, local copies, waits for them, and re-layouts: 9.84 us -> 4.97 us  [gather_rows(): full = lax.dynamic_update_slice(full, pieces[k][None], (at, 0, 0))]
    dynamic_update_slice x0 -> x2, local copies, waits for them, and re-layouts: none -> 1.68 us  [shards(): full_both = lax.dynamic_update_slice(full_both, pieces[k][None], (at, 0, 0))]
    ppermute x8, waiting for transfers between devices: 7.52 us -> 6.5 us  [send(): return lax.ppermute(value, axis, pairs)]
    dot_general x1 -> x2, matrix products: 4.52 us -> 5.27 us  [the longest x1 4.52 us: shards(): jnp.dot(receptor, full_both.reshape(-1, full_both.shape[2]), preferred_el...]
  transfers between devices with their start and end apart: 13 -> 13, of which waited for: 6 -> 7; matrix products, arithmetic and copies ran while one was open for 13% -> 17% of each run, Pallas kernels for 0% -> 0%
where the time goes in v11:
time: 95.9 us; the launch traced here: 94.2 us
  starting transfers between devices  26 us (27%)
  waiting for transfers between devices  19.6 us (20%)
  local copies, waits for them, and re-layouts  15 us (16%)
  Pallas kernels  14.4 us (15%)
  matrix products  7.22 us (8%)
  other arithmetic  6.7 us (7%)
  between operations  5.29 us (6%)
    ppermute x8, starting transfers between devices, send(): return lax.ppermute(value, axis, pairs)  22.9 us
    ppermute x1, waiting for transfers between devices, gather_rows(): lax.ppermute(jnp.stack([shard, early]), 'blk', [(s, s ^ (2 if s % 2 else...  10.5 us
    pallas_call x1, Pallas kernels, back_fused(): pl.pallas_call(back_kernel, out_shape=jax.ShapeDtypeStruct((rows, width),...  7.63 us
    pallas_call x1, Pallas kernels, pose_fused(): pl.pallas_call(pose_kernel, out_shape=(jax.ShapeDtypeStruct((1, pair_rows...  6.79 us
    ppermute x8, waiting for transfers between devices, send(): return lax.ppermute(value, axis, pairs)  6.5 us
    dynamic_update_slice x6, local copies, waits for them, and re-layouts, gather_rows(): full = lax.dynamic_update_slice(full, pieces[k][None], (at, 0, 0))  4.97 us
    dot_general x1, matrix products, shards(): jnp.dot(receptor, full_both.reshape(-1, full_both.shape[2]), preferred_el...  4.52 us
    broadcast_in_dim x1, local copies, waits for them, and re-layouts, gather_rows(): full = jnp.zeros((count,) + shard.shape, shard.dtype)  2.47 us
  transfers between devices with their start and end apart: 13, of which 7 were waited for; matrix products, arithmetic and copies ran while one was open for 17% of the time, Pallas kernels for 0%

profile of v11, /device:TPU:16, one launch (start us, length us, event | category | flops | bytes accessed | tf_op | source)
XLA Modules:
  0.0 94.2 jit_solution(10402155445367310610)
XLA Ops:
  0.7 1.1 %constant_dynamic-update-slice_fusion.1 = bf16[128,2048]{1,0:T(8,128)(2,1)S(1)} fusion(bf16[128,1024]{1,0:T(8,128)(2,1)} %param.12), kind=kLoop, calls=%fused_computation.38 | loop fusion | bytes 524288
  1.7 1.0 %constant_dynamic-update-slice_fusion = bf16[128,2048]{1,0:T(8,128)(2,1)S(1)} fusion(bf16[128,2048]{1,0:T(8,128)(2,1)S(1)} %constant_dynamic-update-slice_fusion.1, bf16[128,1024]{1,0:T(8,128)(2,1)} %param.13), kind=kLoop, calls=%fused_computation.37 | loop fusion | bytes 524288 | tf_op jit(solution)/shard_map/concatenate | solution.py:283
  2.7 1.6 %collective-permute-start.1 = (bf16[128,2048]{1,0:T(8,128)(2,1)S(1)}, bf16[128,2048]{1,0:T(8,128)(2,1)S(1)}, u32[]{:S(2)}, u32[]{:S(2)}) collective-permute-start(bf16[128,2048]{1,0:T(8,128)(2,1)S(1)} %constant_dynamic-update-slice_fusion), channel_id=1, source_target_pairs={{0,2},{1,5},{2,0},{3,7},{4,6},{5,1},{6,4},{7,3},{8,10},{9,13},{10,... | collective-permute-start | bytes 1572872 | tf_op jit(solution)/shard_map/ppermute | solution.py:262
  4.2 2.5 %broadcast_in_dim.72 = bf16[8,128,2048]{2,1,0:T(8,128)(2,1)} broadcast(bf16[]{:T(256)} %constant.198.clone.1), dimensions={} | broadcast | bytes 4194306 | tf_op jit(solution)/shard_map/broadcast_in_dim | solution.py:273
  6.7 0.8 constant_dynamic-update-slice_fusion.3
  7.6 0.7 fusion.14
  9.6 0.1 constant_dynamic-slice_fusion.1
  9.6 2.3 %collective-permute-done.1 = bf16[128,2048]{1,0:T(8,128)(2,1)S(1)} collective-permute-done((bf16[128,2048]{1,0:T(8,128)(2,1)S(1)}, bf16[128,2048]{1,0:T(8,128)(2,1)S(1)}, u32[]{:S(2)}, u32[]{:S(2)}) %collective-permute-start.1) | collective-permute-done | bytes 524320 | tf_op jit(solution)/shard_map/ppermute | solution.py:262
  11.9 0.1 pad_maximum_fusion
  12.0 1.6 %collective-permute-start.3 = (bf16[2,128,2048]{2,1,0:T(8,128)(2,1)S(1)}, bf16[2,128,2048]{2,1,0:T(8,128)(2,1)S(1)}, u32[]{:S(2)}, u32[]{:S(2)}) collective-permute-start(bf16[2,128,2048]{2,1,0:T(8,128)(2,1)S(1)} %pad_maximum_fusion), channel_id=1, source_target_pairs={{0,4},{1,3},{2,6},{3,1},{4,0},{5,7},{6,2},{7,5},{8,12},{9,11},{10,... | collective-permute-start | bytes 3145736 | tf_op jit(solution)/shard_map/ppermute | solution.py:264
  13.6 0.8 bitcast_dynamic-update-slice_fusion.1
  14.4 0.8 constant_dynamic-update-slice_fusion.2
  15.3 0.2 collective-permute-done.2
  15.5 0.8 bitcast_dynamic-update-slice_fusion
  16.4 10.5 %collective-permute-done.3 = bf16[2,128,2048]{2,1,0:T(8,128)(2,1)S(1)} collective-permute-done((bf16[2,128,2048]{2,1,0:T(8,128)(2,1)S(1)}, bf16[2,128,2048]{2,1,0:T(8,128)(2,1)S(1)}, u32[]{:S(2)}, u32[]{:S(2)}) %collective-permute-start.3) | collective-permute-done | bytes 1048608 | tf_op jit(solution)/shard_map/ppermute | solution.py:264
  26.9 0.0 collective-permute-start.4
  26.9 0.8 slice_dynamic-update-slice_fusion.3
  27.7 0.8 slice_dynamic-update-slice_fusion.2
  28.5 4.5 %fusion.16 = f32[2048,512]{0,1:T(8,128)S(1)} fusion(bf16[512,1024]{1,0:T(8,128)(2,1)S(1)} %copy-done.2, bf16[1024,2048]{1,0:T(8,128)(2,1)} %bitcast.5), kind=kOutput, calls=%fused_computation.46 | convolution fusion | flops 2147483648 | bytes 9437184 | tf_op jit(solution)/shard_map/dot_general | solution.py:289
  33.1 0.8 bitcast_add_fusion
  33.8 0.2 slice.72.val_ref
  34.0 1.8 %convert_reduce_fusion = (f32[1024]{0:T(1024)S(1)}, bf16[512,1024]{1,0:T(8,128)(2,1)S(1)}, f32[512,1024]{1,0:T(8,128)}) fusion(f32[512,2048]{1,0:T(8,128)S(1)} %bitcast_add_fusion), kind=kLoop, calls=%fused_computation.2 | loop fusion | flops 3668992 | bytes 5246976 | tf_op jit(solution)/shard_map/reduce_sum | solution.py:37
  35.9 1.4 %copy.17 = bf16[512,1024]{0,1:T(8,128)(2,1)} copy(bf16[512,1024]{1,0:T(8,128)(2,1)S(1)} %get-tuple-element.87.feat_ref) | data formatting | bytes 2097152 | tf_op jit(solution)/shard_map/convert_element_type | solution.py:303
  37.3 1.3 %copy.16 = bf16[512,1024]{0,1:T(8,128)(2,1)} copy(bf16[512,1024]{1,0:T(8,128)(2,1)S(1)} %slice.72.val_ref) | data formatting | bytes 2097152 | tf_op jit(solution)/shard_map/slice | solution.py:302
  38.6 2.0 %fusion.15 = f32[16,64,64]{2,1,0:T(8,128)S(1)} fusion(bf16[512,16,64]{0,2,1:T(8,128)(2,1)} %bitcast.42, bf16[512,16,64]{0,2,1:T(8,128)(2,1)} %bitcast.41), kind=kOutput, calls=%fused_computation.45 | convolution fusion | flops 67108864 | bytes 2359296 | tf_op jit(solution)/shard_map/thd,the->dhe/dot_general | solution.py:34
  40.5 0.2 copy.20
  40.8 0.6 collective-permute-start.5
  44.5 2.9 %collective-permute-start.8 = (bf16[65,1024]{1,0:T(8,128)(2,1)S(1)}, bf16[65,1024]{1,0:T(8,128)(2,1)S(1)}, u32[]{:S(2)}, u32[]{:S(2)}) collective-permute-start(bf16[65,1024]{1,0:T(8,128)(2,1)S(1)} %get-tuple-element.95), channel_id=1, source_target_pairs={{1,4},{3,6},{5,8},{7,10},{9,12},{11,14},{13,16},{15,18},{17,20},{1... | collective-permute-start | bytes 399368 | tf_op jit(solution)/shard_map/ppermute | solution.py:58
  47.5 0.1 add_convert_fusion.3
  47.6 3.4 %collective-permute-start.6 = (bf16[65,1024]{1,0:T(8,128)(2,1)S(1)}, bf16[65,1024]{1,0:T(8,128)(2,1)S(1)}, u32[]{:S(2)}, u32[]{:S(2)}) collective-permute-start(bf16[65,1024]{1,0:T(8,128)(2,1)S(1)} %get-tuple-element.93), channel_id=1, source_target_pairs={{0,2},{1,3},{2,4},{3,5},{4,6},{5,7},{6,8},{7,9},{8,10},{9,11},{10,... | collective-permute-start | bytes 399368 | tf_op jit(solution)/shard_map/ppermute | solution.py:58
  51.0 4.3 %collective-permute-start.7 = (bf16[65,1024]{1,0:T(8,128)(2,1)S(1)}, bf16[65,1024]{1,0:T(8,128)(2,1)S(1)}, u32[]{:S(2)}, u32[]{:S(2)}) collective-permute-start(bf16[65,1024]{1,0:T(8,128)(2,1)S(1)} %get-tuple-element.94), channel_id=1, source_target_pairs={{2,0},{3,1},{4,2},{5,3},{6,4},{7,5},{8,6},{9,7},{10,8},{11,9},{12,... | collective-permute-start | bytes 399368 | tf_op jit(solution)/shard_map/ppermute | solution.py:58
  55.2 0.9 slice_dynamic-update-slice_fusion.1
  56.1 0.0 collective-permute-done.8
  56.1 1.6 %collective-permute-done.6 = bf16[65,1024]{1,0:T(8,128)(2,1)S(1)} collective-permute-done((bf16[65,1024]{1,0:T(8,128)(2,1)S(1)}, bf16[65,1024]{1,0:T(8,128)(2,1)S(1)}, u32[]{:S(2)}, u32[]{:S(2)}) %collective-permute-start.6) | collective-permute-done | bytes 133152 | tf_op jit(solution)/shard_map/ppermute | solution.py:58
  57.7 1.7 %collective-permute-done.7 = bf16[65,1024]{1,0:T(8,128)(2,1)S(1)} collective-permute-done((bf16[65,1024]{1,0:T(8,128)(2,1)S(1)}, bf16[65,1024]{1,0:T(8,128)(2,1)S(1)}, u32[]{:S(2)}, u32[]{:S(2)}) %collective-permute-start.7) | collective-permute-done | bytes 133152 | tf_op jit(solution)/shard_map/ppermute | solution.py:58
  59.4 0.8 fusion.3.state_ref
  60.2 6.8 %shard_map.103 = (f32[1,256]{1,0:T(1,128)}, bf16[128,1024]{1,0:T(8,128)(2,1)}, f32[65,1024]{1,0:T(8,128)}) custom-call(bf16[128,1024]{1,0:T(8,128)(2,1)} %pose_ref.1, s32[2,256]{1,0:T(2,128)} %bitcast.50, f32[65,1024]{1,0:T(8,128)} %fusion.3.state_ref, bf16[1024,1024]{1,0:T(8,128)(2,1)} %query_ref.1, f32[1,1024]{1,0:T(1,128)} %bitcast.49), custom_call_target="tpu_custom_call" | custom-call | tf_op jit(solution)/shard_map/pallas_call | solution.py:206
  67.0 1.0 %convert_element_type.68 = bf16[65,1024]{1,0:T(8,128)(2,1)S(1)} convert(f32[65,1024]{1,0:T(8,128)} %get-tuple-element.8) | non-fusion elementwise | flops 66560 | bytes 399360 | tf_op jit(solution)/shard_map/convert_element_type | solution.py:74
  68.0 0.1 collective-permute-start.9
  68.1 3.8 %collective-permute-start.12 = (bf16[65,1024]{1,0:T(8,128)(2,1)S(1)}, bf16[65,1024]{1,0:T(8,128)(2,1)S(1)}, u32[]{:S(2)}, u32[]{:S(2)}) collective-permute-start(bf16[65,1024]{1,0:T(8,128)(2,1)S(1)} %select_convert_fusion.1), channel_id=1, source_target_pairs={{1,4},{3,6},{5,8},{7,10},{9,12},{11,14},{13,16},{15,18},{17,20},{1... | collective-permute-start | bytes 399368 | tf_op jit(solution)/shard_map/ppermute | solution.py:58
  71.9 1.1 %add_convert_fusion.1 = (bf16[65,1024]{1,0:T(8,128)(2,1)S(1)}, bf16[65,1024]{1,0:T(8,128)(2,1)S(1)}) fusion(f32[65,1024]{1,0:T(8,128)} %get-tuple-element.8, bf16[65,1024]{1,0:T(8,128)(2,1)S(1)} %collective-permute-done.9, pred[]{:T(512)S(6)} %and.108, pred[]{:T(512)S(6)} %eq.40, pred[]{:T(512)S(6)} %and.106, pred[]{:T(512)S(6)} %and.112, pred[]{:T(512)S(6)} %and.111), kind=kLoop, calls=%fused_computation.29 | loop fusion | flops 732160 | bytes 665605 | tf_op jit(solution)/shard_map/convert_element_type | solution.py:89
  73.0 4.3 %collective-permute-start.10 = (bf16[65,1024]{1,0:T(8,128)(2,1)S(1)}, bf16[65,1024]{1,0:T(8,128)(2,1)S(1)}, u32[]{:S(2)}, u32[]{:S(2)}) collective-permute-start(bf16[65,1024]{1,0:T(8,128)(2,1)S(1)} %get-tuple-element.91), channel_id=1, source_target_pairs={{0,2},{1,3},{2,4},{3,5},{4,6},{5,7},{6,8},{7,9},{8,10},{9,11},{10,... | collective-permute-start | bytes 399368 | tf_op jit(solution)/shard_map/ppermute | solution.py:58
  77.4 3.5 %collective-permute-start.11 = (bf16[65,1024]{1,0:T(8,128)(2,1)S(1)}, bf16[65,1024]{1,0:T(8,128)(2,1)S(1)}, u32[]{:S(2)}, u32[]{:S(2)}) collective-permute-start(bf16[65,1024]{1,0:T(8,128)(2,1)S(1)} %get-tuple-element.92), channel_id=1, source_target_pairs={{2,0},{3,1},{4,2},{5,3},{6,4},{7,5},{8,6},{9,7},{10,8},{11,9},{12,... | collective-permute-start | bytes 399368 | tf_op jit(solution)/shard_map/ppermute | solution.py:58
  80.8 0.8 slice_dynamic-update-slice_fusion
  81.7 1.1 %collective-permute-done.10 = bf16[65,1024]{1,0:T(8,128)(2,1)S(1)} collective-permute-done((bf16[65,1024]{1,0:T(8,128)(2,1)S(1)}, bf16[65,1024]{1,0:T(8,128)(2,1)S(1)}, u32[]{:S(2)}, u32[]{:S(2)}) %collective-permute-start.10) | collective-permute-done | bytes 133152 | tf_op jit(solution)/shard_map/ppermute | solution.py:58
  82.8 2.1 %collective-permute-done.11 = bf16[65,1024]{1,0:T(8,128)(2,1)S(1)} collective-permute-done((bf16[65,1024]{1,0:T(8,128)(2,1)S(1)}, bf16[65,1024]{1,0:T(8,128)(2,1)S(1)}, u32[]{:S(2)}, u32[]{:S(2)}) %collective-permute-start.11) | collective-permute-done | bytes 133152 | tf_op jit(solution)/shard_map/ppermute | solution.py:58
  84.9 1.7 %fusion.8.grad_ref = bf16[65,1024]{1,0:T(8,128)(2,1)} fusion(f32[65,1024]{1,0:T(8,128)} %get-tuple-element.8, bf16[65,1024]{1,0:T(8,128)(2,1)S(1)} %collective-permute-done.9, bf16[65,1024]{1,0:T(8,128)(2,1)S(1)} %collective-permute-done.12, bf16[65,1024]{1,0:T(8,128)(2,1)S(1)} %collective-permute-done.11, bf16[65,1024]{1,0:T(8,128)(2,1)S(1)} %collective-permute-done.10, ...), kind=kLoop, calls=%fused_computation.25 | loop fusion | flops 665600 | bytes 931841 | tf_op jit(solution)/shard_map/convert_element_type | solution.py:307
  86.6 7.6 %shard_map.104 = bf16[512,1024]{1,0:T(8,128)(2,1)} custom-call(bf16[512,1024]{1,0:T(8,128)(2,1)} %copy-done.1, bf16[512,1024]{1,0:T(8,128)(2,1)} %copy-done, f32[512,1024]{1,0:T(8,128)} %get-tuple-element.88.keys_ref, bf16[65,1024]{1,0:T(8,128)(2,1)} %fusion.8.grad_ref, bf16[1024,2048]{1,0:T(8,128)(2,1)} %bitcast.28.full_ref), custom_call_target="tpu_custom_call" | custom-call | tf_op jit(solution)/shard_map/pallas_call | solution.py:243
  (17 shorter events, 0.1 us)
Async XLA Ops:
  0.6 6.9 %copy-start.3 = (s32[32]{0:T(128)S(1)}, s32[32]{0:T(128)}, u32[]{:S(2)}) copy-start(s32[32]{0:T(128)} %param.11) | copy-start | bytes 388
  0.6 8.9 %copy-start.2 = (bf16[512,1024]{1,0:T(8,128)(2,1)S(1)}, bf16[512,1024]{1,0:T(8,128)(2,1)}, u32[]{:S(2)}) copy-start(bf16[512,1024]{1,0:T(8,128)(2,1)} %param.8) | copy-start | bytes 3145732
  2.7 9.2 %collective-permute-start.1 = (bf16[128,2048]{1,0:T(8,128)(2,1)S(1)}, bf16[128,2048]{1,0:T(8,128)(2,1)S(1)}, u32[]{:S(2)}, u32[]{:S(2)}) collective-permute-start(bf16[128,2048]{1,0:T(8,128)(2,1)S(1)} %constant_dynamic-update-slice_fusion), channel_id=1, source_target_pairs={{0,2},{1,5},{2,0},{3,7},{4,6},{5,1},{6,4},{7,3},{8,10},{9,13},{10,... | collective-permute-start | bytes 1572872 | tf_op jit(solution)/shard_map/ppermute | solution.py:262
  4.2 9.4 %collective-permute-start = (bf16[128,2048]{1,0:T(8,128)(2,1)S(1)}, bf16[128,2048]{1,0:T(8,128)(2,1)S(1)}, u32[]{:S(2)}, u32[]{:S(2)}) collective-permute-start(bf16[128,2048]{1,0:T(8,128)(2,1)S(1)} %constant_dynamic-update-slice_fusion), channel_id=1, source_target_pairs={{0,1},{1,0},{2,3},{3,2},{4,5},{5,4},{6,7},{7,6},{8,9},{9,8},{10,11... | collective-permute-start | bytes 1572872 | tf_op jit(solution)/shard_map/ppermute | solution.py:261
  12.0 14.9 %collective-permute-start.3 = (bf16[2,128,2048]{2,1,0:T(8,128)(2,1)S(1)}, bf16[2,128,2048]{2,1,0:T(8,128)(2,1)S(1)}, u32[]{:S(2)}, u32[]{:S(2)}) collective-permute-start(bf16[2,128,2048]{2,1,0:T(8,128)(2,1)S(1)} %pad_maximum_fusion), channel_id=1, source_target_pairs={{0,4},{1,3},{2,6},{3,1},{4,0},{5,7},{6,2},{7,5},{8,12},{9,11},{10,... | collective-permute-start | bytes 3145736 | tf_op jit(solution)/shard_map/ppermute | solution.py:264
  13.6 1.9 %collective-permute-start.2 = (bf16[128,2048]{1,0:T(8,128)(2,1)S(1)}, bf16[128,2048]{1,0:T(8,128)(2,1)S(1)}, u32[]{:S(2)}, u32[]{:S(2)}) collective-permute-start(bf16[128,2048]{1,0:T(8,128)(2,1)S(1)} %collective-permute-done.1), channel_id=1, source_target_pairs={{0,1},{1,0},{2,3},{3,2},{4,5},{5,4},{6,7},{7,6},{8,9},{9,8},{10,11... | collective-permute-start | bytes 1572872 | tf_op jit(solution)/shard_map/ppermute | solution.py:263
  26.9 6.2 %collective-permute-start.4 = (bf16[2,128,2048]{2,1,0:T(8,128)(2,1)S(1)}, bf16[2,128,2048]{2,1,0:T(8,128)(2,1)S(1)}, u32[]{:S(2)}, u32[]{:S(2)}) collective-permute-start(bf16[2,128,2048]{2,1,0:T(8,128)(2,1)S(1)} %collective-permute-done.3), channel_id=1, source_target_pairs={{0,1},{1,0},{2,3},{3,2},{4,5},{5,4},{6,7},{7,6},{8,9},{9,8},{10,11... | collective-permute-start | bytes 3145736 | tf_op jit(solution)/shard_map/ppermute | solution.py:267
  34.0 4.6 %copy-start = (bf16[512,1024]{1,0:T(8,128)(2,1)}, bf16[512,1024]{1,0:T(8,128)(2,1)S(1)}, u32[]{:S(2)}) copy-start(bf16[512,1024]{1,0:T(8,128)(2,1)S(1)} %slice.72.val_ref) | copy-start | bytes 3145732
  35.9 11.7 %copy-start.1 = (bf16[512,1024]{1,0:T(8,128)(2,1)}, bf16[512,1024]{1,0:T(8,128)(2,1)S(1)}, u32[]{:S(2)}) copy-start(bf16[512,1024]{1,0:T(8,128)(2,1)S(1)} %get-tuple-element.87.feat_ref) | copy-start | bytes 3145732
  40.8 6.7 %collective-permute-start.5 = (bf16[65,1024]{1,0:T(8,128)(2,1)S(1)}, bf16[65,1024]{1,0:T(8,128)(2,1)S(1)}, u32[]{:S(2)}, u32[]{:S(2)}) collective-permute-start(bf16[65,1024]{1,0:T(8,128)(2,1)S(1)} %get-tuple-element.96), channel_id=1, source_target_pairs={{0,1},{1,0},{2,3},{3,2},{4,5},{5,4},{6,7},{7,6},{8,9},{9,8},{10,11... | collective-permute-start | bytes 399368 | tf_op jit(solution)/shard_map/ppermute | solution.py:58
  44.5 11.6 %collective-permute-start.8 = (bf16[65,1024]{1,0:T(8,128)(2,1)S(1)}, bf16[65,1024]{1,0:T(8,128)(2,1)S(1)}, u32[]{:S(2)}, u32[]{:S(2)}) collective-permute-start(bf16[65,1024]{1,0:T(8,128)(2,1)S(1)} %get-tuple-element.95), channel_id=1, source_target_pairs={{1,4},{3,6},{5,8},{7,10},{9,12},{11,14},{13,16},{15,18},{17,20},{1... | collective-permute-start | bytes 399368 | tf_op jit(solution)/shard_map/ppermute | solution.py:58
  47.6 10.1 %collective-permute-start.6 = (bf16[65,1024]{1,0:T(8,128)(2,1)S(1)}, bf16[65,1024]{1,0:T(8,128)(2,1)S(1)}, u32[]{:S(2)}, u32[]{:S(2)}) collective-permute-start(bf16[65,1024]{1,0:T(8,128)(2,1)S(1)} %get-tuple-element.93), channel_id=1, source_target_pairs={{0,2},{1,3},{2,4},{3,5},{4,6},{5,7},{6,8},{7,9},{8,10},{9,11},{10,... | collective-permute-start | bytes 399368 | tf_op jit(solution)/shard_map/ppermute | solution.py:58
  51.0 8.4 %collective-permute-start.7 = (bf16[65,1024]{1,0:T(8,128)(2,1)S(1)}, bf16[65,1024]{1,0:T(8,128)(2,1)S(1)}, u32[]{:S(2)}, u32[]{:S(2)}) collective-permute-start(bf16[65,1024]{1,0:T(8,128)(2,1)S(1)} %get-tuple-element.94), channel_id=1, source_target_pairs={{2,0},{3,1},{4,2},{5,3},{6,4},{7,5},{8,6},{9,7},{10,8},{11,9},{12,... | collective-permute-start | bytes 399368 | tf_op jit(solution)/shard_map/ppermute | solution.py:58
  68.0 3.9 %collective-permute-start.9 = (bf16[65,1024]{1,0:T(8,128)(2,1)S(1)}, bf16[65,1024]{1,0:T(8,128)(2,1)S(1)}, u32[]{:S(2)}, u32[]{:S(2)}) collective-permute-start(bf16[65,1024]{1,0:T(8,128)(2,1)S(1)} %convert_element_type.68), channel_id=1, source_target_pairs={{0,1},{1,0},{2,3},{3,2},{4,5},{5,4},{6,7},{7,6},{8,9},{9,8},{10,11... | collective-permute-start | bytes 399368 | tf_op jit(solution)/shard_map/ppermute | solution.py:58
  68.1 13.6 %collective-permute-start.12 = (bf16[65,1024]{1,0:T(8,128)(2,1)S(1)}, bf16[65,1024]{1,0:T(8,128)(2,1)S(1)}, u32[]{:S(2)}, u32[]{:S(2)}) collective-permute-start(bf16[65,1024]{1,0:T(8,128)(2,1)S(1)} %select_convert_fusion.1), channel_id=1, source_target_pairs={{1,4},{3,6},{5,8},{7,10},{9,12},{11,14},{13,16},{15,18},{17,20},{1... | collective-permute-start | bytes 399368 | tf_op jit(solution)/shard_map/ppermute | solution.py:58
  73.0 9.8 %collective-permute-start.10 = (bf16[65,1024]{1,0:T(8,128)(2,1)S(1)}, bf16[65,1024]{1,0:T(8,128)(2,1)S(1)}, u32[]{:S(2)}, u32[]{:S(2)}) collective-permute-start(bf16[65,1024]{1,0:T(8,128)(2,1)S(1)} %get-tuple-element.91), channel_id=1, source_target_pairs={{0,2},{1,3},{2,4},{3,5},{4,6},{5,7},{6,8},{7,9},{8,10},{9,11},{10,... | collective-permute-start | bytes 399368 | tf_op jit(solution)/shard_map/ppermute | solution.py:58
  77.4 7.5 %collective-permute-start.11 = (bf16[65,1024]{1,0:T(8,128)(2,1)S(1)}, bf16[65,1024]{1,0:T(8,128)(2,1)S(1)}, u32[]{:S(2)}, u32[]{:S(2)}) collective-permute-start(bf16[65,1024]{1,0:T(8,128)(2,1)S(1)} %get-tuple-element.92), channel_id=1, source_target_pairs={{2,0},{3,1},{4,2},{5,3},{6,4},{7,5},{8,6},{9,7},{10,8},{11,9},{12,... | collective-permute-start | bytes 399368 | tf_op jit(solution)/shard_map/ppermute | solution.py:58

commit v12 on v11

--- a/solution.py
+++ b/solution.py
@@ -268,13 +268,12 @@
     twin = position ^ 1
     sources = [
         ([shard, twin_own, early, twin_early], [position, twin, position ^ first, twin ^ second]),
-        ([late[0], late[1]], [position ^ second, position ^ 6]),
     ]
     full = jnp.zeros((count,) + shard.shape, shard.dtype)
     for pieces, where in sources:
         for k, at in enumerate(where):
             full = lax.dynamic_update_slice(full, pieces[k][None], (at, 0, 0))
-    return full, (twin_late, [twin ^ first, twin ^ 6])
+    return full, [(late, [position ^ second, position ^ 6]), (twin_late, [twin ^ first, twin ^ 6])]
 
 
 def shards(receptor, poses, pairs, block_complex, w_key, w_value, w_query, score_weight):
@@ -284,19 +283,20 @@
     if rest is None:
         both = jnp.dot(receptor, full_both, preferred_element_type=jnp.float32)
     else:
-        pieces, where = rest
         part = full_both.shape[1]
         both = jnp.dot(
             receptor, full_both.reshape(-1, full_both.shape[2]), preferred_element_type=jnp.float32
         )
-        picked = jnp.concatenate(
-            [lax.dynamic_slice_in_dim(receptor, at * part, part, axis=1) for at in where], axis=1
-        )
-        both = both + jnp.dot(
-            picked, pieces.reshape(-1, pieces.shape[2]), preferred_element_type=jnp.float32
-        )
-        for k, at in enumerate(where):
-            full_both = lax.dynamic_update_slice(full_both, pieces[k][None], (at, 0, 0))
+        for pieces, where in rest:
+            picked = jnp.concatenate(
+                [lax.dynamic_slice_in_dim(receptor, at * part, part, axis=1) for at in where], axis=1
+            )
+            both = both + jnp.dot(
+                picked, pieces.reshape(-1, pieces.shape[2]), preferred_element_type=jnp.float32
+            )
+        for pieces, where in rest:
+            for k, at in enumerate(where):
+                full_both = lax.dynamic_update_slice(full_both, pieces[k][None], (at, 0, 0))
         full_both = full_both.reshape(-1, full_both.shape[2])
     keys = both[:, :width]
     values = both[:, width:]

time: 95.9 us -> 97.8 us (1.020)
  starting transfers between devices: 26 us -> 20.5 us
  waiting for transfers between devices: 19.6 us -> 23.4 us
  local copies, waits for them, and re-layouts: 15 us -> 17.8 us
  matrix products: 7.22 us -> 8.78 us
    ppermute x8, waiting for transfers between devices: 6.5 us -> 12.6 us  [send(): return lax.ppermute(value, axis, pairs)]
    ppermute x8, starting transfers between devices: 22.9 us -> 17.3 us  [send(): return lax.ppermute(value, axis, pairs)]
    dynamic_update_slice x2 -> x4, local copies, waits for them, and re-layouts: 1.68 us -> 5.55 us  [shards(): full_both = lax.dynamic_update_slice(full_both, pieces[k][None], (at, 0, 0))]
    ppermute x1, waiting for transfers between devices: 2.29 us -> 0.01 us  [gather_rows(): lax.ppermute(shard, 'blk', [(s, s ^ (4 if s % 2 else 2)) for s in range(c...]
    dynamic_update_slice x6 -> x4, local copies, waits for them, and re-layouts: 4.97 us -> 3.34 us  [gather_rows(): full = lax.dynamic_update_slice(full, pieces[k][None], (at, 0, 0))]
    reshape x1, local copies, waits for them, and re-layouts: 0.18 us -> 1.22 us  [local_state(): outer = jnp.einsum('thd,the->dhe', key_heads, val_heads, preferred_elemen...]
  transfers between devices with their start and end apart: 13 -> 13, of which waited for: 7 -> 6; matrix products, arithmetic and copies ran while one was open for 17% -> 20% of each run, Pallas kernels for 0% -> 0%
where the time goes in v12:
time: 97.8 us; the launch traced here: 97 us
  waiting for transfers between devices  23.4 us (24%)
  starting transfers between devices  20.5 us (21%)
  local copies, waits for them, and re-layouts  17.8 us (18%)
  Pallas kernels  14.4 us (15%)
  matrix products  8.78 us (9%)
  other arithmetic  6.69 us (7%)
  between operations  5.45 us (6%)
    ppermute x8, starting transfers between devices, send(): return lax.ppermute(value, axis, pairs)  17.3 us
    ppermute x8, waiting for transfers between devices, send(): return lax.ppermute(value, axis, pairs)  12.6 us
    ppermute x1, waiting for transfers between devices, gather_rows(): lax.ppermute(jnp.stack([shard, early]), 'blk', [(s, s ^ (2 if s % 2 else...  10.5 us
    pallas_call x1, Pallas kernels, back_fused(): pl.pallas_call(back_kernel, out_shape=jax.ShapeDtypeStruct((rows, width),...  7.63 us
    pallas_call x1, Pallas kernels, pose_fused(): pl.pallas_call(pose_kernel, out_shape=(jax.ShapeDtypeStruct((1, pair_rows...  6.79 us
    dynamic_update_slice x4, local copies, waits for them, and re-layouts, shards(): full_both = lax.dynamic_update_slice(full_both, pieces[k][None], (at, 0, 0))  5.55 us
    dot_general x1, matrix products, shards(): jnp.dot(receptor, full_both.reshape(-1, full_both.shape[2]), preferred_el...  4.9 us
    dynamic_update_slice x4, local copies, waits for them, and re-layouts, gather_rows(): full = lax.dynamic_update_slice(full, pieces[k][None], (at, 0, 0))  3.34 us
  transfers between devices with their start and end apart: 13, of which 6 were waited for; matrix products, arithmetic and copies ran while one was open for 20% of the time, Pallas kernels for 0%

profile of v12, /device:TPU:16, one launch (start us, length us, event | category | flops | bytes accessed | tf_op | source)
XLA Modules:
  0.0 97.0 jit_solution(6591446334158518410)
XLA Ops:
  0.7 1.1 %constant_dynamic-update-slice_fusion.1 = bf16[128,2048]{1,0:T(8,128)(2,1)S(1)} fusion(bf16[128,1024]{1,0:T(8,128)(2,1)} %param.12), kind=kLoop, calls=%fused_computation.43 | loop fusion | bytes 524288
  1.7 1.0 constant_dynamic-update-slice_fusion
  2.7 1.6 %collective-permute-start.1 = (bf16[128,2048]{1,0:T(8,128)(2,1)S(1)}, bf16[128,2048]{1,0:T(8,128)(2,1)S(1)}, u32[]{:S(2)}, u32[]{:S(2)}) collective-permute-start(bf16[128,2048]{1,0:T(8,128)(2,1)S(1)} %constant_dynamic-update-slice_fusion), channel_id=1, source_target_pairs={{0,2},{1,5},{2,0},{3,7},{4,6},{5,1},{6,4},{7,3},{8,10},{9,13},{10,... | collective-permute-start | bytes 1572872 | tf_op jit(solution)/shard_map/ppermute | solution.py:262
  4.2 0.0 collective-permute-start
  4.2 2.5 %broadcast_in_dim.72 = bf16[8,128,2048]{2,1,0:T(8,128)(2,1)} broadcast(bf16[]{:T(256)} %constant.198.clone.1), dimensions={} | broadcast | bytes 4194306 | tf_op jit(solution)/shard_map/broadcast_in_dim | solution.py:272
  6.7 0.8 constant_dynamic-update-slice_fusion.3
  7.6 0.7 fusion.20
  12.8 0.1 constant_dynamic-slice_fusion.1
  13.0 0.1 pad_maximum_fusion
  13.1 1.6 %collective-permute-start.3 = (bf16[2,128,2048]{2,1,0:T(8,128)(2,1)S(1)}, bf16[2,128,2048]{2,1,0:T(8,128)(2,1)S(1)}, u32[]{:S(2)}, u32[]{:S(2)}) collective-permute-start(bf16[2,128,2048]{2,1,0:T(8,128)(2,1)S(1)} %pad_maximum_fusion), channel_id=1, source_target_pairs={{0,4},{1,3},{2,6},{3,1},{4,0},{5,7},{6,2},{7,5},{8,12},{9,11},{10,... | collective-permute-start | bytes 3145736 | tf_op jit(solution)/shard_map/ppermute | solution.py:264
  14.7 0.8 bitcast_dynamic-update-slice_fusion.1
  15.5 0.8 constant_dynamic-update-slice_fusion.2
  16.3 0.2 collective-permute-done.2
  16.6 0.8 bitcast_dynamic-update-slice_fusion
  17.4 10.5 %collective-permute-done.3 = bf16[2,128,2048]{2,1,0:T(8,128)(2,1)S(1)} collective-permute-done((bf16[2,128,2048]{2,1,0:T(8,128)(2,1)S(1)}, bf16[2,128,2048]{2,1,0:T(8,128)(2,1)S(1)}, u32[]{:S(2)}, u32[]{:S(2)}) %collective-permute-start.3) | collective-permute-done | bytes 1048608 | tf_op jit(solution)/shard_map/ppermute | solution.py:264
  28.0 4.9 %fusion.22 = f32[2048,512]{0,1:T(8,128)S(1)} fusion(bf16[512,1024]{1,0:T(8,128)(2,1)S(1)} %copy-done.5, bf16[1024,2048]{1,0:T(8,128)(2,1)} %bitcast.5), kind=kOutput, calls=%fused_computation.54 | convolution fusion | flops 2147483648 | bytes 9437184 | tf_op jit(solution)/shard_map/dot_general | solution.py:287
  32.9 0.7 fusion.10
  33.6 0.8 slice_dynamic-update-slice_fusion.3
  34.4 0.7 fusion
  35.2 0.3 copy-done.2
  35.5 1.8 %convert_reduce_fusion = (f32[1024]{0:T(1024)S(1)}, bf16[512,1024]{1,0:T(8,128)(2,1)S(1)}, f32[512,1024]{1,0:T(8,128)}) fusion(f32[512,2048]{1,0:T(8,128)S(1)} %fusion), kind=kLoop, calls=%fused_computation.3 | loop fusion | flops 3668992 | bytes 5246976 | tf_op jit(solution)/shard_map/reduce_sum | solution.py:37
  37.3 0.1 slice.72.val_ref
  37.5 0.5 copy.16
  38.0 1.3 %copy.17 = bf16[512,1024]{0,1:T(8,128)(2,1)} copy(bf16[512,1024]{1,0:T(8,128)(2,1)S(1)} %get-tuple-element.87.feat_ref) | data formatting | bytes 2097152 | tf_op jit(solution)/shard_map/convert_element_type | solution.py:303
  39.4 2.4 %fusion.21 = f32[16,64,64]{2,1,0:T(8,128)} fusion(bf16[512,16,64]{0,2,1:T(8,128)(2,1)S(1)} %bitcast.44, bf16[512,16,64]{0,2,1:T(8,128)(2,1)} %bitcast.45), kind=kOutput, calls=%fused_computation.53 | convolution fusion | flops 67108864 | bytes 2359296 | tf_op jit(solution)/shard_map/thd,the->dhe/dot_general | solution.py:34
  41.8 1.2 %copy.20 = f32[64,1024]{1,0:T(8,128)S(1)} copy(f32[64,1024]{0,1:T(8,128)} %bitcast.49) | data formatting | bytes 524288 | tf_op jit(solution)/shard_map/reshape | solution.py:36
  43.1 0.2 collective-permute-start.5
  43.3 2.0 %slice_dynamic-update-slice_fusion.2 = bf16[8,128,2048]{2,1,0:T(8,128)(2,1)} fusion(bf16[8,128,2048]{2,1,0:T(8,128)(2,1)} %slice_dynamic-update-slice_fusion.3, s32[]{:T(128)S(6)} %select_n.255, bf16[2,128,2048]{2,1,0:T(8,128)(2,1)} %copy-done.4), kind=kLoop, calls=%fused_computation.8 | loop fusion | bytes 1048580 | tf_op jit(solution)/shard_map/dynamic_update_slice | solution.py:299
  45.3 3.2 %collective-permute-start.8 = (bf16[65,1024]{1,0:T(8,128)(2,1)S(1)}, bf16[65,1024]{1,0:T(8,128)(2,1)S(1)}, u32[]{:S(2)}, u32[]{:S(2)}) collective-permute-start(bf16[65,1024]{1,0:T(8,128)(2,1)S(1)} %get-tuple-element.97), channel_id=1, source_target_pairs={{1,4},{3,6},{5,8},{7,10},{9,12},{11,14},{13,16},{15,18},{17,20},{1... | collective-permute-start | bytes 399368 | tf_op jit(solution)/shard_map/ppermute | solution.py:58
  48.5 0.1 add_convert_fusion.3
  48.6 2.9 %collective-permute-start.7 = (bf16[65,1024]{1,0:T(8,128)(2,1)S(1)}, bf16[65,1024]{1,0:T(8,128)(2,1)S(1)}, u32[]{:S(2)}, u32[]{:S(2)}) collective-permute-start(bf16[65,1024]{1,0:T(8,128)(2,1)S(1)} %get-tuple-element.96), channel_id=1, source_target_pairs={{2,0},{3,1},{4,2},{5,3},{6,4},{7,5},{8,6},{9,7},{10,8},{11,9},{12,... | collective-permute-start | bytes 399368 | tf_op jit(solution)/shard_map/ppermute | solution.py:58
  51.5 2.9 %collective-permute-start.6 = (bf16[65,1024]{1,0:T(8,128)(2,1)S(1)}, bf16[65,1024]{1,0:T(8,128)(2,1)S(1)}, u32[]{:S(2)}, u32[]{:S(2)}) collective-permute-start(bf16[65,1024]{1,0:T(8,128)(2,1)S(1)} %get-tuple-element.95), channel_id=1, source_target_pairs={{0,2},{1,3},{2,4},{3,5},{4,6},{5,7},{6,8},{7,9},{8,10},{9,11},{10,... | collective-permute-start | bytes 399368 | tf_op jit(solution)/shard_map/ppermute | solution.py:58
  54.4 1.9 %slice_dynamic-update-slice_fusion.1 = bf16[8,128,2048]{2,1,0:T(8,128)(2,1)} fusion(bf16[8,128,2048]{2,1,0:T(8,128)(2,1)} %slice_dynamic-update-slice_fusion.2, s32[]{:T(128)S(6)} %select_n.256, bf16[2,128,2048]{2,1,0:T(8,128)(2,1)} %copy-done.2), kind=kLoop, calls=%fused_computation.7 | loop fusion | bytes 1048580 | tf_op jit(solution)/shard_map/dynamic_update_slice | solution.py:299
  56.3 0.2 collective-permute-done.7
  56.5 5.4 %collective-permute-done.6 = bf16[65,1024]{1,0:T(8,128)(2,1)S(1)} collective-permute-done((bf16[65,1024]{1,0:T(8,128)(2,1)S(1)}, bf16[65,1024]{1,0:T(8,128)(2,1)S(1)}, u32[]{:S(2)}, u32[]{:S(2)}) %collective-permute-start.6) | collective-permute-done | bytes 133152 | tf_op jit(solution)/shard_map/ppermute | solution.py:58
  61.9 0.8 fusion.4.state_ref
  62.7 6.8 %shard_map.103 = (f32[1,256]{1,0:T(1,128)}, bf16[128,1024]{1,0:T(8,128)(2,1)}, f32[65,1024]{1,0:T(8,128)}) custom-call(bf16[128,1024]{1,0:T(8,128)(2,1)} %pose_ref.1, s32[2,256]{1,0:T(2,128)} %bitcast.55, f32[65,1024]{1,0:T(8,128)} %fusion.4.state_ref, bf16[1024,1024]{1,0:T(8,128)(2,1)} %query_ref.1, f32[1,1024]{1,0:T(1,128)} %bitcast.54), custom_call_target="tpu_custom_call" | custom-call | tf_op jit(solution)/shard_map/pallas_call | solution.py:206
  69.5 1.0 %convert_element_type.68 = bf16[65,1024]{1,0:T(8,128)(2,1)S(1)} convert(f32[65,1024]{1,0:T(8,128)} %get-tuple-element.8) | non-fusion elementwise | flops 66560 | bytes 399360 | tf_op jit(solution)/shard_map/convert_element_type | solution.py:74
  70.5 0.2 collective-permute-start.9
  70.7 1.9 %collective-permute-start.12 = (bf16[65,1024]{1,0:T(8,128)(2,1)S(1)}, bf16[65,1024]{1,0:T(8,128)(2,1)S(1)}, u32[]{:S(2)}, u32[]{:S(2)}) collective-permute-start(bf16[65,1024]{1,0:T(8,128)(2,1)S(1)} %select_convert_fusion.1), channel_id=1, source_target_pairs={{1,4},{3,6},{5,8},{7,10},{9,12},{11,14},{13,16},{15,18},{17,20},{1... | collective-permute-start | bytes 399368 | tf_op jit(solution)/shard_map/ppermute | solution.py:58
  72.6 1.1 %add_convert_fusion.1 = (bf16[65,1024]{1,0:T(8,128)(2,1)S(1)}, bf16[65,1024]{1,0:T(8,128)(2,1)S(1)}) fusion(f32[65,1024]{1,0:T(8,128)} %get-tuple-element.8, bf16[65,1024]{1,0:T(8,128)(2,1)S(1)} %collective-permute-done.9, pred[]{:T(512)S(6)} %and.108, pred[]{:T(512)S(6)} %eq.40, pred[]{:T(512)S(6)} %and.106, pred[]{:T(512)S(6)} %and.112, pred[]{:T(512)S(6)} %and.111), kind=kLoop, calls=%fused_computation.30 | loop fusion | flops 732160 | bytes 665605 | tf_op jit(solution)/shard_map/convert_element_type | solution.py:89
  73.7 3.7 %collective-permute-start.11 = (bf16[65,1024]{1,0:T(8,128)(2,1)S(1)}, bf16[65,1024]{1,0:T(8,128)(2,1)S(1)}, u32[]{:S(2)}, u32[]{:S(2)}) collective-permute-start(bf16[65,1024]{1,0:T(8,128)(2,1)S(1)} %get-tuple-element.94), channel_id=1, source_target_pairs={{2,0},{3,1},{4,2},{5,3},{6,4},{7,5},{8,6},{9,7},{10,8},{11,9},{12,... | collective-permute-start | bytes 399368 | tf_op jit(solution)/shard_map/ppermute | solution.py:58
  77.4 2.3 %collective-permute-start.10 = (bf16[65,1024]{1,0:T(8,128)(2,1)S(1)}, bf16[65,1024]{1,0:T(8,128)(2,1)S(1)}, u32[]{:S(2)}, u32[]{:S(2)}) collective-permute-start(bf16[65,1024]{1,0:T(8,128)(2,1)S(1)} %get-tuple-element.93), channel_id=1, source_target_pairs={{0,2},{1,3},{2,4},{3,5},{4,6},{5,7},{6,8},{7,9},{8,10},{9,11},{10,... | collective-permute-start | bytes 399368 | tf_op jit(solution)/shard_map/ppermute | solution.py:58
  79.8 0.8 slice_dynamic-update-slice_fusion
  80.6 1.2 %collective-permute-done.11 = bf16[65,1024]{1,0:T(8,128)(2,1)S(1)} collective-permute-done((bf16[65,1024]{1,0:T(8,128)(2,1)S(1)}, bf16[65,1024]{1,0:T(8,128)(2,1)S(1)}, u32[]{:S(2)}, u32[]{:S(2)}) %collective-permute-start.11) | collective-permute-done | bytes 133152 | tf_op jit(solution)/shard_map/ppermute | solution.py:58
  81.8 5.9 %collective-permute-done.10 = bf16[65,1024]{1,0:T(8,128)(2,1)S(1)} collective-permute-done((bf16[65,1024]{1,0:T(8,128)(2,1)S(1)}, bf16[65,1024]{1,0:T(8,128)(2,1)S(1)}, u32[]{:S(2)}, u32[]{:S(2)}) %collective-permute-start.10) | collective-permute-done | bytes 133152 | tf_op jit(solution)/shard_map/ppermute | solution.py:58
  87.7 1.7 %fusion.9.grad_ref = bf16[65,1024]{1,0:T(8,128)(2,1)} fusion(f32[65,1024]{1,0:T(8,128)} %get-tuple-element.8, bf16[65,1024]{1,0:T(8,128)(2,1)S(1)} %collective-permute-done.9, bf16[65,1024]{1,0:T(8,128)(2,1)S(1)} %collective-permute-done.12, bf16[65,1024]{1,0:T(8,128)(2,1)S(1)} %collective-permute-done.11, bf16[65,1024]{1,0:T(8,128)(2,1)S(1)} %collective-permute-done.10, ...), kind=kLoop, calls=%fused_computation.26 | loop fusion | flops 665600 | bytes 931841 | tf_op jit(solution)/shard_map/convert_element_type | solution.py:307
  89.4 7.6 %shard_map.104 = bf16[512,1024]{1,0:T(8,128)(2,1)} custom-call(bf16[512,1024]{1,0:T(8,128)(2,1)} %copy-done.1, bf16[512,1024]{1,0:T(8,128)(2,1)} %copy-done, f32[512,1024]{1,0:T(8,128)} %get-tuple-element.88.keys_ref, bf16[65,1024]{1,0:T(8,128)(2,1)} %fusion.9.grad_ref, bf16[1024,2048]{1,0:T(8,128)(2,1)} %bitcast.29.full_ref), custom_call_target="tpu_custom_call" | custom-call | tf_op jit(solution)/shard_map/pallas_call | solution.py:243
  (24 shorter events, 0.1 us)
Async XLA Ops:
  0.6 6.9 %copy-start.6 = (s32[32]{0:T(128)S(1)}, s32[32]{0:T(128)}, u32[]{:S(2)}) copy-start(s32[32]{0:T(128)} %param.11) | copy-start | bytes 388
  0.6 12.2 %copy-start.5 = (bf16[512,1024]{1,0:T(8,128)(2,1)S(1)}, bf16[512,1024]{1,0:T(8,128)(2,1)}, u32[]{:S(2)}) copy-start(bf16[512,1024]{1,0:T(8,128)(2,1)} %param.8) | copy-start | bytes 3145732
  2.7 10.3 %collective-permute-start.1 = (bf16[128,2048]{1,0:T(8,128)(2,1)S(1)}, bf16[128,2048]{1,0:T(8,128)(2,1)S(1)}, u32[]{:S(2)}, u32[]{:S(2)}) collective-permute-start(bf16[128,2048]{1,0:T(8,128)(2,1)S(1)} %constant_dynamic-update-slice_fusion), channel_id=1, source_target_pairs={{0,2},{1,5},{2,0},{3,7},{4,6},{5,1},{6,4},{7,3},{8,10},{9,13},{10,... | collective-permute-start | bytes 1572872 | tf_op jit(solution)/shard_map/ppermute | solution.py:262
  4.2 10.4 %collective-permute-start = (bf16[128,2048]{1,0:T(8,128)(2,1)S(1)}, bf16[128,2048]{1,0:T(8,128)(2,1)S(1)}, u32[]{:S(2)}, u32[]{:S(2)}) collective-permute-start(bf16[128,2048]{1,0:T(8,128)(2,1)S(1)} %constant_dynamic-update-slice_fusion), channel_id=1, source_target_pairs={{0,1},{1,0},{2,3},{3,2},{4,5},{5,4},{6,7},{7,6},{8,9},{9,8},{10,11... | collective-permute-start | bytes 1572872 | tf_op jit(solution)/shard_map/ppermute | solution.py:261
  13.1 14.9 %collective-permute-start.3 = (bf16[2,128,2048]{2,1,0:T(8,128)(2,1)S(1)}, bf16[2,128,2048]{2,1,0:T(8,128)(2,1)S(1)}, u32[]{:S(2)}, u32[]{:S(2)}) collective-permute-start(bf16[2,128,2048]{2,1,0:T(8,128)(2,1)S(1)} %pad_maximum_fusion), channel_id=1, source_target_pairs={{0,4},{1,3},{2,6},{3,1},{4,0},{5,7},{6,2},{7,5},{8,12},{9,11},{10,... | collective-permute-start | bytes 3145736 | tf_op jit(solution)/shard_map/ppermute | solution.py:264
  14.7 1.9 %collective-permute-start.2 = (bf16[128,2048]{1,0:T(8,128)(2,1)S(1)}, bf16[128,2048]{1,0:T(8,128)(2,1)S(1)}, u32[]{:S(2)}, u32[]{:S(2)}) collective-permute-start(bf16[128,2048]{1,0:T(8,128)(2,1)S(1)} %collective-permute-done.1), channel_id=1, source_target_pairs={{0,1},{1,0},{2,3},{3,2},{4,5},{5,4},{6,7},{7,6},{8,9},{9,8},{10,11... | collective-permute-start | bytes 1572872 | tf_op jit(solution)/shard_map/ppermute | solution.py:263
  28.0 5.6 %copy-start.4 = (bf16[2,128,2048]{2,1,0:T(8,128)(2,1)}, bf16[2,128,2048]{2,1,0:T(8,128)(2,1)S(1)}, u32[]{:S(2)}) copy-start(bf16[2,128,2048]{2,1,0:T(8,128)(2,1)S(1)} %collective-permute-done.3) | copy-start | bytes 3145732
  28.0 6.5 %collective-permute-start.4 = (bf16[2,128,2048]{2,1,0:T(8,128)(2,1)S(1)}, bf16[2,128,2048]{2,1,0:T(8,128)(2,1)S(1)}, u32[]{:S(2)}, u32[]{:S(2)}) collective-permute-start(bf16[2,128,2048]{2,1,0:T(8,128)(2,1)S(1)} %collective-permute-done.3), channel_id=1, source_target_pairs={{0,1},{1,0},{2,3},{3,2},{4,5},{5,4},{6,7},{7,6},{8,9},{9,8},{10,11... | collective-permute-start | bytes 3145736 | tf_op jit(solution)/shard_map/ppermute | solution.py:267
  34.4 1.0 %copy-start.2 = (bf16[2,128,2048]{2,1,0:T(8,128)(2,1)}, bf16[2,128,2048]{2,1,0:T(8,128)(2,1)S(1)}, u32[]{:S(2)}) copy-start(bf16[2,128,2048]{2,1,0:T(8,128)(2,1)S(1)} %collective-permute-done.4) | copy-start | bytes 3145732
  37.3 4.5 %copy-start.1 = (bf16[512,1024]{1,0:T(8,128)(2,1)}, bf16[512,1024]{1,0:T(8,128)(2,1)S(1)}, u32[]{:S(2)}) copy-start(bf16[512,1024]{1,0:T(8,128)(2,1)S(1)} %get-tuple-element.87.feat_ref) | copy-start | bytes 3145732
  37.5 7.8 %copy-start = (bf16[512,1024]{1,0:T(8,128)(2,1)}, bf16[512,1024]{1,0:T(8,128)(2,1)S(1)}, u32[]{:S(2)}) copy-start(bf16[512,1024]{1,0:T(8,128)(2,1)S(1)} %slice.72.val_ref) | copy-start | bytes 3145732
  43.1 36.7 %copy-start.3 = (bf16[2,128,2048]{2,1,0:T(8,128)(2,1)S(1)}, bf16[2,128,2048]{2,1,0:T(8,128)(2,1)}, u32[]{:S(2)}) copy-start(bf16[2,128,2048]{2,1,0:T(8,128)(2,1)} %copy-done.2) | copy-start | bytes 3145732
  43.1 5.4 %collective-permute-start.5 = (bf16[65,1024]{1,0:T(8,128)(2,1)S(1)}, bf16[65,1024]{1,0:T(8,128)(2,1)S(1)}, u32[]{:S(2)}, u32[]{:S(2)}) collective-permute-start(bf16[65,1024]{1,0:T(8,128)(2,1)S(1)} %get-tuple-element.98), channel_id=1, source_target_pairs={{0,1},{1,0},{2,3},{3,2},{4,5},{5,4},{6,7},{7,6},{8,9},{9,8},{10,11... | collective-permute-start | bytes 399368 | tf_op jit(solution)/shard_map/ppermute | solution.py:58
  45.3 11.1 %collective-permute-start.8 = (bf16[65,1024]{1,0:T(8,128)(2,1)S(1)}, bf16[65,1024]{1,0:T(8,128)(2,1)S(1)}, u32[]{:S(2)}, u32[]{:S(2)}) collective-permute-start(bf16[65,1024]{1,0:T(8,128)(2,1)S(1)} %get-tuple-element.97), channel_id=1, source_target_pairs={{1,4},{3,6},{5,8},{7,10},{9,12},{11,14},{13,16},{15,18},{17,20},{1... | collective-permute-start | bytes 399368 | tf_op jit(solution)/shard_map/ppermute | solution.py:58
  48.6 7.9 %collective-permute-start.7 = (bf16[65,1024]{1,0:T(8,128)(2,1)S(1)}, bf16[65,1024]{1,0:T(8,128)(2,1)S(1)}, u32[]{:S(2)}, u32[]{:S(2)}) collective-permute-start(bf16[65,1024]{1,0:T(8,128)(2,1)S(1)} %get-tuple-element.96), channel_id=1, source_target_pairs={{2,0},{3,1},{4,2},{5,3},{6,4},{7,5},{8,6},{9,7},{10,8},{11,9},{12,... | collective-permute-start | bytes 399368 | tf_op jit(solution)/shard_map/ppermute | solution.py:58
  51.5 10.4 %collective-permute-start.6 = (bf16[65,1024]{1,0:T(8,128)(2,1)S(1)}, bf16[65,1024]{1,0:T(8,128)(2,1)S(1)}, u32[]{:S(2)}, u32[]{:S(2)}) collective-permute-start(bf16[65,1024]{1,0:T(8,128)(2,1)S(1)} %get-tuple-element.95), channel_id=1, source_target_pairs={{0,2},{1,3},{2,4},{3,5},{4,6},{5,7},{6,8},{7,9},{8,10},{9,11},{10,... | collective-permute-start | bytes 399368 | tf_op jit(solution)/shard_map/ppermute | solution.py:58
  70.5 2.1 %collective-permute-start.9 = (bf16[65,1024]{1,0:T(8,128)(2,1)S(1)}, bf16[65,1024]{1,0:T(8,128)(2,1)S(1)}, u32[]{:S(2)}, u32[]{:S(2)}) collective-permute-start(bf16[65,1024]{1,0:T(8,128)(2,1)S(1)} %convert_element_type.68), channel_id=1, source_target_pairs={{0,1},{1,0},{2,3},{3,2},{4,5},{5,4},{6,7},{7,6},{8,9},{9,8},{10,11... | collective-permute-start | bytes 399368 | tf_op jit(solution)/shard_map/ppermute | solution.py:58
  70.7 9.9 %collective-permute-start.12 = (bf16[65,1024]{1,0:T(8,128)(2,1)S(1)}, bf16[65,1024]{1,0:T(8,128)(2,1)S(1)}, u32[]{:S(2)}, u32[]{:S(2)}) collective-permute-start(bf16[65,1024]{1,0:T(8,128)(2,1)S(1)} %select_convert_fusion.1), channel_id=1, source_target_pairs={{1,4},{3,6},{5,8},{7,10},{9,12},{11,14},{13,16},{15,18},{17,20},{1... | collective-permute-start | bytes 399368 | tf_op jit(solution)/shard_map/ppermute | solution.py:58
  73.7 8.1 %collective-permute-start.11 = (bf16[65,1024]{1,0:T(8,128)(2,1)S(1)}, bf16[65,1024]{1,0:T(8,128)(2,1)S(1)}, u32[]{:S(2)}, u32[]{:S(2)}) collective-permute-start(bf16[65,1024]{1,0:T(8,128)(2,1)S(1)} %get-tuple-element.94), channel_id=1, source_target_pairs={{2,0},{3,1},{4,2},{5,3},{6,4},{7,5},{8,6},{9,7},{10,8},{11,9},{12,... | collective-permute-start | bytes 399368 | tf_op jit(solution)/shard_map/ppermute | solution.py:58
  77.4 10.2 %collective-permute-start.10 = (bf16[65,1024]{1,0:T(8,128)(2,1)S(1)}, bf16[65,1024]{1,0:T(8,128)(2,1)S(1)}, u32[]{:S(2)}, u32[]{:S(2)}) collective-permute-start(bf16[65,1024]{1,0:T(8,128)(2,1)S(1)} %get-tuple-element.93), channel_id=1, source_target_pairs={{0,2},{1,3},{2,4},{3,5},{4,6},{5,7},{6,8},{7,9},{8,10},{9,11},{10,... | collective-permute-start | bytes 399368 | tf_op jit(solution)/shard_map/ppermute | solution.py:58

commit v13 on v12

--- a/solution.py
+++ b/solution.py
@@ -264,7 +264,6 @@
     late = lax.ppermute(
         jnp.stack([shard, early]), "blk", [(s, s ^ (2 if s % 2 else 4)) for s in range(count)]
     )
-    twin_late = lax.ppermute(late, "blk", swap)
     twin = position ^ 1
     sources = [
         ([shard, twin_own, early, twin_early], [position, twin, position ^ first, twin ^ second]),
@@ -273,7 +272,7 @@
     for pieces, where in sources:
         for k, at in enumerate(where):
             full = lax.dynamic_update_slice(full, pieces[k][None], (at, 0, 0))
-    return full, [(late, [position ^ second, position ^ 6]), (twin_late, [twin ^ first, twin ^ 6])]
+    return full, (late, [position ^ second, position ^ 6], [twin ^ first, twin ^ 6])
 
 
 def shards(receptor, poses, pairs, block_complex, w_key, w_value, w_query, score_weight):
@@ -287,6 +286,11 @@
         both = jnp.dot(
             receptor, full_both.reshape(-1, full_both.shape[2]), preferred_element_type=jnp.float32
         )
+        late, mine, theirs = rest
+        both, late = lax.optimization_barrier((both, late))
+        count = lax.axis_size("blk")
+        twin_late = lax.ppermute(late, "blk", [(s, s ^ 1) for s in range(count)])
+        rest = [(late, mine), (twin_late, theirs)]
         for pieces, where in rest:
             picked = jnp.concatenate(
                 [lax.dynamic_slice_in_dim(receptor, at * part, part, axis=1) for at in where], axis=1

time: 97.8 us -> 98.4 us (level)
  waiting for transfers between devices: 23.4 us -> 20.5 us
  matrix products: 8.78 us -> 10.5 us
    ppermute x1, waiting for transfers between devices: 10.5 us -> 3.97 us  [gather_rows(): lax.ppermute(jnp.stack([shard, early]), 'blk', [(s, s ^ (2 if s % 2 else...]
    ppermute x1, waiting for transfers between devices: 0.01 us -> 4.28 us  [gather_rows(): lax.ppermute(shard, 'blk', [(s, s ^ (4 if s % 2 else 2)) for s in range(c...]
    dot_general x1, matrix products: 4.9 us -> 6.56 us  [shards(): jnp.dot(receptor, full_both.reshape(-1, full_both.shape[2]), preferred_el...]
  transfers between devices with their start and end apart: 13 -> 13, of which waited for: 6 -> 7; matrix products, arithmetic and copies ran while one was open for 20% -> 23% of each run, Pallas kernels for 0% -> 0%
where the time goes in v13:
time: 98.4 us; the launch traced here: 97.6 us
  starting transfers between devices  20.7 us (21%)
  waiting for transfers between devices  20.5 us (21%)
  local copies, waits for them, and re-layouts  18.4 us (19%)
  Pallas kernels  14.4 us (15%)
  matrix products  10.5 us (11%)
  other arithmetic  7.63 us (8%)
  between operations  5.35 us (5%)
    ppermute x8, starting transfers between devices, send(): return lax.ppermute(value, axis, pairs)  17.6 us
    ppermute x8, waiting for transfers between devices, send(): return lax.ppermute(value, axis, pairs)  12 us
    pallas_call x1, Pallas kernels, back_fused(): pl.pallas_call(back_kernel, out_shape=jax.ShapeDtypeStruct((rows, width),...  7.63 us
    pallas_call x1, Pallas kernels, pose_fused(): pl.pallas_call(pose_kernel, out_shape=(jax.ShapeDtypeStruct((1, pair_rows...  6.81 us
    dot_general x1, matrix products, shards(): jnp.dot(receptor, full_both.reshape(-1, full_both.shape[2]), preferred_el...  6.56 us
    dynamic_update_slice x4, local copies, waits for them, and re-layouts, shards(): full_both = lax.dynamic_update_slice(full_both, pieces[k][None], (at, 0, 0))  5.56 us
    ppermute x1, waiting for transfers between devices, gather_rows(): lax.ppermute(shard, 'blk', [(s, s ^ (4 if s % 2 else 2)) for s in range(c...  4.28 us
    ppermute x1, waiting for transfers between devices, gather_rows(): lax.ppermute(jnp.stack([shard, early]), 'blk', [(s, s ^ (2 if s % 2 else...  3.97 us
  transfers between devices with their start and end apart: 13, of which 7 were waited for; matrix products, arithmetic and copies ran while one was open for 23% of the time, Pallas kernels for 0%

profile of v13, /device:TPU:16, one launch (start us, length us, event | category | flops | bytes accessed | tf_op | source)
XLA Modules:
  0.0 97.6 jit_solution(9681532461434072996)
XLA Ops:
  0.6 1.0 constant_dynamic-update-slice_fusion.1
  1.6 1.0 constant_dynamic-update-slice_fusion
  2.6 1.6 %collective-permute-start.1 = (bf16[128,2048]{1,0:T(8,128)(2,1)S(1)}, bf16[128,2048]{1,0:T(8,128)(2,1)S(1)}, u32[]{:S(2)}, u32[]{:S(2)}) collective-permute-start(bf16[128,2048]{1,0:T(8,128)(2,1)S(1)} %constant_dynamic-update-slice_fusion), channel_id=1, source_target_pairs={{0,2},{1,5},{2,0},{3,7},{4,6},{5,1},{6,4},{7,3},{8,10},{9,13},{10,... | collective-permute-start | bytes 1572872 | tf_op jit(solution)/shard_map/ppermute | solution.py:262
  4.1 2.5 %broadcast_in_dim.72 = bf16[8,128,2048]{2,1,0:T(8,128)(2,1)} broadcast(bf16[]{:T(256)} %constant.198.clone.1), dimensions={} | broadcast | bytes 4194306 | tf_op jit(solution)/shard_map/broadcast_in_dim | solution.py:271
  6.7 0.9 constant_dynamic-update-slice_fusion.3
  7.5 4.3 %collective-permute-done.1 = bf16[128,2048]{1,0:T(8,128)(2,1)S(1)} collective-permute-done((bf16[128,2048]{1,0:T(8,128)(2,1)S(1)}, bf16[128,2048]{1,0:T(8,128)(2,1)S(1)}, u32[]{:S(2)}, u32[]{:S(2)}) %collective-permute-start.1) | collective-permute-done | bytes 524320 | tf_op jit(solution)/shard_map/ppermute | solution.py:262
  11.9 1.6 %collective-permute-start.3 = (bf16[2,128,2048]{2,1,0:T(8,128)(2,1)S(1)}, bf16[2,128,2048]{2,1,0:T(8,128)(2,1)S(1)}, u32[]{:S(2)}, u32[]{:S(2)}) collective-permute-start(bf16[2,128,2048]{2,1,0:T(8,128)(2,1)S(1)} %pad_maximum_fusion), channel_id=1, source_target_pairs={{0,4},{1,3},{2,6},{3,1},{4,0},{5,7},{6,2},{7,5},{8,12},{9,11},{10,... | collective-permute-start | bytes 3145736 | tf_op jit(solution)/shard_map/ppermute | solution.py:264
  13.5 0.8 bitcast_dynamic-update-slice_fusion.1
  14.4 0.8 constant_dynamic-update-slice_fusion.2
  15.2 0.2 collective-permute-done.2
  15.4 0.8 bitcast_dynamic-update-slice_fusion
  16.3 6.6 %convolution_bitcast_fusion = f32[512,2048]{1,0:T(8,128)} fusion(bf16[512,1024]{1,0:T(8,128)(2,1)S(1)} %copy-done.6, bf16[1024,2048]{1,0:T(8,128)(2,1)} %bitcast.5), kind=kOutput, calls=%fused_computation.1 | convolution fusion | flops 2147483648 | bytes 9437184 | tf_op jit(solution)/shard_map/dot_general | solution.py:286
  22.8 4.0 %collective-permute-done.3 = bf16[2,128,2048]{2,1,0:T(8,128)(2,1)S(1)} collective-permute-done((bf16[2,128,2048]{2,1,0:T(8,128)(2,1)S(1)}, bf16[2,128,2048]{2,1,0:T(8,128)(2,1)S(1)}, u32[]{:S(2)}, u32[]{:S(2)}) %collective-permute-start.3) | collective-permute-done | bytes 1048608 | tf_op jit(solution)/shard_map/ppermute | solution.py:264
  26.8 0.8 fusion.22
  32.1 0.1 constant_dynamic-slice_fusion.1
  32.3 0.7 fusion.9
  33.0 0.9 slice_dynamic-update-slice_fusion.3
  33.9 0.8 copy-done.2
  34.7 0.8 add_add_fusion
  35.5 1.8 %convert_reduce_fusion = (f32[1024]{0:T(1024)S(1)}, bf16[512,1024]{1,0:T(8,128)(2,1)S(1)}, f32[512,1024]{1,0:T(8,128)}) fusion(f32[512,2048]{1,0:T(8,128)S(1)} %add_add_fusion), kind=kLoop, calls=%fused_computation.3 | loop fusion | flops 3668992 | bytes 5246976 | tf_op jit(solution)/shard_map/reduce_sum | solution.py:37
  37.3 0.1 slice.70.val_ref
  37.5 0.5 copy.16
  38.0 1.3 %copy.17 = bf16[512,1024]{0,1:T(8,128)(2,1)} copy(bf16[512,1024]{1,0:T(8,128)(2,1)S(1)} %get-tuple-element.91.feat_ref) | data formatting | bytes 2097152 | tf_op jit(solution)/shard_map/convert_element_type | solution.py:307
  39.3 2.5 %fusion.23 = f32[16,64,64]{2,1,0:T(8,128)} fusion(bf16[512,16,64]{0,2,1:T(8,128)(2,1)S(1)} %bitcast.42, bf16[512,16,64]{0,2,1:T(8,128)(2,1)} %bitcast.43), kind=kOutput, calls=%fused_computation.54 | convolution fusion | flops 67108864 | bytes 2359296 | tf_op jit(solution)/shard_map/thd,the->dhe/dot_general | solution.py:34
  41.8 1.2 %copy.20 = f32[64,1024]{1,0:T(8,128)S(1)} copy(f32[64,1024]{0,1:T(8,128)} %bitcast.47) | data formatting | bytes 524288 | tf_op jit(solution)/shard_map/reshape | solution.py:36
  43.1 0.4 collective-permute-start.5
  43.5 1.9 %slice_dynamic-update-slice_fusion.2 = bf16[8,128,2048]{2,1,0:T(8,128)(2,1)} fusion(bf16[8,128,2048]{2,1,0:T(8,128)(2,1)} %slice_dynamic-update-slice_fusion.3, s32[]{:T(128)S(6)} %select_n.255, bf16[2,128,2048]{2,1,0:T(8,128)(2,1)} %copy-done.5), kind=kLoop, calls=%fused_computation.10 | loop fusion | bytes 1048580 | tf_op jit(solution)/shard_map/dynamic_update_slice | solution.py:303
  45.4 3.2 %collective-permute-start.8 = (bf16[65,1024]{1,0:T(8,128)(2,1)S(1)}, bf16[65,1024]{1,0:T(8,128)(2,1)S(1)}, u32[]{:S(2)}, u32[]{:S(2)}) collective-permute-start(bf16[65,1024]{1,0:T(8,128)(2,1)S(1)} %get-tuple-element.101), channel_id=1, source_target_pairs={{1,4},{3,6},{5,8},{7,10},{9,12},{11,14},{13,16},{15,18},{17,20},{1... | collective-permute-start | bytes 399368 | tf_op jit(solution)/shard_map/ppermute | solution.py:58
  48.6 0.1 add_convert_fusion.3
  48.7 3.3 %collective-permute-start.7 = (bf16[65,1024]{1,0:T(8,128)(2,1)S(1)}, bf16[65,1024]{1,0:T(8,128)(2,1)S(1)}, u32[]{:S(2)}, u32[]{:S(2)}) collective-permute-start(bf16[65,1024]{1,0:T(8,128)(2,1)S(1)} %get-tuple-element.100), channel_id=1, source_target_pairs={{2,0},{3,1},{4,2},{5,3},{6,4},{7,5},{8,6},{9,7},{10,8},{11,9},{12,... | collective-permute-start | bytes 399368 | tf_op jit(solution)/shard_map/ppermute | solution.py:58
  52.0 2.5 %collective-permute-start.6 = (bf16[65,1024]{1,0:T(8,128)(2,1)S(1)}, bf16[65,1024]{1,0:T(8,128)(2,1)S(1)}, u32[]{:S(2)}, u32[]{:S(2)}) collective-permute-start(bf16[65,1024]{1,0:T(8,128)(2,1)S(1)} %get-tuple-element.99), channel_id=1, source_target_pairs={{0,2},{1,3},{2,4},{3,5},{4,6},{5,7},{6,8},{7,9},{8,10},{9,11},{10,... | collective-permute-start | bytes 399368 | tf_op jit(solution)/shard_map/ppermute | solution.py:58
  54.6 1.9 %slice_dynamic-update-slice_fusion.1 = bf16[8,128,2048]{2,1,0:T(8,128)(2,1)} fusion(bf16[8,128,2048]{2,1,0:T(8,128)(2,1)} %slice_dynamic-update-slice_fusion.2, s32[]{:T(128)S(6)} %select_n.256, bf16[2,128,2048]{2,1,0:T(8,128)(2,1)} %copy-done.3), kind=kLoop, calls=%fused_computation.7 | loop fusion | bytes 1048580 | tf_op jit(solution)/shard_map/dynamic_update_slice | solution.py:303
  56.5 0.2 collective-permute-done.7
  56.7 5.7 %collective-permute-done.6 = bf16[65,1024]{1,0:T(8,128)(2,1)S(1)} collective-permute-done((bf16[65,1024]{1,0:T(8,128)(2,1)S(1)}, bf16[65,1024]{1,0:T(8,128)(2,1)S(1)}, u32[]{:S(2)}, u32[]{:S(2)}) %collective-permute-start.6) | collective-permute-done | bytes 133152 | tf_op jit(solution)/shard_map/ppermute | solution.py:58
  62.4 0.8 fusion.3.state_ref
  63.2 6.8 %shard_map.103 = (f32[1,256]{1,0:T(1,128)}, bf16[128,1024]{1,0:T(8,128)(2,1)}, f32[65,1024]{1,0:T(8,128)}) custom-call(bf16[128,1024]{1,0:T(8,128)(2,1)} %pose_ref.1, s32[2,256]{1,0:T(2,128)} %bitcast.53, f32[65,1024]{1,0:T(8,128)} %fusion.3.state_ref, bf16[1024,1024]{1,0:T(8,128)(2,1)} %query_ref.1, f32[1,1024]{1,0:T(1,128)} %bitcast.52), custom_call_target="tpu_custom_call" | custom-call | tf_op jit(solution)/shard_map/pallas_call | solution.py:206
  70.0 1.0 %convert_element_type.68 = bf16[65,1024]{1,0:T(8,128)(2,1)S(1)} convert(f32[65,1024]{1,0:T(8,128)} %get-tuple-element.12) | non-fusion elementwise | flops 66560 | bytes 399360 | tf_op jit(solution)/shard_map/convert_element_type | solution.py:74
  71.0 0.2 collective-permute-start.9
  71.2 1.0 %select_convert_fusion.1 = bf16[65,1024]{1,0:T(8,128)(2,1)S(1)} fusion(f32[65,1024]{1,0:T(8,128)} %get-tuple-element.12, pred[]{:T(512)S(6)} %and.115), kind=kLoop, calls=%fused_computation.28 | loop fusion | flops 66560 | bytes 399361 | tf_op jit(solution)/shard_map/convert_element_type | solution.py:80
  72.2 1.9 %collective-permute-start.12 = (bf16[65,1024]{1,0:T(8,128)(2,1)S(1)}, bf16[65,1024]{1,0:T(8,128)(2,1)S(1)}, u32[]{:S(2)}, u32[]{:S(2)}) collective-permute-start(bf16[65,1024]{1,0:T(8,128)(2,1)S(1)} %select_convert_fusion.1), channel_id=1, source_target_pairs={{1,4},{3,6},{5,8},{7,10},{9,12},{11,14},{13,16},{15,18},{17,20},{1... | collective-permute-start | bytes 399368 | tf_op jit(solution)/shard_map/ppermute | solution.py:58
  74.1 1.1 %add_convert_fusion.1 = (bf16[65,1024]{1,0:T(8,128)(2,1)S(1)}, bf16[65,1024]{1,0:T(8,128)(2,1)S(1)}) fusion(f32[65,1024]{1,0:T(8,128)} %get-tuple-element.12, bf16[65,1024]{1,0:T(8,128)(2,1)S(1)} %collective-permute-done.9, pred[]{:T(512)S(6)} %and.108, pred[]{:T(512)S(6)} %eq.40, pred[]{:T(512)S(6)} %and.106, pred[]{:T(512)S(6)} %and.112, pred[]{:T(512)S(6)} %and.111), kind=kLoop, calls=%fused_computation.30 | loop fusion | flops 732160 | bytes 665605 | tf_op jit(solution)/shard_map/convert_element_type | solution.py:89
  75.2 2.8 %collective-permute-start.11 = (bf16[65,1024]{1,0:T(8,128)(2,1)S(1)}, bf16[65,1024]{1,0:T(8,128)(2,1)S(1)}, u32[]{:S(2)}, u32[]{:S(2)}) collective-permute-start(bf16[65,1024]{1,0:T(8,128)(2,1)S(1)} %get-tuple-element.98), channel_id=1, source_target_pairs={{2,0},{3,1},{4,2},{5,3},{6,4},{7,5},{8,6},{9,7},{10,8},{11,9},{12,... | collective-permute-start | bytes 399368 | tf_op jit(solution)/shard_map/ppermute | solution.py:58
  78.0 3.2 %collective-permute-start.10 = (bf16[65,1024]{1,0:T(8,128)(2,1)S(1)}, bf16[65,1024]{1,0:T(8,128)(2,1)S(1)}, u32[]{:S(2)}, u32[]{:S(2)}) collective-permute-start(bf16[65,1024]{1,0:T(8,128)(2,1)S(1)} %get-tuple-element.97), channel_id=1, source_target_pairs={{0,2},{1,3},{2,4},{3,5},{4,6},{5,7},{6,8},{7,9},{8,10},{9,11},{10,... | collective-permute-start | bytes 399368 | tf_op jit(solution)/shard_map/ppermute | solution.py:58
  81.2 0.9 slice_dynamic-update-slice_fusion
  82.1 0.1 collective-permute-done.11
  82.3 6.0 %collective-permute-done.10 = bf16[65,1024]{1,0:T(8,128)(2,1)S(1)} collective-permute-done((bf16[65,1024]{1,0:T(8,128)(2,1)S(1)}, bf16[65,1024]{1,0:T(8,128)(2,1)S(1)}, u32[]{:S(2)}, u32[]{:S(2)}) %collective-permute-start.10) | collective-permute-done | bytes 133152 | tf_op jit(solution)/shard_map/ppermute | solution.py:58
  88.2 1.7 %fusion.8.grad_ref = bf16[65,1024]{1,0:T(8,128)(2,1)} fusion(f32[65,1024]{1,0:T(8,128)} %get-tuple-element.12, bf16[65,1024]{1,0:T(8,128)(2,1)S(1)} %collective-permute-done.9, bf16[65,1024]{1,0:T(8,128)(2,1)S(1)} %collective-permute-done.12, bf16[65,1024]{1,0:T(8,128)(2,1)S(1)} %collective-permute-done.11, bf16[65,1024]{1,0:T(8,128)(2,1)S(1)} %collective-permute-done.10, ...), kind=kLoop, calls=%fused_computation.26 | loop fusion | flops 665600 | bytes 931841 | tf_op jit(solution)/shard_map/convert_element_type | solution.py:311
  90.0 7.6 %shard_map.104 = bf16[512,1024]{1,0:T(8,128)(2,1)} custom-call(bf16[512,1024]{1,0:T(8,128)(2,1)} %copy-done.1, bf16[512,1024]{1,0:T(8,128)(2,1)} %copy-done, f32[512,1024]{1,0:T(8,128)} %get-tuple-element.92.keys_ref, bf16[65,1024]{1,0:T(8,128)(2,1)} %fusion.8.grad_ref, bf16[1024,2048]{1,0:T(8,128)(2,1)} %bitcast.29.full_ref), custom_call_target="tpu_custom_call" | custom-call | tf_op jit(solution)/shard_map/pallas_call | solution.py:243
  (28 shorter events, 0.2 us)
Async XLA Ops:
  2.6 9.2 %collective-permute-start.1 = (bf16[128,2048]{1,0:T(8,128)(2,1)S(1)}, bf16[128,2048]{1,0:T(8,128)(2,1)S(1)}, u32[]{:S(2)}, u32[]{:S(2)}) collective-permute-start(bf16[128,2048]{1,0:T(8,128)(2,1)S(1)} %constant_dynamic-update-slice_fusion), channel_id=1, source_target_pairs={{0,2},{1,5},{2,0},{3,7},{4,6},{5,1},{6,4},{7,3},{8,10},{9,13},{10,... | collective-permute-start | bytes 1572872 | tf_op jit(solution)/shard_map/ppermute | solution.py:262
  4.1 9.4 %collective-permute-start = (bf16[128,2048]{1,0:T(8,128)(2,1)S(1)}, bf16[128,2048]{1,0:T(8,128)(2,1)S(1)}, u32[]{:S(2)}, u32[]{:S(2)}) collective-permute-start(bf16[128,2048]{1,0:T(8,128)(2,1)S(1)} %constant_dynamic-update-slice_fusion), channel_id=1, source_target_pairs={{0,1},{1,0},{2,3},{3,2},{4,5},{5,4},{6,7},{7,6},{8,9},{9,8},{10,11... | collective-permute-start | bytes 1572872 | tf_op jit(solution)/shard_map/ppermute | solution.py:261
  6.7 9.6 %copy-start.6 = (bf16[512,1024]{1,0:T(8,128)(2,1)S(1)}, bf16[512,1024]{1,0:T(8,128)(2,1)}, u32[]{:S(2)}) copy-start(bf16[512,1024]{1,0:T(8,128)(2,1)} %param.8) | copy-start | bytes 3145732
  11.9 14.9 %collective-permute-start.3 = (bf16[2,128,2048]{2,1,0:T(8,128)(2,1)S(1)}, bf16[2,128,2048]{2,1,0:T(8,128)(2,1)S(1)}, u32[]{:S(2)}, u32[]{:S(2)}) collective-permute-start(bf16[2,128,2048]{2,1,0:T(8,128)(2,1)S(1)} %pad_maximum_fusion), channel_id=1, source_target_pairs={{0,4},{1,3},{2,6},{3,1},{4,0},{5,7},{6,2},{7,5},{8,12},{9,11},{10,... | collective-permute-start | bytes 3145736 | tf_op jit(solution)/shard_map/ppermute | solution.py:264
  13.5 1.9 %collective-permute-start.2 = (bf16[128,2048]{1,0:T(8,128)(2,1)S(1)}, bf16[128,2048]{1,0:T(8,128)(2,1)S(1)}, u32[]{:S(2)}, u32[]{:S(2)}) collective-permute-start(bf16[128,2048]{1,0:T(8,128)(2,1)S(1)} %collective-permute-done.1), channel_id=1, source_target_pairs={{0,1},{1,0},{2,3},{3,2},{4,5},{5,4},{6,7},{7,6},{8,9},{9,8},{10,11... | collective-permute-start | bytes 1572872 | tf_op jit(solution)/shard_map/ppermute | solution.py:263
  16.3 10.5 %copy-start.8 = (s32[32]{0:T(128)S(1)}, s32[32]{0:T(128)}, u32[]{:S(2)}) copy-start(s32[32]{0:T(128)} %param.11) | copy-start | bytes 388
  16.3 15.9 %copy-start.7 = (bf16[512,1024]{1,0:T(8,128)(2,1)S(1)}, bf16[512,1024]{1,0:T(8,128)(2,1)}, u32[]{:S(2)}) copy-start(bf16[512,1024]{1,0:T(8,128)(2,1)} %param.8) | copy-start | bytes 3145732
  26.8 6.2 %copy-start.5 = (bf16[2,128,2048]{2,1,0:T(8,128)(2,1)}, bf16[2,128,2048]{2,1,0:T(8,128)(2,1)S(1)}, u32[]{:S(2)}) copy-start(bf16[2,128,2048]{2,1,0:T(8,128)(2,1)S(1)} %collective-permute-done.3) | copy-start | bytes 3145732
  26.8 7.1 %collective-permute-start.4 = (bf16[2,128,2048]{2,1,0:T(8,128)(2,1)S(1)}, bf16[2,128,2048]{2,1,0:T(8,128)(2,1)S(1)}, u32[]{:S(2)}, u32[]{:S(2)}) collective-permute-start(bf16[2,128,2048]{2,1,0:T(8,128)(2,1)S(1)} %collective-permute-done.3), channel_id=1, source_target_pairs={{0,1},{1,0},{2,3},{3,2},{4,5},{5,4},{6,7},{7,6},{8,9},{9,8},{10,11... | collective-permute-start | bytes 3145736 | tf_op jit(solution)/shard_map/ppermute | solution.py:292
  32.3 2.4 %copy-start.2 = (f32[512,2048]{1,0:T(8,128)S(1)}, f32[512,2048]{1,0:T(8,128)}, u32[]{:S(2)}) copy-start(f32[512,2048]{1,0:T(8,128)} %convolution_bitcast_fusion) | copy-start | bytes 12582916
  33.9 1.6 %copy-start.3 = (bf16[2,128,2048]{2,1,0:T(8,128)(2,1)}, bf16[2,128,2048]{2,1,0:T(8,128)(2,1)S(1)}, u32[]{:S(2)}) copy-start(bf16[2,128,2048]{2,1,0:T(8,128)(2,1)S(1)} %collective-permute-done.4) | copy-start | bytes 3145732
  37.3 4.5 %copy-start.1 = (bf16[512,1024]{1,0:T(8,128)(2,1)}, bf16[512,1024]{1,0:T(8,128)(2,1)S(1)}, u32[]{:S(2)}) copy-start(bf16[512,1024]{1,0:T(8,128)(2,1)S(1)} %get-tuple-element.91.feat_ref) | copy-start | bytes 3145732
  37.4 8.0 %copy-start = (bf16[512,1024]{1,0:T(8,128)(2,1)}, bf16[512,1024]{1,0:T(8,128)(2,1)S(1)}, u32[]{:S(2)}) copy-start(bf16[512,1024]{1,0:T(8,128)(2,1)S(1)} %slice.70.val_ref) | copy-start | bytes 3145732
  43.1 38.1 %copy-start.4 = (bf16[2,128,2048]{2,1,0:T(8,128)(2,1)S(1)}, bf16[2,128,2048]{2,1,0:T(8,128)(2,1)}, u32[]{:S(2)}) copy-start(bf16[2,128,2048]{2,1,0:T(8,128)(2,1)} %copy-done.3) | copy-start | bytes 3145732
  43.1 5.5 %collective-permute-start.5 = (bf16[65,1024]{1,0:T(8,128)(2,1)S(1)}, bf16[65,1024]{1,0:T(8,128)(2,1)S(1)}, u32[]{:S(2)}, u32[]{:S(2)}) collective-permute-start(bf16[65,1024]{1,0:T(8,128)(2,1)S(1)} %get-tuple-element.102), channel_id=1, source_target_pairs={{0,1},{1,0},{2,3},{3,2},{4,5},{5,4},{6,7},{7,6},{8,9},{9,8},{10,11... | collective-permute-start | bytes 399368 | tf_op jit(solution)/shard_map/ppermute | solution.py:58
  45.4 11.1 %collective-permute-start.8 = (bf16[65,1024]{1,0:T(8,128)(2,1)S(1)}, bf16[65,1024]{1,0:T(8,128)(2,1)S(1)}, u32[]{:S(2)}, u32[]{:S(2)}) collective-permute-start(bf16[65,1024]{1,0:T(8,128)(2,1)S(1)} %get-tuple-element.101), channel_id=1, source_target_pairs={{1,4},{3,6},{5,8},{7,10},{9,12},{11,14},{13,16},{15,18},{17,20},{1... | collective-permute-start | bytes 399368 | tf_op jit(solution)/shard_map/ppermute | solution.py:58
  48.7 8.0 %collective-permute-start.7 = (bf16[65,1024]{1,0:T(8,128)(2,1)S(1)}, bf16[65,1024]{1,0:T(8,128)(2,1)S(1)}, u32[]{:S(2)}, u32[]{:S(2)}) collective-permute-start(bf16[65,1024]{1,0:T(8,128)(2,1)S(1)} %get-tuple-element.100), channel_id=1, source_target_pairs={{2,0},{3,1},{4,2},{5,3},{6,4},{7,5},{8,6},{9,7},{10,8},{11,9},{12,... | collective-permute-start | bytes 399368 | tf_op jit(solution)/shard_map/ppermute | solution.py:58
  52.0 10.4 %collective-permute-start.6 = (bf16[65,1024]{1,0:T(8,128)(2,1)S(1)}, bf16[65,1024]{1,0:T(8,128)(2,1)S(1)}, u32[]{:S(2)}, u32[]{:S(2)}) collective-permute-start(bf16[65,1024]{1,0:T(8,128)(2,1)S(1)} %get-tuple-element.99), channel_id=1, source_target_pairs={{0,2},{1,3},{2,4},{3,5},{4,6},{5,7},{6,8},{7,9},{8,10},{9,11},{10,... | collective-permute-start | bytes 399368 | tf_op jit(solution)/shard_map/ppermute | solution.py:58
  71.0 3.1 %collective-permute-start.9 = (bf16[65,1024]{1,0:T(8,128)(2,1)S(1)}, bf16[65,1024]{1,0:T(8,128)(2,1)S(1)}, u32[]{:S(2)}, u32[]{:S(2)}) collective-permute-start(bf16[65,1024]{1,0:T(8,128)(2,1)S(1)} %convert_element_type.68), channel_id=1, source_target_pairs={{0,1},{1,0},{2,3},{3,2},{4,5},{5,4},{6,7},{7,6},{8,9},{9,8},{10,11... | collective-permute-start | bytes 399368 | tf_op jit(solution)/shard_map/ppermute | solution.py:58
  72.2 10.0 %collective-permute-start.12 = (bf16[65,1024]{1,0:T(8,128)(2,1)S(1)}, bf16[65,1024]{1,0:T(8,128)(2,1)S(1)}, u32[]{:S(2)}, u32[]{:S(2)}) collective-permute-start(bf16[65,1024]{1,0:T(8,128)(2,1)S(1)} %select_convert_fusion.1), channel_id=1, source_target_pairs={{1,4},{3,6},{5,8},{7,10},{9,12},{11,14},{13,16},{15,18},{17,20},{1... | collective-permute-start | bytes 399368 | tf_op jit(solution)/shard_map/ppermute | solution.py:58
  75.2 7.1 %collective-permute-start.11 = (bf16[65,1024]{1,0:T(8,128)(2,1)S(1)}, bf16[65,1024]{1,0:T(8,128)(2,1)S(1)}, u32[]{:S(2)}, u32[]{:S(2)}) collective-permute-start(bf16[65,1024]{1,0:T(8,128)(2,1)S(1)} %get-tuple-element.98), channel_id=1, source_target_pairs={{2,0},{3,1},{4,2},{5,3},{6,4},{7,5},{8,6},{9,7},{10,8},{11,9},{12,... | collective-permute-start | bytes 399368 | tf_op jit(solution)/shard_map/ppermute | solution.py:58
  78.0 10.3 %collective-permute-start.10 = (bf16[65,1024]{1,0:T(8,128)(2,1)S(1)}, bf16[65,1024]{1,0:T(8,128)(2,1)S(1)}, u32[]{:S(2)}, u32[]{:S(2)}) collective-permute-start(bf16[65,1024]{1,0:T(8,128)(2,1)S(1)} %get-tuple-element.97), channel_id=1, source_target_pairs={{0,2},{1,3},{2,4},{3,5},{4,6},{5,7},{6,8},{7,9},{8,10},{9,11},{10,... | collective-permute-start | bytes 399368 | tf_op jit(solution)/shard_map/ppermute | solution.py:58

commit v14 on v11

--- a/solution.py
+++ b/solution.py
@@ -28,14 +28,15 @@
 
 
 def local_state(key_feat, val_round):
-    rows = key_feat.shape[0]
-    key_heads = key_feat.reshape(rows, H, DH)
-    val_heads = val_round.reshape(rows, H, DH)
-    outer = jnp.einsum(
-        "thd,the->dhe", key_heads, val_heads, preferred_element_type=jnp.float32
-    ).reshape(DH, H * DH)
+    width = key_feat.shape[1]
+    outer = lax.dot_general(
+        key_feat, val_round, (((0,), (0,)), ((), ())), preferred_element_type=jnp.float32
+    )
+    head_row = lax.broadcasted_iota(jnp.int32, (width, width), 0) // DH
+    head_col = lax.broadcasted_iota(jnp.int32, (width, width), 1) // DH
+    diagonal = jnp.where(head_row == head_col, outer, 0.0).reshape(width // DH, DH, width)
     norm_row = jnp.sum(key_feat, axis=0, dtype=jnp.float32)
-    return jnp.concatenate([outer, norm_row[None, :]], axis=0)
+    return jnp.concatenate([jnp.sum(diagonal, axis=0), norm_row[None, :]], axis=0)
 
 
 def complex_total(own, block_complex):

time: 95.9 us -> 96 us (level)
  waiting for transfers between devices: 19.6 us -> 16.7 us
  other arithmetic: 6.7 us -> 8.7 us
    ppermute x8, waiting for transfers between devices: 6.5 us -> 3.63 us  [send(): return lax.ppermute(value, axis, pairs)]
    reduce_sum x0 -> x1, other arithmetic: none -> 2.48 us  [local_state(): jnp.sum(diagonal, axis=0)]
    convert_element_type x1 -> x0, local copies, waits for them, and re-layouts: 1.42 us -> none  [shards(): key_feat = features(keys).astype(jnp.bfloat16)]
    slice x2 -> x1, local copies, waits for them, and re-layouts: 1.47 us -> 2.83 us  [shards(): values = both[:, width:]]
    convert_element_type x1, other arithmetic: 1.73 us -> 0.76 us  [shards(): state_grad = complex_sum(pose_state, block_complex).astype(jnp.bfloat16)]
  transfers between devices with their start and end apart: 13 -> 13, of which waited for: 7 -> 6; matrix products, arithmetic and copies ran while one was open for 17% -> 20% of each run, Pallas kernels for 0% -> 0%
where the time goes in v14:
time: 96 us; the launch traced here: 94.2 us
  starting transfers between devices  26 us (27%)
  waiting for transfers between devices  16.7 us (17%)
  local copies, waits for them, and re-layouts  14.9 us (16%)
  Pallas kernels  14.4 us (15%)
  other arithmetic  8.7 us (9%)
  matrix products  8.15 us (8%)
  between operations  5.29 us (6%)
    ppermute x8, starting transfers between devices, send(): return lax.ppermute(value, axis, pairs)  22.9 us
    ppermute x1, waiting for transfers between devices, gather_rows(): lax.ppermute(jnp.stack([shard, early]), 'blk', [(s, s ^ (2 if s % 2 else...  10.5 us
    pallas_call x1, Pallas kernels, back_fused(): pl.pallas_call(back_kernel, out_shape=jax.ShapeDtypeStruct((rows, width),...  7.63 us
    pallas_call x1, Pallas kernels, pose_fused(): pl.pallas_call(pose_kernel, out_shape=(jax.ShapeDtypeStruct((1, pair_rows...  6.76 us
    dynamic_update_slice x6, local copies, waits for them, and re-layouts, gather_rows(): full = lax.dynamic_update_slice(full, pieces[k][None], (at, 0, 0))  5.03 us
    dot_general x1, matrix products, shards(): jnp.dot(receptor, full_both.reshape(-1, full_both.shape[2]), preferred_el...  4.52 us
    ppermute x8, waiting for transfers between devices, send(): return lax.ppermute(value, axis, pairs)  3.63 us
    dot_general x1, matrix products, local_state(): lax.dot_general(key_feat, val_round, (((0,), (0,)), ((), ())), preferred_...  2.88 us
  transfers between devices with their start and end apart: 13, of which 6 were waited for; matrix products, arithmetic and copies ran while one was open for 20% of the time, Pallas kernels for 0%

profile of v14, /device:TPU:16, one launch (start us, length us, event | category | flops | bytes accessed | tf_op | source)
XLA Modules:
  0.0 94.2 jit_solution(8257296944228214270)
XLA Ops:
  0.7 1.1 %constant_dynamic-update-slice_fusion.1 = bf16[128,2048]{1,0:T(8,128)(2,1)S(1)} fusion(bf16[128,1024]{1,0:T(8,128)(2,1)} %param.12), kind=kLoop, calls=%fused_computation.43 | loop fusion | bytes 524288
  1.7 1.0 %constant_dynamic-update-slice_fusion = bf16[128,2048]{1,0:T(8,128)(2,1)S(1)} fusion(bf16[128,2048]{1,0:T(8,128)(2,1)S(1)} %constant_dynamic-update-slice_fusion.1, bf16[128,1024]{1,0:T(8,128)(2,1)} %param.13), kind=kLoop, calls=%fused_computation.42 | loop fusion | bytes 524288 | tf_op jit(solution)/shard_map/concatenate | solution.py:284
  2.7 1.6 %collective-permute-start.1 = (bf16[128,2048]{1,0:T(8,128)(2,1)S(1)}, bf16[128,2048]{1,0:T(8,128)(2,1)S(1)}, u32[]{:S(2)}, u32[]{:S(2)}) collective-permute-start(bf16[128,2048]{1,0:T(8,128)(2,1)S(1)} %constant_dynamic-update-slice_fusion), channel_id=1, source_target_pairs={{0,2},{1,5},{2,0},{3,7},{4,6},{5,1},{6,4},{7,3},{8,10},{9,13},{10,... | collective-permute-start | bytes 1572872 | tf_op jit(solution)/shard_map/ppermute | solution.py:263
  4.2 0.0 collective-permute-start
  4.2 2.5 %broadcast_in_dim.76 = bf16[8,128,2048]{2,1,0:T(8,128)(2,1)} broadcast(bf16[]{:T(256)} %constant.229.clone.1), dimensions={} | broadcast | bytes 4194306 | tf_op jit(solution)/shard_map/broadcast_in_dim | solution.py:274
  6.7 0.8 constant_dynamic-update-slice_fusion.3
  7.6 0.7 fusion.18
  9.5 0.1 constant_dynamic-slice_fusion.1
  9.6 2.3 %collective-permute-done.1 = bf16[128,2048]{1,0:T(8,128)(2,1)S(1)} collective-permute-done((bf16[128,2048]{1,0:T(8,128)(2,1)S(1)}, bf16[128,2048]{1,0:T(8,128)(2,1)S(1)}, u32[]{:S(2)}, u32[]{:S(2)}) %collective-permute-start.1) | collective-permute-done | bytes 524320 | tf_op jit(solution)/shard_map/ppermute | solution.py:263
  11.9 0.1 pad_maximum_fusion
  12.0 1.6 %collective-permute-start.3 = (bf16[2,128,2048]{2,1,0:T(8,128)(2,1)S(1)}, bf16[2,128,2048]{2,1,0:T(8,128)(2,1)S(1)}, u32[]{:S(2)}, u32[]{:S(2)}) collective-permute-start(bf16[2,128,2048]{2,1,0:T(8,128)(2,1)S(1)} %pad_maximum_fusion), channel_id=1, source_target_pairs={{0,4},{1,3},{2,6},{3,1},{4,0},{5,7},{6,2},{7,5},{8,12},{9,11},{10,... | collective-permute-start | bytes 3145736 | tf_op jit(solution)/shard_map/ppermute | solution.py:265
  13.6 0.8 bitcast_dynamic-update-slice_fusion.1
  14.5 0.8 constant_dynamic-update-slice_fusion.2
  15.3 0.2 collective-permute-done.2
  15.5 0.8 bitcast_dynamic-update-slice_fusion
  16.4 10.5 %collective-permute-done.3 = bf16[2,128,2048]{2,1,0:T(8,128)(2,1)S(1)} collective-permute-done((bf16[2,128,2048]{2,1,0:T(8,128)(2,1)S(1)}, bf16[2,128,2048]{2,1,0:T(8,128)(2,1)S(1)}, u32[]{:S(2)}, u32[]{:S(2)}) %collective-permute-start.3) | collective-permute-done | bytes 1048608 | tf_op jit(solution)/shard_map/ppermute | solution.py:265
  26.9 0.0 collective-permute-start.4
  26.9 0.8 slice_dynamic-update-slice_fusion.3
  27.7 0.8 slice_dynamic-update-slice_fusion.2
  28.6 4.5 %fusion.20 = f32[2048,512]{0,1:T(8,128)S(1)} fusion(bf16[512,1024]{1,0:T(8,128)(2,1)S(1)} %copy-done.3, bf16[1024,2048]{1,0:T(8,128)(2,1)} %bitcast.5), kind=kOutput, calls=%fused_computation.55 | convolution fusion | flops 2147483648 | bytes 9437184 | tf_op jit(solution)/shard_map/dot_general | solution.py:290
  33.1 0.7 bitcast_add_fusion
  33.9 2.2 %convert_reduce_fusion = (f32[1024]{0:T(1024)S(1)}, bf16[512,1024]{1,0:T(8,128)(2,1)S(1)}, f32[512,1024]{1,0:T(8,128)}) fusion(f32[512,2048]{1,0:T(8,128)S(1)} %bitcast_add_fusion), kind=kLoop, calls=%fused_computation.4 | loop fusion | flops 3668992 | bytes 5246976 | tf_op jit(solution)/shard_map/reduce_sum | solution.py:38
  36.1 2.9 %fusion = f32[1024,1024]{1,0:T(8,128)} fusion(bf16[512,1024]{1,0:T(8,128)(2,1)S(1)} %get-tuple-element.87.feat_ref, s32[1024]{0:T(1024)S(1)} %get-tuple-element.104, s32[1024]{0:T(1024)S(1)} %get-tuple-element.105, pred[1024]{0:T(1024)(128)(4,1)S(1)} %fusion.16, f32[512,2048]{1,0:T(8,128)S(1)} %bitcast_add_fusion), kind=kOutput, calls=%fused_computation.2 | convolution fusion | flops 1077936128 | bytes 6309888 | tf_op jit(solution)/shard_map/dot_general | solution.py:32
  39.0 2.5 %reduce_sum.18 = f32[64,1024]{1,0:T(8,128)S(1)} reduce(f32[16,64,1024]{2,1,0:T(8,128)} %bitcast.35, f32[]{:T(128)} %constant.236.clone.1), dimensions={0}, to_apply=%region_0.1 | reduce | flops 983040 | bytes 4456452 | tf_op jit(solution)/shard_map/reduce_sum | solution.py:39
  41.5 0.6 collective-permute-start.5
  45.4 2.9 %collective-permute-start.8 = (bf16[65,1024]{1,0:T(8,128)(2,1)S(1)}, bf16[65,1024]{1,0:T(8,128)(2,1)S(1)}, u32[]{:S(2)}, u32[]{:S(2)}) collective-permute-start(bf16[65,1024]{1,0:T(8,128)(2,1)S(1)} %get-tuple-element.95), channel_id=1, source_target_pairs={{1,4},{3,6},{5,8},{7,10},{9,12},{11,14},{13,16},{15,18},{17,20},{1... | collective-permute-start | bytes 399368 | tf_op jit(solution)/shard_map/ppermute | solution.py:59
  48.4 0.1 add_convert_fusion.3
  48.5 3.4 %collective-permute-start.6 = (bf16[65,1024]{1,0:T(8,128)(2,1)S(1)}, bf16[65,1024]{1,0:T(8,128)(2,1)S(1)}, u32[]{:S(2)}, u32[]{:S(2)}) collective-permute-start(bf16[65,1024]{1,0:T(8,128)(2,1)S(1)} %get-tuple-element.93), channel_id=1, source_target_pairs={{0,2},{1,3},{2,4},{3,5},{4,6},{5,7},{6,8},{7,9},{8,10},{9,11},{10,... | collective-permute-start | bytes 399368 | tf_op jit(solution)/shard_map/ppermute | solution.py:59
  51.9 4.3 %collective-permute-start.7 = (bf16[65,1024]{1,0:T(8,128)(2,1)S(1)}, bf16[65,1024]{1,0:T(8,128)(2,1)S(1)}, u32[]{:S(2)}, u32[]{:S(2)}) collective-permute-start(bf16[65,1024]{1,0:T(8,128)(2,1)S(1)} %get-tuple-element.94), channel_id=1, source_target_pairs={{2,0},{3,1},{4,2},{5,3},{6,4},{7,5},{8,6},{9,7},{10,8},{11,9},{12,... | collective-permute-start | bytes 399368 | tf_op jit(solution)/shard_map/ppermute | solution.py:59
  56.1 0.8 slice_dynamic-update-slice_fusion.1
  57.0 0.0 collective-permute-done.8
  57.0 1.6 %collective-permute-done.6 = bf16[65,1024]{1,0:T(8,128)(2,1)S(1)} collective-permute-done((bf16[65,1024]{1,0:T(8,128)(2,1)S(1)}, bf16[65,1024]{1,0:T(8,128)(2,1)S(1)}, u32[]{:S(2)}, u32[]{:S(2)}) %collective-permute-start.6) | collective-permute-done | bytes 133152 | tf_op jit(solution)/shard_map/ppermute | solution.py:59
  58.6 1.7 %collective-permute-done.7 = bf16[65,1024]{1,0:T(8,128)(2,1)S(1)} collective-permute-done((bf16[65,1024]{1,0:T(8,128)(2,1)S(1)}, bf16[65,1024]{1,0:T(8,128)(2,1)S(1)}, u32[]{:S(2)}, u32[]{:S(2)}) %collective-permute-start.7) | collective-permute-done | bytes 133152 | tf_op jit(solution)/shard_map/ppermute | solution.py:59
  60.3 0.8 fusion.4.state_ref
  61.1 6.8 %shard_map.103 = (f32[1,256]{1,0:T(1,128)}, bf16[128,1024]{1,0:T(8,128)(2,1)}, f32[65,1024]{1,0:T(8,128)}) custom-call(bf16[128,1024]{1,0:T(8,128)(2,1)} %pose_ref.1, s32[2,256]{1,0:T(2,128)} %bitcast.43, f32[65,1024]{1,0:T(8,128)} %fusion.4.state_ref, bf16[1024,1024]{1,0:T(8,128)(2,1)} %query_ref.1, f32[1,1024]{1,0:T(1,128)} %bitcast.42), custom_call_target="tpu_custom_call" | custom-call | tf_op jit(solution)/shard_map/pallas_call | solution.py:207
  67.9 1.0 %convert_element_type.68 = bf16[65,1024]{1,0:T(8,128)(2,1)S(1)} convert(f32[65,1024]{1,0:T(8,128)} %get-tuple-element.8) | non-fusion elementwise | flops 66560 | bytes 399360 | tf_op jit(solution)/shard_map/convert_element_type | solution.py:75
  69.0 0.1 collective-permute-start.9
  69.1 3.8 %collective-permute-start.12 = (bf16[65,1024]{1,0:T(8,128)(2,1)S(1)}, bf16[65,1024]{1,0:T(8,128)(2,1)S(1)}, u32[]{:S(2)}, u32[]{:S(2)}) collective-permute-start(bf16[65,1024]{1,0:T(8,128)(2,1)S(1)} %select_convert_fusion.1), channel_id=1, source_target_pairs={{1,4},{3,6},{5,8},{7,10},{9,12},{11,14},{13,16},{15,18},{17,20},{1... | collective-permute-start | bytes 399368 | tf_op jit(solution)/shard_map/ppermute | solution.py:59
  72.9 0.0 collective-permute-done.9
  72.9 1.1 %add_convert_fusion.1 = (bf16[65,1024]{1,0:T(8,128)(2,1)S(1)}, bf16[65,1024]{1,0:T(8,128)(2,1)S(1)}) fusion(f32[65,1024]{1,0:T(8,128)} %get-tuple-element.8, bf16[65,1024]{1,0:T(8,128)(2,1)S(1)} %collective-permute-done.9, pred[]{:T(512)S(6)} %and.118, pred[]{:T(512)S(6)} %eq.44, pred[]{:T(512)S(6)} %and.116, pred[]{:T(512)S(6)} %and.122, pred[]{:T(512)S(6)} %and.121), kind=kLoop, calls=%fused_computation.31 | loop fusion | flops 732160 | bytes 665605 | tf_op jit(solution)/shard_map/convert_element_type | solution.py:90
  74.0 4.3 %collective-permute-start.10 = (bf16[65,1024]{1,0:T(8,128)(2,1)S(1)}, bf16[65,1024]{1,0:T(8,128)(2,1)S(1)}, u32[]{:S(2)}, u32[]{:S(2)}) collective-permute-start(bf16[65,1024]{1,0:T(8,128)(2,1)S(1)} %get-tuple-element.91), channel_id=1, source_target_pairs={{0,2},{1,3},{2,4},{3,5},{4,6},{5,7},{6,8},{7,9},{8,10},{9,11},{10,... | collective-permute-start | bytes 399368 | tf_op jit(solution)/shard_map/ppermute | solution.py:59
  78.3 3.5 %collective-permute-start.11 = (bf16[65,1024]{1,0:T(8,128)(2,1)S(1)}, bf16[65,1024]{1,0:T(8,128)(2,1)S(1)}, u32[]{:S(2)}, u32[]{:S(2)}) collective-permute-start(bf16[65,1024]{1,0:T(8,128)(2,1)S(1)} %get-tuple-element.92), channel_id=1, source_target_pairs={{2,0},{3,1},{4,2},{5,3},{6,4},{7,5},{8,6},{9,7},{10,8},{11,9},{12,... | collective-permute-start | bytes 399368 | tf_op jit(solution)/shard_map/ppermute | solution.py:59
  81.8 0.9 slice_dynamic-update-slice_fusion
  82.7 2.8 %slice.72.val_ref = bf16[512,1024]{1,0:T(8,128)(2,1)} slice(f32[512,2048]{1,0:T(8,128)} %copy-done), slice={[0:512], [1024:2048]} | slice | bytes 2097152 | tf_op jit(solution)/shard_map/slice | solution.py:303
  85.5 0.0 collective-permute-done.10
  85.5 0.3 collective-permute-done.11
  85.8 0.8 fusion.9.grad_ref
  86.6 7.6 %shard_map.104 = bf16[512,1024]{1,0:T(8,128)(2,1)} custom-call(bf16[512,1024]{1,0:T(8,128)(2,1)} %copy-done.2, bf16[512,1024]{1,0:T(8,128)(2,1)} %slice.72.val_ref, f32[512,1024]{1,0:T(8,128)} %get-tuple-element.88.keys_ref, bf16[65,1024]{1,0:T(8,128)(2,1)} %fusion.9.grad_ref, bf16[1024,2048]{1,0:T(8,128)(2,1)} %bitcast.25.full_ref), custom_call_target="tpu_custom_call" | custom-call | tf_op jit(solution)/shard_map/pallas_call | solution.py:244
  (19 shorter events, 0.1 us)
Async XLA Ops:
  0.6 7.0 %copy-start.4 = (s32[32]{0:T(128)S(1)}, s32[32]{0:T(128)}, u32[]{:S(2)}) copy-start(s32[32]{0:T(128)} %param.11) | copy-start | bytes 388
  0.6 8.8 %copy-start.3 = (bf16[512,1024]{1,0:T(8,128)(2,1)S(1)}, bf16[512,1024]{1,0:T(8,128)(2,1)}, u32[]{:S(2)}) copy-start(bf16[512,1024]{1,0:T(8,128)(2,1)} %param.8) | copy-start | bytes 3145732
  2.7 9.2 %collective-permute-start.1 = (bf16[128,2048]{1,0:T(8,128)(2,1)S(1)}, bf16[128,2048]{1,0:T(8,128)(2,1)S(1)}, u32[]{:S(2)}, u32[]{:S(2)}) collective-permute-start(bf16[128,2048]{1,0:T(8,128)(2,1)S(1)} %constant_dynamic-update-slice_fusion), channel_id=1, source_target_pairs={{0,2},{1,5},{2,0},{3,7},{4,6},{5,1},{6,4},{7,3},{8,10},{9,13},{10,... | collective-permute-start | bytes 1572872 | tf_op jit(solution)/shard_map/ppermute | solution.py:263
  4.2 9.4 %collective-permute-start = (bf16[128,2048]{1,0:T(8,128)(2,1)S(1)}, bf16[128,2048]{1,0:T(8,128)(2,1)S(1)}, u32[]{:S(2)}, u32[]{:S(2)}) collective-permute-start(bf16[128,2048]{1,0:T(8,128)(2,1)S(1)} %constant_dynamic-update-slice_fusion), channel_id=1, source_target_pairs={{0,1},{1,0},{2,3},{3,2},{4,5},{5,4},{6,7},{7,6},{8,9},{9,8},{10,11... | collective-permute-start | bytes 1572872 | tf_op jit(solution)/shard_map/ppermute | solution.py:262
  12.0 14.9 %collective-permute-start.3 = (bf16[2,128,2048]{2,1,0:T(8,128)(2,1)S(1)}, bf16[2,128,2048]{2,1,0:T(8,128)(2,1)S(1)}, u32[]{:S(2)}, u32[]{:S(2)}) collective-permute-start(bf16[2,128,2048]{2,1,0:T(8,128)(2,1)S(1)} %pad_maximum_fusion), channel_id=1, source_target_pairs={{0,4},{1,3},{2,6},{3,1},{4,0},{5,7},{6,2},{7,5},{8,12},{9,11},{10,... | collective-permute-start | bytes 3145736 | tf_op jit(solution)/shard_map/ppermute | solution.py:265
  13.6 1.9 %collective-permute-start.2 = (bf16[128,2048]{1,0:T(8,128)(2,1)S(1)}, bf16[128,2048]{1,0:T(8,128)(2,1)S(1)}, u32[]{:S(2)}, u32[]{:S(2)}) collective-permute-start(bf16[128,2048]{1,0:T(8,128)(2,1)S(1)} %collective-permute-done.1), channel_id=1, source_target_pairs={{0,1},{1,0},{2,3},{3,2},{4,5},{5,4},{6,7},{7,6},{8,9},{9,8},{10,11... | collective-permute-start | bytes 1572872 | tf_op jit(solution)/shard_map/ppermute | solution.py:264
  26.9 6.2 %collective-permute-start.4 = (bf16[2,128,2048]{2,1,0:T(8,128)(2,1)S(1)}, bf16[2,128,2048]{2,1,0:T(8,128)(2,1)S(1)}, u32[]{:S(2)}, u32[]{:S(2)}) collective-permute-start(bf16[2,128,2048]{2,1,0:T(8,128)(2,1)S(1)} %collective-permute-done.3), channel_id=1, source_target_pairs={{0,1},{1,0},{2,3},{3,2},{4,5},{5,4},{6,7},{7,6},{8,9},{9,8},{10,11... | collective-permute-start | bytes 3145736 | tf_op jit(solution)/shard_map/ppermute | solution.py:268
  33.9 5.1 %copy-start = (f32[512,2048]{1,0:T(8,128)}, f32[512,2048]{1,0:T(8,128)S(1)}, u32[]{:S(2)}) copy-start(f32[512,2048]{1,0:T(8,128)S(1)} %bitcast_add_fusion) | copy-start | bytes 12582916
  36.1 2.9 %copy-start.2 = (bf16[512,1024]{1,0:T(8,128)(2,1)}, bf16[512,1024]{1,0:T(8,128)(2,1)S(1)}, u32[]{:S(2)}) copy-start(bf16[512,1024]{1,0:T(8,128)(2,1)S(1)} %get-tuple-element.87.feat_ref) | copy-start | bytes 3145732
  41.5 6.8 %collective-permute-start.5 = (bf16[65,1024]{1,0:T(8,128)(2,1)S(1)}, bf16[65,1024]{1,0:T(8,128)(2,1)S(1)}, u32[]{:S(2)}, u32[]{:S(2)}) collective-permute-start(bf16[65,1024]{1,0:T(8,128)(2,1)S(1)} %get-tuple-element.96), channel_id=1, source_target_pairs={{0,1},{1,0},{2,3},{3,2},{4,5},{5,4},{6,7},{7,6},{8,9},{9,8},{10,11... | collective-permute-start | bytes 399368 | tf_op jit(solution)/shard_map/ppermute | solution.py:59
  45.4 11.6 %collective-permute-start.8 = (bf16[65,1024]{1,0:T(8,128)(2,1)S(1)}, bf16[65,1024]{1,0:T(8,128)(2,1)S(1)}, u32[]{:S(2)}, u32[]{:S(2)}) collective-permute-start(bf16[65,1024]{1,0:T(8,128)(2,1)S(1)} %get-tuple-element.95), channel_id=1, source_target_pairs={{1,4},{3,6},{5,8},{7,10},{9,12},{11,14},{13,16},{15,18},{17,20},{1... | collective-permute-start | bytes 399368 | tf_op jit(solution)/shard_map/ppermute | solution.py:59
  48.5 10.1 %collective-permute-start.6 = (bf16[65,1024]{1,0:T(8,128)(2,1)S(1)}, bf16[65,1024]{1,0:T(8,128)(2,1)S(1)}, u32[]{:S(2)}, u32[]{:S(2)}) collective-permute-start(bf16[65,1024]{1,0:T(8,128)(2,1)S(1)} %get-tuple-element.93), channel_id=1, source_target_pairs={{0,2},{1,3},{2,4},{3,5},{4,6},{5,7},{6,8},{7,9},{8,10},{9,11},{10,... | collective-permute-start | bytes 399368 | tf_op jit(solution)/shard_map/ppermute | solution.py:59
  51.9 8.5 %collective-permute-start.7 = (bf16[65,1024]{1,0:T(8,128)(2,1)S(1)}, bf16[65,1024]{1,0:T(8,128)(2,1)S(1)}, u32[]{:S(2)}, u32[]{:S(2)}) collective-permute-start(bf16[65,1024]{1,0:T(8,128)(2,1)S(1)} %get-tuple-element.94), channel_id=1, source_target_pairs={{2,0},{3,1},{4,2},{5,3},{6,4},{7,5},{8,6},{9,7},{10,8},{11,9},{12,... | collective-permute-start | bytes 399368 | tf_op jit(solution)/shard_map/ppermute | solution.py:59
  67.9 17.9 %copy-start.1 = (f32[65,1024]{1,0:T(8,128)S(1)}, f32[65,1024]{1,0:T(8,128)}, u32[]{:S(2)}) copy-start(f32[65,1024]{1,0:T(8,128)} %get-tuple-element.8) | copy-start | bytes 798724
  69.0 3.9 %collective-permute-start.9 = (bf16[65,1024]{1,0:T(8,128)(2,1)S(1)}, bf16[65,1024]{1,0:T(8,128)(2,1)S(1)}, u32[]{:S(2)}, u32[]{:S(2)}) collective-permute-start(bf16[65,1024]{1,0:T(8,128)(2,1)S(1)} %convert_element_type.68), channel_id=1, source_target_pairs={{0,1},{1,0},{2,3},{3,2},{4,5},{5,4},{6,7},{7,6},{8,9},{9,8},{10,11... | collective-permute-start | bytes 399368 | tf_op jit(solution)/shard_map/ppermute | solution.py:59
  69.1 16.5 %collective-permute-start.12 = (bf16[65,1024]{1,0:T(8,128)(2,1)S(1)}, bf16[65,1024]{1,0:T(8,128)(2,1)S(1)}, u32[]{:S(2)}, u32[]{:S(2)}) collective-permute-start(bf16[65,1024]{1,0:T(8,128)(2,1)S(1)} %select_convert_fusion.1), channel_id=1, source_target_pairs={{1,4},{3,6},{5,8},{7,10},{9,12},{11,14},{13,16},{15,18},{17,20},{1... | collective-permute-start | bytes 399368 | tf_op jit(solution)/shard_map/ppermute | solution.py:59
  74.0 11.5 %collective-permute-start.10 = (bf16[65,1024]{1,0:T(8,128)(2,1)S(1)}, bf16[65,1024]{1,0:T(8,128)(2,1)S(1)}, u32[]{:S(2)}, u32[]{:S(2)}) collective-permute-start(bf16[65,1024]{1,0:T(8,128)(2,1)S(1)} %get-tuple-element.91), channel_id=1, source_target_pairs={{0,2},{1,3},{2,4},{3,5},{4,6},{5,7},{6,8},{7,9},{8,10},{9,11},{10,... | collective-permute-start | bytes 399368 | tf_op jit(solution)/shard_map/ppermute | solution.py:59
  78.3 7.5 %collective-permute-start.11 = (bf16[65,1024]{1,0:T(8,128)(2,1)S(1)}, bf16[65,1024]{1,0:T(8,128)(2,1)S(1)}, u32[]{:S(2)}, u32[]{:S(2)}) collective-permute-start(bf16[65,1024]{1,0:T(8,128)(2,1)S(1)} %get-tuple-element.92), channel_id=1, source_target_pairs={{2,0},{3,1},{4,2},{5,3},{6,4},{7,5},{8,6},{9,7},{10,8},{11,9},{12,... | collective-permute-start | bytes 399368 | tf_op jit(solution)/shard_map/ppermute | solution.py:59

commit v15 on v11

--- a/solution.py
+++ b/solution.py
@@ -232,9 +232,7 @@
         both_ref[:, cols] = (feat_grad * slope(keys_ref[:, cols])).astype(both_ref.dtype)
         value_grad = jnp.dot(feat_ref[:, cols], block, preferred_element_type=jnp.float32)
         both_ref[:, width + g * lanes : width + (g + 1) * lanes] = value_grad.astype(both_ref.dtype)
-    total = lax.dot_general(
-        both_ref[...], full_ref[...], (((1,), (1,)), ((), ())), preferred_element_type=jnp.float32
-    )
+    total = jnp.dot(both_ref[...], full_ref[...], preferred_element_type=jnp.float32)
     out_ref[...] = total.astype(out_ref.dtype)
 
 
@@ -245,7 +243,7 @@
         out_shape=jax.ShapeDtypeStruct((rows, width), jnp.bfloat16),
         scratch_shapes=[pltpu.VMEM((rows, 2 * width), jnp.bfloat16)],
         interpret=interpret,
-    )(key_feat, val_round, keys, state_grad, full_both)
+    )(key_feat, val_round, keys, state_grad, full_both.T)
 
 
 def gather_rows(shard):

time: 95.9 us -> 326 us (3.40)
  the two profiles are of different devices: /device:TPU:16 before, /device:TPU:7 now
where the time goes in v15:
time: 326 us; the launch traced here: 320 us
  local copies, waits for them, and re-layouts  246 us (75%)
  starting transfers between devices  27.1 us (8%)
  Pallas kernels  14.4 us (4%)
  waiting for transfers between devices  10.6 us (3%)
  matrix products  8.36 us (3%)
  other arithmetic  7.4 us (2%)
  between operations  5.57 us (2%)
    dynamic_update_slice x6, local copies, waits for them, and re-layouts, gather_rows(): full = lax.dynamic_update_slice(full, pieces[k][None], (at, 0, 0))  163 us
    dynamic_update_slice x2, local copies, waits for them, and re-layouts, shards(): full_both = lax.dynamic_update_slice(full_both, pieces[k][None], (at, 0, 0))  54.3 us
    ppermute x8, starting transfers between devices, send(): return lax.ppermute(value, axis, pairs)  24.3 us
    ppermute x1, waiting for transfers between devices, gather_rows(): lax.ppermute(shard, 'blk', [(s, s ^ (4 if s % 2 else 2)) for s in range(c...  8.1 us
    pallas_call x1, Pallas kernels, back_fused(): pl.pallas_call(back_kernel, out_shape=jax.ShapeDtypeStruct((rows, width),...  7.63 us
    unnamed x12, local copies, waits for them, and re-layouts  7.06 us
    pallas_call x1, Pallas kernels, pose_fused(): pl.pallas_call(pose_kernel, out_shape=(jax.ShapeDtypeStruct((1, pair_rows...  6.77 us
  transfers between devices with their start and end apart: 13, of which 3 were waited for; matrix products, arithmetic and copies ran while one was open for 77% of the time, Pallas kernels for 0%

profile of v15, /device:TPU:7, one launch (start us, length us, event | category | flops | bytes accessed | tf_op | source)
XLA Modules:
  0.0 319.9 jit_solution(8992460542338075244)
XLA Ops:
  0.6 1.0 constant_dynamic-update-slice_fusion.1
  1.6 1.0 constant_dynamic-update-slice_fusion
  2.9 8.1 %collective-permute-done.1 = bf16[128,2048]{1,0:T(8,128)(2,1)S(1)} collective-permute-done((bf16[128,2048]{1,0:T(8,128)(2,1)S(1)}, bf16[128,2048]{1,0:T(8,128)(2,1)S(1)}, u32[]{:S(2)}, u32[]{:S(2)}) %collective-permute-start.1) | collective-permute-done | bytes 524320 | tf_op jit(solution)/shard_map/ppermute | solution.py:260
  11.0 1.1 pad_maximum_fusion
  12.3 1.8 collective-permute-start
  14.1 0.7 copy.23
  14.9 0.7 fusion.19
  16.9 2.3 broadcast_in_dim.72
  19.2 27.1 %dynamic_update_slice.24 = bf16[8,128,2048]{1,0,2:T(8,128)(2,1)} dynamic-update-slice(bf16[8,128,2048]{1,0,2:T(8,128)(2,1)} %broadcast_in_dim.72, bf16[1,128,2048]{1,0,2:T(2,128)(2,1)S(1)} %copy.23, s32[]{:T(128)S(6)} %select_n.205, s32[]{:T(128)} %constant.200.clone.1, s32[]{:T(128)} %constant.200.clone.1) | dynamic-update-slice | bytes 1048580 | tf_op jit(solution)/shard_map/dynamic_update_slice | solution.py:274
  46.4 1.0 constant_dynamic-slice_fusion.1
  47.3 0.8 copy.25
  48.1 0.8 copy-done.3
  48.9 2.3 copy.24
  51.3 27.2 %dynamic_update_slice.25 = bf16[8,128,2048]{1,0,2:T(8,128)(2,1)} dynamic-update-slice(bf16[8,128,2048]{1,0,2:T(8,128)(2,1)} %dynamic_update_slice.24, bf16[1,128,2048]{1,0,2:T(2,128)(2,1)S(1)} %copy.24, s32[]{:T(128)S(6)} %select_n.206, s32[]{:T(128)} %constant.200.clone.1, s32[]{:T(128)} %constant.200.clone.1) | dynamic-update-slice | bytes 1048580 | tf_op jit(solution)/shard_map/dynamic_update_slice | solution.py:274
  78.4 27.1 %dynamic_update_slice.26 = bf16[8,128,2048]{1,0,2:T(8,128)(2,1)} dynamic-update-slice(bf16[8,128,2048]{1,0,2:T(8,128)(2,1)} %dynamic_update_slice.25, bf16[1,128,2048]{1,0,2:T(2,128)(2,1)S(1)} %copy.25, s32[]{:T(128)S(6)} %select_n.209, s32[]{:T(128)} %constant.200.clone.1, s32[]{:T(128)} %constant.200.clone.1) | dynamic-update-slice | bytes 1048580 | tf_op jit(solution)/shard_map/dynamic_update_slice | solution.py:274
  105.6 2.3 copy.26
  107.9 27.2 %dynamic_update_slice.27 = bf16[8,128,2048]{1,0,2:T(8,128)(2,1)} dynamic-update-slice(bf16[8,128,2048]{1,0,2:T(8,128)(2,1)} %dynamic_update_slice.26, bf16[1,128,2048]{1,0,2:T(2,128)(2,1)S(1)} %copy.26, s32[]{:T(128)S(6)} %select_n.210, s32[]{:T(128)} %constant.200.clone.1, s32[]{:T(128)} %constant.200.clone.1) | dynamic-update-slice | bytes 1048580 | tf_op jit(solution)/shard_map/dynamic_update_slice | solution.py:274
  135.6 2.1 fusion.18
  137.7 0.7 copy.27
  138.4 2.4 copy.28
  140.8 27.2 %dynamic_update_slice.28 = bf16[8,128,2048]{1,0,2:T(8,128)(2,1)} dynamic-update-slice(bf16[8,128,2048]{1,0,2:T(8,128)(2,1)} %dynamic_update_slice.27, bf16[1,128,2048]{1,0,2:T(2,128)(2,1)S(1)} %copy.27, s32[]{:T(128)S(6)} %select_n.211, s32[]{:T(128)} %constant.200.clone.1, s32[]{:T(128)} %constant.200.clone.1) | dynamic-update-slice | bytes 1048580 | tf_op jit(solution)/shard_map/dynamic_update_slice | solution.py:274
  168.0 27.1 %dynamic_update_slice.29 = bf16[8,128,2048]{1,0,2:T(8,128)(2,1)} dynamic-update-slice(bf16[8,128,2048]{1,0,2:T(8,128)(2,1)} %dynamic_update_slice.28, bf16[1,128,2048]{1,0,2:T(2,128)(2,1)S(1)} %copy.28, s32[]{:T(128)S(6)} %select_n.212, s32[]{:T(128)} %constant.200.clone.1, s32[]{:T(128)} %constant.200.clone.1) | dynamic-update-slice | bytes 1048580 | tf_op jit(solution)/shard_map/dynamic_update_slice | solution.py:274
  195.1 4.9 %fusion = f32[2048,512]{0,1:T(8,128)S(1)} fusion(bf16[512,1024]{1,0:T(8,128)(2,1)} %param.8, bf16[256,8,8,128]{3,2,1,0:T(8,128)(2,1)} %bitcast.49), kind=kOutput, calls=%fused_computation.1 | convolution fusion | flops 2147483648 | bytes 9437184 | tf_op jit(solution)/shard_map/dot_general | solution.py:287
  200.0 0.8 bitcast_add_fusion
  200.7 1.9 convert_reduce_fusion
  202.8 1.5 copy.30
  204.3 1.3 copy.31
  205.6 2.8 fusion.20
  208.4 1.2 copy.36
  212.3 4.5 %collective-permute-start.8 = (bf16[65,1024]{1,0:T(8,128)(2,1)S(1)}, bf16[65,1024]{1,0:T(8,128)(2,1)S(1)}, u32[]{:S(2)}, u32[]{:S(2)}) collective-permute-start(bf16[65,1024]{1,0:T(8,128)(2,1)S(1)} %get-tuple-element.99), channel_id=1, source_target_pairs={{1,4},{3,6},{5,8},{7,10},{9,12},{11,14},{13,16},{15,18},{17,20},{1... | collective-permute-start | bytes 399368 | tf_op jit(solution)/shard_map/ppermute | solution.py:58
  217.0 2.2 collective-permute-start.7
  219.2 5.1 %collective-permute-start.6 = (bf16[65,1024]{1,0:T(8,128)(2,1)S(1)}, bf16[65,1024]{1,0:T(8,128)(2,1)S(1)}, u32[]{:S(2)}, u32[]{:S(2)}) collective-permute-start(bf16[65,1024]{1,0:T(8,128)(2,1)S(1)} %get-tuple-element.97), channel_id=1, source_target_pairs={{0,2},{1,3},{2,4},{3,5},{4,6},{5,7},{6,8},{7,9},{8,10},{9,11},{10,... | collective-permute-start | bytes 399368 | tf_op jit(solution)/shard_map/ppermute | solution.py:58
  225.0 0.9 collective-permute-done.7
  225.8 1.7 collective-permute-done.6
  227.5 0.8 fusion.6.state_ref
  228.3 6.8 %shard_map.103 = (f32[1,256]{1,0:T(1,128)}, bf16[128,1024]{1,0:T(8,128)(2,1)}, f32[65,1024]{1,0:T(8,128)}) custom-call(bf16[128,1024]{1,0:T(8,128)(2,1)} %pose_ref.1, s32[2,256]{1,0:T(2,128)} %bitcast.64, f32[65,1024]{1,0:T(8,128)} %fusion.6.state_ref, bf16[1024,1024]{1,0:T(8,128)(2,1)} %query_ref.1, f32[1,1024]{1,0:T(1,128)} %bitcast.63), custom_call_target="tpu_custom_call" | custom-call | tf_op jit(solution)/shard_map/pallas_call | solution.py:206
  235.1 1.0 convert_element_type.68
  236.9 5.1 %collective-permute-start.12 = (bf16[65,1024]{1,0:T(8,128)(2,1)}, bf16[65,1024]{1,0:T(8,128)(2,1)S(1)}, u32[]{:S(2)}, u32[]{:S(2)}) collective-permute-start(bf16[65,1024]{1,0:T(8,128)(2,1)} %select_convert_fusion.1), channel_id=1, source_target_pairs={{1,4},{3,6},{5,8},{7,10},{9,12},{11,14},{13,16},{15,18},{17,20},{1... | collective-permute-start | bytes 399368 | tf_op jit(solution)/shard_map/ppermute | solution.py:58
  242.1 1.1 add_convert_fusion.1
  243.1 3.0 collective-permute-start.11
  246.1 4.1 %collective-permute-start.10 = (bf16[65,1024]{1,0:T(8,128)(2,1)S(1)}, bf16[65,1024]{1,0:T(8,128)(2,1)S(1)}, u32[]{:S(2)}, u32[]{:S(2)}) collective-permute-start(bf16[65,1024]{1,0:T(8,128)(2,1)S(1)} %get-tuple-element.95), channel_id=1, source_target_pairs={{0,2},{1,3},{2,4},{3,5},{4,6},{5,7},{6,8},{7,9},{8,10},{9,11},{10,... | collective-permute-start | bytes 399368 | tf_op jit(solution)/shard_map/ppermute | solution.py:58
  250.3 0.8 copy.33
  251.1 0.8 copy.34
  251.9 27.2 %dynamic_update_slice.30 = bf16[8,128,2048]{1,0,2:T(8,128)(2,1)} dynamic-update-slice(bf16[8,128,2048]{1,0,2:T(8,128)(2,1)} %dynamic_update_slice.29, bf16[1,128,2048]{1,0,2:T(2,128)(2,1)S(1)} %copy.33, s32[]{:T(128)S(6)} %select_n.248, s32[]{:T(128)} %constant.200.clone.1, s32[]{:T(128)} %constant.200.clone.1) | dynamic-update-slice | bytes 1048580 | tf_op jit(solution)/shard_map/dynamic_update_slice | solution.py:297
  279.0 27.1 %dynamic_update_slice.31 = bf16[8,128,2048]{1,0,2:T(8,128)(2,1)} dynamic-update-slice(bf16[8,128,2048]{1,0,2:T(8,128)(2,1)} %dynamic_update_slice.30, bf16[1,128,2048]{1,0,2:T(2,128)(2,1)S(1)} %copy.34, s32[]{:T(128)S(6)} %select_n.249, s32[]{:T(128)} %constant.200.clone.1, s32[]{:T(128)} %constant.200.clone.1) | dynamic-update-slice | bytes 1048580 | tf_op jit(solution)/shard_map/dynamic_update_slice | solution.py:297
  306.2 5.3 %copy.44 = bf16[256,8,8,128]{3,1,2,0:T(8,128)(2,1)} copy(bf16[256,8,8,128]{3,2,1,0:T(8,128)(2,1)} %bitcast.50) | data formatting | bytes 8388608
  311.5 0.8 fusion.11.grad_ref
  312.2 7.6 %shard_map.104 = bf16[512,1024]{1,0:T(8,128)(2,1)} custom-call(bf16[512,1024]{1,0:T(8,128)(2,1)} %copy-done.1, bf16[512,1024]{1,0:T(8,128)(2,1)} %copy-done, f32[512,1024]{1,0:T(8,128)} %get-tuple-element.88.keys_ref, bf16[65,1024]{1,0:T(8,128)(2,1)} %fusion.11.grad_ref, bf16[2048,1024]{1,0:T(8,128)(2,1)} %bitcast.48), custom_call_target="tpu_custom_call" | custom-call | tf_op jit(solution)/shard_map/pallas_call | solution.py:241
  (30 shorter events, 2.5 us)
Async XLA Ops:
  0.6 14.3 %copy-start.4 = (s32[32]{0:T(128)S(1)}, s32[32]{0:T(128)}, u32[]{:S(2)}) copy-start(s32[32]{0:T(128)} %param.11) | copy-start | bytes 388
  2.6 8.4 %collective-permute-start.1 = (bf16[128,2048]{1,0:T(8,128)(2,1)S(1)}, bf16[128,2048]{1,0:T(8,128)(2,1)S(1)}, u32[]{:S(2)}, u32[]{:S(2)}) collective-permute-start(bf16[128,2048]{1,0:T(8,128)(2,1)S(1)} %constant_dynamic-update-slice_fusion), channel_id=1, source_target_pairs={{0,2},{1,5},{2,0},{3,7},{4,6},{5,1},{6,4},{7,3},{8,10},{9,13},{10,... | collective-permute-start | bytes 1572872 | tf_op jit(solution)/shard_map/ppermute | solution.py:260
  12.0 123.1 %collective-permute-start.3 = (bf16[2,128,2048]{2,1,0:T(8,128)(2,1)}, bf16[2,128,2048]{2,1,0:T(8,128)(2,1)}, u32[]{:S(2)}, u32[]{:S(2)}) collective-permute-start(bf16[2,128,2048]{2,1,0:T(8,128)(2,1)} %pad_maximum_fusion), channel_id=1, source_target_pairs={{0,4},{1,3},{2,6},{3,1},{4,0},{5,7},{6,2},{7,5},{8,12},{9,11},{10,... | collective-permute-start | bytes 3145736 | tf_op jit(solution)/shard_map/ppermute | solution.py:262
  12.3 35.8 %collective-permute-start = (bf16[128,2048]{1,0:T(8,128)(2,1)S(1)}, bf16[128,2048]{1,0:T(8,128)(2,1)S(1)}, u32[]{:S(2)}, u32[]{:S(2)}) collective-permute-start(bf16[128,2048]{1,0:T(8,128)(2,1)S(1)} %constant_dynamic-update-slice_fusion), channel_id=1, source_target_pairs={{0,1},{1,0},{2,3},{3,2},{4,5},{5,4},{6,7},{7,6},{8,9},{9,8},{10,11... | collective-permute-start | bytes 1572872 | tf_op jit(solution)/shard_map/ppermute | solution.py:259
  14.1 91.5 %collective-permute-start.2 = (bf16[128,2048]{1,0:T(8,128)(2,1)S(1)}, bf16[128,2048]{1,0:T(8,128)(2,1)}, u32[]{:S(2)}, u32[]{:S(2)}) collective-permute-start(bf16[128,2048]{1,0:T(8,128)(2,1)S(1)} %collective-permute-done.1), channel_id=1, source_target_pairs={{0,1},{1,0},{2,3},{3,2},{4,5},{5,4},{6,7},{7,6},{8,9},{9,8},{10,11... | collective-permute-start | bytes 1572872 | tf_op jit(solution)/shard_map/ppermute | solution.py:261
  48.1 0.8 copy-start.3
  135.1 64.9 %collective-permute-start.4 = (bf16[2,128,2048]{2,1,0:T(8,128)(2,1)}, bf16[2,128,2048]{2,1,0:T(8,128)(2,1)S(1)}, u32[]{:S(2)}, u32[]{:S(2)}) collective-permute-start(bf16[2,128,2048]{2,1,0:T(8,128)(2,1)} %collective-permute-done.3), channel_id=1, source_target_pairs={{0,1},{1,0},{2,3},{3,2},{4,5},{5,4},{6,7},{7,6},{8,9},{9,8},{10,11... | collective-permute-start | bytes 3145736 | tf_op jit(solution)/shard_map/ppermute | solution.py:265
  202.6 5.8 %copy-start.1 = (bf16[512,1024]{1,0:T(8,128)(2,1)}, bf16[512,1024]{1,0:T(8,128)(2,1)S(1)}, u32[]{:S(2)}) copy-start(bf16[512,1024]{1,0:T(8,128)(2,1)S(1)} %get-tuple-element.87.feat_ref) | copy-start | bytes 3145732
  202.8 14.2 %copy-start = (bf16[512,1024]{1,0:T(8,128)(2,1)}, bf16[512,1024]{1,0:T(8,128)(2,1)S(1)}, u32[]{:S(2)}) copy-start(bf16[512,1024]{1,0:T(8,128)(2,1)S(1)} %slice.68.val_ref) | copy-start | bytes 3145732
  209.6 7.2 %collective-permute-start.5 = (bf16[65,1024]{1,0:T(8,128)(2,1)S(1)}, bf16[65,1024]{1,0:T(8,128)(2,1)S(1)}, u32[]{:S(2)}, u32[]{:S(2)}) collective-permute-start(bf16[65,1024]{1,0:T(8,128)(2,1)S(1)} %get-tuple-element.100), channel_id=1, source_target_pairs={{0,1},{1,0},{2,3},{3,2},{4,5},{5,4},{6,7},{7,6},{8,9},{9,8},{10,11... | collective-permute-start | bytes 399368 | tf_op jit(solution)/shard_map/ppermute | solution.py:58
  212.3 12.6 %collective-permute-start.8 = (bf16[65,1024]{1,0:T(8,128)(2,1)S(1)}, bf16[65,1024]{1,0:T(8,128)(2,1)S(1)}, u32[]{:S(2)}, u32[]{:S(2)}) collective-permute-start(bf16[65,1024]{1,0:T(8,128)(2,1)S(1)} %get-tuple-element.99), channel_id=1, source_target_pairs={{1,4},{3,6},{5,8},{7,10},{9,12},{11,14},{13,16},{15,18},{17,20},{1... | collective-permute-start | bytes 399368 | tf_op jit(solution)/shard_map/ppermute | solution.py:58
  217.0 8.8 %collective-permute-start.7 = (bf16[65,1024]{1,0:T(8,128)(2,1)S(1)}, bf16[65,1024]{1,0:T(8,128)(2,1)S(1)}, u32[]{:S(2)}, u32[]{:S(2)}) collective-permute-start(bf16[65,1024]{1,0:T(8,128)(2,1)S(1)} %get-tuple-element.98), channel_id=1, source_target_pairs={{2,0},{3,1},{4,2},{5,3},{6,4},{7,5},{8,6},{9,7},{10,8},{11,9},{12,... | collective-permute-start | bytes 399368 | tf_op jit(solution)/shard_map/ppermute | solution.py:58
  219.2 8.3 %collective-permute-start.6 = (bf16[65,1024]{1,0:T(8,128)(2,1)S(1)}, bf16[65,1024]{1,0:T(8,128)(2,1)S(1)}, u32[]{:S(2)}, u32[]{:S(2)}) collective-permute-start(bf16[65,1024]{1,0:T(8,128)(2,1)S(1)} %get-tuple-element.97), channel_id=1, source_target_pairs={{0,2},{1,3},{2,4},{3,5},{4,6},{5,7},{6,8},{7,9},{8,10},{9,11},{10,... | collective-permute-start | bytes 399368 | tf_op jit(solution)/shard_map/ppermute | solution.py:58
  236.0 6.0 %collective-permute-start.9 = (bf16[65,1024]{1,0:T(8,128)(2,1)S(1)}, bf16[65,1024]{1,0:T(8,128)(2,1)S(1)}, u32[]{:S(2)}, u32[]{:S(2)}) collective-permute-start(bf16[65,1024]{1,0:T(8,128)(2,1)S(1)} %convert_element_type.68), channel_id=1, source_target_pairs={{0,1},{1,0},{2,3},{3,2},{4,5},{5,4},{6,7},{7,6},{8,9},{9,8},{10,11... | collective-permute-start | bytes 399368 | tf_op jit(solution)/shard_map/ppermute | solution.py:58
  236.9 74.5 %collective-permute-start.12 = (bf16[65,1024]{1,0:T(8,128)(2,1)}, bf16[65,1024]{1,0:T(8,128)(2,1)S(1)}, u32[]{:S(2)}, u32[]{:S(2)}) collective-permute-start(bf16[65,1024]{1,0:T(8,128)(2,1)} %select_convert_fusion.1), channel_id=1, source_target_pairs={{1,4},{3,6},{5,8},{7,10},{9,12},{11,14},{13,16},{15,18},{17,20},{1... | collective-permute-start | bytes 399368 | tf_op jit(solution)/shard_map/ppermute | solution.py:58
  243.1 68.3 %collective-permute-start.11 = (bf16[65,1024]{1,0:T(8,128)(2,1)S(1)}, bf16[65,1024]{1,0:T(8,128)(2,1)S(1)}, u32[]{:S(2)}, u32[]{:S(2)}) collective-permute-start(bf16[65,1024]{1,0:T(8,128)(2,1)S(1)} %get-tuple-element.96), channel_id=1, source_target_pairs={{2,0},{3,1},{4,2},{5,3},{6,4},{7,5},{8,6},{9,7},{10,8},{11,9},{12,... | collective-permute-start | bytes 399368 | tf_op jit(solution)/shard_map/ppermute | solution.py:58
  246.1 65.3 %collective-permute-start.10 = (bf16[65,1024]{1,0:T(8,128)(2,1)S(1)}, bf16[65,1024]{1,0:T(8,128)(2,1)S(1)}, u32[]{:S(2)}, u32[]{:S(2)}) collective-permute-start(bf16[65,1024]{1,0:T(8,128)(2,1)S(1)} %get-tuple-element.95), channel_id=1, source_target_pairs={{0,2},{1,3},{2,4},{3,5},{4,6},{5,7},{6,8},{7,9},{8,10},{9,11},{10,... | collective-permute-start | bytes 399368 | tf_op jit(solution)/shard_map/ppermute | solution.py:58
  306.2 5.3 %copy-start.2 = (f32[65,1024]{1,0:T(8,128)S(1)}, f32[65,1024]{1,0:T(8,128)}, u32[]{:S(2)}) copy-start(f32[65,1024]{1,0:T(8,128)} %get-tuple-element.8) | copy-start | bytes 798724

commit v16 on v11

--- a/solution.py
+++ b/solution.py
@@ -90,8 +90,15 @@
 
     up = send(chip_part(position + 2), axis, [(s, s + 2) for s in range(count - 2)])
     down = send(chip_part(position - 2), axis, [(s, s - 2) for s in range(2, count)])
-    total = own + kept(sibling, twin, position)
-    return total + up.astype(own.dtype) + down.astype(own.dtype) + far.astype(own.dtype)
+    alike = jnp.logical_and(twin <= last, complex_of(twin) == complex_of(position))
+    return own, sibling, alike.astype(own.dtype).reshape(1, 1), up, down, far
+
+
+def add_terms(own_ref, twin_ref, alike_ref, up_ref, down_ref, far_ref):
+    total = own_ref[...] + twin_ref[...].astype(jnp.float32) * alike_ref[...]
+    for ref in (up_ref, down_ref, far_ref):
+        total = total + ref[...].astype(jnp.float32)
+    return total
 
 
 def pose_side(pose_rows, pair_rows, state, w_query, score_weight):
@@ -136,7 +143,12 @@
     return (pair_loss, pose_grad.astype(jnp.bfloat16), pose_state)
 
 
-def pose_kernel(pose_ref, pair_ref, state_ref, query_ref, weight_ref, loss_ref, grad_ref, back_ref, feat_ref):
+def pose_kernel(
+    pose_ref, pair_ref, *refs
+):
+    terms = refs[:6]
+    query_ref, weight_ref, loss_ref, grad_ref, back_ref, feat_ref, state_ref = refs[6:]
+    state_ref[...] = add_terms(*terms)
     count, width = pose_ref.shape
     lanes = 2 * DH
     queries = jnp.dot(pose_ref[...], query_ref[...], preferred_element_type=jnp.float32)
@@ -208,15 +220,21 @@
         out_shape=(
             jax.ShapeDtypeStruct((1, pair_rows.shape[0]), jnp.float32),
             jax.ShapeDtypeStruct((count, width), jnp.bfloat16),
-            jax.ShapeDtypeStruct(state.shape, jnp.float32),
+            jax.ShapeDtypeStruct(state[0].shape, jnp.float32),
         ),
-        scratch_shapes=[pltpu.VMEM((count, width), jnp.bfloat16)],
+        scratch_shapes=[
+            pltpu.VMEM((count, width), jnp.bfloat16),
+            pltpu.VMEM(state[0].shape, jnp.float32),
+        ],
         interpret=interpret,
-    )(pose_rows, pairs_t, state, w_query, score_weight.reshape(1, width))
+    )(pose_rows, pairs_t, *state, w_query, score_weight.reshape(1, width))
     return (loss.reshape(pair_rows.shape[0]), grad, back)
 
 
-def back_kernel(feat_ref, val_ref, keys_ref, grad_ref, full_ref, out_ref, both_ref):
+def back_kernel(feat_ref, val_ref, keys_ref, *refs):
+    terms = refs[:6]
+    full_ref, out_ref, both_ref, grad_ref = refs[6:]
+    grad_ref[...] = add_terms(*terms).astype(grad_ref.dtype)
     width = feat_ref.shape[1]
     lanes = 2 * DH
     head_row = lax.broadcasted_iota(jnp.int32, (lanes, lanes), 0) // DH
@@ -243,9 +261,12 @@
     return pl.pallas_call(
         back_kernel,
         out_shape=jax.ShapeDtypeStruct((rows, width), jnp.bfloat16),
-        scratch_shapes=[pltpu.VMEM((rows, 2 * width), jnp.bfloat16)],
+        scratch_shapes=[
+            pltpu.VMEM((rows, 2 * width), jnp.bfloat16),
+            pltpu.VMEM(state_grad[0].shape, jnp.bfloat16),
+        ],
         interpret=interpret,
-    )(key_feat, val_round, keys, state_grad, full_both)
+    )(key_feat, val_round, keys, *state_grad, full_both)
 
 
 def gather_rows(shard):
@@ -304,7 +325,7 @@
     val_round = values.astype(jnp.bfloat16)
     state = complex_sum(local_state(key_feat, val_round), block_complex)
     pair_loss, pose_grad, pose_state = pose_fused(poses, pairs, state, w_query, score_weight)
-    state_grad = complex_sum(pose_state, block_complex).astype(jnp.bfloat16)
+    state_grad = complex_sum(pose_state, block_complex)
     total = back_fused(key_feat, val_round, keys, state_grad, full_both)
     return (pair_loss, pose_grad, total)
 

time: 95.9 us -> 97.3 us (1.015); the launches traced: 94.2 us -> 96.6 us
  waiting for transfers between devices: 19.6 us -> 25.7 us
  starting transfers between devices: 26 us -> 20.7 us
  local copies, waits for them, and re-layouts: 15 us -> 16.3 us
    ppermute x8, waiting for transfers between devices: 6.5 us -> 12.6 us  [send(): return lax.ppermute(value, axis, pairs)]
    ppermute x8, starting transfers between devices: 22.9 us -> 17.6 us  [send(): return lax.ppermute(value, axis, pairs)]
    unnamed x9 -> x21, local copies, waits for them, and re-layouts: 1.07 us -> 2.41 us
  transfers between devices with their start and end apart: 13 -> 13, of which waited for: 7 -> 7; matrix products, arithmetic and copies ran while one was open for 17% -> 19% of each run, Pallas kernels for 0% -> 0%
where the time goes in v16:
time: 97.3 us; the launch traced here: 96.6 us
  waiting for transfers between devices  25.7 us (26%)
  starting transfers between devices  20.7 us (21%)
  local copies, waits for them, and re-layouts  16.3 us (17%)
  Pallas kernels  15.1 us (16%)
  matrix products  7.23 us (7%)
  other arithmetic  6.4 us (7%)
  between operations  5.22 us (5%)
    ppermute x8, starting transfers between devices, send(): return lax.ppermute(value, axis, pairs)  17.6 us
    ppermute x8, waiting for transfers between devices, send(): return lax.ppermute(value, axis, pairs)  12.6 us
    ppermute x1, waiting for transfers between devices, gather_rows(): lax.ppermute(jnp.stack([shard, early]), 'blk', [(s, s ^ (2 if s % 2 else...  10.5 us
    pallas_call x1, Pallas kernels, back_fused(): pl.pallas_call(back_kernel, out_shape=jax.ShapeDtypeStruct((rows, width),...  8.02 us
    pallas_call x1, Pallas kernels, pose_fused(): pl.pallas_call(pose_kernel, out_shape=(jax.ShapeDtypeStruct((1, pair_rows...  7.04 us
    dynamic_update_slice x6, local copies, waits for them, and re-layouts, gather_rows(): full = lax.dynamic_update_slice(full, pieces[k][None], (at, 0, 0))  5.02 us
    dot_general x1, matrix products, shards(): jnp.dot(receptor, full_both.reshape(-1, full_both.shape[2]), preferred_el...  4.52 us
    broadcast_in_dim x1, local copies, waits for them, and re-layouts, gather_rows(): full = jnp.zeros((count,) + shard.shape, shard.dtype)  2.48 us
  transfers between devices with their start and end apart: 13, of which 7 were waited for; matrix products, arithmetic and copies ran while one was open for 19% of the time, Pallas kernels for 0%

profile of v16, /device:TPU:16, one launch (start us, length us, event | category | flops | bytes accessed | tf_op | source)
XLA Modules:
  0.0 96.6 jit_solution(294833980019382219)
XLA Ops:
  0.7 1.1 %constant_dynamic-update-slice_fusion.1 = bf16[128,2048]{1,0:T(8,128)(2,1)S(1)} fusion(bf16[128,1024]{1,0:T(8,128)(2,1)} %param.12), kind=kLoop, calls=%fused_computation.26 | loop fusion | bytes 524288
  1.7 1.0 %constant_dynamic-update-slice_fusion = bf16[128,2048]{1,0:T(8,128)(2,1)S(1)} fusion(bf16[128,2048]{1,0:T(8,128)(2,1)S(1)} %constant_dynamic-update-slice_fusion.1, bf16[128,1024]{1,0:T(8,128)(2,1)} %param.13), kind=kLoop, calls=%fused_computation.25 | loop fusion | bytes 524288 | tf_op jit(solution)/shard_map/concatenate | solution.py:304
  2.7 1.6 %collective-permute-start.1 = (bf16[128,2048]{1,0:T(8,128)(2,1)S(1)}, bf16[128,2048]{1,0:T(8,128)(2,1)S(1)}, u32[]{:S(2)}, u32[]{:S(2)}) collective-permute-start(bf16[128,2048]{1,0:T(8,128)(2,1)S(1)} %constant_dynamic-update-slice_fusion), channel_id=1, source_target_pairs={{0,2},{1,5},{2,0},{3,7},{4,6},{5,1},{6,4},{7,3},{8,10},{9,13},{10,... | collective-permute-start | bytes 1572872 | tf_op jit(solution)/shard_map/ppermute | solution.py:283
  4.2 2.5 %broadcast_in_dim.70 = bf16[8,128,2048]{2,1,0:T(8,128)(2,1)} broadcast(bf16[]{:T(256)} %constant.198.clone.1), dimensions={} | broadcast | bytes 4194306 | tf_op jit(solution)/shard_map/broadcast_in_dim | solution.py:294
  6.7 0.8 constant_dynamic-update-slice_fusion.3
  7.6 0.7 fusion.5
  9.6 0.1 constant_dynamic-slice_fusion.1
  9.6 2.3 %collective-permute-done.1 = bf16[128,2048]{1,0:T(8,128)(2,1)S(1)} collective-permute-done((bf16[128,2048]{1,0:T(8,128)(2,1)S(1)}, bf16[128,2048]{1,0:T(8,128)(2,1)S(1)}, u32[]{:S(2)}, u32[]{:S(2)}) %collective-permute-start.1) | collective-permute-done | bytes 524320 | tf_op jit(solution)/shard_map/ppermute | solution.py:283
  11.9 0.1 pad_maximum_fusion
  12.0 1.6 %collective-permute-start.3 = (bf16[2,128,2048]{2,1,0:T(8,128)(2,1)S(1)}, bf16[2,128,2048]{2,1,0:T(8,128)(2,1)S(1)}, u32[]{:S(2)}, u32[]{:S(2)}) collective-permute-start(bf16[2,128,2048]{2,1,0:T(8,128)(2,1)S(1)} %pad_maximum_fusion), channel_id=1, source_target_pairs={{0,4},{1,3},{2,6},{3,1},{4,0},{5,7},{6,2},{7,5},{8,12},{9,11},{10,... | collective-permute-start | bytes 3145736 | tf_op jit(solution)/shard_map/ppermute | solution.py:285
  13.6 0.8 bitcast_dynamic-update-slice_fusion.1
  14.5 0.8 constant_dynamic-update-slice_fusion.2
  15.3 0.2 collective-permute-done.2
  15.5 0.8 bitcast_dynamic-update-slice_fusion
  16.4 10.5 %collective-permute-done.3 = bf16[2,128,2048]{2,1,0:T(8,128)(2,1)S(1)} collective-permute-done((bf16[2,128,2048]{2,1,0:T(8,128)(2,1)S(1)}, bf16[2,128,2048]{2,1,0:T(8,128)(2,1)S(1)}, u32[]{:S(2)}, u32[]{:S(2)}) %collective-permute-start.3) | collective-permute-done | bytes 1048608 | tf_op jit(solution)/shard_map/ppermute | solution.py:285
  26.9 0.8 slice_dynamic-update-slice_fusion.3
  27.7 0.8 slice_dynamic-update-slice_fusion.2
  28.6 4.5 %fusion.7 = f32[2048,512]{0,1:T(8,128)S(1)} fusion(bf16[512,1024]{1,0:T(8,128)(2,1)S(1)} %copy-done.8, bf16[1024,2048]{1,0:T(8,128)(2,1)} %bitcast.5), kind=kOutput, calls=%fused_computation.35 | convolution fusion | flops 2147483648 | bytes 9437184 | tf_op jit(solution)/shard_map/dot_general | solution.py:310
  33.1 0.8 bitcast_add_fusion
  33.9 0.2 slice.72.val_ref
  34.0 1.8 %convert_reduce_fusion = (f32[1024]{0:T(1024)S(1)}, bf16[512,1024]{1,0:T(8,128)(2,1)S(1)}, f32[512,1024]{1,0:T(8,128)}) fusion(f32[512,2048]{1,0:T(8,128)S(1)} %bitcast_add_fusion), kind=kLoop, calls=%fused_computation.2 | loop fusion | flops 3668992 | bytes 5246976 | tf_op jit(solution)/shard_map/reduce_sum | solution.py:37
  35.9 1.4 %copy.17 = bf16[512,1024]{0,1:T(8,128)(2,1)} copy(bf16[512,1024]{1,0:T(8,128)(2,1)S(1)} %get-tuple-element.87.feat_ref) | data formatting | bytes 2097152 | tf_op jit(solution)/shard_map/convert_element_type | solution.py:324
  37.3 1.3 %copy.16 = bf16[512,1024]{0,1:T(8,128)(2,1)} copy(bf16[512,1024]{1,0:T(8,128)(2,1)S(1)} %slice.72.val_ref) | data formatting | bytes 2097152 | tf_op jit(solution)/shard_map/slice | solution.py:323
  38.6 2.0 %fusion.6 = f32[16,64,64]{2,1,0:T(8,128)S(1)} fusion(bf16[512,16,64]{0,2,1:T(8,128)(2,1)} %bitcast.43, bf16[512,16,64]{0,2,1:T(8,128)(2,1)} %bitcast.42), kind=kOutput, calls=%fused_computation.34 | convolution fusion | flops 67108864 | bytes 2359296 | tf_op jit(solution)/shard_map/thd,the->dhe/dot_general | solution.py:34
  40.6 0.2 copy.20
  40.8 0.6 collective-permute-start.5
  44.4 3.0 %collective-permute-start.8 = (bf16[65,1024]{1,0:T(8,128)(2,1)S(1)}, bf16[65,1024]{1,0:T(8,128)(2,1)S(1)}, u32[]{:S(2)}, u32[]{:S(2)}) collective-permute-start(bf16[65,1024]{1,0:T(8,128)(2,1)S(1)} %get-tuple-element.95), channel_id=1, source_target_pairs={{1,4},{3,6},{5,8},{7,10},{9,12},{11,14},{13,16},{15,18},{17,20},{1... | collective-permute-start | bytes 399368 | tf_op jit(solution)/shard_map/ppermute | solution.py:58
  47.4 0.8 add_convert_fusion.2
  48.2 3.3 %collective-permute-start.7 = (bf16[65,1024]{1,0:T(8,128)(2,1)S(1)}, bf16[65,1024]{1,0:T(8,128)(2,1)S(1)}, u32[]{:S(2)}, u32[]{:S(2)}) collective-permute-start(bf16[65,1024]{1,0:T(8,128)(2,1)S(1)} %get-tuple-element.93), channel_id=1, source_target_pairs={{2,0},{3,1},{4,2},{5,3},{6,4},{7,5},{8,6},{9,7},{10,8},{11,9},{12,... | collective-permute-start | bytes 399368 | tf_op jit(solution)/shard_map/ppermute | solution.py:58
  51.6 2.5 %collective-permute-start.6 = (bf16[65,1024]{1,0:T(8,128)(2,1)S(1)}, bf16[65,1024]{1,0:T(8,128)(2,1)S(1)}, u32[]{:S(2)}, u32[]{:S(2)}) collective-permute-start(bf16[65,1024]{1,0:T(8,128)(2,1)S(1)} %get-tuple-element.94), channel_id=1, source_target_pairs={{0,2},{1,3},{2,4},{3,5},{4,6},{5,7},{6,8},{7,9},{8,10},{9,11},{10,... | collective-permute-start | bytes 399368 | tf_op jit(solution)/shard_map/ppermute | solution.py:58
  54.1 0.8 slice_dynamic-update-slice_fusion.1
  54.9 0.8 convert_element_type.42.refs_1_
  55.7 0.8 collective-permute-done.7.refs_4_
  56.5 5.3 %collective-permute-done.6.refs_3_ = bf16[65,1024]{1,0:T(8,128)(2,1)S(1)} collective-permute-done((bf16[65,1024]{1,0:T(8,128)(2,1)S(1)}, bf16[65,1024]{1,0:T(8,128)(2,1)S(1)}, u32[]{:S(2)}, u32[]{:S(2)}) %collective-permute-start.6) | collective-permute-done | bytes 133152 | tf_op jit(solution)/shard_map/ppermute | solution.py:58
  61.8 0.7 copy-done.4
  62.4 7.0 %shard_map.103 = (f32[1,256]{1,0:T(1,128)}, bf16[128,1024]{1,0:T(8,128)(2,1)}, f32[65,1024]{1,0:T(8,128)}) custom-call(bf16[128,1024]{1,0:T(8,128)(2,1)} %pose_ref.1, s32[2,256]{1,0:T(2,128)} %bitcast.50, f32[65,1024]{1,0:T(8,128)} %get-tuple-element.97.refs_0_, f32[65,1024]{1,0:T(8,128)} %convert_element_type.42.refs_1_, f32[1,1]{1,0:T(1,128)} %bitcast.16.refs_2_, ...), custom_call_target="tpu_custom_call" | custom-call | tf_op jit(solution)/shard_map/pallas_call | solution.py:218
  69.5 1.0 %convert_element_type.46 = bf16[65,1024]{1,0:T(8,128)(2,1)S(1)} convert(f32[65,1024]{1,0:T(8,128)} %get-tuple-element.8.refs_0_) | non-fusion elementwise | flops 66560 | bytes 399360 | tf_op jit(solution)/shard_map/convert_element_type | solution.py:74
  70.4 0.2 collective-permute-start.9
  70.7 2.0 %collective-permute-start.12 = (bf16[65,1024]{1,0:T(8,128)(2,1)S(1)}, bf16[65,1024]{1,0:T(8,128)(2,1)S(1)}, u32[]{:S(2)}, u32[]{:S(2)}) collective-permute-start(bf16[65,1024]{1,0:T(8,128)(2,1)S(1)} %select_convert_fusion.1), channel_id=1, source_target_pairs={{1,4},{3,6},{5,8},{7,10},{9,12},{11,14},{13,16},{15,18},{17,20},{1... | collective-permute-start | bytes 399368 | tf_op jit(solution)/shard_map/ppermute | solution.py:58
  72.7 1.1 %add_convert_fusion = (bf16[65,1024]{1,0:T(8,128)(2,1)S(1)}, bf16[65,1024]{1,0:T(8,128)(2,1)S(1)}) fusion(f32[65,1024]{1,0:T(8,128)} %get-tuple-element.8.refs_0_, bf16[65,1024]{1,0:T(8,128)(2,1)S(1)} %collective-permute-done.9, pred[]{:T(512)S(6)} %and.107, pred[]{:T(512)S(6)} %and.106, pred[]{:T(512)S(6)} %eq.40, pred[]{:T(512)S(6)} %and.103, pred[]{:T(512)S(6)} %and.101), kind=kLoop, calls=%fused_computation.13 | loop fusion | flops 732160 | bytes 665605 | tf_op jit(solution)/shard_map/convert_element_type | solution.py:89
  73.8 3.9 %collective-permute-start.11 = (bf16[65,1024]{1,0:T(8,128)(2,1)S(1)}, bf16[65,1024]{1,0:T(8,128)(2,1)S(1)}, u32[]{:S(2)}, u32[]{:S(2)}) collective-permute-start(bf16[65,1024]{1,0:T(8,128)(2,1)S(1)} %get-tuple-element.91), channel_id=1, source_target_pairs={{2,0},{3,1},{4,2},{5,3},{6,4},{7,5},{8,6},{9,7},{10,8},{11,9},{12,... | collective-permute-start | bytes 399368 | tf_op jit(solution)/shard_map/ppermute | solution.py:58
  77.6 2.2 %collective-permute-start.10 = (bf16[65,1024]{1,0:T(8,128)(2,1)S(1)}, bf16[65,1024]{1,0:T(8,128)(2,1)S(1)}, u32[]{:S(2)}, u32[]{:S(2)}) collective-permute-start(bf16[65,1024]{1,0:T(8,128)(2,1)S(1)} %get-tuple-element.92), channel_id=1, source_target_pairs={{0,2},{1,3},{2,4},{3,5},{4,6},{5,7},{6,8},{7,9},{8,10},{9,11},{10,... | collective-permute-start | bytes 399368 | tf_op jit(solution)/shard_map/ppermute | solution.py:58
  79.8 0.8 slice_dynamic-update-slice_fusion
  80.6 0.8 convert_element_type.47.refs_1_
  81.4 0.3 collective-permute-done.11.refs_4_
  81.7 6.2 %collective-permute-done.10.refs_3_ = bf16[65,1024]{1,0:T(8,128)(2,1)S(1)} collective-permute-done((bf16[65,1024]{1,0:T(8,128)(2,1)S(1)}, bf16[65,1024]{1,0:T(8,128)(2,1)S(1)}, u32[]{:S(2)}, u32[]{:S(2)}) %collective-permute-start.10) | collective-permute-done | bytes 133152 | tf_op jit(solution)/shard_map/ppermute | solution.py:58
  87.9 0.7 copy-done.7
  88.6 8.0 %shard_map.104 = bf16[512,1024]{1,0:T(8,128)(2,1)} custom-call(bf16[512,1024]{1,0:T(8,128)(2,1)} %copy-done.1, bf16[512,1024]{1,0:T(8,128)(2,1)} %copy-done, f32[512,1024]{1,0:T(8,128)} %get-tuple-element.88.keys_ref, f32[65,1024]{1,0:T(8,128)} %get-tuple-element.8.refs_0_, f32[65,1024]{1,0:T(8,128)} %convert_element_type.47.refs_1_, ...), custom_call_target="tpu_custom_call" | custom-call | tf_op jit(solution)/shard_map/pallas_call | solution.py:261
  (29 shorter events, 0.1 us)
Async XLA Ops:
  0.6 6.9 %copy-start.9 = (s32[32]{0:T(128)S(1)}, s32[32]{0:T(128)}, u32[]{:S(2)}) copy-start(s32[32]{0:T(128)} %param.11) | copy-start | bytes 388
  0.6 8.9 %copy-start.8 = (bf16[512,1024]{1,0:T(8,128)(2,1)S(1)}, bf16[512,1024]{1,0:T(8,128)(2,1)}, u32[]{:S(2)}) copy-start(bf16[512,1024]{1,0:T(8,128)(2,1)} %param.8) | copy-start | bytes 3145732
  2.7 9.2 %collective-permute-start.1 = (bf16[128,2048]{1,0:T(8,128)(2,1)S(1)}, bf16[128,2048]{1,0:T(8,128)(2,1)S(1)}, u32[]{:S(2)}, u32[]{:S(2)}) collective-permute-start(bf16[128,2048]{1,0:T(8,128)(2,1)S(1)} %constant_dynamic-update-slice_fusion), channel_id=1, source_target_pairs={{0,2},{1,5},{2,0},{3,7},{4,6},{5,1},{6,4},{7,3},{8,10},{9,13},{10,... | collective-permute-start | bytes 1572872 | tf_op jit(solution)/shard_map/ppermute | solution.py:283
  4.2 9.4 %collective-permute-start = (bf16[128,2048]{1,0:T(8,128)(2,1)S(1)}, bf16[128,2048]{1,0:T(8,128)(2,1)S(1)}, u32[]{:S(2)}, u32[]{:S(2)}) collective-permute-start(bf16[128,2048]{1,0:T(8,128)(2,1)S(1)} %constant_dynamic-update-slice_fusion), channel_id=1, source_target_pairs={{0,1},{1,0},{2,3},{3,2},{4,5},{5,4},{6,7},{7,6},{8,9},{9,8},{10,11... | collective-permute-start | bytes 1572872 | tf_op jit(solution)/shard_map/ppermute | solution.py:282
  12.0 14.9 %collective-permute-start.3 = (bf16[2,128,2048]{2,1,0:T(8,128)(2,1)S(1)}, bf16[2,128,2048]{2,1,0:T(8,128)(2,1)S(1)}, u32[]{:S(2)}, u32[]{:S(2)}) collective-permute-start(bf16[2,128,2048]{2,1,0:T(8,128)(2,1)S(1)} %pad_maximum_fusion), channel_id=1, source_target_pairs={{0,4},{1,3},{2,6},{3,1},{4,0},{5,7},{6,2},{7,5},{8,12},{9,11},{10,... | collective-permute-start | bytes 3145736 | tf_op jit(solution)/shard_map/ppermute | solution.py:285
  13.6 1.9 %collective-permute-start.2 = (bf16[128,2048]{1,0:T(8,128)(2,1)S(1)}, bf16[128,2048]{1,0:T(8,128)(2,1)S(1)}, u32[]{:S(2)}, u32[]{:S(2)}) collective-permute-start(bf16[128,2048]{1,0:T(8,128)(2,1)S(1)} %collective-permute-done.1), channel_id=1, source_target_pairs={{0,1},{1,0},{2,3},{3,2},{4,5},{5,4},{6,7},{7,6},{8,9},{9,8},{10,11... | collective-permute-start | bytes 1572872 | tf_op jit(solution)/shard_map/ppermute | solution.py:284
  26.9 6.2 %collective-permute-start.4 = (bf16[2,128,2048]{2,1,0:T(8,128)(2,1)S(1)}, bf16[2,128,2048]{2,1,0:T(8,128)(2,1)S(1)}, u32[]{:S(2)}, u32[]{:S(2)}) collective-permute-start(bf16[2,128,2048]{2,1,0:T(8,128)(2,1)S(1)} %collective-permute-done.3), channel_id=1, source_target_pairs={{0,1},{1,0},{2,3},{3,2},{4,5},{5,4},{6,7},{7,6},{8,9},{9,8},{10,11... | collective-permute-start | bytes 3145736 | tf_op jit(solution)/shard_map/ppermute | solution.py:288
  34.0 4.6 %copy-start = (bf16[512,1024]{1,0:T(8,128)(2,1)}, bf16[512,1024]{1,0:T(8,128)(2,1)S(1)}, u32[]{:S(2)}) copy-start(bf16[512,1024]{1,0:T(8,128)(2,1)S(1)} %slice.72.val_ref) | copy-start | bytes 3145732
  35.9 12.4 %copy-start.1 = (bf16[512,1024]{1,0:T(8,128)(2,1)}, bf16[512,1024]{1,0:T(8,128)(2,1)S(1)}, u32[]{:S(2)}) copy-start(bf16[512,1024]{1,0:T(8,128)(2,1)S(1)} %get-tuple-element.87.feat_ref) | copy-start | bytes 3145732
  40.8 6.6 %collective-permute-start.5 = (bf16[65,1024]{1,0:T(8,128)(2,1)S(1)}, bf16[65,1024]{1,0:T(8,128)(2,1)S(1)}, u32[]{:S(2)}, u32[]{:S(2)}) collective-permute-start(bf16[65,1024]{1,0:T(8,128)(2,1)S(1)} %get-tuple-element.96), channel_id=1, source_target_pairs={{0,1},{1,0},{2,3},{3,2},{4,5},{5,4},{6,7},{7,6},{8,9},{9,8},{10,11... | collective-permute-start | bytes 399368 | tf_op jit(solution)/shard_map/ppermute | solution.py:58
  44.4 11.2 %collective-permute-start.8 = (bf16[65,1024]{1,0:T(8,128)(2,1)S(1)}, bf16[65,1024]{1,0:T(8,128)(2,1)S(1)}, u32[]{:S(2)}, u32[]{:S(2)}) collective-permute-start(bf16[65,1024]{1,0:T(8,128)(2,1)S(1)} %get-tuple-element.95), channel_id=1, source_target_pairs={{1,4},{3,6},{5,8},{7,10},{9,12},{11,14},{13,16},{15,18},{17,20},{1... | collective-permute-start | bytes 399368 | tf_op jit(solution)/shard_map/ppermute | solution.py:58
  48.2 8.2 %collective-permute-start.7 = (bf16[65,1024]{1,0:T(8,128)(2,1)S(1)}, bf16[65,1024]{1,0:T(8,128)(2,1)S(1)}, u32[]{:S(2)}, u32[]{:S(2)}) collective-permute-start(bf16[65,1024]{1,0:T(8,128)(2,1)S(1)} %get-tuple-element.93), channel_id=1, source_target_pairs={{2,0},{3,1},{4,2},{5,3},{6,4},{7,5},{8,6},{9,7},{10,8},{11,9},{12,... | collective-permute-start | bytes 399368 | tf_op jit(solution)/shard_map/ppermute | solution.py:58
  51.6 10.2 %collective-permute-start.6 = (bf16[65,1024]{1,0:T(8,128)(2,1)S(1)}, bf16[65,1024]{1,0:T(8,128)(2,1)S(1)}, u32[]{:S(2)}, u32[]{:S(2)}) collective-permute-start(bf16[65,1024]{1,0:T(8,128)(2,1)S(1)} %get-tuple-element.94), channel_id=1, source_target_pairs={{0,2},{1,3},{2,4},{3,5},{4,6},{5,7},{6,8},{7,9},{8,10},{9,11},{10,... | collective-permute-start | bytes 399368 | tf_op jit(solution)/shard_map/ppermute | solution.py:58
  55.7 6.1 %copy-start.2 = (bf16[65,1024]{1,0:T(8,128)(2,1)}, bf16[65,1024]{1,0:T(8,128)(2,1)S(1)}, u32[]{:S(2)}) copy-start(bf16[65,1024]{1,0:T(8,128)(2,1)S(1)} %collective-permute-done.8.refs_5_) | copy-start | bytes 399364
  56.5 5.3 %copy-start.3 = (bf16[65,1024]{1,0:T(8,128)(2,1)}, bf16[65,1024]{1,0:T(8,128)(2,1)S(1)}, u32[]{:S(2)}) copy-start(bf16[65,1024]{1,0:T(8,128)(2,1)S(1)} %collective-permute-done.7.refs_4_) | copy-start | bytes 399364
  61.8 0.7 copy-start.4
  70.4 2.2 %collective-permute-start.9 = (bf16[65,1024]{1,0:T(8,128)(2,1)S(1)}, bf16[65,1024]{1,0:T(8,128)(2,1)S(1)}, u32[]{:S(2)}, u32[]{:S(2)}) collective-permute-start(bf16[65,1024]{1,0:T(8,128)(2,1)S(1)} %convert_element_type.46), channel_id=1, source_target_pairs={{0,1},{1,0},{2,3},{3,2},{4,5},{5,4},{6,7},{7,6},{8,9},{9,8},{10,11... | collective-permute-start | bytes 399368 | tf_op jit(solution)/shard_map/ppermute | solution.py:58
  70.7 10.7 %collective-permute-start.12 = (bf16[65,1024]{1,0:T(8,128)(2,1)S(1)}, bf16[65,1024]{1,0:T(8,128)(2,1)S(1)}, u32[]{:S(2)}, u32[]{:S(2)}) collective-permute-start(bf16[65,1024]{1,0:T(8,128)(2,1)S(1)} %select_convert_fusion.1), channel_id=1, source_target_pairs={{1,4},{3,6},{5,8},{7,10},{9,12},{11,14},{13,16},{15,18},{17,20},{1... | collective-permute-start | bytes 399368 | tf_op jit(solution)/shard_map/ppermute | solution.py:58
  73.8 8.0 %collective-permute-start.11 = (bf16[65,1024]{1,0:T(8,128)(2,1)S(1)}, bf16[65,1024]{1,0:T(8,128)(2,1)S(1)}, u32[]{:S(2)}, u32[]{:S(2)}) collective-permute-start(bf16[65,1024]{1,0:T(8,128)(2,1)S(1)} %get-tuple-element.91), channel_id=1, source_target_pairs={{2,0},{3,1},{4,2},{5,3},{6,4},{7,5},{8,6},{9,7},{10,8},{11,9},{12,... | collective-permute-start | bytes 399368 | tf_op jit(solution)/shard_map/ppermute | solution.py:58
  77.6 10.3 %collective-permute-start.10 = (bf16[65,1024]{1,0:T(8,128)(2,1)S(1)}, bf16[65,1024]{1,0:T(8,128)(2,1)S(1)}, u32[]{:S(2)}, u32[]{:S(2)}) collective-permute-start(bf16[65,1024]{1,0:T(8,128)(2,1)S(1)} %get-tuple-element.92), channel_id=1, source_target_pairs={{0,2},{1,3},{2,4},{3,5},{4,6},{5,7},{6,8},{7,9},{8,10},{9,11},{10,... | collective-permute-start | bytes 399368 | tf_op jit(solution)/shard_map/ppermute | solution.py:58
  81.4 6.5 %copy-start.5 = (bf16[65,1024]{1,0:T(8,128)(2,1)}, bf16[65,1024]{1,0:T(8,128)(2,1)S(1)}, u32[]{:S(2)}) copy-start(bf16[65,1024]{1,0:T(8,128)(2,1)S(1)} %collective-permute-done.12.refs_5_) | copy-start | bytes 399364
  81.7 6.2 %copy-start.6 = (bf16[65,1024]{1,0:T(8,128)(2,1)}, bf16[65,1024]{1,0:T(8,128)(2,1)S(1)}, u32[]{:S(2)}) copy-start(bf16[65,1024]{1,0:T(8,128)(2,1)S(1)} %collective-permute-done.11.refs_4_) | copy-start | bytes 399364
  87.9 0.7 copy-start.7

commit v17 on v11

--- a/solution.py
+++ b/solution.py
@@ -88,8 +88,19 @@
     def chip_part(target):
         return (kept(low, first, target) + kept(high, first + 1, target)).astype(jnp.bfloat16)
 
-    up = send(chip_part(position + 2), axis, [(s, s + 2) for s in range(count - 2)])
-    down = send(chip_part(position - 2), axis, [(s, s - 2) for s in range(2, count)])
+    even_chip = (position // 2) % 2 == 0
+    pairs_a = [(s, s + 2 if (s // 2) % 2 == 0 else s - 2) for s in range(count)]
+    pairs_b = [
+        (s, s + 2 if (s // 2) % 2 else s - 2)
+        for s in range(count)
+        if 0 <= (s + 2 if (s // 2) % 2 else s - 2) < count
+    ]
+    up = send(
+        chip_part(jnp.where(even_chip, position + 2, position - 2)), axis, pairs_a
+    )
+    down = send(
+        chip_part(jnp.where(even_chip, position - 2, position + 2)), axis, pairs_b
+    )
     total = own + kept(sibling, twin, position)
     return total + up.astype(own.dtype) + down.astype(own.dtype) + far.astype(own.dtype)
 

time: 95.9 us -> 91.9 us (0.958)
  starting transfers between devices: 26 us -> 18.2 us
  waiting for transfers between devices: 19.6 us -> 24.2 us
    ppermute x8, starting transfers between devices: 22.9 us -> 15.1 us  [send(): return lax.ppermute(value, axis, pairs)]
    ppermute x8, waiting for transfers between devices: 6.5 us -> 11.2 us  [send(): return lax.ppermute(value, axis, pairs)]
  transfers between devices with their start and end apart: 13 -> 13, of which waited for: 7 -> 6; matrix products, arithmetic and copies ran while one was open for 17% -> 17% of each run, Pallas kernels for 0% -> 0%
where the time goes in v17:
time: 91.9 us; the launch traced here: 91 us
  waiting for transfers between devices  24.2 us (26%)
  starting transfers between devices  18.2 us (20%)
  local copies, waits for them, and re-layouts  15 us (16%)
  Pallas kernels  14.4 us (16%)
  matrix products  7.22 us (8%)
  other arithmetic  6.7 us (7%)
  between operations  5.28 us (6%)
    ppermute x8, starting transfers between devices, send(): return lax.ppermute(value, axis, pairs)  15.1 us
    ppermute x8, waiting for transfers between devices, send(): return lax.ppermute(value, axis, pairs)  11.2 us
    ppermute x1, waiting for transfers between devices, gather_rows(): lax.ppermute(jnp.stack([shard, early]), 'blk', [(s, s ^ (2 if s % 2 else...  10.5 us
    pallas_call x1, Pallas kernels, back_fused(): pl.pallas_call(back_kernel, out_shape=jax.ShapeDtypeStruct((rows, width),...  7.63 us
    pallas_call x1, Pallas kernels, pose_fused(): pl.pallas_call(pose_kernel, out_shape=(jax.ShapeDtypeStruct((1, pair_rows...  6.79 us
    dynamic_update_slice x6, local copies, waits for them, and re-layouts, gather_rows(): full = lax.dynamic_update_slice(full, pieces[k][None], (at, 0, 0))  4.97 us
    dot_general x1, matrix products, shards(): jnp.dot(receptor, full_both.reshape(-1, full_both.shape[2]), preferred_el...  4.52 us
    broadcast_in_dim x1, local copies, waits for them, and re-layouts, gather_rows(): full = jnp.zeros((count,) + shard.shape, shard.dtype)  2.47 us
  transfers between devices with their start and end apart: 13, of which 6 were waited for; matrix products, arithmetic and copies ran while one was open for 17% of the time, Pallas kernels for 0%

profile of v17, /device:TPU:16, one launch (start us, length us, event | category | flops | bytes accessed | tf_op | source)
XLA Modules:
  0.0 91.0 jit_solution(12609896665266588515)
XLA Ops:
  0.7 1.1 %constant_dynamic-update-slice_fusion.1 = bf16[128,2048]{1,0:T(8,128)(2,1)S(1)} fusion(bf16[128,1024]{1,0:T(8,128)(2,1)} %param.12), kind=kLoop, calls=%fused_computation.38 | loop fusion | bytes 524288
  1.7 1.0 %constant_dynamic-update-slice_fusion = bf16[128,2048]{1,0:T(8,128)(2,1)S(1)} fusion(bf16[128,2048]{1,0:T(8,128)(2,1)S(1)} %constant_dynamic-update-slice_fusion.1, bf16[128,1024]{1,0:T(8,128)(2,1)} %param.13), kind=kLoop, calls=%fused_computation.37 | loop fusion | bytes 524288 | tf_op jit(solution)/shard_map/concatenate | solution.py:294
  2.7 1.6 %collective-permute-start.1 = (bf16[128,2048]{1,0:T(8,128)(2,1)S(1)}, bf16[128,2048]{1,0:T(8,128)(2,1)S(1)}, u32[]{:S(2)}, u32[]{:S(2)}) collective-permute-start(bf16[128,2048]{1,0:T(8,128)(2,1)S(1)} %constant_dynamic-update-slice_fusion), channel_id=1, source_target_pairs={{0,2},{1,5},{2,0},{3,7},{4,6},{5,1},{6,4},{7,3},{8,10},{9,13},{10,... | collective-permute-start | bytes 1572872 | tf_op jit(solution)/shard_map/ppermute | solution.py:273
  4.2 2.5 %broadcast_in_dim.72 = bf16[8,128,2048]{2,1,0:T(8,128)(2,1)} broadcast(bf16[]{:T(256)} %constant.216.clone.1), dimensions={} | broadcast | bytes 4194306 | tf_op jit(solution)/shard_map/broadcast_in_dim | solution.py:284
  6.7 0.8 constant_dynamic-update-slice_fusion.3
  7.6 0.7 fusion.14
  9.6 0.1 constant_dynamic-slice_fusion.1
  9.6 2.3 %collective-permute-done.1 = bf16[128,2048]{1,0:T(8,128)(2,1)S(1)} collective-permute-done((bf16[128,2048]{1,0:T(8,128)(2,1)S(1)}, bf16[128,2048]{1,0:T(8,128)(2,1)S(1)}, u32[]{:S(2)}, u32[]{:S(2)}) %collective-permute-start.1) | collective-permute-done | bytes 524320 | tf_op jit(solution)/shard_map/ppermute | solution.py:273
  11.9 0.1 pad_maximum_fusion
  12.0 1.6 %collective-permute-start.3 = (bf16[2,128,2048]{2,1,0:T(8,128)(2,1)S(1)}, bf16[2,128,2048]{2,1,0:T(8,128)(2,1)S(1)}, u32[]{:S(2)}, u32[]{:S(2)}) collective-permute-start(bf16[2,128,2048]{2,1,0:T(8,128)(2,1)S(1)} %pad_maximum_fusion), channel_id=1, source_target_pairs={{0,4},{1,3},{2,6},{3,1},{4,0},{5,7},{6,2},{7,5},{8,12},{9,11},{10,... | collective-permute-start | bytes 3145736 | tf_op jit(solution)/shard_map/ppermute | solution.py:275
  13.6 0.8 bitcast_dynamic-update-slice_fusion.1
  14.4 0.8 constant_dynamic-update-slice_fusion.2
  15.3 0.2 collective-permute-done.2
  15.5 0.8 bitcast_dynamic-update-slice_fusion
  16.4 10.5 %collective-permute-done.3 = bf16[2,128,2048]{2,1,0:T(8,128)(2,1)S(1)} collective-permute-done((bf16[2,128,2048]{2,1,0:T(8,128)(2,1)S(1)}, bf16[2,128,2048]{2,1,0:T(8,128)(2,1)S(1)}, u32[]{:S(2)}, u32[]{:S(2)}) %collective-permute-start.3) | collective-permute-done | bytes 1048608 | tf_op jit(solution)/shard_map/ppermute | solution.py:275
  26.9 0.0 collective-permute-start.4
  26.9 0.8 slice_dynamic-update-slice_fusion.3
  27.7 0.8 slice_dynamic-update-slice_fusion.2
  28.5 4.5 %fusion.16 = f32[2048,512]{0,1:T(8,128)S(1)} fusion(bf16[512,1024]{1,0:T(8,128)(2,1)S(1)} %copy-done.2, bf16[1024,2048]{1,0:T(8,128)(2,1)} %bitcast.5), kind=kOutput, calls=%fused_computation.46 | convolution fusion | flops 2147483648 | bytes 9437184 | tf_op jit(solution)/shard_map/dot_general | solution.py:300
  33.1 0.8 bitcast_add_fusion
  33.8 0.2 slice.72.val_ref
  34.0 1.8 %convert_reduce_fusion = (f32[1024]{0:T(1024)S(1)}, bf16[512,1024]{1,0:T(8,128)(2,1)S(1)}, f32[512,1024]{1,0:T(8,128)}) fusion(f32[512,2048]{1,0:T(8,128)S(1)} %bitcast_add_fusion), kind=kLoop, calls=%fused_computation.2 | loop fusion | flops 3668992 | bytes 5246976 | tf_op jit(solution)/shard_map/reduce_sum | solution.py:37
  35.9 1.4 %copy.17 = bf16[512,1024]{0,1:T(8,128)(2,1)} copy(bf16[512,1024]{1,0:T(8,128)(2,1)S(1)} %get-tuple-element.87.feat_ref) | data formatting | bytes 2097152 | tf_op jit(solution)/shard_map/convert_element_type | solution.py:314
  37.3 1.3 %copy.16 = bf16[512,1024]{0,1:T(8,128)(2,1)} copy(bf16[512,1024]{1,0:T(8,128)(2,1)S(1)} %slice.72.val_ref) | data formatting | bytes 2097152 | tf_op jit(solution)/shard_map/slice | solution.py:313
  38.6 2.0 %fusion.15 = f32[16,64,64]{2,1,0:T(8,128)S(1)} fusion(bf16[512,16,64]{0,2,1:T(8,128)(2,1)} %bitcast.42, bf16[512,16,64]{0,2,1:T(8,128)(2,1)} %bitcast.41), kind=kOutput, calls=%fused_computation.45 | convolution fusion | flops 67108864 | bytes 2359296 | tf_op jit(solution)/shard_map/thd,the->dhe/dot_general | solution.py:34
  40.5 0.2 copy.20
  40.8 0.6 collective-permute-start.5
  44.5 3.0 %collective-permute-start.8 = (bf16[65,1024]{1,0:T(8,128)(2,1)S(1)}, bf16[65,1024]{1,0:T(8,128)(2,1)S(1)}, u32[]{:S(2)}, u32[]{:S(2)}) collective-permute-start(bf16[65,1024]{1,0:T(8,128)(2,1)S(1)} %get-tuple-element.95), channel_id=1, source_target_pairs={{1,4},{3,6},{5,8},{7,10},{9,12},{11,14},{13,16},{15,18},{17,20},{1... | collective-permute-start | bytes 399368 | tf_op jit(solution)/shard_map/ppermute | solution.py:58
  47.4 0.0 collective-permute-done.5
  47.5 0.1 add_convert_fusion.3
  47.6 1.5 %collective-permute-start.6 = (bf16[65,1024]{1,0:T(8,128)(2,1)S(1)}, bf16[65,1024]{1,0:T(8,128)(2,1)S(1)}, u32[]{:S(2)}, u32[]{:S(2)}) collective-permute-start(bf16[65,1024]{1,0:T(8,128)(2,1)S(1)} %get-tuple-element.93), channel_id=1, source_target_pairs={{0,2},{1,3},{2,0},{3,1},{4,6},{5,7},{6,4},{7,5},{8,10},{9,11},{10,... | collective-permute-start | bytes 399368 | tf_op jit(solution)/shard_map/ppermute | solution.py:58
  49.1 2.4 %collective-permute-start.7 = (bf16[65,1024]{1,0:T(8,128)(2,1)S(1)}, bf16[65,1024]{1,0:T(8,128)(2,1)S(1)}, u32[]{:S(2)}, u32[]{:S(2)}) collective-permute-start(bf16[65,1024]{1,0:T(8,128)(2,1)S(1)} %get-tuple-element.94), channel_id=1, source_target_pairs={{2,4},{3,5},{4,2},{5,3},{6,8},{7,9},{8,6},{9,7},{10,12},{11,13},{1... | collective-permute-start | bytes 399368 | tf_op jit(solution)/shard_map/ppermute | solution.py:58
  51.5 0.9 slice_dynamic-update-slice_fusion.1
  52.4 1.6 %collective-permute-done.6 = bf16[65,1024]{1,0:T(8,128)(2,1)S(1)} collective-permute-done((bf16[65,1024]{1,0:T(8,128)(2,1)S(1)}, bf16[65,1024]{1,0:T(8,128)(2,1)S(1)}, u32[]{:S(2)}, u32[]{:S(2)}) %collective-permute-start.6) | collective-permute-done | bytes 133152 | tf_op jit(solution)/shard_map/ppermute | solution.py:58
  54.0 4.9 %collective-permute-done.7 = bf16[65,1024]{1,0:T(8,128)(2,1)S(1)} collective-permute-done((bf16[65,1024]{1,0:T(8,128)(2,1)S(1)}, bf16[65,1024]{1,0:T(8,128)(2,1)S(1)}, u32[]{:S(2)}, u32[]{:S(2)}) %collective-permute-start.7) | collective-permute-done | bytes 133152 | tf_op jit(solution)/shard_map/ppermute | solution.py:58
  58.9 0.8 fusion.3.state_ref
  59.7 6.8 %shard_map.103 = (f32[1,256]{1,0:T(1,128)}, bf16[128,1024]{1,0:T(8,128)(2,1)}, f32[65,1024]{1,0:T(8,128)}) custom-call(bf16[128,1024]{1,0:T(8,128)(2,1)} %pose_ref.1, s32[2,256]{1,0:T(2,128)} %bitcast.50, f32[65,1024]{1,0:T(8,128)} %fusion.3.state_ref, bf16[1024,1024]{1,0:T(8,128)(2,1)} %query_ref.1, f32[1,1024]{1,0:T(1,128)} %bitcast.49), custom_call_target="tpu_custom_call" | custom-call | tf_op jit(solution)/shard_map/pallas_call | solution.py:217
  66.5 1.0 %convert_element_type.68 = bf16[65,1024]{1,0:T(8,128)(2,1)S(1)} convert(f32[65,1024]{1,0:T(8,128)} %get-tuple-element.8) | non-fusion elementwise | flops 66560 | bytes 399360 | tf_op jit(solution)/shard_map/convert_element_type | solution.py:74
  67.4 0.1 collective-permute-start.9
  67.6 2.0 %collective-permute-start.12 = (bf16[65,1024]{1,0:T(8,128)(2,1)S(1)}, bf16[65,1024]{1,0:T(8,128)(2,1)S(1)}, u32[]{:S(2)}, u32[]{:S(2)}) collective-permute-start(bf16[65,1024]{1,0:T(8,128)(2,1)S(1)} %select_convert_fusion.1), channel_id=1, source_target_pairs={{1,4},{3,6},{5,8},{7,10},{9,12},{11,14},{13,16},{15,18},{17,20},{1... | collective-permute-start | bytes 399368 | tf_op jit(solution)/shard_map/ppermute | solution.py:58
  69.6 1.1 %add_convert_fusion.1 = (bf16[65,1024]{1,0:T(8,128)(2,1)S(1)}, bf16[65,1024]{1,0:T(8,128)(2,1)S(1)}) fusion(f32[65,1024]{1,0:T(8,128)} %get-tuple-element.8, bf16[65,1024]{1,0:T(8,128)(2,1)S(1)} %collective-permute-done.9, pred[]{:T(512)S(6)} %and.121, pred[]{:T(512)S(6)} %eq.47, pred[]{:T(512)S(6)} %and.119, pred[]{:T(512)S(6)} %and.125, pred[]{:T(512)S(6)} %and.124), kind=kLoop, calls=%fused_computation.29 | loop fusion | flops 732160 | bytes 665605 | tf_op jit(solution)/shard_map/convert_element_type | solution.py:89
  70.7 1.5 %collective-permute-start.10 = (bf16[65,1024]{1,0:T(8,128)(2,1)S(1)}, bf16[65,1024]{1,0:T(8,128)(2,1)S(1)}, u32[]{:S(2)}, u32[]{:S(2)}) collective-permute-start(bf16[65,1024]{1,0:T(8,128)(2,1)S(1)} %get-tuple-element.91), channel_id=1, source_target_pairs={{0,2},{1,3},{2,0},{3,1},{4,6},{5,7},{6,4},{7,5},{8,10},{9,11},{10,... | collective-permute-start | bytes 399368 | tf_op jit(solution)/shard_map/ppermute | solution.py:58
  72.2 4.0 %collective-permute-start.11 = (bf16[65,1024]{1,0:T(8,128)(2,1)S(1)}, bf16[65,1024]{1,0:T(8,128)(2,1)S(1)}, u32[]{:S(2)}, u32[]{:S(2)}) collective-permute-start(bf16[65,1024]{1,0:T(8,128)(2,1)S(1)} %get-tuple-element.92), channel_id=1, source_target_pairs={{2,4},{3,5},{4,2},{5,3},{6,8},{7,9},{8,6},{9,7},{10,12},{11,13},{1... | collective-permute-start | bytes 399368 | tf_op jit(solution)/shard_map/ppermute | solution.py:58
  76.2 0.8 slice_dynamic-update-slice_fusion
  77.0 0.0 collective-permute-done.12
  77.0 4.7 %collective-permute-done.11 = bf16[65,1024]{1,0:T(8,128)(2,1)S(1)} collective-permute-done((bf16[65,1024]{1,0:T(8,128)(2,1)S(1)}, bf16[65,1024]{1,0:T(8,128)(2,1)S(1)}, u32[]{:S(2)}, u32[]{:S(2)}) %collective-permute-start.11) | collective-permute-done | bytes 133152 | tf_op jit(solution)/shard_map/ppermute | solution.py:58
  81.7 1.7 %fusion.8.grad_ref = bf16[65,1024]{1,0:T(8,128)(2,1)} fusion(f32[65,1024]{1,0:T(8,128)} %get-tuple-element.8, bf16[65,1024]{1,0:T(8,128)(2,1)S(1)} %collective-permute-done.9, bf16[65,1024]{1,0:T(8,128)(2,1)S(1)} %collective-permute-done.12, bf16[65,1024]{1,0:T(8,128)(2,1)S(1)} %collective-permute-done.11, bf16[65,1024]{1,0:T(8,128)(2,1)S(1)} %collective-permute-done.10, ...), kind=kLoop, calls=%fused_computation.25 | loop fusion | flops 665600 | bytes 931841 | tf_op jit(solution)/shard_map/convert_element_type | solution.py:318
  83.4 7.6 %shard_map.104 = bf16[512,1024]{1,0:T(8,128)(2,1)} custom-call(bf16[512,1024]{1,0:T(8,128)(2,1)} %copy-done.1, bf16[512,1024]{1,0:T(8,128)(2,1)} %copy-done, f32[512,1024]{1,0:T(8,128)} %get-tuple-element.88.keys_ref, bf16[65,1024]{1,0:T(8,128)(2,1)} %fusion.8.grad_ref, bf16[1024,2048]{1,0:T(8,128)(2,1)} %bitcast.28.full_ref), custom_call_target="tpu_custom_call" | custom-call | tf_op jit(solution)/shard_map/pallas_call | solution.py:254
  (17 shorter events, 0.1 us)
Async XLA Ops:
  0.6 6.9 %copy-start.3 = (s32[32]{0:T(128)S(1)}, s32[32]{0:T(128)}, u32[]{:S(2)}) copy-start(s32[32]{0:T(128)} %param.11) | copy-start | bytes 388
  0.6 8.9 %copy-start.2 = (bf16[512,1024]{1,0:T(8,128)(2,1)S(1)}, bf16[512,1024]{1,0:T(8,128)(2,1)}, u32[]{:S(2)}) copy-start(bf16[512,1024]{1,0:T(8,128)(2,1)} %param.8) | copy-start | bytes 3145732
  2.7 9.2 %collective-permute-start.1 = (bf16[128,2048]{1,0:T(8,128)(2,1)S(1)}, bf16[128,2048]{1,0:T(8,128)(2,1)S(1)}, u32[]{:S(2)}, u32[]{:S(2)}) collective-permute-start(bf16[128,2048]{1,0:T(8,128)(2,1)S(1)} %constant_dynamic-update-slice_fusion), channel_id=1, source_target_pairs={{0,2},{1,5},{2,0},{3,7},{4,6},{5,1},{6,4},{7,3},{8,10},{9,13},{10,... | collective-permute-start | bytes 1572872 | tf_op jit(solution)/shard_map/ppermute | solution.py:273
  4.2 9.4 %collective-permute-start = (bf16[128,2048]{1,0:T(8,128)(2,1)S(1)}, bf16[128,2048]{1,0:T(8,128)(2,1)S(1)}, u32[]{:S(2)}, u32[]{:S(2)}) collective-permute-start(bf16[128,2048]{1,0:T(8,128)(2,1)S(1)} %constant_dynamic-update-slice_fusion), channel_id=1, source_target_pairs={{0,1},{1,0},{2,3},{3,2},{4,5},{5,4},{6,7},{7,6},{8,9},{9,8},{10,11... | collective-permute-start | bytes 1572872 | tf_op jit(solution)/shard_map/ppermute | solution.py:272
  12.0 14.9 %collective-permute-start.3 = (bf16[2,128,2048]{2,1,0:T(8,128)(2,1)S(1)}, bf16[2,128,2048]{2,1,0:T(8,128)(2,1)S(1)}, u32[]{:S(2)}, u32[]{:S(2)}) collective-permute-start(bf16[2,128,2048]{2,1,0:T(8,128)(2,1)S(1)} %pad_maximum_fusion), channel_id=1, source_target_pairs={{0,4},{1,3},{2,6},{3,1},{4,0},{5,7},{6,2},{7,5},{8,12},{9,11},{10,... | collective-permute-start | bytes 3145736 | tf_op jit(solution)/shard_map/ppermute | solution.py:275
  13.6 1.9 %collective-permute-start.2 = (bf16[128,2048]{1,0:T(8,128)(2,1)S(1)}, bf16[128,2048]{1,0:T(8,128)(2,1)S(1)}, u32[]{:S(2)}, u32[]{:S(2)}) collective-permute-start(bf16[128,2048]{1,0:T(8,128)(2,1)S(1)} %collective-permute-done.1), channel_id=1, source_target_pairs={{0,1},{1,0},{2,3},{3,2},{4,5},{5,4},{6,7},{7,6},{8,9},{9,8},{10,11... | collective-permute-start | bytes 1572872 | tf_op jit(solution)/shard_map/ppermute | solution.py:274
  26.9 6.2 %collective-permute-start.4 = (bf16[2,128,2048]{2,1,0:T(8,128)(2,1)S(1)}, bf16[2,128,2048]{2,1,0:T(8,128)(2,1)S(1)}, u32[]{:S(2)}, u32[]{:S(2)}) collective-permute-start(bf16[2,128,2048]{2,1,0:T(8,128)(2,1)S(1)} %collective-permute-done.3), channel_id=1, source_target_pairs={{0,1},{1,0},{2,3},{3,2},{4,5},{5,4},{6,7},{7,6},{8,9},{9,8},{10,11... | collective-permute-start | bytes 3145736 | tf_op jit(solution)/shard_map/ppermute | solution.py:278
  34.0 4.6 %copy-start = (bf16[512,1024]{1,0:T(8,128)(2,1)}, bf16[512,1024]{1,0:T(8,128)(2,1)S(1)}, u32[]{:S(2)}) copy-start(bf16[512,1024]{1,0:T(8,128)(2,1)S(1)} %slice.72.val_ref) | copy-start | bytes 3145732
  35.9 11.7 %copy-start.1 = (bf16[512,1024]{1,0:T(8,128)(2,1)}, bf16[512,1024]{1,0:T(8,128)(2,1)S(1)}, u32[]{:S(2)}) copy-start(bf16[512,1024]{1,0:T(8,128)(2,1)S(1)} %get-tuple-element.87.feat_ref) | copy-start | bytes 3145732
  40.8 6.7 %collective-permute-start.5 = (bf16[65,1024]{1,0:T(8,128)(2,1)S(1)}, bf16[65,1024]{1,0:T(8,128)(2,1)S(1)}, u32[]{:S(2)}, u32[]{:S(2)}) collective-permute-start(bf16[65,1024]{1,0:T(8,128)(2,1)S(1)} %get-tuple-element.96), channel_id=1, source_target_pairs={{0,1},{1,0},{2,3},{3,2},{4,5},{5,4},{6,7},{7,6},{8,9},{9,8},{10,11... | collective-permute-start | bytes 399368 | tf_op jit(solution)/shard_map/ppermute | solution.py:58
  44.5 7.9 %collective-permute-start.8 = (bf16[65,1024]{1,0:T(8,128)(2,1)S(1)}, bf16[65,1024]{1,0:T(8,128)(2,1)S(1)}, u32[]{:S(2)}, u32[]{:S(2)}) collective-permute-start(bf16[65,1024]{1,0:T(8,128)(2,1)S(1)} %get-tuple-element.95), channel_id=1, source_target_pairs={{1,4},{3,6},{5,8},{7,10},{9,12},{11,14},{13,16},{15,18},{17,20},{1... | collective-permute-start | bytes 399368 | tf_op jit(solution)/shard_map/ppermute | solution.py:58
  47.6 6.4 %collective-permute-start.6 = (bf16[65,1024]{1,0:T(8,128)(2,1)S(1)}, bf16[65,1024]{1,0:T(8,128)(2,1)S(1)}, u32[]{:S(2)}, u32[]{:S(2)}) collective-permute-start(bf16[65,1024]{1,0:T(8,128)(2,1)S(1)} %get-tuple-element.93), channel_id=1, source_target_pairs={{0,2},{1,3},{2,0},{3,1},{4,6},{5,7},{6,4},{7,5},{8,10},{9,11},{10,... | collective-permute-start | bytes 399368 | tf_op jit(solution)/shard_map/ppermute | solution.py:58
  49.1 9.7 %collective-permute-start.7 = (bf16[65,1024]{1,0:T(8,128)(2,1)S(1)}, bf16[65,1024]{1,0:T(8,128)(2,1)S(1)}, u32[]{:S(2)}, u32[]{:S(2)}) collective-permute-start(bf16[65,1024]{1,0:T(8,128)(2,1)S(1)} %get-tuple-element.94), channel_id=1, source_target_pairs={{2,4},{3,5},{4,2},{5,3},{6,8},{7,9},{8,6},{9,7},{10,12},{11,13},{1... | collective-permute-start | bytes 399368 | tf_op jit(solution)/shard_map/ppermute | solution.py:58
  67.4 2.1 %collective-permute-start.9 = (bf16[65,1024]{1,0:T(8,128)(2,1)S(1)}, bf16[65,1024]{1,0:T(8,128)(2,1)S(1)}, u32[]{:S(2)}, u32[]{:S(2)}) collective-permute-start(bf16[65,1024]{1,0:T(8,128)(2,1)S(1)} %convert_element_type.68), channel_id=1, source_target_pairs={{0,1},{1,0},{2,3},{3,2},{4,5},{5,4},{6,7},{7,6},{8,9},{9,8},{10,11... | collective-permute-start | bytes 399368 | tf_op jit(solution)/shard_map/ppermute | solution.py:58
  67.6 9.4 %collective-permute-start.12 = (bf16[65,1024]{1,0:T(8,128)(2,1)S(1)}, bf16[65,1024]{1,0:T(8,128)(2,1)S(1)}, u32[]{:S(2)}, u32[]{:S(2)}) collective-permute-start(bf16[65,1024]{1,0:T(8,128)(2,1)S(1)} %select_convert_fusion.1), channel_id=1, source_target_pairs={{1,4},{3,6},{5,8},{7,10},{9,12},{11,14},{13,16},{15,18},{17,20},{1... | collective-permute-start | bytes 399368 | tf_op jit(solution)/shard_map/ppermute | solution.py:58
  70.7 6.3 %collective-permute-start.10 = (bf16[65,1024]{1,0:T(8,128)(2,1)S(1)}, bf16[65,1024]{1,0:T(8,128)(2,1)S(1)}, u32[]{:S(2)}, u32[]{:S(2)}) collective-permute-start(bf16[65,1024]{1,0:T(8,128)(2,1)S(1)} %get-tuple-element.91), channel_id=1, source_target_pairs={{0,2},{1,3},{2,0},{3,1},{4,6},{5,7},{6,4},{7,5},{8,10},{9,11},{10,... | collective-permute-start | bytes 399368 | tf_op jit(solution)/shard_map/ppermute | solution.py:58
  72.2 9.5 %collective-permute-start.11 = (bf16[65,1024]{1,0:T(8,128)(2,1)S(1)}, bf16[65,1024]{1,0:T(8,128)(2,1)S(1)}, u32[]{:S(2)}, u32[]{:S(2)}) collective-permute-start(bf16[65,1024]{1,0:T(8,128)(2,1)S(1)} %get-tuple-element.92), channel_id=1, source_target_pairs={{2,4},{3,5},{4,2},{5,3},{6,8},{7,9},{8,6},{9,7},{10,12},{11,13},{1... | collective-permute-start | bytes 399368 | tf_op jit(solution)/shard_map/ppermute | solution.py:58

commit v18 on v17

--- a/solution.py
+++ b/solution.py
@@ -58,7 +58,7 @@
     return lax.ppermute(value, axis, pairs)
 
 
-def complex_sum(own, block_complex):
+def complex_sum(own, block_complex, narrow=None):
     axis = ("sec", "blk")
     count = lax.axis_size(axis)
     position = lax.axis_index(axis)
@@ -71,7 +71,8 @@
         inside = jnp.logical_and(target >= 0, target <= last)
         return jnp.where(jnp.logical_and(inside, complex_of(block) == complex_of(target)), value, 0.0)
 
-    narrow = own.astype(jnp.bfloat16)
+    if narrow is None:
+        narrow = own.astype(jnp.bfloat16)
     twin = position ^ 1
     sibling = send(narrow, axis, [(s, s ^ 1) for s in range(count)]).astype(own.dtype)
     odd = position % 2 == 1
@@ -147,7 +148,10 @@
     return (pair_loss, pose_grad.astype(jnp.bfloat16), pose_state)
 
 
-def pose_kernel(pose_ref, pair_ref, state_ref, query_ref, weight_ref, loss_ref, grad_ref, back_ref, feat_ref):
+def pose_kernel(
+    pose_ref, pair_ref, state_ref, query_ref, weight_ref, loss_ref, grad_ref, back_ref, narrow_ref,
+    feat_ref,
+):
     count, width = pose_ref.shape
     lanes = 2 * DH
     queries = jnp.dot(pose_ref[...], query_ref[...], preferred_element_type=jnp.float32)
@@ -205,6 +209,7 @@
             preferred_element_type=jnp.float32,
         ) + denom_grad * norm[:, cols]
         feat_ref[:, cols] = (feat_grad * slope(queries[:, cols])).astype(feat_ref.dtype)
+    narrow_ref[...] = back_ref[...].astype(narrow_ref.dtype)
     grad = lax.dot_general(
         feat_ref[...], query_ref[...], (((1,), (1,)), ((), ())), preferred_element_type=jnp.float32
     )
@@ -214,17 +219,18 @@
 def pose_fused(pose_rows, pair_rows, state, w_query, score_weight, interpret=False):
     count, width = pose_rows.shape
     pairs_t = pair_rows.T
-    loss, grad, back = pl.pallas_call(
+    loss, grad, back, narrow = pl.pallas_call(
         pose_kernel,
         out_shape=(
             jax.ShapeDtypeStruct((1, pair_rows.shape[0]), jnp.float32),
             jax.ShapeDtypeStruct((count, width), jnp.bfloat16),
             jax.ShapeDtypeStruct(state.shape, jnp.float32),
+            jax.ShapeDtypeStruct(state.shape, jnp.bfloat16),
         ),
         scratch_shapes=[pltpu.VMEM((count, width), jnp.bfloat16)],
         interpret=interpret,
     )(pose_rows, pairs_t, state, w_query, score_weight.reshape(1, width))
-    return (loss.reshape(pair_rows.shape[0]), grad, back)
+    return (loss.reshape(pair_rows.shape[0]), grad, (back, narrow))
 
 
 def back_kernel(feat_ref, val_ref, keys_ref, grad_ref, full_ref, out_ref, both_ref):
@@ -315,7 +321,7 @@
     val_round = values.astype(jnp.bfloat16)
     state = complex_sum(local_state(key_feat, val_round), block_complex)
     pair_loss, pose_grad, pose_state = pose_fused(poses, pairs, state, w_query, score_weight)
-    state_grad = complex_sum(pose_state, block_complex).astype(jnp.bfloat16)
+    state_grad = complex_sum(pose_state[0], block_complex, pose_state[1]).astype(jnp.bfloat16)
     total = back_fused(key_feat, val_round, keys, state_grad, full_both)
     return (pair_loss, pose_grad, total)
 

time: 91.9 us -> 90.8 us (0.988)
  other arithmetic: 6.7 us -> 5.72 us
    convert_element_type x2 -> x1, other arithmetic: 2.71 us -> 1.73 us  [shards(): complex_sum(pose_state[0], block_complex, pose_state[1])]
where the time goes in v18:
time: 90.8 us; the launch traced here: 90 us
  waiting for transfers between devices  24.2 us (27%)
  starting transfers between devices  18.2 us (20%)
  local copies, waits for them, and re-layouts  15 us (17%)
  Pallas kernels  14.4 us (16%)
  matrix products  7.22 us (8%)
  other arithmetic  5.72 us (6%)
  between operations  5.27 us (6%)
    ppermute x8, starting transfers between devices, send(): return lax.ppermute(value, axis, pairs)  15 us
    ppermute x8, waiting for transfers between devices, send(): return lax.ppermute(value, axis, pairs)  11.2 us
    ppermute x1, waiting for transfers between devices, gather_rows(): lax.ppermute(jnp.stack([shard, early]), 'blk', [(s, s ^ (2 if s % 2 else...  10.5 us
    pallas_call x1, Pallas kernels, back_fused(): pl.pallas_call(back_kernel, out_shape=jax.ShapeDtypeStruct((rows, width),...  7.63 us
    pallas_call x1, Pallas kernels, pose_fused(): pl.pallas_call(pose_kernel, out_shape=(jax.ShapeDtypeStruct((1, pair_rows...  6.78 us
    dynamic_update_slice x6, local copies, waits for them, and re-layouts, gather_rows(): full = lax.dynamic_update_slice(full, pieces[k][None], (at, 0, 0))  4.97 us
    dot_general x1, matrix products, shards(): jnp.dot(receptor, full_both.reshape(-1, full_both.shape[2]), preferred_el...  4.52 us
    broadcast_in_dim x1, local copies, waits for them, and re-layouts, gather_rows(): full = jnp.zeros((count,) + shard.shape, shard.dtype)  2.47 us
  transfers between devices with their start and end apart: 13, of which 6 were waited for; matrix products, arithmetic and copies ran while one was open for 17% of the time, Pallas kernels for 0%

profile of v18, /device:TPU:16, one launch (start us, length us, event | category | flops | bytes accessed | tf_op | source)
XLA Modules:
  0.0 90.0 jit_solution(2031296684445012882)
XLA Ops:
  0.7 1.1 %constant_dynamic-update-slice_fusion.1 = bf16[128,2048]{1,0:T(8,128)(2,1)S(1)} fusion(bf16[128,1024]{1,0:T(8,128)(2,1)} %param.12), kind=kLoop, calls=%fused_computation.38 | loop fusion | bytes 524288
  1.7 1.0 %constant_dynamic-update-slice_fusion = bf16[128,2048]{1,0:T(8,128)(2,1)S(1)} fusion(bf16[128,2048]{1,0:T(8,128)(2,1)S(1)} %constant_dynamic-update-slice_fusion.1, bf16[128,1024]{1,0:T(8,128)(2,1)} %param.13), kind=kLoop, calls=%fused_computation.37 | loop fusion | bytes 524288 | tf_op jit(solution)/shard_map/concatenate | solution.py:300
  2.7 1.6 %collective-permute-start.1 = (bf16[128,2048]{1,0:T(8,128)(2,1)S(1)}, bf16[128,2048]{1,0:T(8,128)(2,1)S(1)}, u32[]{:S(2)}, u32[]{:S(2)}) collective-permute-start(bf16[128,2048]{1,0:T(8,128)(2,1)S(1)} %constant_dynamic-update-slice_fusion), channel_id=1, source_target_pairs={{0,2},{1,5},{2,0},{3,7},{4,6},{5,1},{6,4},{7,3},{8,10},{9,13},{10,... | collective-permute-start | bytes 1572872 | tf_op jit(solution)/shard_map/ppermute | solution.py:279
  4.2 0.0 collective-permute-start
  4.2 2.5 %broadcast_in_dim.72 = bf16[8,128,2048]{2,1,0:T(8,128)(2,1)} broadcast(bf16[]{:T(256)} %constant.216.clone.1), dimensions={} | broadcast | bytes 4194306 | tf_op jit(solution)/shard_map/broadcast_in_dim | solution.py:290
  6.7 0.8 constant_dynamic-update-slice_fusion.3
  7.6 0.7 fusion.14
  9.6 0.1 constant_dynamic-slice_fusion.1
  9.6 2.3 %collective-permute-done.1 = bf16[128,2048]{1,0:T(8,128)(2,1)S(1)} collective-permute-done((bf16[128,2048]{1,0:T(8,128)(2,1)S(1)}, bf16[128,2048]{1,0:T(8,128)(2,1)S(1)}, u32[]{:S(2)}, u32[]{:S(2)}) %collective-permute-start.1) | collective-permute-done | bytes 524320 | tf_op jit(solution)/shard_map/ppermute | solution.py:279
  11.9 0.1 pad_maximum_fusion
  12.0 1.6 %collective-permute-start.3 = (bf16[2,128,2048]{2,1,0:T(8,128)(2,1)S(1)}, bf16[2,128,2048]{2,1,0:T(8,128)(2,1)S(1)}, u32[]{:S(2)}, u32[]{:S(2)}) collective-permute-start(bf16[2,128,2048]{2,1,0:T(8,128)(2,1)S(1)} %pad_maximum_fusion), channel_id=1, source_target_pairs={{0,4},{1,3},{2,6},{3,1},{4,0},{5,7},{6,2},{7,5},{8,12},{9,11},{10,... | collective-permute-start | bytes 3145736 | tf_op jit(solution)/shard_map/ppermute | solution.py:281
  13.6 0.0 collective-permute-start.2
  13.6 0.0 collective-permute-done
  13.6 0.8 bitcast_dynamic-update-slice_fusion.1
  14.4 0.8 constant_dynamic-update-slice_fusion.2
  15.3 0.2 collective-permute-done.2
  15.5 0.8 bitcast_dynamic-update-slice_fusion
  16.4 10.5 %collective-permute-done.3 = bf16[2,128,2048]{2,1,0:T(8,128)(2,1)S(1)} collective-permute-done((bf16[2,128,2048]{2,1,0:T(8,128)(2,1)S(1)}, bf16[2,128,2048]{2,1,0:T(8,128)(2,1)S(1)}, u32[]{:S(2)}, u32[]{:S(2)}) %collective-permute-start.3) | collective-permute-done | bytes 1048608 | tf_op jit(solution)/shard_map/ppermute | solution.py:281
  26.9 0.8 slice_dynamic-update-slice_fusion.3
  27.7 0.8 slice_dynamic-update-slice_fusion.2
  28.5 4.5 %fusion.16 = f32[2048,512]{0,1:T(8,128)S(1)} fusion(bf16[512,1024]{1,0:T(8,128)(2,1)S(1)} %copy-done.2, bf16[1024,2048]{1,0:T(8,128)(2,1)} %bitcast.5), kind=kOutput, calls=%fused_computation.46 | convolution fusion | flops 2147483648 | bytes 9437184 | tf_op jit(solution)/shard_map/dot_general | solution.py:306
  33.1 0.0 collective-permute-done.4
  33.1 0.8 bitcast_add_fusion
  33.8 0.2 slice.72.val_ref
  34.0 1.8 %convert_reduce_fusion = (f32[1024]{0:T(1024)S(1)}, bf16[512,1024]{1,0:T(8,128)(2,1)S(1)}, f32[512,1024]{1,0:T(8,128)}) fusion(f32[512,2048]{1,0:T(8,128)S(1)} %bitcast_add_fusion), kind=kLoop, calls=%fused_computation.2 | loop fusion | flops 3668992 | bytes 5246976 | tf_op jit(solution)/shard_map/reduce_sum | solution.py:37
  35.9 1.4 %copy.17 = bf16[512,1024]{0,1:T(8,128)(2,1)} copy(bf16[512,1024]{1,0:T(8,128)(2,1)S(1)} %get-tuple-element.89.feat_ref) | data formatting | bytes 2097152 | tf_op jit(solution)/shard_map/convert_element_type | solution.py:320
  37.3 1.3 %copy.16 = bf16[512,1024]{0,1:T(8,128)(2,1)} copy(bf16[512,1024]{1,0:T(8,128)(2,1)S(1)} %slice.72.val_ref) | data formatting | bytes 2097152 | tf_op jit(solution)/shard_map/slice | solution.py:319
  38.6 2.0 %fusion.15 = f32[16,64,64]{2,1,0:T(8,128)S(1)} fusion(bf16[512,16,64]{0,2,1:T(8,128)(2,1)} %bitcast.42, bf16[512,16,64]{0,2,1:T(8,128)(2,1)} %bitcast.41), kind=kOutput, calls=%fused_computation.45 | convolution fusion | flops 67108864 | bytes 2359296 | tf_op jit(solution)/shard_map/thd,the->dhe/dot_general | solution.py:34
  40.5 0.2 copy.20
  40.8 0.6 collective-permute-start.5
  44.5 3.0 %collective-permute-start.8 = (bf16[65,1024]{1,0:T(8,128)(2,1)S(1)}, bf16[65,1024]{1,0:T(8,128)(2,1)S(1)}, u32[]{:S(2)}, u32[]{:S(2)}) collective-permute-start(bf16[65,1024]{1,0:T(8,128)(2,1)S(1)} %get-tuple-element.97), channel_id=1, source_target_pairs={{1,4},{3,6},{5,8},{7,10},{9,12},{11,14},{13,16},{15,18},{17,20},{1... | collective-permute-start | bytes 399368 | tf_op jit(solution)/shard_map/ppermute | solution.py:58
  47.5 0.1 add_convert_fusion.3
  47.6 1.5 %collective-permute-start.6 = (bf16[65,1024]{1,0:T(8,128)(2,1)S(1)}, bf16[65,1024]{1,0:T(8,128)(2,1)S(1)}, u32[]{:S(2)}, u32[]{:S(2)}) collective-permute-start(bf16[65,1024]{1,0:T(8,128)(2,1)S(1)} %get-tuple-element.95), channel_id=1, source_target_pairs={{0,2},{1,3},{2,0},{3,1},{4,6},{5,7},{6,4},{7,5},{8,10},{9,11},{10,... | collective-permute-start | bytes 399368 | tf_op jit(solution)/shard_map/ppermute | solution.py:58
  49.1 2.4 %collective-permute-start.7 = (bf16[65,1024]{1,0:T(8,128)(2,1)S(1)}, bf16[65,1024]{1,0:T(8,128)(2,1)S(1)}, u32[]{:S(2)}, u32[]{:S(2)}) collective-permute-start(bf16[65,1024]{1,0:T(8,128)(2,1)S(1)} %get-tuple-element.96), channel_id=1, source_target_pairs={{2,4},{3,5},{4,2},{5,3},{6,8},{7,9},{8,6},{9,7},{10,12},{11,13},{1... | collective-permute-start | bytes 399368 | tf_op jit(solution)/shard_map/ppermute | solution.py:58
  51.5 0.9 slice_dynamic-update-slice_fusion.1
  52.4 0.0 collective-permute-done.8
  52.4 1.6 %collective-permute-done.6 = bf16[65,1024]{1,0:T(8,128)(2,1)S(1)} collective-permute-done((bf16[65,1024]{1,0:T(8,128)(2,1)S(1)}, bf16[65,1024]{1,0:T(8,128)(2,1)S(1)}, u32[]{:S(2)}, u32[]{:S(2)}) %collective-permute-start.6) | collective-permute-done | bytes 133152 | tf_op jit(solution)/shard_map/ppermute | solution.py:58
  54.0 4.9 %collective-permute-done.7 = bf16[65,1024]{1,0:T(8,128)(2,1)S(1)} collective-permute-done((bf16[65,1024]{1,0:T(8,128)(2,1)S(1)}, bf16[65,1024]{1,0:T(8,128)(2,1)S(1)}, u32[]{:S(2)}, u32[]{:S(2)}) %collective-permute-start.7) | collective-permute-done | bytes 133152 | tf_op jit(solution)/shard_map/ppermute | solution.py:58
  58.9 0.8 fusion.3.state_ref
  59.7 6.8 %shard_map.103 = (f32[1,256]{1,0:T(1,128)}, bf16[128,1024]{1,0:T(8,128)(2,1)}, f32[65,1024]{1,0:T(8,128)}, bf16[65,1024]{1,0:T(8,128)(2,1)}) custom-call(bf16[128,1024]{1,0:T(8,128)(2,1)} %pose_ref.1, s32[2,256]{1,0:T(2,128)} %bitcast.50, f32[65,1024]{1,0:T(8,128)} %fusion.3.state_ref, bf16[1024,1024]{1,0:T(8,128)(2,1)} %query_ref.1, f32[1,1024]{1,0:T(1,128)} %bitcast.49), custom_call_target="tpu_custom_call" | custom-call | tf_op jit(solution)/shard_map/pallas_call | solution.py:222
  66.5 2.0 %collective-permute-start.12 = (bf16[65,1024]{1,0:T(8,128)(2,1)S(1)}, bf16[65,1024]{1,0:T(8,128)(2,1)S(1)}, u32[]{:S(2)}, u32[]{:S(2)}) collective-permute-start(bf16[65,1024]{1,0:T(8,128)(2,1)S(1)} %select_convert_fusion.1), channel_id=1, source_target_pairs={{1,4},{3,6},{5,8},{7,10},{9,12},{11,14},{13,16},{15,18},{17,20},{1... | collective-permute-start | bytes 399368 | tf_op jit(solution)/shard_map/ppermute | solution.py:58
  68.5 1.1 %add_convert_fusion.1 = (bf16[65,1024]{1,0:T(8,128)(2,1)S(1)}, bf16[65,1024]{1,0:T(8,128)(2,1)S(1)}) fusion(f32[65,1024]{1,0:T(8,128)} %get-tuple-element.9, bf16[65,1024]{1,0:T(8,128)(2,1)S(1)} %collective-permute-done.9, pred[]{:T(512)S(6)} %and.121, pred[]{:T(512)S(6)} %eq.47, pred[]{:T(512)S(6)} %and.119, pred[]{:T(512)S(6)} %and.125, pred[]{:T(512)S(6)} %and.124), kind=kLoop, calls=%fused_computation.29 | loop fusion | flops 732160 | bytes 665605 | tf_op jit(solution)/shard_map/convert_element_type | solution.py:90
  69.6 1.5 %collective-permute-start.10 = (bf16[65,1024]{1,0:T(8,128)(2,1)S(1)}, bf16[65,1024]{1,0:T(8,128)(2,1)S(1)}, u32[]{:S(2)}, u32[]{:S(2)}) collective-permute-start(bf16[65,1024]{1,0:T(8,128)(2,1)S(1)} %get-tuple-element.93), channel_id=1, source_target_pairs={{0,2},{1,3},{2,0},{3,1},{4,6},{5,7},{6,4},{7,5},{8,10},{9,11},{10,... | collective-permute-start | bytes 399368 | tf_op jit(solution)/shard_map/ppermute | solution.py:58
  71.1 4.0 %collective-permute-start.11 = (bf16[65,1024]{1,0:T(8,128)(2,1)S(1)}, bf16[65,1024]{1,0:T(8,128)(2,1)S(1)}, u32[]{:S(2)}, u32[]{:S(2)}) collective-permute-start(bf16[65,1024]{1,0:T(8,128)(2,1)S(1)} %get-tuple-element.94), channel_id=1, source_target_pairs={{2,4},{3,5},{4,2},{5,3},{6,8},{7,9},{8,6},{9,7},{10,12},{11,13},{1... | collective-permute-start | bytes 399368 | tf_op jit(solution)/shard_map/ppermute | solution.py:58
  75.1 0.8 slice_dynamic-update-slice_fusion
  76.0 4.7 %collective-permute-done.11 = bf16[65,1024]{1,0:T(8,128)(2,1)S(1)} collective-permute-done((bf16[65,1024]{1,0:T(8,128)(2,1)S(1)}, bf16[65,1024]{1,0:T(8,128)(2,1)S(1)}, u32[]{:S(2)}, u32[]{:S(2)}) %collective-permute-start.11) | collective-permute-done | bytes 133152 | tf_op jit(solution)/shard_map/ppermute | solution.py:58
  80.6 1.7 %fusion.8.grad_ref = bf16[65,1024]{1,0:T(8,128)(2,1)} fusion(f32[65,1024]{1,0:T(8,128)} %get-tuple-element.9, bf16[65,1024]{1,0:T(8,128)(2,1)S(1)} %collective-permute-done.9, bf16[65,1024]{1,0:T(8,128)(2,1)S(1)} %collective-permute-done.12, bf16[65,1024]{1,0:T(8,128)(2,1)S(1)} %collective-permute-done.11, bf16[65,1024]{1,0:T(8,128)(2,1)S(1)} %collective-permute-done.10, ...), kind=kLoop, calls=%fused_computation.25 | loop fusion | flops 665600 | bytes 931841 | tf_op jit(solution)/shard_map/convert_element_type | solution.py:324
  82.4 7.6 %shard_map.104 = bf16[512,1024]{1,0:T(8,128)(2,1)} custom-call(bf16[512,1024]{1,0:T(8,128)(2,1)} %copy-done.1, bf16[512,1024]{1,0:T(8,128)(2,1)} %copy-done, f32[512,1024]{1,0:T(8,128)} %get-tuple-element.90.keys_ref, bf16[65,1024]{1,0:T(8,128)(2,1)} %fusion.8.grad_ref, bf16[1024,2048]{1,0:T(8,128)(2,1)} %bitcast.28.full_ref), custom_call_target="tpu_custom_call" | custom-call | tf_op jit(solution)/shard_map/pallas_call | solution.py:260
  (16 shorter events, 0.1 us)
Async XLA Ops:
  0.6 6.9 %copy-start.3 = (s32[32]{0:T(128)S(1)}, s32[32]{0:T(128)}, u32[]{:S(2)}) copy-start(s32[32]{0:T(128)} %param.11) | copy-start | bytes 388
  0.6 8.9 %copy-start.2 = (bf16[512,1024]{1,0:T(8,128)(2,1)S(1)}, bf16[512,1024]{1,0:T(8,128)(2,1)}, u32[]{:S(2)}) copy-start(bf16[512,1024]{1,0:T(8,128)(2,1)} %param.8) | copy-start | bytes 3145732
  2.7 9.2 %collective-permute-start.1 = (bf16[128,2048]{1,0:T(8,128)(2,1)S(1)}, bf16[128,2048]{1,0:T(8,128)(2,1)S(1)}, u32[]{:S(2)}, u32[]{:S(2)}) collective-permute-start(bf16[128,2048]{1,0:T(8,128)(2,1)S(1)} %constant_dynamic-update-slice_fusion), channel_id=1, source_target_pairs={{0,2},{1,5},{2,0},{3,7},{4,6},{5,1},{6,4},{7,3},{8,10},{9,13},{10,... | collective-permute-start | bytes 1572872 | tf_op jit(solution)/shard_map/ppermute | solution.py:279
  4.2 9.4 %collective-permute-start = (bf16[128,2048]{1,0:T(8,128)(2,1)S(1)}, bf16[128,2048]{1,0:T(8,128)(2,1)S(1)}, u32[]{:S(2)}, u32[]{:S(2)}) collective-permute-start(bf16[128,2048]{1,0:T(8,128)(2,1)S(1)} %constant_dynamic-update-slice_fusion), channel_id=1, source_target_pairs={{0,1},{1,0},{2,3},{3,2},{4,5},{5,4},{6,7},{7,6},{8,9},{9,8},{10,11... | collective-permute-start | bytes 1572872 | tf_op jit(solution)/shard_map/ppermute | solution.py:278
  12.0 14.9 %collective-permute-start.3 = (bf16[2,128,2048]{2,1,0:T(8,128)(2,1)S(1)}, bf16[2,128,2048]{2,1,0:T(8,128)(2,1)S(1)}, u32[]{:S(2)}, u32[]{:S(2)}) collective-permute-start(bf16[2,128,2048]{2,1,0:T(8,128)(2,1)S(1)} %pad_maximum_fusion), channel_id=1, source_target_pairs={{0,4},{1,3},{2,6},{3,1},{4,0},{5,7},{6,2},{7,5},{8,12},{9,11},{10,... | collective-permute-start | bytes 3145736 | tf_op jit(solution)/shard_map/ppermute | solution.py:281
  13.6 1.9 %collective-permute-start.2 = (bf16[128,2048]{1,0:T(8,128)(2,1)S(1)}, bf16[128,2048]{1,0:T(8,128)(2,1)S(1)}, u32[]{:S(2)}, u32[]{:S(2)}) collective-permute-start(bf16[128,2048]{1,0:T(8,128)(2,1)S(1)} %collective-permute-done.1), channel_id=1, source_target_pairs={{0,1},{1,0},{2,3},{3,2},{4,5},{5,4},{6,7},{7,6},{8,9},{9,8},{10,11... | collective-permute-start | bytes 1572872 | tf_op jit(solution)/shard_map/ppermute | solution.py:280
  26.9 6.2 %collective-permute-start.4 = (bf16[2,128,2048]{2,1,0:T(8,128)(2,1)S(1)}, bf16[2,128,2048]{2,1,0:T(8,128)(2,1)S(1)}, u32[]{:S(2)}, u32[]{:S(2)}) collective-permute-start(bf16[2,128,2048]{2,1,0:T(8,128)(2,1)S(1)} %collective-permute-done.3), channel_id=1, source_target_pairs={{0,1},{1,0},{2,3},{3,2},{4,5},{5,4},{6,7},{7,6},{8,9},{9,8},{10,11... | collective-permute-start | bytes 3145736 | tf_op jit(solution)/shard_map/ppermute | solution.py:284
  34.0 4.6 %copy-start = (bf16[512,1024]{1,0:T(8,128)(2,1)}, bf16[512,1024]{1,0:T(8,128)(2,1)S(1)}, u32[]{:S(2)}) copy-start(bf16[512,1024]{1,0:T(8,128)(2,1)S(1)} %slice.72.val_ref) | copy-start | bytes 3145732
  35.9 11.7 %copy-start.1 = (bf16[512,1024]{1,0:T(8,128)(2,1)}, bf16[512,1024]{1,0:T(8,128)(2,1)S(1)}, u32[]{:S(2)}) copy-start(bf16[512,1024]{1,0:T(8,128)(2,1)S(1)} %get-tuple-element.89.feat_ref) | copy-start | bytes 3145732
  40.8 6.7 %collective-permute-start.5 = (bf16[65,1024]{1,0:T(8,128)(2,1)S(1)}, bf16[65,1024]{1,0:T(8,128)(2,1)S(1)}, u32[]{:S(2)}, u32[]{:S(2)}) collective-permute-start(bf16[65,1024]{1,0:T(8,128)(2,1)S(1)} %get-tuple-element.98), channel_id=1, source_target_pairs={{0,1},{1,0},{2,3},{3,2},{4,5},{5,4},{6,7},{7,6},{8,9},{9,8},{10,11... | collective-permute-start | bytes 399368 | tf_op jit(solution)/shard_map/ppermute | solution.py:58
  44.5 7.9 %collective-permute-start.8 = (bf16[65,1024]{1,0:T(8,128)(2,1)S(1)}, bf16[65,1024]{1,0:T(8,128)(2,1)S(1)}, u32[]{:S(2)}, u32[]{:S(2)}) collective-permute-start(bf16[65,1024]{1,0:T(8,128)(2,1)S(1)} %get-tuple-element.97), channel_id=1, source_target_pairs={{1,4},{3,6},{5,8},{7,10},{9,12},{11,14},{13,16},{15,18},{17,20},{1... | collective-permute-start | bytes 399368 | tf_op jit(solution)/shard_map/ppermute | solution.py:58
  47.6 6.4 %collective-permute-start.6 = (bf16[65,1024]{1,0:T(8,128)(2,1)S(1)}, bf16[65,1024]{1,0:T(8,128)(2,1)S(1)}, u32[]{:S(2)}, u32[]{:S(2)}) collective-permute-start(bf16[65,1024]{1,0:T(8,128)(2,1)S(1)} %get-tuple-element.95), channel_id=1, source_target_pairs={{0,2},{1,3},{2,0},{3,1},{4,6},{5,7},{6,4},{7,5},{8,10},{9,11},{10,... | collective-permute-start | bytes 399368 | tf_op jit(solution)/shard_map/ppermute | solution.py:58
  49.1 9.7 %collective-permute-start.7 = (bf16[65,1024]{1,0:T(8,128)(2,1)S(1)}, bf16[65,1024]{1,0:T(8,128)(2,1)S(1)}, u32[]{:S(2)}, u32[]{:S(2)}) collective-permute-start(bf16[65,1024]{1,0:T(8,128)(2,1)S(1)} %get-tuple-element.96), channel_id=1, source_target_pairs={{2,4},{3,5},{4,2},{5,3},{6,8},{7,9},{8,6},{9,7},{10,12},{11,13},{1... | collective-permute-start | bytes 399368 | tf_op jit(solution)/shard_map/ppermute | solution.py:58
  66.5 2.1 %collective-permute-start.9 = (bf16[65,1024]{1,0:T(8,128)(2,1)}, bf16[65,1024]{1,0:T(8,128)(2,1)S(1)}, u32[]{:S(2)}, u32[]{:S(2)}) collective-permute-start(bf16[65,1024]{1,0:T(8,128)(2,1)} %get-tuple-element.10), channel_id=1, source_target_pairs={{0,1},{1,0},{2,3},{3,2},{4,5},{5,4},{6,7},{7,6},{8,9},{9,8},{10,11... | collective-permute-start | bytes 399368 | tf_op jit(solution)/shard_map/ppermute | solution.py:58
  66.5 9.5 %collective-permute-start.12 = (bf16[65,1024]{1,0:T(8,128)(2,1)S(1)}, bf16[65,1024]{1,0:T(8,128)(2,1)S(1)}, u32[]{:S(2)}, u32[]{:S(2)}) collective-permute-start(bf16[65,1024]{1,0:T(8,128)(2,1)S(1)} %select_convert_fusion.1), channel_id=1, source_target_pairs={{1,4},{3,6},{5,8},{7,10},{9,12},{11,14},{13,16},{15,18},{17,20},{1... | collective-permute-start | bytes 399368 | tf_op jit(solution)/shard_map/ppermute | solution.py:58
  69.6 6.4 %collective-permute-start.10 = (bf16[65,1024]{1,0:T(8,128)(2,1)S(1)}, bf16[65,1024]{1,0:T(8,128)(2,1)S(1)}, u32[]{:S(2)}, u32[]{:S(2)}) collective-permute-start(bf16[65,1024]{1,0:T(8,128)(2,1)S(1)} %get-tuple-element.93), channel_id=1, source_target_pairs={{0,2},{1,3},{2,0},{3,1},{4,6},{5,7},{6,4},{7,5},{8,10},{9,11},{10,... | collective-permute-start | bytes 399368 | tf_op jit(solution)/shard_map/ppermute | solution.py:58
  71.1 9.5 %collective-permute-start.11 = (bf16[65,1024]{1,0:T(8,128)(2,1)S(1)}, bf16[65,1024]{1,0:T(8,128)(2,1)S(1)}, u32[]{:S(2)}, u32[]{:S(2)}) collective-permute-start(bf16[65,1024]{1,0:T(8,128)(2,1)S(1)} %get-tuple-element.94), channel_id=1, source_target_pairs={{2,4},{3,5},{4,2},{5,3},{6,8},{7,9},{8,6},{9,7},{10,12},{11,13},{1... | collective-permute-start | bytes 399368 | tf_op jit(solution)/shard_map/ppermute | solution.py:58

commit v19 on v18

--- a/solution.py
+++ b/solution.py
@@ -58,7 +58,7 @@
     return lax.ppermute(value, axis, pairs)
 
 
-def complex_sum(own, block_complex, narrow=None):
+def complex_sum(own, block_complex, narrow=None, split=False):
     axis = ("sec", "blk")
     count = lax.axis_size(axis)
     position = lax.axis_index(axis)
@@ -102,8 +102,18 @@
     down = send(
         chip_part(jnp.where(even_chip, position - 2, position + 2)), axis, pairs_b
     )
+    if split:
+        alike = jnp.logical_and(twin <= last, complex_of(twin) == complex_of(position))
+        return own, sibling, alike.astype(own.dtype).reshape(1, 1), up, down, far
     total = own + kept(sibling, twin, position)
     return total + up.astype(own.dtype) + down.astype(own.dtype) + far.astype(own.dtype)
+
+
+def add_terms(own_ref, twin_ref, alike_ref, up_ref, down_ref, far_ref):
+    total = own_ref[...] + twin_ref[...].astype(jnp.float32) * alike_ref[...]
+    for ref in (up_ref, down_ref, far_ref):
+        total = total + ref[...].astype(jnp.float32)
+    return total
 
 
 def pose_side(pose_rows, pair_rows, state, w_query, score_weight):
@@ -233,7 +243,10 @@
     return (loss.reshape(pair_rows.shape[0]), grad, (back, narrow))
 
 
-def back_kernel(feat_ref, val_ref, keys_ref, grad_ref, full_ref, out_ref, both_ref):
+def back_kernel(feat_ref, val_ref, keys_ref, *refs):
+    terms = refs[:6]
+    full_ref, out_ref, both_ref, grad_ref = refs[6:]
+    grad_ref[...] = add_terms(*terms).astype(grad_ref.dtype)
     width = feat_ref.shape[1]
     lanes = 2 * DH
     head_row = lax.broadcasted_iota(jnp.int32, (lanes, lanes), 0) // DH
@@ -260,9 +273,12 @@
     return pl.pallas_call(
         back_kernel,
         out_shape=jax.ShapeDtypeStruct((rows, width), jnp.bfloat16),
-        scratch_shapes=[pltpu.VMEM((rows, 2 * width), jnp.bfloat16)],
+        scratch_shapes=[
+            pltpu.VMEM((rows, 2 * width), jnp.bfloat16),
+            pltpu.VMEM(state_grad[0].shape, jnp.bfloat16),
+        ],
         interpret=interpret,
-    )(key_feat, val_round, keys, state_grad, full_both)
+    )(key_feat, val_round, keys, *state_grad, full_both)
 
 
 def gather_rows(shard):
@@ -321,7 +337,7 @@
     val_round = values.astype(jnp.bfloat16)
     state = complex_sum(local_state(key_feat, val_round), block_complex)
     pair_loss, pose_grad, pose_state = pose_fused(poses, pairs, state, w_query, score_weight)
-    state_grad = complex_sum(pose_state[0], block_complex, pose_state[1]).astype(jnp.bfloat16)
+    state_grad = complex_sum(pose_state[0], block_complex, pose_state[1], split=True)
     total = back_fused(key_feat, val_round, keys, state_grad, full_both)
     return (pair_loss, pose_grad, total)
 

time: 90.8 us -> 92.2 us (1.015)
  waiting for transfers between devices: 24.2 us -> 25.5 us
  other arithmetic: 5.72 us -> 4.74 us
    ppermute x8, waiting for transfers between devices: 11.2 us -> 12.5 us  [send(): return lax.ppermute(value, axis, pairs)]
    convert_element_type x1, other arithmetic: 1.73 us -> 0.76 us  [complex_sum(): send(narrow, axis, [(s, s ^ 1) for s in range(count)]).astype(own.dtype)]
  transfers between devices with their start and end apart: 13 -> 13, of which waited for: 6 -> 7; matrix products, arithmetic and copies ran while one was open for 17% -> 18% of each run, Pallas kernels for 0% -> 0%
where the time goes in v19:
time: 92.2 us; the launch traced here: 91.5 us
  waiting for transfers between devices  25.5 us (28%)
  starting transfers between devices  18.2 us (20%)
  local copies, waits for them, and re-layouts  15.6 us (17%)
  Pallas kernels  14.8 us (16%)
  matrix products  7.23 us (8%)
  between operations  5.36 us (6%)
  other arithmetic  4.74 us (5%)
    ppermute x8, starting transfers between devices, send(): return lax.ppermute(value, axis, pairs)  15.1 us
    ppermute x8, waiting for transfers between devices, send(): return lax.ppermute(value, axis, pairs)  12.5 us
    ppermute x1, waiting for transfers between devices, gather_rows(): lax.ppermute(jnp.stack([shard, early]), 'blk', [(s, s ^ (2 if s % 2 else...  10.5 us
    pallas_call x1, Pallas kernels, back_fused(): pl.pallas_call(back_kernel, out_shape=jax.ShapeDtypeStruct((rows, width),...  8.02 us
    pallas_call x1, Pallas kernels, pose_fused(): pl.pallas_call(pose_kernel, out_shape=(jax.ShapeDtypeStruct((1, pair_rows...  6.78 us
    dynamic_update_slice x6, local copies, waits for them, and re-layouts, gather_rows(): full = lax.dynamic_update_slice(full, pieces[k][None], (at, 0, 0))  5.01 us
    dot_general x1, matrix products, shards(): jnp.dot(receptor, full_both.reshape(-1, full_both.shape[2]), preferred_el...  4.52 us
    broadcast_in_dim x1, local copies, waits for them, and re-layouts, gather_rows(): full = jnp.zeros((count,) + shard.shape, shard.dtype)  2.47 us
  transfers between devices with their start and end apart: 13, of which 7 were waited for; matrix products, arithmetic and copies ran while one was open for 18% of the time, Pallas kernels for 0%

profile of v19, /device:TPU:16, one launch (start us, length us, event | category | flops | bytes accessed | tf_op | source)
XLA Modules:
  0.0 91.5 jit_solution(13541078503956294409)
XLA Ops:
  0.7 1.1 %constant_dynamic-update-slice_fusion.1 = bf16[128,2048]{1,0:T(8,128)(2,1)S(1)} fusion(bf16[128,1024]{1,0:T(8,128)(2,1)} %param.12), kind=kLoop, calls=%fused_computation.32 | loop fusion | bytes 524288
  1.7 1.0 %constant_dynamic-update-slice_fusion = bf16[128,2048]{1,0:T(8,128)(2,1)S(1)} fusion(bf16[128,2048]{1,0:T(8,128)(2,1)S(1)} %constant_dynamic-update-slice_fusion.1, bf16[128,1024]{1,0:T(8,128)(2,1)} %param.13), kind=kLoop, calls=%fused_computation.31 | loop fusion | bytes 524288 | tf_op jit(solution)/shard_map/concatenate | solution.py:316
  2.7 1.6 %collective-permute-start.1 = (bf16[128,2048]{1,0:T(8,128)(2,1)S(1)}, bf16[128,2048]{1,0:T(8,128)(2,1)S(1)}, u32[]{:S(2)}, u32[]{:S(2)}) collective-permute-start(bf16[128,2048]{1,0:T(8,128)(2,1)S(1)} %constant_dynamic-update-slice_fusion), channel_id=1, source_target_pairs={{0,2},{1,5},{2,0},{3,7},{4,6},{5,1},{6,4},{7,3},{8,10},{9,13},{10,... | collective-permute-start | bytes 1572872 | tf_op jit(solution)/shard_map/ppermute | solution.py:295
  4.2 0.0 collective-permute-start
  4.2 2.5 %broadcast_in_dim.71 = bf16[8,128,2048]{2,1,0:T(8,128)(2,1)} broadcast(bf16[]{:T(256)} %constant.216.clone.1), dimensions={} | broadcast | bytes 4194306 | tf_op jit(solution)/shard_map/broadcast_in_dim | solution.py:306
  6.7 0.8 constant_dynamic-update-slice_fusion.3
  7.6 0.7 fusion.9
  9.6 0.1 constant_dynamic-slice_fusion.1
  9.7 2.3 %collective-permute-done.1 = bf16[128,2048]{1,0:T(8,128)(2,1)S(1)} collective-permute-done((bf16[128,2048]{1,0:T(8,128)(2,1)S(1)}, bf16[128,2048]{1,0:T(8,128)(2,1)S(1)}, u32[]{:S(2)}, u32[]{:S(2)}) %collective-permute-start.1) | collective-permute-done | bytes 524320 | tf_op jit(solution)/shard_map/ppermute | solution.py:295
  11.9 0.1 pad_maximum_fusion
  12.0 1.6 %collective-permute-start.3 = (bf16[2,128,2048]{2,1,0:T(8,128)(2,1)S(1)}, bf16[2,128,2048]{2,1,0:T(8,128)(2,1)S(1)}, u32[]{:S(2)}, u32[]{:S(2)}) collective-permute-start(bf16[2,128,2048]{2,1,0:T(8,128)(2,1)S(1)} %pad_maximum_fusion), channel_id=1, source_target_pairs={{0,4},{1,3},{2,6},{3,1},{4,0},{5,7},{6,2},{7,5},{8,12},{9,11},{10,... | collective-permute-start | bytes 3145736 | tf_op jit(solution)/shard_map/ppermute | solution.py:297
  13.6 0.0 collective-permute-start.2
  13.6 0.0 collective-permute-done
  13.6 0.8 bitcast_dynamic-update-slice_fusion.1
  14.5 0.8 constant_dynamic-update-slice_fusion.2
  15.3 0.2 collective-permute-done.2
  15.5 0.8 bitcast_dynamic-update-slice_fusion
  16.4 10.5 %collective-permute-done.3 = bf16[2,128,2048]{2,1,0:T(8,128)(2,1)S(1)} collective-permute-done((bf16[2,128,2048]{2,1,0:T(8,128)(2,1)S(1)}, bf16[2,128,2048]{2,1,0:T(8,128)(2,1)S(1)}, u32[]{:S(2)}, u32[]{:S(2)}) %collective-permute-start.3) | collective-permute-done | bytes 1048608 | tf_op jit(solution)/shard_map/ppermute | solution.py:297
  26.9 0.8 slice_dynamic-update-slice_fusion.3
  27.7 0.8 slice_dynamic-update-slice_fusion.2
  28.6 4.5 %fusion.11 = f32[2048,512]{0,1:T(8,128)S(1)} fusion(bf16[512,1024]{1,0:T(8,128)(2,1)S(1)} %copy-done.5, bf16[1024,2048]{1,0:T(8,128)(2,1)} %bitcast.5), kind=kOutput, calls=%fused_computation.40 | convolution fusion | flops 2147483648 | bytes 9437184 | tf_op jit(solution)/shard_map/dot_general | solution.py:322
  33.1 0.8 bitcast_add_fusion
  33.9 0.2 slice.72.val_ref
  34.0 1.8 %convert_reduce_fusion = (f32[1024]{0:T(1024)S(1)}, bf16[512,1024]{1,0:T(8,128)(2,1)S(1)}, f32[512,1024]{1,0:T(8,128)}) fusion(f32[512,2048]{1,0:T(8,128)S(1)} %bitcast_add_fusion), kind=kLoop, calls=%fused_computation.2 | loop fusion | flops 3668992 | bytes 5246976 | tf_op jit(solution)/shard_map/reduce_sum | solution.py:37
  35.9 1.4 %copy.17 = bf16[512,1024]{0,1:T(8,128)(2,1)} copy(bf16[512,1024]{1,0:T(8,128)(2,1)S(1)} %get-tuple-element.89.feat_ref) | data formatting | bytes 2097152 | tf_op jit(solution)/shard_map/convert_element_type | solution.py:336
  37.3 1.3 %copy.16 = bf16[512,1024]{0,1:T(8,128)(2,1)} copy(bf16[512,1024]{1,0:T(8,128)(2,1)S(1)} %slice.72.val_ref) | data formatting | bytes 2097152 | tf_op jit(solution)/shard_map/slice | solution.py:335
  38.6 2.0 %fusion.10 = f32[16,64,64]{2,1,0:T(8,128)S(1)} fusion(bf16[512,16,64]{0,2,1:T(8,128)(2,1)} %bitcast.43, bf16[512,16,64]{0,2,1:T(8,128)(2,1)} %bitcast.42), kind=kOutput, calls=%fused_computation.39 | convolution fusion | flops 67108864 | bytes 2359296 | tf_op jit(solution)/shard_map/thd,the->dhe/dot_general | solution.py:34
  40.5 0.2 copy.20
  40.8 0.6 collective-permute-start.5
  44.5 3.0 %collective-permute-start.8 = (bf16[65,1024]{1,0:T(8,128)(2,1)S(1)}, bf16[65,1024]{1,0:T(8,128)(2,1)S(1)}, u32[]{:S(2)}, u32[]{:S(2)}) collective-permute-start(bf16[65,1024]{1,0:T(8,128)(2,1)S(1)} %get-tuple-element.97), channel_id=1, source_target_pairs={{1,4},{3,6},{5,8},{7,10},{9,12},{11,14},{13,16},{15,18},{17,20},{1... | collective-permute-start | bytes 399368 | tf_op jit(solution)/shard_map/ppermute | solution.py:58
  47.5 0.1 add_convert_fusion.3
  47.6 1.6 %collective-permute-start.6 = (bf16[65,1024]{1,0:T(8,128)(2,1)S(1)}, bf16[65,1024]{1,0:T(8,128)(2,1)S(1)}, u32[]{:S(2)}, u32[]{:S(2)}) collective-permute-start(bf16[65,1024]{1,0:T(8,128)(2,1)S(1)} %get-tuple-element.95), channel_id=1, source_target_pairs={{0,2},{1,3},{2,0},{3,1},{4,6},{5,7},{6,4},{7,5},{8,10},{9,11},{10,... | collective-permute-start | bytes 399368 | tf_op jit(solution)/shard_map/ppermute | solution.py:58
  49.2 2.4 %collective-permute-start.7 = (bf16[65,1024]{1,0:T(8,128)(2,1)S(1)}, bf16[65,1024]{1,0:T(8,128)(2,1)S(1)}, u32[]{:S(2)}, u32[]{:S(2)}) collective-permute-start(bf16[65,1024]{1,0:T(8,128)(2,1)S(1)} %get-tuple-element.96), channel_id=1, source_target_pairs={{2,4},{3,5},{4,2},{5,3},{6,8},{7,9},{8,6},{9,7},{10,12},{11,13},{1... | collective-permute-start | bytes 399368 | tf_op jit(solution)/shard_map/ppermute | solution.py:58
  51.6 0.8 slice_dynamic-update-slice_fusion.1
  52.4 1.6 %collective-permute-done.6 = bf16[65,1024]{1,0:T(8,128)(2,1)S(1)} collective-permute-done((bf16[65,1024]{1,0:T(8,128)(2,1)S(1)}, bf16[65,1024]{1,0:T(8,128)(2,1)S(1)}, u32[]{:S(2)}, u32[]{:S(2)}) %collective-permute-start.6) | collective-permute-done | bytes 133152 | tf_op jit(solution)/shard_map/ppermute | solution.py:58
  54.0 4.9 %collective-permute-done.7 = bf16[65,1024]{1,0:T(8,128)(2,1)S(1)} collective-permute-done((bf16[65,1024]{1,0:T(8,128)(2,1)S(1)}, bf16[65,1024]{1,0:T(8,128)(2,1)S(1)}, u32[]{:S(2)}, u32[]{:S(2)}) %collective-permute-start.7) | collective-permute-done | bytes 133152 | tf_op jit(solution)/shard_map/ppermute | solution.py:58
  58.9 0.8 fusion.3.state_ref
  59.8 6.8 %shard_map.103 = (f32[1,256]{1,0:T(1,128)}, bf16[128,1024]{1,0:T(8,128)(2,1)}, f32[65,1024]{1,0:T(8,128)}, bf16[65,1024]{1,0:T(8,128)(2,1)}) custom-call(bf16[128,1024]{1,0:T(8,128)(2,1)} %pose_ref.1, s32[2,256]{1,0:T(2,128)} %bitcast.51, f32[65,1024]{1,0:T(8,128)} %fusion.3.state_ref, bf16[1024,1024]{1,0:T(8,128)(2,1)} %query_ref.1, f32[1,1024]{1,0:T(1,128)} %bitcast.50), custom_call_target="tpu_custom_call" | custom-call | tf_op jit(solution)/shard_map/pallas_call | solution.py:232
  66.6 2.0 %collective-permute-start.12 = (bf16[65,1024]{1,0:T(8,128)(2,1)S(1)}, bf16[65,1024]{1,0:T(8,128)(2,1)S(1)}, u32[]{:S(2)}, u32[]{:S(2)}) collective-permute-start(bf16[65,1024]{1,0:T(8,128)(2,1)S(1)} %select_convert_fusion.1), channel_id=1, source_target_pairs={{1,4},{3,6},{5,8},{7,10},{9,12},{11,14},{13,16},{15,18},{17,20},{1... | collective-permute-start | bytes 399368 | tf_op jit(solution)/shard_map/ppermute | solution.py:58
  68.6 1.1 %add_convert_fusion = (bf16[65,1024]{1,0:T(8,128)(2,1)S(1)}, bf16[65,1024]{1,0:T(8,128)(2,1)S(1)}) fusion(f32[65,1024]{1,0:T(8,128)} %get-tuple-element.9.refs_0_, bf16[65,1024]{1,0:T(8,128)(2,1)S(1)} %collective-permute-done.9, pred[]{:T(512)S(6)} %and.126, pred[]{:T(512)S(6)} %and.125, pred[]{:T(512)S(6)} %eq.47, pred[]{:T(512)S(6)} %and.122, pred[]{:T(512)S(6)} %and.120), kind=kLoop, calls=%fused_computation.20 | loop fusion | flops 732160 | bytes 665605 | tf_op jit(solution)/shard_map/convert_element_type | solution.py:90
  69.7 3.6 %collective-permute-start.11 = (bf16[65,1024]{1,0:T(8,128)(2,1)S(1)}, bf16[65,1024]{1,0:T(8,128)(2,1)S(1)}, u32[]{:S(2)}, u32[]{:S(2)}) collective-permute-start(bf16[65,1024]{1,0:T(8,128)(2,1)S(1)} %get-tuple-element.93), channel_id=1, source_target_pairs={{2,4},{3,5},{4,2},{5,3},{6,8},{7,9},{8,6},{9,7},{10,12},{11,13},{1... | collective-permute-start | bytes 399368 | tf_op jit(solution)/shard_map/ppermute | solution.py:58
  73.3 2.0 %collective-permute-start.10 = (bf16[65,1024]{1,0:T(8,128)(2,1)S(1)}, bf16[65,1024]{1,0:T(8,128)(2,1)S(1)}, u32[]{:S(2)}, u32[]{:S(2)}) collective-permute-start(bf16[65,1024]{1,0:T(8,128)(2,1)S(1)} %get-tuple-element.94), channel_id=1, source_target_pairs={{0,2},{1,3},{2,0},{3,1},{4,6},{5,7},{6,4},{7,5},{8,10},{9,11},{10,... | collective-permute-start | bytes 399368 | tf_op jit(solution)/shard_map/ppermute | solution.py:58
  75.3 0.8 slice_dynamic-update-slice_fusion
  76.1 0.8 convert_element_type.54.refs_1_
  76.9 2.7 %collective-permute-done.11.refs_4_ = bf16[65,1024]{1,0:T(8,128)(2,1)S(1)} collective-permute-done((bf16[65,1024]{1,0:T(8,128)(2,1)S(1)}, bf16[65,1024]{1,0:T(8,128)(2,1)S(1)}, u32[]{:S(2)}, u32[]{:S(2)}) %collective-permute-start.11) | collective-permute-done | bytes 133152 | tf_op jit(solution)/shard_map/ppermute | solution.py:58
  79.6 3.2 %collective-permute-done.10.refs_3_ = bf16[65,1024]{1,0:T(8,128)(2,1)S(1)} collective-permute-done((bf16[65,1024]{1,0:T(8,128)(2,1)S(1)}, bf16[65,1024]{1,0:T(8,128)(2,1)S(1)}, u32[]{:S(2)}, u32[]{:S(2)}) %collective-permute-start.10) | collective-permute-done | bytes 133152 | tf_op jit(solution)/shard_map/ppermute | solution.py:58
  82.9 0.6 copy-done.4
  83.5 8.0 %shard_map.104 = bf16[512,1024]{1,0:T(8,128)(2,1)} custom-call(bf16[512,1024]{1,0:T(8,128)(2,1)} %copy-done.1, bf16[512,1024]{1,0:T(8,128)(2,1)} %copy-done, f32[512,1024]{1,0:T(8,128)} %get-tuple-element.90.keys_ref, f32[65,1024]{1,0:T(8,128)} %get-tuple-element.9.refs_0_, f32[65,1024]{1,0:T(8,128)} %convert_element_type.54.refs_1_, ...), custom_call_target="tpu_custom_call" | custom-call | tf_op jit(solution)/shard_map/pallas_call | solution.py:273
  (22 shorter events, 0.1 us)
Async XLA Ops:
  0.6 6.9 %copy-start.6 = (s32[32]{0:T(128)S(1)}, s32[32]{0:T(128)}, u32[]{:S(2)}) copy-start(s32[32]{0:T(128)} %param.11) | copy-start | bytes 388
  0.6 8.9 %copy-start.5 = (bf16[512,1024]{1,0:T(8,128)(2,1)S(1)}, bf16[512,1024]{1,0:T(8,128)(2,1)}, u32[]{:S(2)}) copy-start(bf16[512,1024]{1,0:T(8,128)(2,1)} %param.8) | copy-start | bytes 3145732
  2.7 9.2 %collective-permute-start.1 = (bf16[128,2048]{1,0:T(8,128)(2,1)S(1)}, bf16[128,2048]{1,0:T(8,128)(2,1)S(1)}, u32[]{:S(2)}, u32[]{:S(2)}) collective-permute-start(bf16[128,2048]{1,0:T(8,128)(2,1)S(1)} %constant_dynamic-update-slice_fusion), channel_id=1, source_target_pairs={{0,2},{1,5},{2,0},{3,7},{4,6},{5,1},{6,4},{7,3},{8,10},{9,13},{10,... | collective-permute-start | bytes 1572872 | tf_op jit(solution)/shard_map/ppermute | solution.py:295
  4.2 9.4 %collective-permute-start = (bf16[128,2048]{1,0:T(8,128)(2,1)S(1)}, bf16[128,2048]{1,0:T(8,128)(2,1)S(1)}, u32[]{:S(2)}, u32[]{:S(2)}) collective-permute-start(bf16[128,2048]{1,0:T(8,128)(2,1)S(1)} %constant_dynamic-update-slice_fusion), channel_id=1, source_target_pairs={{0,1},{1,0},{2,3},{3,2},{4,5},{5,4},{6,7},{7,6},{8,9},{9,8},{10,11... | collective-permute-start | bytes 1572872 | tf_op jit(solution)/shard_map/ppermute | solution.py:294
  12.0 14.9 %collective-permute-start.3 = (bf16[2,128,2048]{2,1,0:T(8,128)(2,1)S(1)}, bf16[2,128,2048]{2,1,0:T(8,128)(2,1)S(1)}, u32[]{:S(2)}, u32[]{:S(2)}) collective-permute-start(bf16[2,128,2048]{2,1,0:T(8,128)(2,1)S(1)} %pad_maximum_fusion), channel_id=1, source_target_pairs={{0,4},{1,3},{2,6},{3,1},{4,0},{5,7},{6,2},{7,5},{8,12},{9,11},{10,... | collective-permute-start | bytes 3145736 | tf_op jit(solution)/shard_map/ppermute | solution.py:297
  13.6 1.9 %collective-permute-start.2 = (bf16[128,2048]{1,0:T(8,128)(2,1)S(1)}, bf16[128,2048]{1,0:T(8,128)(2,1)S(1)}, u32[]{:S(2)}, u32[]{:S(2)}) collective-permute-start(bf16[128,2048]{1,0:T(8,128)(2,1)S(1)} %collective-permute-done.1), channel_id=1, source_target_pairs={{0,1},{1,0},{2,3},{3,2},{4,5},{5,4},{6,7},{7,6},{8,9},{9,8},{10,11... | collective-permute-start | bytes 1572872 | tf_op jit(solution)/shard_map/ppermute | solution.py:296
  26.9 6.2 %collective-permute-start.4 = (bf16[2,128,2048]{2,1,0:T(8,128)(2,1)S(1)}, bf16[2,128,2048]{2,1,0:T(8,128)(2,1)S(1)}, u32[]{:S(2)}, u32[]{:S(2)}) collective-permute-start(bf16[2,128,2048]{2,1,0:T(8,128)(2,1)S(1)} %collective-permute-done.3), channel_id=1, source_target_pairs={{0,1},{1,0},{2,3},{3,2},{4,5},{5,4},{6,7},{7,6},{8,9},{9,8},{10,11... | collective-permute-start | bytes 3145736 | tf_op jit(solution)/shard_map/ppermute | solution.py:300
  34.0 4.5 %copy-start = (bf16[512,1024]{1,0:T(8,128)(2,1)}, bf16[512,1024]{1,0:T(8,128)(2,1)S(1)}, u32[]{:S(2)}) copy-start(bf16[512,1024]{1,0:T(8,128)(2,1)S(1)} %slice.72.val_ref) | copy-start | bytes 3145732
  35.9 11.8 %copy-start.1 = (bf16[512,1024]{1,0:T(8,128)(2,1)}, bf16[512,1024]{1,0:T(8,128)(2,1)S(1)}, u32[]{:S(2)}) copy-start(bf16[512,1024]{1,0:T(8,128)(2,1)S(1)} %get-tuple-element.89.feat_ref) | copy-start | bytes 3145732
  40.8 6.7 %collective-permute-start.5 = (bf16[65,1024]{1,0:T(8,128)(2,1)S(1)}, bf16[65,1024]{1,0:T(8,128)(2,1)S(1)}, u32[]{:S(2)}, u32[]{:S(2)}) collective-permute-start(bf16[65,1024]{1,0:T(8,128)(2,1)S(1)} %get-tuple-element.98), channel_id=1, source_target_pairs={{0,1},{1,0},{2,3},{3,2},{4,5},{5,4},{6,7},{7,6},{8,9},{9,8},{10,11... | collective-permute-start | bytes 399368 | tf_op jit(solution)/shard_map/ppermute | solution.py:58
  44.5 7.9 %collective-permute-start.8 = (bf16[65,1024]{1,0:T(8,128)(2,1)S(1)}, bf16[65,1024]{1,0:T(8,128)(2,1)S(1)}, u32[]{:S(2)}, u32[]{:S(2)}) collective-permute-start(bf16[65,1024]{1,0:T(8,128)(2,1)S(1)} %get-tuple-element.97), channel_id=1, source_target_pairs={{1,4},{3,6},{5,8},{7,10},{9,12},{11,14},{13,16},{15,18},{17,20},{1... | collective-permute-start | bytes 399368 | tf_op jit(solution)/shard_map/ppermute | solution.py:58
  47.6 6.4 %collective-permute-start.6 = (bf16[65,1024]{1,0:T(8,128)(2,1)S(1)}, bf16[65,1024]{1,0:T(8,128)(2,1)S(1)}, u32[]{:S(2)}, u32[]{:S(2)}) collective-permute-start(bf16[65,1024]{1,0:T(8,128)(2,1)S(1)} %get-tuple-element.95), channel_id=1, source_target_pairs={{0,2},{1,3},{2,0},{3,1},{4,6},{5,7},{6,4},{7,5},{8,10},{9,11},{10,... | collective-permute-start | bytes 399368 | tf_op jit(solution)/shard_map/ppermute | solution.py:58
  49.2 9.7 %collective-permute-start.7 = (bf16[65,1024]{1,0:T(8,128)(2,1)S(1)}, bf16[65,1024]{1,0:T(8,128)(2,1)S(1)}, u32[]{:S(2)}, u32[]{:S(2)}) collective-permute-start(bf16[65,1024]{1,0:T(8,128)(2,1)S(1)} %get-tuple-element.96), channel_id=1, source_target_pairs={{2,4},{3,5},{4,2},{5,3},{6,8},{7,9},{8,6},{9,7},{10,12},{11,13},{1... | collective-permute-start | bytes 399368 | tf_op jit(solution)/shard_map/ppermute | solution.py:58
  66.5 2.1 %collective-permute-start.9 = (bf16[65,1024]{1,0:T(8,128)(2,1)}, bf16[65,1024]{1,0:T(8,128)(2,1)S(1)}, u32[]{:S(2)}, u32[]{:S(2)}) collective-permute-start(bf16[65,1024]{1,0:T(8,128)(2,1)} %get-tuple-element.10), channel_id=1, source_target_pairs={{0,1},{1,0},{2,3},{3,2},{4,5},{5,4},{6,7},{7,6},{8,9},{9,8},{10,11... | collective-permute-start | bytes 399368 | tf_op jit(solution)/shard_map/ppermute | solution.py:58
  66.6 10.3 %collective-permute-start.12 = (bf16[65,1024]{1,0:T(8,128)(2,1)S(1)}, bf16[65,1024]{1,0:T(8,128)(2,1)S(1)}, u32[]{:S(2)}, u32[]{:S(2)}) collective-permute-start(bf16[65,1024]{1,0:T(8,128)(2,1)S(1)} %select_convert_fusion.1), channel_id=1, source_target_pairs={{1,4},{3,6},{5,8},{7,10},{9,12},{11,14},{13,16},{15,18},{17,20},{1... | collective-permute-start | bytes 399368 | tf_op jit(solution)/shard_map/ppermute | solution.py:58
  69.7 9.9 %collective-permute-start.11 = (bf16[65,1024]{1,0:T(8,128)(2,1)S(1)}, bf16[65,1024]{1,0:T(8,128)(2,1)S(1)}, u32[]{:S(2)}, u32[]{:S(2)}) collective-permute-start(bf16[65,1024]{1,0:T(8,128)(2,1)S(1)} %get-tuple-element.93), channel_id=1, source_target_pairs={{2,4},{3,5},{4,2},{5,3},{6,8},{7,9},{8,6},{9,7},{10,12},{11,13},{1... | collective-permute-start | bytes 399368 | tf_op jit(solution)/shard_map/ppermute | solution.py:58
  73.3 9.5 %collective-permute-start.10 = (bf16[65,1024]{1,0:T(8,128)(2,1)S(1)}, bf16[65,1024]{1,0:T(8,128)(2,1)S(1)}, u32[]{:S(2)}, u32[]{:S(2)}) collective-permute-start(bf16[65,1024]{1,0:T(8,128)(2,1)S(1)} %get-tuple-element.94), channel_id=1, source_target_pairs={{0,2},{1,3},{2,0},{3,1},{4,6},{5,7},{6,4},{7,5},{8,10},{9,11},{10,... | collective-permute-start | bytes 399368 | tf_op jit(solution)/shard_map/ppermute | solution.py:58
  76.9 6.0 %copy-start.2 = (bf16[65,1024]{1,0:T(8,128)(2,1)}, bf16[65,1024]{1,0:T(8,128)(2,1)S(1)}, u32[]{:S(2)}) copy-start(bf16[65,1024]{1,0:T(8,128)(2,1)S(1)} %collective-permute-done.12.refs_5_) | copy-start | bytes 399364
  79.6 3.2 %copy-start.3 = (bf16[65,1024]{1,0:T(8,128)(2,1)}, bf16[65,1024]{1,0:T(8,128)(2,1)S(1)}, u32[]{:S(2)}) copy-start(bf16[65,1024]{1,0:T(8,128)(2,1)S(1)} %collective-permute-done.11.refs_4_) | copy-start | bytes 399364
  82.9 0.6 copy-start.4

commit v20 on v18

--- a/solution.py
+++ b/solution.py
@@ -265,7 +265,7 @@
     )(key_feat, val_round, keys, state_grad, full_both)
 
 
-def gather_rows(shard):
+def gather_rows(shard, halves):
     count = lax.axis_size("blk")
     if count != 8:
         return lax.all_gather(shard, "blk", axis=0, tiled=True), None
@@ -276,7 +276,9 @@
     second = 6 - first
     swap = [(s, s ^ 1) for s in range(count)]
     twin_own = lax.ppermute(shard, "blk", swap)
-    early = lax.ppermute(shard, "blk", [(s, s ^ (4 if s % 2 else 2)) for s in range(count)])
+    early = jnp.concatenate(
+        lax.ppermute(halves, "blk", [(s, s ^ (4 if s % 2 else 2)) for s in range(count)]), axis=1
+    )
     twin_early = lax.ppermute(early, "blk", swap)
     late = lax.ppermute(
         jnp.stack([shard, early]), "blk", [(s, s ^ (2 if s % 2 else 4)) for s in range(count)]
@@ -297,7 +299,7 @@
 def shards(receptor, poses, pairs, block_complex, w_key, w_value, w_query, score_weight):
     rows = receptor.shape[0]
     width = receptor.shape[1]
-    full_both, rest = gather_rows(jnp.concatenate([w_key, w_value], axis=1))
+    full_both, rest = gather_rows(jnp.concatenate([w_key, w_value], axis=1), (w_key, w_value))
     if rest is None:
         both = jnp.dot(receptor, full_both, preferred_element_type=jnp.float32)
     else:

time: 90.8 us -> 89.8 us (0.989)
  waiting for transfers between devices: 24.2 us -> 21.9 us
  starting transfers between devices: 18.2 us -> 19.3 us
    ppermute x1 -> x2, waiting for transfers between devices: 2.29 us -> 0.01 us  [gather_rows(): lax.ppermute(halves, 'blk', [(s, s ^ (4 if s % 2 else 2)) for s in range(...]
    ppermute x1 -> x2, starting transfers between devices: 1.56 us -> 2.09 us  [gather_rows(): lax.ppermute(halves, 'blk', [(s, s ^ (4 if s % 2 else 2)) for s in range(...]
  transfers between devices with their start and end apart: 13 -> 14, of which waited for: 6 -> 4; matrix products, arithmetic and copies ran while one was open for 17% -> 20% of each run, Pallas kernels for 0% -> 0%
where the time goes in v20:
time: 89.8 us; the launch traced here: 89 us
  waiting for transfers between devices  21.9 us (24%)
  starting transfers between devices  19.3 us (21%)
  local copies, waits for them, and re-layouts  14.9 us (17%)
  Pallas kernels  14.4 us (16%)
  matrix products  7.23 us (8%)
  other arithmetic  5.72 us (6%)
  between operations  5.46 us (6%)
    ppermute x8, starting transfers between devices, send(): return lax.ppermute(value, axis, pairs)  15 us
    ppermute x8, waiting for transfers between devices, send(): return lax.ppermute(value, axis, pairs)  11.1 us
    ppermute x1, waiting for transfers between devices, gather_rows(): lax.ppermute(jnp.stack([shard, early]), 'blk', [(s, s ^ (2 if s % 2 else...  10.8 us
    pallas_call x1, Pallas kernels, back_fused(): pl.pallas_call(back_kernel, out_shape=jax.ShapeDtypeStruct((rows, width),...  7.63 us
    pallas_call x1, Pallas kernels, pose_fused(): pl.pallas_call(pose_kernel, out_shape=(jax.ShapeDtypeStruct((1, pair_rows...  6.76 us
    dynamic_update_slice x6, local copies, waits for them, and re-layouts, gather_rows(): full = lax.dynamic_update_slice(full, pieces[k][None], (at, 0, 0))  4.98 us
    dot_general x1, matrix products, shards(): jnp.dot(receptor, full_both.reshape(-1, full_both.shape[2]), preferred_el...  4.52 us
    broadcast_in_dim x1, local copies, waits for them, and re-layouts, gather_rows(): full = jnp.zeros((count,) + shard.shape, shard.dtype)  2.46 us
  transfers between devices with their start and end apart: 14, of which 4 were waited for; matrix products, arithmetic and copies ran while one was open for 20% of the time, Pallas kernels for 0%

profile of v20, /device:TPU:16, one launch (start us, length us, event | category | flops | bytes accessed | tf_op | source)
XLA Modules:
  0.0 89.0 jit_solution(2702166653729574520)
XLA Ops:
  0.7 1.6 %collective-permute-start.1 = (bf16[128,1024]{1,0:T(8,128)(2,1)}, bf16[128,1024]{1,0:T(8,128)(2,1)S(1)}, u32[]{:S(2)}, u32[]{:S(2)}) collective-permute-start(bf16[128,1024]{1,0:T(8,128)(2,1)} %param.12), channel_id=1, source_target_pairs={{0,2},{1,5},{2,0},{3,7},{4,6},{5,1},{6,4},{7,3},{8,10},{9,13},{10,... | collective-permute-start | bytes 786440 | tf_op jit(solution)/shard_map/ppermute | solution.py:280
  2.2 0.5 collective-permute-start.2
  2.7 1.0 %constant_dynamic-update-slice_fusion.1 = bf16[128,2048]{1,0:T(8,128)(2,1)S(1)} fusion(bf16[128,1024]{1,0:T(8,128)(2,1)} %param.12), kind=kLoop, calls=%fused_computation.38 | loop fusion | bytes 524288
  3.7 1.0 %constant_dynamic-update-slice_fusion = bf16[128,2048]{1,0:T(8,128)(2,1)S(1)} fusion(bf16[128,2048]{1,0:T(8,128)(2,1)S(1)} %constant_dynamic-update-slice_fusion.1, bf16[128,1024]{1,0:T(8,128)(2,1)} %param.13), kind=kLoop, calls=%fused_computation.37 | loop fusion | bytes 524288 | tf_op jit(solution)/shard_map/concatenate | solution.py:302
  4.7 0.1 collective-permute-start
  4.8 2.5 %broadcast_in_dim.72 = bf16[8,128,2048]{2,1,0:T(8,128)(2,1)} broadcast(bf16[]{:T(256)} %constant.216.clone.1), dimensions={} | broadcast | bytes 4194306 | tf_op jit(solution)/shard_map/broadcast_in_dim | solution.py:292
  7.2 0.8 constant_dynamic-update-slice_fusion.5
  8.1 0.1 constant_dynamic-slice_fusion.1
  8.3 0.7 fusion.14
  10.3 0.0 collective-permute-done.1
  10.4 0.0 collective-permute-done.2
  10.4 0.5 collective-permute-start.3
  10.9 0.1 pad_maximum_fusion
  11.0 1.6 %collective-permute-start.4 = (bf16[2,128,2048]{2,1,0:T(8,128)(2,1)S(1)}, bf16[2,128,2048]{2,1,0:T(8,128)(2,1)S(1)}, u32[]{:S(2)}, u32[]{:S(2)}) collective-permute-start(bf16[2,128,2048]{2,1,0:T(8,128)(2,1)S(1)} %pad_maximum_fusion), channel_id=1, source_target_pairs={{0,4},{1,3},{2,6},{3,1},{4,0},{5,7},{6,2},{7,5},{8,12},{9,11},{10,... | collective-permute-start | bytes 3145736 | tf_op jit(solution)/shard_map/ppermute | solution.py:283
  12.6 0.0 collective-permute-done
  12.6 0.8 bitcast_dynamic-update-slice_fusion.1
  13.5 0.8 constant_dynamic-update-slice_fusion.4
  14.3 0.8 bitcast_dynamic-update-slice_fusion
  15.1 10.8 %collective-permute-done.4 = bf16[2,128,2048]{2,1,0:T(8,128)(2,1)S(1)} collective-permute-done((bf16[2,128,2048]{2,1,0:T(8,128)(2,1)S(1)}, bf16[2,128,2048]{2,1,0:T(8,128)(2,1)S(1)}, u32[]{:S(2)}, u32[]{:S(2)}) %collective-permute-start.4) | collective-permute-done | bytes 1048608 | tf_op jit(solution)/shard_map/ppermute | solution.py:283
  25.9 0.0 collective-permute-start.5
  25.9 0.8 slice_dynamic-update-slice_fusion.3
  26.7 0.8 slice_dynamic-update-slice_fusion.2
  27.6 4.5 %fusion.16 = f32[2048,512]{0,1:T(8,128)S(1)} fusion(bf16[512,1024]{1,0:T(8,128)(2,1)S(1)} %copy-done.2, bf16[1024,2048]{1,0:T(8,128)(2,1)} %bitcast.5), kind=kOutput, calls=%fused_computation.48 | convolution fusion | flops 2147483648 | bytes 9437184 | tf_op jit(solution)/shard_map/dot_general | solution.py:308
  32.1 0.8 bitcast_add_fusion
  32.9 0.2 slice.72.val_ref
  33.0 1.8 %convert_reduce_fusion = (f32[1024]{0:T(1024)S(1)}, bf16[512,1024]{1,0:T(8,128)(2,1)S(1)}, f32[512,1024]{1,0:T(8,128)}) fusion(f32[512,2048]{1,0:T(8,128)S(1)} %bitcast_add_fusion), kind=kLoop, calls=%fused_computation.2 | loop fusion | flops 3668992 | bytes 5246976 | tf_op jit(solution)/shard_map/reduce_sum | solution.py:37
  34.9 1.4 %copy.17 = bf16[512,1024]{0,1:T(8,128)(2,1)} copy(bf16[512,1024]{1,0:T(8,128)(2,1)S(1)} %get-tuple-element.89.feat_ref) | data formatting | bytes 2097152 | tf_op jit(solution)/shard_map/convert_element_type | solution.py:322
  36.3 1.3 %copy.16 = bf16[512,1024]{0,1:T(8,128)(2,1)} copy(bf16[512,1024]{1,0:T(8,128)(2,1)S(1)} %slice.72.val_ref) | data formatting | bytes 2097152 | tf_op jit(solution)/shard_map/slice | solution.py:321
  37.6 1.9 %fusion.15 = f32[16,64,64]{2,1,0:T(8,128)S(1)} fusion(bf16[512,16,64]{0,2,1:T(8,128)(2,1)} %bitcast.42, bf16[512,16,64]{0,2,1:T(8,128)(2,1)} %bitcast.41), kind=kOutput, calls=%fused_computation.47 | convolution fusion | flops 67108864 | bytes 2359296 | tf_op jit(solution)/shard_map/thd,the->dhe/dot_general | solution.py:34
  39.5 0.2 copy.20
  39.8 0.6 collective-permute-start.6
  43.5 3.0 %collective-permute-start.9 = (bf16[65,1024]{1,0:T(8,128)(2,1)S(1)}, bf16[65,1024]{1,0:T(8,128)(2,1)S(1)}, u32[]{:S(2)}, u32[]{:S(2)}) collective-permute-start(bf16[65,1024]{1,0:T(8,128)(2,1)S(1)} %get-tuple-element.97), channel_id=1, source_target_pairs={{1,4},{3,6},{5,8},{7,10},{9,12},{11,14},{13,16},{15,18},{17,20},{1... | collective-permute-start | bytes 399368 | tf_op jit(solution)/shard_map/ppermute | solution.py:58
  46.5 0.1 add_convert_fusion.3
  46.6 1.5 %collective-permute-start.7 = (bf16[65,1024]{1,0:T(8,128)(2,1)S(1)}, bf16[65,1024]{1,0:T(8,128)(2,1)S(1)}, u32[]{:S(2)}, u32[]{:S(2)}) collective-permute-start(bf16[65,1024]{1,0:T(8,128)(2,1)S(1)} %get-tuple-element.95), channel_id=1, source_target_pairs={{0,2},{1,3},{2,0},{3,1},{4,6},{5,7},{6,4},{7,5},{8,10},{9,11},{10,... | collective-permute-start | bytes 399368 | tf_op jit(solution)/shard_map/ppermute | solution.py:58
  48.1 2.4 %collective-permute-start.8 = (bf16[65,1024]{1,0:T(8,128)(2,1)S(1)}, bf16[65,1024]{1,0:T(8,128)(2,1)S(1)}, u32[]{:S(2)}, u32[]{:S(2)}) collective-permute-start(bf16[65,1024]{1,0:T(8,128)(2,1)S(1)} %get-tuple-element.96), channel_id=1, source_target_pairs={{2,4},{3,5},{4,2},{5,3},{6,8},{7,9},{8,6},{9,7},{10,12},{11,13},{1... | collective-permute-start | bytes 399368 | tf_op jit(solution)/shard_map/ppermute | solution.py:58
  50.5 0.9 slice_dynamic-update-slice_fusion.1
  51.4 1.6 %collective-permute-done.7 = bf16[65,1024]{1,0:T(8,128)(2,1)S(1)} collective-permute-done((bf16[65,1024]{1,0:T(8,128)(2,1)S(1)}, bf16[65,1024]{1,0:T(8,128)(2,1)S(1)}, u32[]{:S(2)}, u32[]{:S(2)}) %collective-permute-start.7) | collective-permute-done | bytes 133152 | tf_op jit(solution)/shard_map/ppermute | solution.py:58
  53.0 4.9 %collective-permute-done.8 = bf16[65,1024]{1,0:T(8,128)(2,1)S(1)} collective-permute-done((bf16[65,1024]{1,0:T(8,128)(2,1)S(1)}, bf16[65,1024]{1,0:T(8,128)(2,1)S(1)}, u32[]{:S(2)}, u32[]{:S(2)}) %collective-permute-start.8) | collective-permute-done | bytes 133152 | tf_op jit(solution)/shard_map/ppermute | solution.py:58
  57.9 0.8 fusion.3.state_ref
  58.7 6.8 %shard_map.103 = (f32[1,256]{1,0:T(1,128)}, bf16[128,1024]{1,0:T(8,128)(2,1)}, f32[65,1024]{1,0:T(8,128)}, bf16[65,1024]{1,0:T(8,128)(2,1)}) custom-call(bf16[128,1024]{1,0:T(8,128)(2,1)} %pose_ref.1, s32[2,256]{1,0:T(2,128)} %bitcast.50, f32[65,1024]{1,0:T(8,128)} %fusion.3.state_ref, bf16[1024,1024]{1,0:T(8,128)(2,1)} %query_ref.1, f32[1,1024]{1,0:T(1,128)} %bitcast.49), custom_call_target="tpu_custom_call" | custom-call | tf_op jit(solution)/shard_map/pallas_call | solution.py:222
  65.5 2.1 %collective-permute-start.13 = (bf16[65,1024]{1,0:T(8,128)(2,1)S(1)}, bf16[65,1024]{1,0:T(8,128)(2,1)S(1)}, u32[]{:S(2)}, u32[]{:S(2)}) collective-permute-start(bf16[65,1024]{1,0:T(8,128)(2,1)S(1)} %select_convert_fusion.1), channel_id=1, source_target_pairs={{1,4},{3,6},{5,8},{7,10},{9,12},{11,14},{13,16},{15,18},{17,20},{1... | collective-permute-start | bytes 399368 | tf_op jit(solution)/shard_map/ppermute | solution.py:58
  67.6 1.1 %add_convert_fusion.1 = (bf16[65,1024]{1,0:T(8,128)(2,1)S(1)}, bf16[65,1024]{1,0:T(8,128)(2,1)S(1)}) fusion(f32[65,1024]{1,0:T(8,128)} %get-tuple-element.9, bf16[65,1024]{1,0:T(8,128)(2,1)S(1)} %collective-permute-done.10, pred[]{:T(512)S(6)} %and.121, pred[]{:T(512)S(6)} %eq.47, pred[]{:T(512)S(6)} %and.119, pred[]{:T(512)S(6)} %and.125, pred[]{:T(512)S(6)} %and.124), kind=kLoop, calls=%fused_computation.29 | loop fusion | flops 732160 | bytes 665605 | tf_op jit(solution)/shard_map/convert_element_type | solution.py:90
  68.7 1.5 %collective-permute-start.11 = (bf16[65,1024]{1,0:T(8,128)(2,1)S(1)}, bf16[65,1024]{1,0:T(8,128)(2,1)S(1)}, u32[]{:S(2)}, u32[]{:S(2)}) collective-permute-start(bf16[65,1024]{1,0:T(8,128)(2,1)S(1)} %get-tuple-element.93), channel_id=1, source_target_pairs={{0,2},{1,3},{2,0},{3,1},{4,6},{5,7},{6,4},{7,5},{8,10},{9,11},{10,... | collective-permute-start | bytes 399368 | tf_op jit(solution)/shard_map/ppermute | solution.py:58
  70.1 4.0 %collective-permute-start.12 = (bf16[65,1024]{1,0:T(8,128)(2,1)S(1)}, bf16[65,1024]{1,0:T(8,128)(2,1)S(1)}, u32[]{:S(2)}, u32[]{:S(2)}) collective-permute-start(bf16[65,1024]{1,0:T(8,128)(2,1)S(1)} %get-tuple-element.94), channel_id=1, source_target_pairs={{2,4},{3,5},{4,2},{5,3},{6,8},{7,9},{8,6},{9,7},{10,12},{11,13},{1... | collective-permute-start | bytes 399368 | tf_op jit(solution)/shard_map/ppermute | solution.py:58
  74.1 0.8 slice_dynamic-update-slice_fusion
  75.0 4.6 %collective-permute-done.12 = bf16[65,1024]{1,0:T(8,128)(2,1)S(1)} collective-permute-done((bf16[65,1024]{1,0:T(8,128)(2,1)S(1)}, bf16[65,1024]{1,0:T(8,128)(2,1)S(1)}, u32[]{:S(2)}, u32[]{:S(2)}) %collective-permute-start.12) | collective-permute-done | bytes 133152 | tf_op jit(solution)/shard_map/ppermute | solution.py:58
  79.6 1.7 %fusion.8.grad_ref = bf16[65,1024]{1,0:T(8,128)(2,1)} fusion(f32[65,1024]{1,0:T(8,128)} %get-tuple-element.9, bf16[65,1024]{1,0:T(8,128)(2,1)S(1)} %collective-permute-done.10, bf16[65,1024]{1,0:T(8,128)(2,1)S(1)} %collective-permute-done.13, bf16[65,1024]{1,0:T(8,128)(2,1)S(1)} %collective-permute-done.12, bf16[65,1024]{1,0:T(8,128)(2,1)S(1)} %collective-permute-done.11, ...), kind=kLoop, calls=%fused_computation.25 | loop fusion | flops 665600 | bytes 931841 | tf_op jit(solution)/shard_map/convert_element_type | solution.py:326
  81.4 7.6 %shard_map.104 = bf16[512,1024]{1,0:T(8,128)(2,1)} custom-call(bf16[512,1024]{1,0:T(8,128)(2,1)} %copy-done.1, bf16[512,1024]{1,0:T(8,128)(2,1)} %copy-done, f32[512,1024]{1,0:T(8,128)} %get-tuple-element.90.keys_ref, bf16[65,1024]{1,0:T(8,128)(2,1)} %fusion.8.grad_ref, bf16[1024,2048]{1,0:T(8,128)(2,1)} %bitcast.28.full_ref), custom_call_target="tpu_custom_call" | custom-call | tf_op jit(solution)/shard_map/pallas_call | solution.py:260
  (20 shorter events, 0.1 us)
Async XLA Ops:
  0.6 7.4 %copy-start.2 = (bf16[512,1024]{1,0:T(8,128)(2,1)S(1)}, bf16[512,1024]{1,0:T(8,128)(2,1)}, u32[]{:S(2)}) copy-start(bf16[512,1024]{1,0:T(8,128)(2,1)} %param.8) | copy-start | bytes 3145732
  0.6 7.6 %copy-start.3 = (s32[32]{0:T(128)S(1)}, s32[32]{0:T(128)}, u32[]{:S(2)}) copy-start(s32[32]{0:T(128)} %param.11) | copy-start | bytes 388
  0.7 9.7 %collective-permute-start.1 = (bf16[128,1024]{1,0:T(8,128)(2,1)}, bf16[128,1024]{1,0:T(8,128)(2,1)S(1)}, u32[]{:S(2)}, u32[]{:S(2)}) collective-permute-start(bf16[128,1024]{1,0:T(8,128)(2,1)} %param.12), channel_id=1, source_target_pairs={{0,2},{1,5},{2,0},{3,7},{4,6},{5,1},{6,4},{7,3},{8,10},{9,13},{10,... | collective-permute-start | bytes 786440 | tf_op jit(solution)/shard_map/ppermute | solution.py:280
  2.2 8.1 %collective-permute-start.2 = (bf16[128,1024]{1,0:T(8,128)(2,1)}, bf16[128,1024]{1,0:T(8,128)(2,1)S(1)}, u32[]{:S(2)}, u32[]{:S(2)}) collective-permute-start(bf16[128,1024]{1,0:T(8,128)(2,1)} %param.13), channel_id=1, source_target_pairs={{0,2},{1,5},{2,0},{3,7},{4,6},{5,1},{6,4},{7,3},{8,10},{9,13},{10,... | collective-permute-start | bytes 786440 | tf_op jit(solution)/shard_map/ppermute | solution.py:280
  4.7 7.9 %collective-permute-start = (bf16[128,2048]{1,0:T(8,128)(2,1)S(1)}, bf16[128,2048]{1,0:T(8,128)(2,1)S(1)}, u32[]{:S(2)}, u32[]{:S(2)}) collective-permute-start(bf16[128,2048]{1,0:T(8,128)(2,1)S(1)} %constant_dynamic-update-slice_fusion), channel_id=1, source_target_pairs={{0,1},{1,0},{2,3},{3,2},{4,5},{5,4},{6,7},{7,6},{8,9},{9,8},{10,11... | collective-permute-start | bytes 1572872 | tf_op jit(solution)/shard_map/ppermute | solution.py:278
  10.4 3.9 %collective-permute-start.3 = (bf16[128,2048]{1,0:T(8,128)(2,1)S(1)}, bf16[128,2048]{1,0:T(8,128)(2,1)S(1)}, u32[]{:S(2)}, u32[]{:S(2)}) collective-permute-start(bf16[128,2048]{1,0:T(8,128)(2,1)S(1)} %constant_dynamic-update-slice_fusion.2), channel_id=1, source_target_pairs={{0,1},{1,0},{2,3},{3,2},{4,5},{5,4},{6,7},{7,6},{8,9},{9,8},{10,11... | collective-permute-start | bytes 1572872 | tf_op jit(solution)/shard_map/ppermute | solution.py:282
  11.0 14.9 %collective-permute-start.4 = (bf16[2,128,2048]{2,1,0:T(8,128)(2,1)S(1)}, bf16[2,128,2048]{2,1,0:T(8,128)(2,1)S(1)}, u32[]{:S(2)}, u32[]{:S(2)}) collective-permute-start(bf16[2,128,2048]{2,1,0:T(8,128)(2,1)S(1)} %pad_maximum_fusion), channel_id=1, source_target_pairs={{0,4},{1,3},{2,6},{3,1},{4,0},{5,7},{6,2},{7,5},{8,12},{9,11},{10,... | collective-permute-start | bytes 3145736 | tf_op jit(solution)/shard_map/ppermute | solution.py:283
  25.9 6.2 %collective-permute-start.5 = (bf16[2,128,2048]{2,1,0:T(8,128)(2,1)S(1)}, bf16[2,128,2048]{2,1,0:T(8,128)(2,1)S(1)}, u32[]{:S(2)}, u32[]{:S(2)}) collective-permute-start(bf16[2,128,2048]{2,1,0:T(8,128)(2,1)S(1)} %collective-permute-done.4), channel_id=1, source_target_pairs={{0,1},{1,0},{2,3},{3,2},{4,5},{5,4},{6,7},{7,6},{8,9},{9,8},{10,11... | collective-permute-start | bytes 3145736 | tf_op jit(solution)/shard_map/ppermute | solution.py:286
  33.0 4.6 %copy-start = (bf16[512,1024]{1,0:T(8,128)(2,1)}, bf16[512,1024]{1,0:T(8,128)(2,1)S(1)}, u32[]{:S(2)}) copy-start(bf16[512,1024]{1,0:T(8,128)(2,1)S(1)} %slice.72.val_ref) | copy-start | bytes 3145732
  34.9 11.7 %copy-start.1 = (bf16[512,1024]{1,0:T(8,128)(2,1)}, bf16[512,1024]{1,0:T(8,128)(2,1)S(1)}, u32[]{:S(2)}) copy-start(bf16[512,1024]{1,0:T(8,128)(2,1)S(1)} %get-tuple-element.89.feat_ref) | copy-start | bytes 3145732
  39.8 6.7 %collective-permute-start.6 = (bf16[65,1024]{1,0:T(8,128)(2,1)S(1)}, bf16[65,1024]{1,0:T(8,128)(2,1)S(1)}, u32[]{:S(2)}, u32[]{:S(2)}) collective-permute-start(bf16[65,1024]{1,0:T(8,128)(2,1)S(1)} %get-tuple-element.98), channel_id=1, source_target_pairs={{0,1},{1,0},{2,3},{3,2},{4,5},{5,4},{6,7},{7,6},{8,9},{9,8},{10,11... | collective-permute-start | bytes 399368 | tf_op jit(solution)/shard_map/ppermute | solution.py:58
  43.5 7.9 %collective-permute-start.9 = (bf16[65,1024]{1,0:T(8,128)(2,1)S(1)}, bf16[65,1024]{1,0:T(8,128)(2,1)S(1)}, u32[]{:S(2)}, u32[]{:S(2)}) collective-permute-start(bf16[65,1024]{1,0:T(8,128)(2,1)S(1)} %get-tuple-element.97), channel_id=1, source_target_pairs={{1,4},{3,6},{5,8},{7,10},{9,12},{11,14},{13,16},{15,18},{17,20},{1... | collective-permute-start | bytes 399368 | tf_op jit(solution)/shard_map/ppermute | solution.py:58
  46.6 6.4 %collective-permute-start.7 = (bf16[65,1024]{1,0:T(8,128)(2,1)S(1)}, bf16[65,1024]{1,0:T(8,128)(2,1)S(1)}, u32[]{:S(2)}, u32[]{:S(2)}) collective-permute-start(bf16[65,1024]{1,0:T(8,128)(2,1)S(1)} %get-tuple-element.95), channel_id=1, source_target_pairs={{0,2},{1,3},{2,0},{3,1},{4,6},{5,7},{6,4},{7,5},{8,10},{9,11},{10,... | collective-permute-start | bytes 399368 | tf_op jit(solution)/shard_map/ppermute | solution.py:58
  48.1 9.7 %collective-permute-start.8 = (bf16[65,1024]{1,0:T(8,128)(2,1)S(1)}, bf16[65,1024]{1,0:T(8,128)(2,1)S(1)}, u32[]{:S(2)}, u32[]{:S(2)}) collective-permute-start(bf16[65,1024]{1,0:T(8,128)(2,1)S(1)} %get-tuple-element.96), channel_id=1, source_target_pairs={{2,4},{3,5},{4,2},{5,3},{6,8},{7,9},{8,6},{9,7},{10,12},{11,13},{1... | collective-permute-start | bytes 399368 | tf_op jit(solution)/shard_map/ppermute | solution.py:58
  65.5 2.1 %collective-permute-start.10 = (bf16[65,1024]{1,0:T(8,128)(2,1)}, bf16[65,1024]{1,0:T(8,128)(2,1)S(1)}, u32[]{:S(2)}, u32[]{:S(2)}) collective-permute-start(bf16[65,1024]{1,0:T(8,128)(2,1)} %get-tuple-element.10), channel_id=1, source_target_pairs={{0,1},{1,0},{2,3},{3,2},{4,5},{5,4},{6,7},{7,6},{8,9},{9,8},{10,11... | collective-permute-start | bytes 399368 | tf_op jit(solution)/shard_map/ppermute | solution.py:58
  65.5 9.5 %collective-permute-start.13 = (bf16[65,1024]{1,0:T(8,128)(2,1)S(1)}, bf16[65,1024]{1,0:T(8,128)(2,1)S(1)}, u32[]{:S(2)}, u32[]{:S(2)}) collective-permute-start(bf16[65,1024]{1,0:T(8,128)(2,1)S(1)} %select_convert_fusion.1), channel_id=1, source_target_pairs={{1,4},{3,6},{5,8},{7,10},{9,12},{11,14},{13,16},{15,18},{17,20},{1... | collective-permute-start | bytes 399368 | tf_op jit(solution)/shard_map/ppermute | solution.py:58
  68.7 6.3 %collective-permute-start.11 = (bf16[65,1024]{1,0:T(8,128)(2,1)S(1)}, bf16[65,1024]{1,0:T(8,128)(2,1)S(1)}, u32[]{:S(2)}, u32[]{:S(2)}) collective-permute-start(bf16[65,1024]{1,0:T(8,128)(2,1)S(1)} %get-tuple-element.93), channel_id=1, source_target_pairs={{0,2},{1,3},{2,0},{3,1},{4,6},{5,7},{6,4},{7,5},{8,10},{9,11},{10,... | collective-permute-start | bytes 399368 | tf_op jit(solution)/shard_map/ppermute | solution.py:58
  70.1 9.5 %collective-permute-start.12 = (bf16[65,1024]{1,0:T(8,128)(2,1)S(1)}, bf16[65,1024]{1,0:T(8,128)(2,1)S(1)}, u32[]{:S(2)}, u32[]{:S(2)}) collective-permute-start(bf16[65,1024]{1,0:T(8,128)(2,1)S(1)} %get-tuple-element.94), channel_id=1, source_target_pairs={{2,4},{3,5},{4,2},{5,3},{6,8},{7,9},{8,6},{9,7},{10,12},{11,13},{1... | collective-permute-start | bytes 399368 | tf_op jit(solution)/shard_map/ppermute | solution.py:58
